TPU v7x, 256 devices: a whole 4x4x8 slice. The times are simulated.
256 devices in a mesh: rad: 16 (over z, core), azi: 16 (over x, y).
Axes of the slice: x: 4, y: 4, z: 8, core: 2. Of those that a mesh axis runs over, the one named last changes fastest.
Arguments:
- jacobian: bfloat16 [64, 128, 5, 128, 128], P('rad', 'azi')
- new_block: bfloat16 [64, 128, 32, 128], P('rad', 'azi')
- kept: float32 [64, 128, 192, 128], P('rad', 'azi')
- columns: int32 [64, 128, 5], P('rad', 'azi'), may hold values from 0 to 8, as said below
Outputs:
- basis: float32 [64, 128, 32, 128], P('rad', 'azi')
- coefficients: float32 [192, 32], replicated
- factor: float32 [32, 32], replicated
Inputs may be any that keep to these rules, and one draw needn't show every extreme that they name: `columns`: slot 0 of every element is 4, the element itself; slots 1 to 4 name four different codes other than 4.
All inputs are finite; a program needn't handle non-finite values.
Results may differ from a plain program's by a relative error of at most 0.0003.
Values may be sent and summed in bfloat16 or wider, within the bound.
No kernel may reach another device: no remote copies, remote signals or barrier semaphores. Data moves between devices by JAX's collectives and lax.ppermute only.
A program may use at most 64 MiB of HBM per device.

v0:
```python
import jax
import jax.numpy as jnp
from jax import lax
from jax.sharding import PartitionSpec as P

BLK = 128
NEW = 32
KEEP = 192


def with_halo(cells, sides, width, closed):
    for axis, dim in sides:
        count = lax.axis_size(axis)
        ends = count if closed else count - 1
        head = lax.slice_in_dim(cells, 0, width, axis=dim)
        tail = lax.slice_in_dim(cells, cells.shape[dim] - width, cells.shape[dim], axis=dim)
        cells = jnp.concatenate(
            [
                lax.ppermute(tail, axis, [(i, (i + 1) % count) for i in range(ends)]),
                cells,
                lax.ppermute(head, axis, [((i + 1) % count, i) for i in range(ends)]),
            ],
            axis=dim,
        )
    return cells


def on_device(jacobian, new_block, kept, columns):
    high = lax.Precision.HIGHEST
    rows_r = new_block.shape[0]
    rows_a = new_block.shape[1]
    widened = with_halo(new_block, (("azi", 1),), 1, True)
    padded = with_halo(widened, (("rad", 0),), 1, False)
    nine = jnp.stack(
        [padded[i : i + rows_r, j : j + rows_a] for i in range(3) for j in range(3)], axis=2
    )
    picked = jnp.take_along_axis(nine, columns[:, :, :, None, None], axis=2)
    image = jnp.einsum("rakij,rakvj->ravi", jacobian, picked, preferred_element_type=jnp.float32)
    elements = rows_r * rows_a
    image = image.reshape(elements, NEW, BLK)
    kept_flat = kept.reshape(elements, KEEP, BLK)
    total_rows = elements * BLK * lax.axis_size("rad") * lax.axis_size("azi")

    def inner(left, right):
        return jnp.einsum(
            "epi,evi->pv", left, right, precision=high, preferred_element_type=jnp.float32
        )

    def expand(coeffs):
        return jnp.einsum(
            "epi,pv->evi", kept_flat, coeffs, precision=high, preferred_element_type=jnp.float32
        )

    def project(field):
        return lax.psum(inner(kept_flat, field), ("rad", "azi"))

    first = project(image)
    once = image - expand(first)
    second = project(once)
    twice = once - expand(second)
    coefficients = first + second
    gram = lax.psum(inner(twice, twice), ("rad", "azi")) / total_rows
    lower = jnp.linalg.cholesky(gram)
    flat = jnp.moveaxis(twice, 1, 0).reshape(NEW, elements * BLK)
    solved = lax.linalg.triangular_solve(lower, flat, left_side=True, lower=True)
    basis = jnp.moveaxis(solved.reshape(NEW, elements, BLK), 0, 1).reshape(rows_r, rows_a, NEW, BLK)
    return (basis, coefficients, lower.T)


def solution(mesh):
    return jax.shard_map(
        on_device,
        mesh=mesh,
        in_specs=(
            P("rad", "azi", None, None, None),
            P("rad", "azi", None, None),
            P("rad", "azi", None, None),
            P("rad", "azi", None),
        ),
        out_specs=(P("rad", "azi", None, None), P(), P()),
        check_vma=False,
    )
```

profile of v0, /device:TPU:1, one launch (start us, length us, event | category | flops | bytes accessed | tf_op | source)
XLA Modules:
  0.0 292.3 jit_solution(15747589936277506462)
XLA Ops:
  0.6 0.9 fusion.37
  1.6 2.1 collective-permute-start
  3.7 3.7 %collective-permute-start.1 = (bf16[4,1,32,128]{3,2,1,0:T(8,128)(2,1)S(1)}, bf16[4,1,32,128]{3,2,1,0:T(8,128)(2,1)S(1)}, u32[]{:S(2)}, u32[]{:S(2)}) collective-permute-start(bf16[4,1,32,128]{3,2,1,0:T(8,128)(2,1)S(1)} %get-tuple-element.11), channel_id=1, source_target_pairs={{1,0},{2,1},{3,2},{4,3},{5,4},{6,5},{7,6},{8,7},{9,8},{10,9},{11,1... | collective-permute-start | bytes 98312 | tf_op jit(solution)/shard_map/ppermute | solution.py:21
  8.6 1.0 constant_dynamic-update-slice_fusion.1
  10.3 5.1 %collective-permute-start.2 = (bf16[1,10,32,128]{3,2,1,0:T(8,128)(2,1)}, bf16[1,10,32,128]{3,2,1,0:T(8,128)(2,1)}, u32[]{:S(2)}, u32[]{:S(2)}) collective-permute-start(bf16[1,10,32,128]{3,2,1,0:T(8,128)(2,1)} %get-tuple-element.10), channel_id=1, source_target_pairs={{0,16},{16,32},{32,48},{48,64},{64,80},{80,96},{96,112},{112,128},... | collective-permute-start | bytes 245768 | tf_op jit(solution)/shard_map/ppermute | solution.py:19
  15.4 1.3 compare_and_fusion
  17.4 0.8 reshape.54
  19.0 2.3 collective-permute-start.3
  21.3 1.6 fusion.21
  22.9 1.6 fusion.18
  24.4 1.6 fusion.29
  26.0 1.7 fusion.27
  31.3 5.1 %gather_fusion = bf16[160,32,128]{2,1,0:T(8,128)(2,1)} fusion(bf16[4,8,9,32,128]{4,3,1,0,2:T(8,128)(2,1)} %fusion.23, s32[160]{0:T(256)S(1)} %reshape.54), kind=kCustom, calls=%fused_computation | custom fusion | bytes 2623360 | tf_op jit(solution)/shard_map/jit(take_along_axis)/gather | solution.py:37
  36.4 4.8 %fusion = f32[4,8,32,128,1]{3,2,4,1,0:T(8,128)S(1)} fusion(bf16[4,8,5,128,128]{4,3,2,1,0:T(8,128)(2,1)} %param.4, bf16[4,8,5,32,128]{4,3,2,1,0:T(8,128)(2,1)} %bitcast.119, pred[4,8,5]{2,1,0:T(8,128)(4,1)S(1)} %copy.12), kind=kOutput, calls=%fused_computation.1 | convolution fusion | flops 168427520 | bytes 7078048 | tf_op jit(solution)/shard_map/rakij,rakvj->ravi/dot_general | solution.py:38
  42.0 2.9 %convolution_bitcast_fusion.3 = f32[192,32]{0,1:T(8,128)S(1)} fusion(f32[4,8,192,128]{3,2,1,0:T(8,128)S(1)} %copy-done, f32[4,8,32,128,1]{3,2,4,1,0:T(8,128)S(1)} %fusion), kind=kOutput, calls=%fused_computation.9 | convolution fusion | flops 301989888 | bytes 3694592 | tf_op jit(solution)/shard_map/epi,evi->pv/dot_general | solution.py:45
  45.0 78.9 %psum.21 = f32[192,32]{0,1:T(8,128)S(1)} all-reduce(f32[192,32]{0,1:T(8,128)S(1)} %convolution_bitcast_fusion.3), channel_id=1, replica_groups=mesh['rad'=16,'azi'=16] {'rad','azi'}, use_global_device_ids=true, to_apply=%region_0.0 | all-reduce | flops 6144 | bytes 49152 | tf_op jit(solution)/shard_map/psum | solution.py:55
  123.8 3.0 %fusion.4 = f32[32,32,128]{2,1,0:T(8,128)S(1)} fusion(f32[32,32,128]{2,1,0:T(8,128)} %bitcast.120, f32[32,192,128]{2,1,0:T(8,128)S(1)} %bitcast.116, f32[192,32]{0,1:T(8,128)S(1)} %psum.21), kind=kOutput, calls=%fused_computation.7 | convolution fusion | flops 302120960 | bytes 4218880 | tf_op jit(solution)/shard_map/epi,pv->evi/dot_general | solution.py:50
  127.7 2.9 %convolution_bitcast_fusion.2 = f32[192,32]{0,1:T(8,128)S(1)} fusion(f32[32,32,128]{2,1,0:T(8,128)S(1)} %fusion.4, f32[32,192,128]{2,1,0:T(8,128)S(1)} %bitcast.117), kind=kOutput, calls=%fused_computation.8 | convolution fusion | flops 301989888 | bytes 3694592 | tf_op jit(solution)/shard_map/epi,evi->pv/dot_general | solution.py:45
  130.6 73.1 %psum.22 = f32[192,32]{0,1:T(8,128)S(1)} all-reduce(f32[192,32]{0,1:T(8,128)S(1)} %convolution_bitcast_fusion.2), channel_id=1, replica_groups=mesh['rad'=16,'azi'=16] {'rad','azi'}, use_global_device_ids=true, to_apply=%region_1.2 | all-reduce | flops 6144 | bytes 49152 | tf_op jit(solution)/shard_map/psum | solution.py:55
  204.4 3.0 %fusion.3 = f32[32,32,128]{2,1,0:T(8,128)S(1)} fusion(f32[32,32,128]{2,1,0:T(8,128)} %copy-done.4, f32[32,192,128]{2,1,0:T(8,128)S(1)} %bitcast.118, f32[192,32]{0,1:T(8,128)S(1)} %psum.22), kind=kOutput, calls=%fused_computation.5 | convolution fusion | flops 302120960 | bytes 4218880 | tf_op jit(solution)/shard_map/epi,pv->evi/dot_general | solution.py:50
  208.8 73.6 %psum.23 = f32[32,32]{0,1:T(8,128)S(1)} all-reduce(f32[32,32]{0,1:T(8,128)S(1)} %convolution_bitcast_fusion.4), channel_id=1, replica_groups=mesh['rad'=16,'azi'=16] {'rad','azi'}, use_global_device_ids=true, to_apply=%region_2.3 | all-reduce | flops 1024 | bytes 8192 | tf_op jit(solution)/shard_map/psum | solution.py:62
  282.5 2.9 cholesky.16
  286.7 2.4 custom-call.6
  289.1 2.5 fusion.6
  (34 shorter events, 12.7 us)
Async XLA Ops:
  0.6 41.4 %copy-start = (f32[4,8,192,128]{3,2,1,0:T(8,128)S(1)}, f32[4,8,192,128]{3,2,1,0:T(8,128)}, u32[]{:S(2)}) copy-start(f32[4,8,192,128]{3,2,1,0:T(8,128)} %param.6) | copy-start | bytes 9437188
  1.6 7.1 %collective-permute-start = (bf16[4,1,32,128]{3,2,1,0:T(8,128)(2,1)S(1)}, bf16[4,1,32,128]{3,2,1,0:T(8,128)(2,1)S(1)}, u32[]{:S(2)}, u32[]{:S(2)}) collective-permute-start(bf16[4,1,32,128]{3,2,1,0:T(8,128)(2,1)S(1)} %get-tuple-element.12), channel_id=1, source_target_pairs={{0,1},{1,2},{2,3},{3,4},{4,5},{5,6},{6,7},{7,8},{8,9},{9,10},{10,1... | collective-permute-start | bytes 98312 | tf_op jit(solution)/shard_map/ppermute | solution.py:19
  3.7 5.9 %collective-permute-start.1 = (bf16[4,1,32,128]{3,2,1,0:T(8,128)(2,1)S(1)}, bf16[4,1,32,128]{3,2,1,0:T(8,128)(2,1)S(1)}, u32[]{:S(2)}, u32[]{:S(2)}) collective-permute-start(bf16[4,1,32,128]{3,2,1,0:T(8,128)(2,1)S(1)} %get-tuple-element.11), channel_id=1, source_target_pairs={{1,0},{2,1},{3,2},{4,3},{5,4},{6,5},{7,6},{8,7},{9,8},{10,9},{11,1... | collective-permute-start | bytes 98312 | tf_op jit(solution)/shard_map/ppermute | solution.py:21
  10.3 11.0 %collective-permute-start.2 = (bf16[1,10,32,128]{3,2,1,0:T(8,128)(2,1)}, bf16[1,10,32,128]{3,2,1,0:T(8,128)(2,1)}, u32[]{:S(2)}, u32[]{:S(2)}) collective-permute-start(bf16[1,10,32,128]{3,2,1,0:T(8,128)(2,1)} %get-tuple-element.10), channel_id=1, source_target_pairs={{0,16},{16,32},{32,48},{48,64},{64,80},{80,96},{96,112},{112,128},... | collective-permute-start | bytes 245768 | tf_op jit(solution)/shard_map/ppermute | solution.py:19
  19.0 8.6 %copy-start.2 = (bf16[4,8,32,128]{3,2,1,0:T(8,128)(2,1)S(1)}, bf16[4,8,32,128]{3,2,1,0:T(8,128)(2,1)}, u32[]{:S(2)}) copy-start(bf16[4,8,32,128]{3,2,1,0:T(8,128)(2,1)} %param.5) | copy-start | bytes 786436
  19.0 10.1 %collective-permute-start.3 = (bf16[1,10,32,128]{3,2,1,0:T(8,128)(2,1)}, bf16[1,10,32,128]{3,2,1,0:T(8,128)(2,1)S(1)}, u32[]{:S(2)}, u32[]{:S(2)}) collective-permute-start(bf16[1,10,32,128]{3,2,1,0:T(8,128)(2,1)} %get-tuple-element.9), channel_id=1, source_target_pairs={{16,0},{32,16},{48,32},{64,48},{80,64},{96,80},{112,96},{128,112},... | collective-permute-start | bytes 245768 | tf_op jit(solution)/shard_map/ppermute | solution.py:21
  41.2 0.8 copy-start.3
  126.9 0.8 copy-start.4
  207.4 0.8 copy-start.1
where the time goes:
time: 293 us; the launch traced here: 292 us
  blocking collectives  226 us (77%)
  matrix products  19.8 us (7%)
  other arithmetic  18.6 us (6%)
  local copies, waits for them, and re-layouts  13.9 us (5%)
  starting transfers between devices  13.2 us (5%)
    psum x2, blocking collectives, project(): return lax.psum(inner(kept_flat, field), ('rad', 'azi'))  152 us
    psum x1, blocking collectives, on_device(): gram = lax.psum(inner(twice, twice), ('rad', 'azi')) / total_rows  73.6 us
    unnamed x7, other arithmetic  8.54 us
    ppermute x2, starting transfers between devices, with_halo(): lax.ppermute(tail, axis, [(i, (i + 1) % count) for i in range(ends)])  7.22 us
    gather x3, local copies, waits for them, and re-layouts, on_device(): picked = jnp.take_along_axis(nine, columns[:, :, :, None, None], axis=2)  6.58 us
    dot_general x3, matrix products, inner(): jnp.einsum('epi,evi->pv', left, right, precision=high, preferred_element_...  6.43 us
    dot_general x2, matrix products, expand(): jnp.einsum('epi,pv->evi', kept_flat, coeffs, precision=high, preferred_el...  6.09 us
    ppermute x2, starting transfers between devices, with_halo(): lax.ppermute(head, axis, [((i + 1) % count, i) for i in range(ends)])  5.97 us
  transfers between devices with their start and end apart: 4, of which 1 were waited for; matrix products, arithmetic and copies ran while one was open for 4% of the time, Pallas kernels for 0%

commit v1 on v0

v1 whole, which is shorter than its diff:
```python
import jax
import jax.numpy as jnp
from jax import lax
from jax.sharding import PartitionSpec as P

BLK = 128
NEW = 32
KEEP = 192


def all_sum(x):
    for axis in ("rad", "azi"):
        count = lax.axis_size(axis)
        step = 1
        while step < count:
            x = x + lax.ppermute(x, axis, [(i, i ^ step) for i in range(count)])
            step *= 2
    return x


def with_halo(cells):
    n_r = lax.axis_size("rad")
    n_a = lax.axis_size("azi")
    rows_r, rows_a = cells.shape[0], cells.shape[1]

    def shift_azi(x, d):
        return lax.ppermute(x, "azi", [(i, (i + d) % n_a) for i in range(n_a)])

    def shift_rad(x, d):
        pairs = [(i, i + d) for i in range(n_r) if 0 <= i + d < n_r]
        return lax.ppermute(x, "rad", pairs)

    def shift_both(x, dr, da):
        pairs = []
        for r in range(n_r):
            if 0 <= r + dr < n_r:
                for a in range(n_a):
                    pairs.append((r * n_a + a, (r + dr) * n_a + (a + da) % n_a))
        return lax.ppermute(x, ("rad", "azi"), pairs)

    first_a, last_a = cells[:, :1], cells[:, rows_a - 1 :]
    first_r, last_r = cells[:1], cells[rows_r - 1 :]
    west = shift_azi(last_a, 1)
    east = shift_azi(first_a, -1)
    north = shift_rad(last_r, 1)
    south = shift_rad(first_r, -1)
    nw = shift_both(cells[rows_r - 1 :, rows_a - 1 :], 1, 1)
    ne = shift_both(cells[rows_r - 1 :, :1], 1, -1)
    sw = shift_both(cells[:1, rows_a - 1 :], -1, 1)
    se = shift_both(cells[:1, :1], -1, -1)
    top = jnp.concatenate([nw, north, ne], axis=1)
    middle = jnp.concatenate([west, cells, east], axis=1)
    bottom = jnp.concatenate([sw, south, se], axis=1)
    return jnp.concatenate([top, middle, bottom], axis=0)


def on_device(jacobian, new_block, kept, columns):
    high = lax.Precision.HIGHEST
    rows_r = new_block.shape[0]
    rows_a = new_block.shape[1]
    elements = rows_r * rows_a
    total_rows = elements * BLK * lax.axis_size("rad") * lax.axis_size("azi")
    kept_flat = kept.reshape(elements, KEEP, BLK)

    kept_gram = all_sum(
        jnp.einsum("epi,eqi->pq", kept_flat, kept_flat, precision=high,
                   preferred_element_type=jnp.float32)
    )

    padded = with_halo(new_block)
    shifted = [padded[c // 3 : c // 3 + rows_r, c % 3 : c % 3 + rows_a] for c in range(9)]
    slots = []
    for k in range(5):
        code = columns[:, :, k][:, :, None, None]
        pick = shifted[0]
        for c in range(1, 9):
            pick = jnp.where(code == c, shifted[c], pick)
        slots.append(pick)
    picked = jnp.stack(slots, axis=2)
    image = jnp.einsum("rakij,rakvj->ravi", jacobian, picked, preferred_element_type=jnp.float32)
    image = image.reshape(elements, NEW, BLK)

    first = all_sum(
        jnp.einsum("epi,evi->pv", kept_flat, image, precision=high,
                   preferred_element_type=jnp.float32)
    )
    second = first - jnp.dot(kept_gram, first, precision=high, preferred_element_type=jnp.float32)
    coefficients = first + second
    twice = image - jnp.einsum(
        "epi,pv->evi", kept_flat, coefficients, precision=high, preferred_element_type=jnp.float32
    )
    gram = all_sum(
        jnp.einsum("evi,ewi->vw", twice, twice, precision=high, preferred_element_type=jnp.float32)
    ) / total_rows
    lower = jnp.linalg.cholesky(gram)
    flat = jnp.moveaxis(twice, 1, 0).reshape(NEW, elements * BLK)
    solved = lax.linalg.triangular_solve(lower, flat, left_side=True, lower=True)
    basis = jnp.moveaxis(solved.reshape(NEW, elements, BLK), 0, 1).reshape(rows_r, rows_a, NEW, BLK)
    return (basis, coefficients, lower.T)


def solution(mesh):
    return jax.shard_map(
        on_device,
        mesh=mesh,
        in_specs=(
            P("rad", "azi", None, None, None),
            P("rad", "azi", None, None),
            P("rad", "azi", None, None),
            P("rad", "azi", None),
        ),
        out_specs=(P("rad", "azi", None, None), P(), P()),
        check_vma=False,
    )
```

time: 293 us -> 180 us (0.61)
  the two profiles are of different devices: /device:TPU:1 before, /device:TPU:2 now
where the time goes in v1:
time: 180 us; the launch traced here: 179 us
  waiting for transfers between devices  102 us (57%)
  starting transfers between devices  45.7 us (25%)
  other arithmetic  13.1 us (7%)
  matrix products  12.8 us (7%)
  local copies, waits for them, and re-layouts  4.18 us (2%)
    ppermute x24, waiting for transfers between devices, all_sum(): x = x + lax.ppermute(x, axis, [(i, i ^ step) for i in range(count)])  102 us
    ppermute x24, starting transfers between devices, all_sum(): x = x + lax.ppermute(x, axis, [(i, i ^ step) for i in range(count)])  21 us
    ppermute x4, starting transfers between devices, shift_both(): return lax.ppermute(x, ('rad', 'azi'), pairs)  16.2 us
    ppermute x2, starting transfers between devices, shift_rad(): return lax.ppermute(x, 'rad', pairs)  4.33 us
    ppermute x2, starting transfers between devices, shift_azi(): return lax.ppermute(x, 'azi', [(i, (i + d) % n_a) for i in range(n_a)])  4.14 us
  transfers between devices with their start and end apart: 32, of which 22 were waited for; matrix products, arithmetic and copies ran while one was open for 9% of the time, Pallas kernels for 0%

profile of v1, /device:TPU:2, one launch (start us, length us, event | category | flops | bytes accessed | tf_op | source)
XLA Modules:
  0.0 179.1 jit_solution(15581246858906977544)
XLA Ops:
  9.1 4.3 %collective-permute-start.5 = (bf16[1,1,32,128]{3,2,1,0:T(8,128)(2,1)S(1)}, bf16[1,1,32,128]{3,2,1,0:T(8,128)(2,1)S(1)}, u32[]{:S(2)}, u32[]{:S(2)}) collective-permute-start(bf16[1,1,32,128]{3,2,1,0:T(8,128)(2,1)S(1)} %get-tuple-element.13), channel_id=1, source_target_pairs={{0,17},{1,18},{2,19},{3,20},{4,21},{5,22},{6,23},{7,24},{8,25},{9,... | collective-permute-start | bytes 24584 | tf_op jit(solution)/shard_map/ppermute | solution.py:39
  19.1 9.4 %collective-permute-start.7 = (bf16[1,1,32,128]{3,2,1,0:T(8,128)(2,1)S(1)}, bf16[1,1,32,128]{3,2,1,0:T(8,128)(2,1)S(1)}, u32[]{:S(2)}, u32[]{:S(2)}) collective-permute-start(bf16[1,1,32,128]{3,2,1,0:T(8,128)(2,1)S(1)} %get-tuple-element.12), channel_id=1, source_target_pairs={{0,31},{1,16},{2,17},{3,18},{4,19},{5,20},{6,21},{7,22},{8,23},{9,... | collective-permute-start | bytes 24584 | tf_op jit(solution)/shard_map/ppermute | solution.py:39
  35.7 3.2 %collective-permute-start.17 = (f32[192,192]{1,0:T(8,128)S(1)}, f32[192,192]{1,0:T(8,128)S(1)}, u32[]{:S(2)}, u32[]{:S(2)}) collective-permute-start(f32[192,192]{1,0:T(8,128)S(1)} %add.94), channel_id=1, source_target_pairs={{0,32},{16,48},{32,0},{48,16},{64,96},{80,112},{96,64},{112,80},{1... | collective-permute-start | bytes 442376 | tf_op jit(solution)/shard_map/ppermute | solution.py:16
  39.7 3.9 %collective-permute-done.17 = f32[192,192]{1,0:T(8,128)S(1)} collective-permute-done((f32[192,192]{1,0:T(8,128)S(1)}, f32[192,192]{1,0:T(8,128)S(1)}, u32[]{:S(2)}, u32[]{:S(2)}) %collective-permute-start.17) | collective-permute-done | bytes 147488 | tf_op jit(solution)/shard_map/ppermute | solution.py:16
  43.6 4.8 %collective-permute-start.18 = (f32[192,192]{1,0:T(8,128)S(1)}, f32[192,192]{1,0:T(8,128)S(1)}, u32[]{:S(2)}, u32[]{:S(2)}) collective-permute-start(f32[192,192]{1,0:T(8,128)S(1)} %add.95), channel_id=1, source_target_pairs={{0,64},{16,80},{32,96},{48,112},{64,0},{80,16},{96,32},{112,48},{1... | collective-permute-start | bytes 442376 | tf_op jit(solution)/shard_map/ppermute | solution.py:16
  49.2 7.8 %collective-permute-done.18 = f32[192,192]{1,0:T(8,128)S(1)} collective-permute-done((f32[192,192]{1,0:T(8,128)S(1)}, f32[192,192]{1,0:T(8,128)S(1)}, u32[]{:S(2)}, u32[]{:S(2)}) %collective-permute-start.18) | collective-permute-done | bytes 147488 | tf_op jit(solution)/shard_map/ppermute | solution.py:16
  60.4 10.4 %collective-permute-done.19 = f32[192,192]{1,0:T(8,128)S(1)} collective-permute-done((f32[192,192]{1,0:T(8,128)S(1)}, f32[192,192]{1,0:T(8,128)S(1)}, u32[]{:S(2)}, u32[]{:S(2)}) %collective-permute-start.19) | collective-permute-done | bytes 147488 | tf_op jit(solution)/shard_map/ppermute | solution.py:16
  71.8 4.8 %collective-permute-done.20 = f32[192,192]{1,0:T(8,128)S(1)} collective-permute-done((f32[192,192]{1,0:T(8,128)S(1)}, f32[192,192]{1,0:T(8,128)S(1)}, u32[]{:S(2)}, u32[]{:S(2)}) %collective-permute-start.20) | collective-permute-done | bytes 147488 | tf_op jit(solution)/shard_map/ppermute | solution.py:16
  79.6 4.2 %collective-permute-done.21 = f32[192,192]{1,0:T(8,128)S(1)} collective-permute-done((f32[192,192]{1,0:T(8,128)S(1)}, f32[192,192]{1,0:T(8,128)S(1)}, u32[]{:S(2)}, u32[]{:S(2)}) %collective-permute-start.21) | collective-permute-done | bytes 147488 | tf_op jit(solution)/shard_map/ppermute | solution.py:16
  83.9 6.8 %collective-permute-start.22 = (f32[192,192]{1,0:T(8,128)S(1)}, f32[192,192]{1,0:T(8,128)S(1)}, u32[]{:S(2)}, u32[]{:S(2)}) collective-permute-start(f32[192,192]{1,0:T(8,128)S(1)} %add.99), channel_id=1, source_target_pairs={{0,4},{1,5},{2,6},{3,7},{4,0},{5,1},{6,2},{7,3},{8,12},{9,13},{10,... | collective-permute-start | bytes 442376 | tf_op jit(solution)/shard_map/ppermute | solution.py:16
  95.0 3.9 %collective-permute-done.9 = f32[192,32]{0,1:T(8,128)S(1)} collective-permute-done((f32[192,32]{0,1:T(8,128)S(1)}, f32[192,32]{0,1:T(8,128)S(1)}, u32[]{:S(2)}, u32[]{:S(2)}) %collective-permute-start.9) | collective-permute-done | bytes 24608 | tf_op jit(solution)/shard_map/ppermute | solution.py:16
  99.0 4.7 %collective-permute-done.10 = f32[192,32]{0,1:T(8,128)S(1)} collective-permute-done((f32[192,32]{0,1:T(8,128)S(1)}, f32[192,32]{0,1:T(8,128)S(1)}, u32[]{:S(2)}, u32[]{:S(2)}) %collective-permute-start.10) | collective-permute-done | bytes 24608 | tf_op jit(solution)/shard_map/ppermute | solution.py:16
  103.7 7.8 %collective-permute-done.11 = f32[192,32]{0,1:T(8,128)S(1)} collective-permute-done((f32[192,32]{0,1:T(8,128)S(1)}, f32[192,32]{0,1:T(8,128)S(1)}, u32[]{:S(2)}, u32[]{:S(2)}) %collective-permute-start.11) | collective-permute-done | bytes 24608 | tf_op jit(solution)/shard_map/ppermute | solution.py:16
  111.5 3.9 %collective-permute-done.12 = f32[192,32]{0,1:T(8,128)S(1)} collective-permute-done((f32[192,32]{0,1:T(8,128)S(1)}, f32[192,32]{0,1:T(8,128)S(1)}, u32[]{:S(2)}, u32[]{:S(2)}) %collective-permute-start.12) | collective-permute-done | bytes 24608 | tf_op jit(solution)/shard_map/ppermute | solution.py:16
  115.4 5.4 %collective-permute-done.13 = f32[192,32]{0,1:T(8,128)S(1)} collective-permute-done((f32[192,32]{0,1:T(8,128)S(1)}, f32[192,32]{0,1:T(8,128)S(1)}, u32[]{:S(2)}, u32[]{:S(2)}) %collective-permute-start.13) | collective-permute-done | bytes 24608 | tf_op jit(solution)/shard_map/ppermute | solution.py:16
  120.9 3.9 %collective-permute-done.14 = f32[192,32]{0,1:T(8,128)S(1)} collective-permute-done((f32[192,32]{0,1:T(8,128)S(1)}, f32[192,32]{0,1:T(8,128)S(1)}, u32[]{:S(2)}, u32[]{:S(2)}) %collective-permute-start.14) | collective-permute-done | bytes 24608 | tf_op jit(solution)/shard_map/ppermute | solution.py:16
  124.8 5.4 %collective-permute-done.15 = f32[192,32]{0,1:T(8,128)S(1)} collective-permute-done((f32[192,32]{0,1:T(8,128)S(1)}, f32[192,32]{0,1:T(8,128)S(1)}, u32[]{:S(2)}, u32[]{:S(2)}) %collective-permute-start.15) | collective-permute-done | bytes 24608 | tf_op jit(solution)/shard_map/ppermute | solution.py:16
  135.2 3.7 %collective-permute-done.25 = f32[32,32]{0,1:T(8,128)S(1)} collective-permute-done((f32[32,32]{0,1:T(8,128)S(1)}, f32[32,32]{0,1:T(8,128)S(1)}, u32[]{:S(2)}, u32[]{:S(2)}) %collective-permute-start.25) | collective-permute-done | bytes 4128 | tf_op jit(solution)/shard_map/ppermute | solution.py:16
  138.9 4.6 %collective-permute-done.26 = f32[32,32]{0,1:T(8,128)S(1)} collective-permute-done((f32[32,32]{0,1:T(8,128)S(1)}, f32[32,32]{0,1:T(8,128)S(1)}, u32[]{:S(2)}, u32[]{:S(2)}) %collective-permute-start.26) | collective-permute-done | bytes 4128 | tf_op jit(solution)/shard_map/ppermute | solution.py:16
  143.9 7.3 %collective-permute-done.27 = f32[32,32]{0,1:T(8,128)S(1)} collective-permute-done((f32[32,32]{0,1:T(8,128)S(1)}, f32[32,32]{0,1:T(8,128)S(1)}, u32[]{:S(2)}, u32[]{:S(2)}) %collective-permute-start.27) | collective-permute-done | bytes 4128 | tf_op jit(solution)/shard_map/ppermute | solution.py:16
  151.3 3.6 %collective-permute-done.28 = f32[32,32]{0,1:T(8,128)S(1)} collective-permute-done((f32[32,32]{0,1:T(8,128)S(1)}, f32[32,32]{0,1:T(8,128)S(1)}, u32[]{:S(2)}, u32[]{:S(2)}) %collective-permute-start.28) | collective-permute-done | bytes 4128 | tf_op jit(solution)/shard_map/ppermute | solution.py:16
  154.9 5.2 %collective-permute-done.29 = f32[32,32]{0,1:T(8,128)S(1)} collective-permute-done((f32[32,32]{0,1:T(8,128)S(1)}, f32[32,32]{0,1:T(8,128)S(1)}, u32[]{:S(2)}, u32[]{:S(2)}) %collective-permute-start.29) | collective-permute-done | bytes 4128 | tf_op jit(solution)/shard_map/ppermute | solution.py:16
  160.2 3.7 %collective-permute-done.30 = f32[32,32]{0,1:T(8,128)S(1)} collective-permute-done((f32[32,32]{0,1:T(8,128)S(1)}, f32[32,32]{0,1:T(8,128)S(1)}, u32[]{:S(2)}, u32[]{:S(2)}) %collective-permute-start.30) | collective-permute-done | bytes 4128 | tf_op jit(solution)/shard_map/ppermute | solution.py:16
  163.9 5.2 %collective-permute-done.31 = f32[32,32]{0,1:T(8,128)S(1)} collective-permute-done((f32[32,32]{0,1:T(8,128)S(1)}, f32[32,32]{0,1:T(8,128)S(1)}, u32[]{:S(2)}, u32[]{:S(2)}) %collective-permute-start.31) | collective-permute-done | bytes 4128 | tf_op jit(solution)/shard_map/ppermute | solution.py:16
  (105 shorter events, 50.2 us)
Async XLA Ops:
  1.6 17.6 %collective-permute-start = (bf16[4,1,32,128]{3,2,1,0:T(8,128)(2,1)S(1)}, bf16[4,1,32,128]{3,2,1,0:T(8,128)(2,1)S(1)}, u32[]{:S(2)}, u32[]{:S(2)}) collective-permute-start(bf16[4,1,32,128]{3,2,1,0:T(8,128)(2,1)S(1)} %get-tuple-element.18), channel_id=1, source_target_pairs={{0,1},{1,2},{2,3},{3,4},{4,5},{5,6},{6,7},{7,8},{8,9},{9,10},{10,1... | collective-permute-start | bytes 98312 | tf_op jit(solution)/shard_map/ppermute | solution.py:27
  3.2 26.7 %collective-permute-start.1 = (bf16[4,1,32,128]{3,2,1,0:T(8,128)(2,1)S(1)}, bf16[4,1,32,128]{3,2,1,0:T(8,128)(2,1)S(1)}, u32[]{:S(2)}, u32[]{:S(2)}) collective-permute-start(bf16[4,1,32,128]{3,2,1,0:T(8,128)(2,1)S(1)} %get-tuple-element.17), channel_id=1, source_target_pairs={{0,15},{1,0},{2,1},{3,2},{4,3},{5,4},{6,5},{7,6},{8,7},{9,8},{10,9... | collective-permute-start | bytes 98312 | tf_op jit(solution)/shard_map/ppermute | solution.py:27
  6.5 22.1 %collective-permute-start.2 = (bf16[1,1,32,128]{3,2,1,0:T(8,128)(2,1)S(1)}, bf16[1,1,32,128]{3,2,1,0:T(8,128)(2,1)S(1)}, u32[]{:S(2)}, u32[]{:S(2)}) collective-permute-start(bf16[1,1,32,128]{3,2,1,0:T(8,128)(2,1)S(1)} %get-tuple-element.11), channel_id=1, source_target_pairs={{16,1},{17,2},{18,3},{19,4},{20,5},{21,6},{22,7},{23,8},{24,9},{25... | collective-permute-start | bytes 24584 | tf_op jit(solution)/shard_map/ppermute | solution.py:39
  7.8 25.2 %collective-permute-start.4 = (bf16[1,1,32,128]{3,2,1,0:T(8,128)(2,1)S(1)}, bf16[1,1,32,128]{3,2,1,0:T(8,128)(2,1)S(1)}, u32[]{:S(2)}, u32[]{:S(2)}) collective-permute-start(bf16[1,1,32,128]{3,2,1,0:T(8,128)(2,1)S(1)} %get-tuple-element.14), channel_id=1, source_target_pairs={{16,15},{17,0},{18,1},{19,2},{20,3},{21,4},{22,5},{23,6},{24,7},{2... | collective-permute-start | bytes 24584 | tf_op jit(solution)/shard_map/ppermute | solution.py:39
  9.1 25.6 %collective-permute-start.5 = (bf16[1,1,32,128]{3,2,1,0:T(8,128)(2,1)S(1)}, bf16[1,1,32,128]{3,2,1,0:T(8,128)(2,1)S(1)}, u32[]{:S(2)}, u32[]{:S(2)}) collective-permute-start(bf16[1,1,32,128]{3,2,1,0:T(8,128)(2,1)S(1)} %get-tuple-element.13), channel_id=1, source_target_pairs={{0,17},{1,18},{2,19},{3,20},{4,21},{5,22},{6,23},{7,24},{8,25},{9,... | collective-permute-start | bytes 24584 | tf_op jit(solution)/shard_map/ppermute | solution.py:39
  19.1 15.5 %collective-permute-start.7 = (bf16[1,1,32,128]{3,2,1,0:T(8,128)(2,1)S(1)}, bf16[1,1,32,128]{3,2,1,0:T(8,128)(2,1)S(1)}, u32[]{:S(2)}, u32[]{:S(2)}) collective-permute-start(bf16[1,1,32,128]{3,2,1,0:T(8,128)(2,1)S(1)} %get-tuple-element.12), channel_id=1, source_target_pairs={{0,31},{1,16},{2,17},{3,18},{4,19},{5,20},{6,21},{7,22},{8,23},{9,... | collective-permute-start | bytes 24584 | tf_op jit(solution)/shard_map/ppermute | solution.py:39
  28.6 6.0 %collective-permute-start.3 = (bf16[1,8,32,128]{3,2,1,0:T(8,128)(2,1)S(1)}, bf16[1,8,32,128]{3,2,1,0:T(8,128)(2,1)S(1)}, u32[]{:S(2)}, u32[]{:S(2)}) collective-permute-start(bf16[1,8,32,128]{3,2,1,0:T(8,128)(2,1)S(1)} %get-tuple-element.15), channel_id=1, source_target_pairs={{16,0},{32,16},{48,32},{64,48},{80,64},{96,80},{112,96},{128,112},... | collective-permute-start | bytes 196616 | tf_op jit(solution)/shard_map/ppermute | solution.py:31
  29.9 4.7 %collective-permute-start.6 = (bf16[1,8,32,128]{3,2,1,0:T(8,128)(2,1)S(1)}, bf16[1,8,32,128]{3,2,1,0:T(8,128)(2,1)S(1)}, u32[]{:S(2)}, u32[]{:S(2)}) collective-permute-start(bf16[1,8,32,128]{3,2,1,0:T(8,128)(2,1)S(1)} %get-tuple-element.16), channel_id=1, source_target_pairs={{0,16},{16,32},{32,48},{48,64},{64,80},{80,96},{96,112},{112,128},... | collective-permute-start | bytes 196616 | tf_op jit(solution)/shard_map/ppermute | solution.py:31
  35.7 7.9 %collective-permute-start.17 = (f32[192,192]{1,0:T(8,128)S(1)}, f32[192,192]{1,0:T(8,128)S(1)}, u32[]{:S(2)}, u32[]{:S(2)}) collective-permute-start(f32[192,192]{1,0:T(8,128)S(1)} %add.94), channel_id=1, source_target_pairs={{0,32},{16,48},{32,0},{48,16},{64,96},{80,112},{96,64},{112,80},{1... | collective-permute-start | bytes 442376 | tf_op jit(solution)/shard_map/ppermute | solution.py:16
  43.6 13.3 %collective-permute-start.18 = (f32[192,192]{1,0:T(8,128)S(1)}, f32[192,192]{1,0:T(8,128)S(1)}, u32[]{:S(2)}, u32[]{:S(2)}) collective-permute-start(f32[192,192]{1,0:T(8,128)S(1)} %add.95), channel_id=1, source_target_pairs={{0,64},{16,80},{32,96},{48,112},{64,0},{80,16},{96,32},{112,48},{1... | collective-permute-start | bytes 442376 | tf_op jit(solution)/shard_map/ppermute | solution.py:16
  57.0 13.8 %collective-permute-start.19 = (f32[192,192]{1,0:T(8,128)S(1)}, f32[192,192]{1,0:T(8,128)S(1)}, u32[]{:S(2)}, u32[]{:S(2)}) collective-permute-start(f32[192,192]{1,0:T(8,128)S(1)} %add.96), channel_id=1, source_target_pairs={{0,128},{16,144},{32,160},{48,176},{64,192},{80,208},{96,224},{112... | collective-permute-start | bytes 442376 | tf_op jit(solution)/shard_map/ppermute | solution.py:16
  70.8 5.8 %collective-permute-start.20 = (f32[192,192]{1,0:T(8,128)S(1)}, f32[192,192]{1,0:T(8,128)S(1)}, u32[]{:S(2)}, u32[]{:S(2)}) collective-permute-start(f32[192,192]{1,0:T(8,128)S(1)} %add.97), channel_id=1, source_target_pairs={{0,1},{1,0},{2,3},{3,2},{4,5},{5,4},{6,7},{7,6},{8,9},{9,8},{10,11... | collective-permute-start | bytes 442376 | tf_op jit(solution)/shard_map/ppermute | solution.py:16
  76.6 7.3 %collective-permute-start.21 = (f32[192,192]{1,0:T(8,128)S(1)}, f32[192,192]{1,0:T(8,128)S(1)}, u32[]{:S(2)}, u32[]{:S(2)}) collective-permute-start(f32[192,192]{1,0:T(8,128)S(1)} %add.98), channel_id=1, source_target_pairs={{0,2},{1,3},{2,0},{3,1},{4,6},{5,7},{6,4},{7,5},{8,10},{9,11},{10,... | collective-permute-start | bytes 442376 | tf_op jit(solution)/shard_map/ppermute | solution.py:16
  83.9 15.0 %collective-permute-start.22 = (f32[192,192]{1,0:T(8,128)S(1)}, f32[192,192]{1,0:T(8,128)S(1)}, u32[]{:S(2)}, u32[]{:S(2)}) collective-permute-start(f32[192,192]{1,0:T(8,128)S(1)} %add.99), channel_id=1, source_target_pairs={{0,4},{1,5},{2,6},{3,7},{4,0},{5,1},{6,2},{7,3},{8,12},{9,13},{10,... | collective-permute-start | bytes 442376 | tf_op jit(solution)/shard_map/ppermute | solution.py:16
  94.9 3.9 %collective-permute-start.9 = (f32[192,32]{0,1:T(8,128)S(1)}, f32[192,32]{0,1:T(8,128)S(1)}, u32[]{:S(2)}, u32[]{:S(2)}) collective-permute-start(f32[192,32]{0,1:T(8,128)S(1)} %add.86), channel_id=1, source_target_pairs={{0,32},{16,48},{32,0},{48,16},{64,96},{80,112},{96,64},{112,80},{1... | collective-permute-start | bytes 73736 | tf_op jit(solution)/shard_map/ppermute | solution.py:16
  98.9 4.8 %collective-permute-start.10 = (f32[192,32]{0,1:T(8,128)S(1)}, f32[192,32]{0,1:T(8,128)S(1)}, u32[]{:S(2)}, u32[]{:S(2)}) collective-permute-start(f32[192,32]{0,1:T(8,128)S(1)} %add.87), channel_id=1, source_target_pairs={{0,64},{16,80},{32,96},{48,112},{64,0},{80,16},{96,32},{112,48},{1... | collective-permute-start | bytes 73736 | tf_op jit(solution)/shard_map/ppermute | solution.py:16
  98.9 31.3 %collective-permute-start.23 = (f32[192,192]{1,0:T(8,128)S(1)}, f32[192,192]{1,0:T(8,128)S(1)}, u32[]{:S(2)}, u32[]{:S(2)}) collective-permute-start(f32[192,192]{1,0:T(8,128)S(1)} %add.100), channel_id=1, source_target_pairs={{0,8},{1,9},{2,10},{3,11},{4,12},{5,13},{6,14},{7,15},{8,0},{9,1},... | collective-permute-start | bytes 442376 | tf_op jit(solution)/shard_map/ppermute | solution.py:16
  103.7 7.8 %collective-permute-start.11 = (f32[192,32]{0,1:T(8,128)S(1)}, f32[192,32]{0,1:T(8,128)S(1)}, u32[]{:S(2)}, u32[]{:S(2)}) collective-permute-start(f32[192,32]{0,1:T(8,128)S(1)} %add.88), channel_id=1, source_target_pairs={{0,128},{16,144},{32,160},{48,176},{64,192},{80,208},{96,224},{112... | collective-permute-start | bytes 73736 | tf_op jit(solution)/shard_map/ppermute | solution.py:16
  115.4 5.4 %collective-permute-start.13 = (f32[192,32]{0,1:T(8,128)S(1)}, f32[192,32]{0,1:T(8,128)S(1)}, u32[]{:S(2)}, u32[]{:S(2)}) collective-permute-start(f32[192,32]{0,1:T(8,128)S(1)} %add.90), channel_id=1, source_target_pairs={{0,2},{1,3},{2,0},{3,1},{4,6},{5,7},{6,4},{7,5},{8,10},{9,11},{10,... | collective-permute-start | bytes 73736 | tf_op jit(solution)/shard_map/ppermute | solution.py:16
  124.8 5.4 %collective-permute-start.15 = (f32[192,32]{0,1:T(8,128)S(1)}, f32[192,32]{0,1:T(8,128)S(1)}, u32[]{:S(2)}, u32[]{:S(2)}) collective-permute-start(f32[192,32]{0,1:T(8,128)S(1)} %add.92), channel_id=1, source_target_pairs={{0,8},{1,9},{2,10},{3,11},{4,12},{5,13},{6,14},{7,15},{8,0},{9,1},... | collective-permute-start | bytes 73736 | tf_op jit(solution)/shard_map/ppermute | solution.py:16
  138.9 4.6 %collective-permute-start.26 = (f32[32,32]{0,1:T(8,128)S(1)}, f32[32,32]{0,1:T(8,128)S(1)}, u32[]{:S(2)}, u32[]{:S(2)}) collective-permute-start(f32[32,32]{0,1:T(8,128)S(1)} %add.104), channel_id=1, source_target_pairs={{0,64},{16,80},{32,96},{48,112},{64,0},{80,16},{96,32},{112,48},{1... | collective-permute-start | bytes 12296 | tf_op jit(solution)/shard_map/ppermute | solution.py:16
  143.5 7.6 %collective-permute-start.27 = (f32[32,32]{0,1:T(8,128)S(1)}, f32[32,32]{0,1:T(8,128)S(1)}, u32[]{:S(2)}, u32[]{:S(2)}) collective-permute-start(f32[32,32]{0,1:T(8,128)S(1)} %add.105), channel_id=1, source_target_pairs={{0,128},{16,144},{32,160},{48,176},{64,192},{80,208},{96,224},{112... | collective-permute-start | bytes 12296 | tf_op jit(solution)/shard_map/ppermute | solution.py:16
  154.9 5.2 %collective-permute-start.29 = (f32[32,32]{0,1:T(8,128)S(1)}, f32[32,32]{0,1:T(8,128)S(1)}, u32[]{:S(2)}, u32[]{:S(2)}) collective-permute-start(f32[32,32]{0,1:T(8,128)S(1)} %add.107), channel_id=1, source_target_pairs={{0,2},{1,3},{2,0},{3,1},{4,6},{5,7},{6,4},{7,5},{8,10},{9,11},{10,... | collective-permute-start | bytes 12296 | tf_op jit(solution)/shard_map/ppermute | solution.py:16
  163.9 5.2 %collective-permute-start.31 = (f32[32,32]{0,1:T(8,128)S(1)}, f32[32,32]{0,1:T(8,128)S(1)}, u32[]{:S(2)}, u32[]{:S(2)}) collective-permute-start(f32[32,32]{0,1:T(8,128)S(1)} %add.109), channel_id=1, source_target_pairs={{0,8},{1,9},{2,10},{3,11},{4,12},{5,13},{6,14},{7,15},{8,0},{9,1},... | collective-permute-start | bytes 12296 | tf_op jit(solution)/shard_map/ppermute | solution.py:16
  (14 other events, 127.4 us)

commit v2 on v0

v2 whole, which is shorter than its diff:
```python
import jax
import jax.numpy as jnp
from jax import lax
from jax.sharding import PartitionSpec as P

BLK = 128
NEW = 32
KEEP = 192


def all_sum(x):
    for axis in ("rad", "azi"):
        count = lax.axis_size(axis)
        step = 1
        while step < count:
            x = x + lax.ppermute(x, axis, [(i, i ^ step) for i in range(count)])
            step *= 2
    return x


def with_halo(cells, sides, width, closed):
    for axis, dim in sides:
        count = lax.axis_size(axis)
        ends = count if closed else count - 1
        head = lax.slice_in_dim(cells, 0, width, axis=dim)
        tail = lax.slice_in_dim(cells, cells.shape[dim] - width, cells.shape[dim], axis=dim)
        cells = jnp.concatenate(
            [
                lax.ppermute(tail, axis, [(i, (i + 1) % count) for i in range(ends)]),
                cells,
                lax.ppermute(head, axis, [((i + 1) % count, i) for i in range(ends)]),
            ],
            axis=dim,
        )
    return cells


def mm(spec, a, b):
    return jnp.einsum(spec, a, b, precision=lax.Precision.HIGHEST,
                      preferred_element_type=jnp.float32)


def on_device(jacobian, new_block, kept, columns):
    rows_r = new_block.shape[0]
    rows_a = new_block.shape[1]
    elements = rows_r * rows_a
    total_rows = elements * BLK * lax.axis_size("rad") * lax.axis_size("azi")
    kept_flat = kept.reshape(elements, KEEP, BLK)

    kept_gram = all_sum(mm("epi,eqi->pq", kept_flat, kept_flat))

    widened = with_halo(new_block, (("azi", 1),), 1, True)
    padded = with_halo(widened, (("rad", 0),), 1, False)
    shifted = [padded[c // 3 : c // 3 + rows_r, c % 3 : c % 3 + rows_a] for c in range(9)]
    slots = []
    for k in range(5):
        code = columns[:, :, k][:, :, None, None]
        pick = shifted[0]
        for c in range(1, 9):
            pick = jnp.where(code == c, shifted[c], pick)
        slots.append(pick)
    picked = jnp.stack(slots, axis=2)
    image = jnp.einsum("rakij,rakvj->ravi", jacobian, picked, preferred_element_type=jnp.float32)
    image = image.reshape(elements, NEW, BLK)

    moments = all_sum(
        jnp.concatenate([mm("epi,evi->pv", kept_flat, image), mm("evi,ewi->vw", image, image)], axis=0)
    )
    first, image_gram = moments[:KEEP], moments[KEEP:]
    second = first - mm("pq,qv->pv", kept_gram, first)
    coefficients = first + second
    twice = image - mm("epi,pv->evi", kept_flat, coefficients)

    cross = mm("pv,pw->vw", coefficients, first)
    expanded = (
        image_gram - cross - cross.T
        + mm("pv,pw->vw", coefficients, mm("pq,qw->pw", kept_gram, coefficients))
    ) / total_rows
    kept_share = jnp.diagonal(expanded) * 16.0 >= jnp.diagonal(image_gram) / total_rows
    gram = lax.cond(
        jnp.all(kept_share),
        lambda: expanded,
        lambda: all_sum(mm("evi,ewi->vw", twice, twice)) / total_rows,
    )
    lower = jnp.linalg.cholesky(gram)
    flat = jnp.moveaxis(twice, 1, 0).reshape(NEW, elements * BLK)
    solved = lax.linalg.triangular_solve(lower, flat, left_side=True, lower=True)
    basis = jnp.moveaxis(solved.reshape(NEW, elements, BLK), 0, 1).reshape(rows_r, rows_a, NEW, BLK)
    return (basis, coefficients, lower.T)


def solution(mesh):
    return jax.shard_map(
        on_device,
        mesh=mesh,
        in_specs=(
            P("rad", "azi", None, None, None),
            P("rad", "azi", None, None),
            P("rad", "azi", None, None),
            P("rad", "azi", None),
        ),
        out_specs=(P("rad", "azi", None, None), P(), P()),
        check_vma=False,
    )
```

time: 293 us -> 123 us (0.42)
  the two profiles are of different devices: /device:TPU:1 before, /device:TPU:2 now
where the time goes in v2:
time: 123 us
  waiting for transfers between devices  60.5 us (49%)
  starting transfers between devices  30.2 us (25%)
  matrix products  15.4 us (13%)
  other arithmetic  12.1 us (10%)
  local copies, waits for them, and re-layouts  3.37 us (3%)
  between operations  1.64 us (1%)
    ppermute x16, waiting for transfers between devices, all_sum(): x = x + lax.ppermute(x, axis, [(i, i ^ step) for i in range(count)])  59.6 us
    ppermute x16, starting transfers between devices, all_sum(): x = x + lax.ppermute(x, axis, [(i, i ^ step) for i in range(count)])  21.8 us
    dot_general x8, matrix products, mm(): jnp.einsum(spec, a, b, precision=lax.Precision.HIGHEST, preferred_element...  11 us
    ppermute x2, starting transfers between devices, with_halo(): lax.ppermute(tail, axis, [(i, (i + 1) % count) for i in range(ends)])  4.61 us
    ppermute x2, starting transfers between devices, with_halo(): lax.ppermute(head, axis, [((i + 1) % count, i) for i in range(ends)])  3.85 us
    another operation x3, other arithmetic, on_device(): lower = jnp.linalg.cholesky(gram)  3.6 us
    unnamed x5, other arithmetic  3.36 us
    another operation x1, matrix products, on_device(): lax.linalg.triangular_solve(lower, flat, left_side=True, lower=True)  2.48 us
  transfers between devices with their start and end apart: 20, of which 13 were waited for; matrix products, arithmetic and copies ran while one was open for 10% of the time, Pallas kernels for 0%

profile of v2, /device:TPU:2, one launch (start us, length us, event | category | flops | bytes accessed | tf_op | source)
XLA Modules:
  0.0 123.2 jit_solution(12533136488834938180)
XLA Ops:
  3.2 2.6 %collective-permute-start.9 = (bf16[4,1,32,128]{3,2,1,0:T(8,128)(2,1)S(1)}, bf16[4,1,32,128]{3,2,1,0:T(8,128)(2,1)S(1)}, u32[]{:S(2)}, u32[]{:S(2)}) collective-permute-start(bf16[4,1,32,128]{3,2,1,0:T(8,128)(2,1)S(1)} %get-tuple-element.26), channel_id=1, source_target_pairs={{1,0},{2,1},{3,2},{4,3},{5,4},{6,5},{7,6},{8,7},{9,8},{10,9},{11,1... | collective-permute-start | bytes 98312 | tf_op jit(solution)/shard_map/ppermute | solution.py:31
  5.7 2.7 %convolution_bitcast_fusion.2 = f32[192,192]{1,0:T(8,128)S(1)} fusion(f32[4,8,192,128]{3,2,1,0:T(8,128)S(1)} %copy-done), kind=kOutput, calls=%fused_computation.6 | convolution fusion | flops 1811939328 | bytes 3293184 | tf_op jit(solution)/shard_map/epi,eqi->pq/dot_general | solution.py:39
  10.0 3.0 %collective-permute-start.11 = (bf16[1,10,32,128]{3,2,1,0:T(8,128)(2,1)S(1)}, bf16[1,10,32,128]{3,2,1,0:T(8,128)(2,1)S(1)}, u32[]{:S(2)}, u32[]{:S(2)}) collective-permute-start(bf16[1,10,32,128]{3,2,1,0:T(8,128)(2,1)S(1)} %get-tuple-element.24), channel_id=1, source_target_pairs={{0,16},{16,32},{32,48},{48,64},{64,80},{80,96},{96,112},{112,128},... | collective-permute-start | bytes 245768 | tf_op jit(solution)/shard_map/ppermute | solution.py:29
  16.6 4.6 %collective-permute-start.21 = (f32[192,192]{1,0:T(8,128)S(1)}, f32[192,192]{1,0:T(8,128)S(1)}, u32[]{:S(2)}, u32[]{:S(2)}) collective-permute-start(f32[192,192]{1,0:T(8,128)S(1)} %add.103), channel_id=1, source_target_pairs={{0,32},{16,48},{32,0},{48,16},{64,96},{80,112},{96,64},{112,80},{1... | collective-permute-start | bytes 442376 | tf_op jit(solution)/shard_map/ppermute | solution.py:16
  22.0 3.9 %collective-permute-done.21 = f32[192,192]{1,0:T(8,128)S(1)} collective-permute-done((f32[192,192]{1,0:T(8,128)S(1)}, f32[192,192]{1,0:T(8,128)S(1)}, u32[]{:S(2)}, u32[]{:S(2)}) %collective-permute-start.21) | collective-permute-done | bytes 147488 | tf_op jit(solution)/shard_map/ppermute | solution.py:16
  26.0 4.4 %collective-permute-start.22 = (f32[192,192]{1,0:T(8,128)S(1)}, f32[192,192]{1,0:T(8,128)S(1)}, u32[]{:S(2)}, u32[]{:S(2)}) collective-permute-start(f32[192,192]{1,0:T(8,128)S(1)} %add.104), channel_id=1, source_target_pairs={{0,64},{16,80},{32,96},{48,112},{64,0},{80,16},{96,32},{112,48},{1... | collective-permute-start | bytes 442376 | tf_op jit(solution)/shard_map/ppermute | solution.py:16
  31.2 8.6 %collective-permute-done.22 = f32[192,192]{1,0:T(8,128)S(1)} collective-permute-done((f32[192,192]{1,0:T(8,128)S(1)}, f32[192,192]{1,0:T(8,128)S(1)}, u32[]{:S(2)}, u32[]{:S(2)}) %collective-permute-start.22) | collective-permute-done | bytes 147488 | tf_op jit(solution)/shard_map/ppermute | solution.py:16
  39.8 3.0 %collective-permute-start.23 = (f32[192,192]{1,0:T(8,128)S(1)}, f32[192,192]{1,0:T(8,128)S(1)}, u32[]{:S(2)}, u32[]{:S(2)}) collective-permute-start(f32[192,192]{1,0:T(8,128)S(1)} %add.105), channel_id=1, source_target_pairs={{0,128},{16,144},{32,160},{48,176},{64,192},{80,208},{96,224},{112... | collective-permute-start | bytes 442376 | tf_op jit(solution)/shard_map/ppermute | solution.py:16
  44.7 8.6 %collective-permute-done.23 = f32[192,192]{1,0:T(8,128)S(1)} collective-permute-done((f32[192,192]{1,0:T(8,128)S(1)}, f32[192,192]{1,0:T(8,128)S(1)}, u32[]{:S(2)}, u32[]{:S(2)}) %collective-permute-start.23) | collective-permute-done | bytes 147488 | tf_op jit(solution)/shard_map/ppermute | solution.py:16
  53.6 2.9 %convolution_bitcast_fusion.3 = f32[192,32]{0,1:T(8,128)S(1)} fusion(f32[4,8,192,128]{3,2,1,0:T(8,128)S(1)} %copy-done, f32[4,8,32,128,1]{3,2,4,1,0:T(8,128)S(1)} %fusion.26), kind=kOutput, calls=%fused_computation.9 | convolution fusion | flops 301989888 | bytes 3694592 | tf_op jit(solution)/shard_map/epi,evi->pv/dot_general | solution.py:39
  56.5 3.9 %collective-permute-done.24 = f32[192,192]{1,0:T(8,128)S(1)} collective-permute-done((f32[192,192]{1,0:T(8,128)S(1)}, f32[192,192]{1,0:T(8,128)S(1)}, u32[]{:S(2)}, u32[]{:S(2)}) %collective-permute-start.24) | collective-permute-done | bytes 147488 | tf_op jit(solution)/shard_map/ppermute | solution.py:16
  62.4 5.6 %collective-permute-done.25 = f32[192,192]{1,0:T(8,128)S(1)} collective-permute-done((f32[192,192]{1,0:T(8,128)S(1)}, f32[192,192]{1,0:T(8,128)S(1)}, u32[]{:S(2)}, u32[]{:S(2)}) %collective-permute-start.25) | collective-permute-done | bytes 147488 | tf_op jit(solution)/shard_map/ppermute | solution.py:16
  70.0 3.9 %collective-permute-done.13 = f32[224,32]{0,1:T(8,128)S(1)} collective-permute-done((f32[224,32]{0,1:T(8,128)S(1)}, f32[224,32]{0,1:T(8,128)S(1)}, u32[]{:S(2)}, u32[]{:S(2)}) %collective-permute-start.13) | collective-permute-done | bytes 28704 | tf_op jit(solution)/shard_map/ppermute | solution.py:16
  73.9 4.9 %collective-permute-done.14 = f32[224,32]{0,1:T(8,128)S(1)} collective-permute-done((f32[224,32]{0,1:T(8,128)S(1)}, f32[224,32]{0,1:T(8,128)S(1)}, u32[]{:S(2)}, u32[]{:S(2)}) %collective-permute-start.14) | collective-permute-done | bytes 28704 | tf_op jit(solution)/shard_map/ppermute | solution.py:16
  78.8 2.1 %collective-permute-start.15 = (f32[224,32]{0,1:T(8,128)S(1)}, f32[224,32]{0,1:T(8,128)S(1)}, u32[]{:S(2)}, u32[]{:S(2)}) collective-permute-start(f32[224,32]{0,1:T(8,128)S(1)} %add.97), channel_id=1, source_target_pairs={{0,128},{16,144},{32,160},{48,176},{64,192},{80,208},{96,224},{112... | collective-permute-start | bytes 86024 | tf_op jit(solution)/shard_map/ppermute | solution.py:16
  80.9 5.8 %collective-permute-done.15 = f32[224,32]{0,1:T(8,128)S(1)} collective-permute-done((f32[224,32]{0,1:T(8,128)S(1)}, f32[224,32]{0,1:T(8,128)S(1)}, u32[]{:S(2)}, u32[]{:S(2)}) %collective-permute-start.15) | collective-permute-done | bytes 28704 | tf_op jit(solution)/shard_map/ppermute | solution.py:16
  87.1 3.4 %collective-permute-done.16 = f32[224,32]{0,1:T(8,128)S(1)} collective-permute-done((f32[224,32]{0,1:T(8,128)S(1)}, f32[224,32]{0,1:T(8,128)S(1)}, u32[]{:S(2)}, u32[]{:S(2)}) %collective-permute-start.16) | collective-permute-done | bytes 28704 | tf_op jit(solution)/shard_map/ppermute | solution.py:16
  92.7 3.3 %collective-permute-done.17 = f32[224,32]{0,1:T(8,128)S(1)} collective-permute-done((f32[224,32]{0,1:T(8,128)S(1)}, f32[224,32]{0,1:T(8,128)S(1)}, u32[]{:S(2)}, u32[]{:S(2)}) %collective-permute-start.17) | collective-permute-done | bytes 28704 | tf_op jit(solution)/shard_map/ppermute | solution.py:16
  96.2 3.7 %collective-permute-done.18 = f32[224,32]{0,1:T(8,128)S(1)} collective-permute-done((f32[224,32]{0,1:T(8,128)S(1)}, f32[224,32]{0,1:T(8,128)S(1)}, u32[]{:S(2)}, u32[]{:S(2)}) %collective-permute-start.18) | collective-permute-done | bytes 28704 | tf_op jit(solution)/shard_map/ppermute | solution.py:16
  101.1 4.2 %collective-permute-done.19 = f32[224,32]{0,1:T(8,128)S(1)} collective-permute-done((f32[224,32]{0,1:T(8,128)S(1)}, f32[224,32]{0,1:T(8,128)S(1)}, u32[]{:S(2)}, u32[]{:S(2)}) %collective-permute-start.19) | collective-permute-done | bytes 28704 | tf_op jit(solution)/shard_map/ppermute | solution.py:16
  109.4 3.8 %fusion = f32[32,32,128]{2,1,0:T(8,128)} fusion(f32[32,32,128]{2,1,0:T(8,128)} %bitcast.187, f32[32,192,128]{2,1,0:T(8,128)S(1)} %bitcast.186, f32[192,32]{0,1:T(8,128)S(1)} %fusion.1), kind=kOutput, calls=%fused_computation.5 | convolution fusion | flops 302120960 | bytes 4218880 | tf_op jit(solution)/shard_map/epi,pv->evi/dot_general | solution.py:39
  113.4 2.9 %cholesky.16 = f32[32,32]{1,0:T(8,128)S(1)} custom-call(f32[32,32]{1,0:T(8,128)S(1)} %fusion.16), custom_call_target="Cholesky" | custom-call | tf_op jit(solution)/shard_map/jit(cholesky)/cholesky | solution.py:85
  117.6 2.4 %custom-call.6 = f32[1,32,32]{1,2,0:T(8,128)S(1)} custom-call(f32[1,32,32]{2,1,0:T(8,128)S(1)} %get-tuple-element.30), custom_call_target="InvertDiagBlocksLowerTriangular" | custom-call | tf_op jit(solution)/shard_map/triangular_solve | solution.py:87
  120.1 2.5 %fusion.2 = f32[32,32,128]{2,0,1:T(8,128)} fusion(f32[1,32,32]{1,2,0:T(8,128)S(1)} %custom-call.6, f32[32,32,128]{2,1,0:T(8,128)} %fusion), kind=kOutput, calls=%fused_computation.16 | convolution fusion | flops 50331648 | bytes 1052672 | tf_op jit(solution)/shard_map/triangular_solve | solution.py:87
  (87 shorter events, 25.0 us)
Async XLA Ops:
  1.6 7.0 %collective-permute-start.8 = (bf16[4,1,32,128]{3,2,1,0:T(8,128)(2,1)S(1)}, bf16[4,1,32,128]{3,2,1,0:T(8,128)(2,1)S(1)}, u32[]{:S(2)}, u32[]{:S(2)}) collective-permute-start(bf16[4,1,32,128]{3,2,1,0:T(8,128)(2,1)S(1)} %get-tuple-element.25), channel_id=1, source_target_pairs={{0,1},{1,2},{2,3},{3,4},{4,5},{5,6},{6,7},{7,8},{8,9},{9,10},{10,1... | collective-permute-start | bytes 98312 | tf_op jit(solution)/shard_map/ppermute | solution.py:29
  3.2 5.5 %collective-permute-start.9 = (bf16[4,1,32,128]{3,2,1,0:T(8,128)(2,1)S(1)}, bf16[4,1,32,128]{3,2,1,0:T(8,128)(2,1)S(1)}, u32[]{:S(2)}, u32[]{:S(2)}) collective-permute-start(bf16[4,1,32,128]{3,2,1,0:T(8,128)(2,1)S(1)} %get-tuple-element.26), channel_id=1, source_target_pairs={{1,0},{2,1},{3,2},{4,3},{5,4},{6,5},{7,6},{8,7},{9,8},{10,9},{11,1... | collective-permute-start | bytes 98312 | tf_op jit(solution)/shard_map/ppermute | solution.py:31
  8.4 8.1 %collective-permute-start.20 = (f32[192,192]{1,0:T(8,128)S(1)}, f32[192,192]{1,0:T(8,128)S(1)}, u32[]{:S(2)}, u32[]{:S(2)}) collective-permute-start(f32[192,192]{1,0:T(8,128)S(1)} %convolution_bitcast_fusion.2), channel_id=1, source_target_pairs={{0,16},{16,0},{32,48},{48,32},{64,80},{80,64},{96,112},{112,96},{1... | collective-permute-start | bytes 442376 | tf_op jit(solution)/shard_map/ppermute | solution.py:16
  8.7 4.4 %collective-permute-start.10 = (bf16[1,10,32,128]{3,2,1,0:T(8,128)(2,1)S(1)}, bf16[1,10,32,128]{3,2,1,0:T(8,128)(2,1)S(1)}, u32[]{:S(2)}, u32[]{:S(2)}) collective-permute-start(bf16[1,10,32,128]{3,2,1,0:T(8,128)(2,1)S(1)} %get-tuple-element.23), channel_id=1, source_target_pairs={{16,0},{32,16},{48,32},{64,48},{80,64},{96,80},{112,96},{128,112},... | collective-permute-start | bytes 245768 | tf_op jit(solution)/shard_map/ppermute | solution.py:31
  10.0 3.9 %collective-permute-start.11 = (bf16[1,10,32,128]{3,2,1,0:T(8,128)(2,1)S(1)}, bf16[1,10,32,128]{3,2,1,0:T(8,128)(2,1)S(1)}, u32[]{:S(2)}, u32[]{:S(2)}) collective-permute-start(bf16[1,10,32,128]{3,2,1,0:T(8,128)(2,1)S(1)} %get-tuple-element.24), channel_id=1, source_target_pairs={{0,16},{16,32},{32,48},{48,64},{64,80},{80,96},{96,112},{112,128},... | collective-permute-start | bytes 245768 | tf_op jit(solution)/shard_map/ppermute | solution.py:29
  13.9 28.9 %slice-start = ((s8[5242880]{0:T(1024)(128)(4,1)}), s8[4194304]{0:T(1024)(128)(4,1)S(1)}, s32[]{:S(2)}) async-start(s8[5242880]{0:T(1024)(128)(4,1)} %bitcast.188), calls=%async_computation | async-start | bytes 8388608
  15.7 27.1 %slice-start.1 = ((s8[5242880]{0:T(1024)(128)(4,1)}), s8[1048576]{0:T(1024)(128)(4,1)S(1)}, s32[]{:S(2)}) async-start(s8[5242880]{0:T(1024)(128)(4,1)} %bitcast.188), calls=%async_computation.1 | async-start | bytes 2097152
  16.6 9.3 %collective-permute-start.21 = (f32[192,192]{1,0:T(8,128)S(1)}, f32[192,192]{1,0:T(8,128)S(1)}, u32[]{:S(2)}, u32[]{:S(2)}) collective-permute-start(f32[192,192]{1,0:T(8,128)S(1)} %add.103), channel_id=1, source_target_pairs={{0,32},{16,48},{32,0},{48,16},{64,96},{80,112},{96,64},{112,80},{1... | collective-permute-start | bytes 442376 | tf_op jit(solution)/shard_map/ppermute | solution.py:16
  26.0 13.8 %collective-permute-start.22 = (f32[192,192]{1,0:T(8,128)S(1)}, f32[192,192]{1,0:T(8,128)S(1)}, u32[]{:S(2)}, u32[]{:S(2)}) collective-permute-start(f32[192,192]{1,0:T(8,128)S(1)} %add.104), channel_id=1, source_target_pairs={{0,64},{16,80},{32,96},{48,112},{64,0},{80,16},{96,32},{112,48},{1... | collective-permute-start | bytes 442376 | tf_op jit(solution)/shard_map/ppermute | solution.py:16
  39.8 13.5 %collective-permute-start.23 = (f32[192,192]{1,0:T(8,128)S(1)}, f32[192,192]{1,0:T(8,128)S(1)}, u32[]{:S(2)}, u32[]{:S(2)}) collective-permute-start(f32[192,192]{1,0:T(8,128)S(1)} %add.105), channel_id=1, source_target_pairs={{0,128},{16,144},{32,160},{48,176},{64,192},{80,208},{96,224},{112... | collective-permute-start | bytes 442376 | tf_op jit(solution)/shard_map/ppermute | solution.py:16
  44.7 17.0 %copy-start.2 = (f32[4,8,32,128,1]{3,2,4,1,0:T(8,128)}, f32[4,8,32,128,1]{3,2,4,1,0:T(8,128)S(1)}, u32[]{:S(2)}) copy-start(f32[4,8,32,128,1]{3,2,4,1,0:T(8,128)S(1)} %fusion.26) | copy-start | bytes 1572868
  53.3 7.1 %collective-permute-start.24 = (f32[192,192]{1,0:T(8,128)S(1)}, f32[192,192]{1,0:T(8,128)S(1)}, u32[]{:S(2)}, u32[]{:S(2)}) collective-permute-start(f32[192,192]{1,0:T(8,128)S(1)} %add.106), channel_id=1, source_target_pairs={{0,1},{1,0},{2,3},{3,2},{4,5},{5,4},{6,7},{7,6},{8,9},{9,8},{10,11... | collective-permute-start | bytes 442376 | tf_op jit(solution)/shard_map/ppermute | solution.py:16
  60.4 7.6 %collective-permute-start.25 = (f32[192,192]{1,0:T(8,128)S(1)}, f32[192,192]{1,0:T(8,128)S(1)}, u32[]{:S(2)}, u32[]{:S(2)}) collective-permute-start(f32[192,192]{1,0:T(8,128)S(1)} %add.107), channel_id=1, source_target_pairs={{0,2},{1,3},{2,0},{3,1},{4,6},{5,7},{6,4},{7,5},{8,10},{9,11},{10,... | collective-permute-start | bytes 442376 | tf_op jit(solution)/shard_map/ppermute | solution.py:16
  62.4 7.5 %collective-permute-start.12 = (f32[224,32]{0,1:T(8,128)S(1)}, f32[224,32]{0,1:T(8,128)S(1)}, u32[]{:S(2)}, u32[]{:S(2)}) collective-permute-start(f32[224,32]{0,1:T(8,128)S(1)} %pad_maximum_fusion.4), channel_id=1, source_target_pairs={{0,16},{16,0},{32,48},{48,32},{64,80},{80,64},{96,112},{112,96},{1... | collective-permute-start | bytes 86024 | tf_op jit(solution)/shard_map/ppermute | solution.py:16
  68.0 23.8 %collective-permute-start.26 = (f32[192,192]{1,0:T(8,128)S(1)}, f32[192,192]{1,0:T(8,128)S(1)}, u32[]{:S(2)}, u32[]{:S(2)}) collective-permute-start(f32[192,192]{1,0:T(8,128)S(1)} %add.108), channel_id=1, source_target_pairs={{0,4},{1,5},{2,6},{3,7},{4,0},{5,1},{6,2},{7,3},{8,12},{9,13},{10,... | collective-permute-start | bytes 442376 | tf_op jit(solution)/shard_map/ppermute | solution.py:16
  69.9 3.9 %collective-permute-start.13 = (f32[224,32]{0,1:T(8,128)S(1)}, f32[224,32]{0,1:T(8,128)S(1)}, u32[]{:S(2)}, u32[]{:S(2)}) collective-permute-start(f32[224,32]{0,1:T(8,128)S(1)} %fusion.43), channel_id=1, source_target_pairs={{0,32},{16,48},{32,0},{48,16},{64,96},{80,112},{96,64},{112,80},{1... | collective-permute-start | bytes 86024 | tf_op jit(solution)/shard_map/ppermute | solution.py:16
  73.9 4.9 %collective-permute-start.14 = (f32[224,32]{0,1:T(8,128)S(1)}, f32[224,32]{0,1:T(8,128)S(1)}, u32[]{:S(2)}, u32[]{:S(2)}) collective-permute-start(f32[224,32]{0,1:T(8,128)S(1)} %add.96), channel_id=1, source_target_pairs={{0,64},{16,80},{32,96},{48,112},{64,0},{80,16},{96,32},{112,48},{1... | collective-permute-start | bytes 86024 | tf_op jit(solution)/shard_map/ppermute | solution.py:16
  78.8 7.8 %collective-permute-start.15 = (f32[224,32]{0,1:T(8,128)S(1)}, f32[224,32]{0,1:T(8,128)S(1)}, u32[]{:S(2)}, u32[]{:S(2)}) collective-permute-start(f32[224,32]{0,1:T(8,128)S(1)} %add.97), channel_id=1, source_target_pairs={{0,128},{16,144},{32,160},{48,176},{64,192},{80,208},{96,224},{112... | collective-permute-start | bytes 86024 | tf_op jit(solution)/shard_map/ppermute | solution.py:16
  86.6 3.9 %collective-permute-start.16 = (f32[224,32]{0,1:T(8,128)S(1)}, f32[224,32]{0,1:T(8,128)S(1)}, u32[]{:S(2)}, u32[]{:S(2)}) collective-permute-start(f32[224,32]{0,1:T(8,128)S(1)} %add.98), channel_id=1, source_target_pairs={{0,1},{1,0},{2,3},{3,2},{4,5},{5,4},{6,7},{7,6},{8,9},{9,8},{10,11... | collective-permute-start | bytes 86024 | tf_op jit(solution)/shard_map/ppermute | solution.py:16
  90.6 5.4 %collective-permute-start.17 = (f32[224,32]{0,1:T(8,128)S(1)}, f32[224,32]{0,1:T(8,128)S(1)}, u32[]{:S(2)}, u32[]{:S(2)}) collective-permute-start(f32[224,32]{0,1:T(8,128)S(1)} %add.99), channel_id=1, source_target_pairs={{0,2},{1,3},{2,0},{3,1},{4,6},{5,7},{6,4},{7,5},{8,10},{9,11},{10,... | collective-permute-start | bytes 86024 | tf_op jit(solution)/shard_map/ppermute | solution.py:16
  91.8 13.5 %collective-permute-start.27 = (f32[192,192]{1,0:T(8,128)S(1)}, f32[192,192]{1,0:T(8,128)S(1)}, u32[]{:S(2)}, u32[]{:S(2)}) collective-permute-start(f32[192,192]{1,0:T(8,128)S(1)} %add.109), channel_id=1, source_target_pairs={{0,8},{1,9},{2,10},{3,11},{4,12},{5,13},{6,14},{7,15},{8,0},{9,1},... | collective-permute-start | bytes 442376 | tf_op jit(solution)/shard_map/ppermute | solution.py:16
  96.0 3.9 %collective-permute-start.18 = (f32[224,32]{0,1:T(8,128)S(1)}, f32[224,32]{0,1:T(8,128)S(1)}, u32[]{:S(2)}, u32[]{:S(2)}) collective-permute-start(f32[224,32]{0,1:T(8,128)S(1)} %add.100), channel_id=1, source_target_pairs={{0,4},{1,5},{2,6},{3,7},{4,0},{5,1},{6,2},{7,3},{8,12},{9,13},{10,... | collective-permute-start | bytes 86024 | tf_op jit(solution)/shard_map/ppermute | solution.py:16
  99.9 5.4 %collective-permute-start.19 = (f32[224,32]{0,1:T(8,128)S(1)}, f32[224,32]{0,1:T(8,128)S(1)}, u32[]{:S(2)}, u32[]{:S(2)}) collective-permute-start(f32[224,32]{0,1:T(8,128)S(1)} %add.101), channel_id=1, source_target_pairs={{0,8},{1,9},{2,10},{3,11},{4,12},{5,13},{6,14},{7,15},{8,0},{9,1},... | collective-permute-start | bytes 86024 | tf_op jit(solution)/shard_map/ppermute | solution.py:16
  105.7 7.5 %copy-start.3 = (f32[192,32]{0,1:T(8,128)}, f32[192,32]{0,1:T(8,128)S(1)}, u32[]{:S(2)}) copy-start(f32[192,32]{0,1:T(8,128)S(1)} %fusion.1) | copy-start | bytes 73732
  (3 other events, 15.9 us)

commit v3 on v2

--- a/solution.py
+++ b/solution.py
@@ -6,16 +6,44 @@
 BLK = 128
 NEW = 32
 KEEP = 192
+PIECE = 64
 
 
-def all_sum(x):
+def rounds():
+    out = []
     for axis in ("rad", "azi"):
+        step = 1
+        while step < lax.axis_size(axis):
+            out.append((axis, step))
+            step *= 2
+    return out
+
+
+def all_sum(x, steps):
+    for axis, step in steps:
         count = lax.axis_size(axis)
-        step = 1
-        while step < count:
-            x = x + lax.ppermute(x, axis, [(i, i ^ step) for i in range(count)])
-            step *= 2
+        x = x + lax.ppermute(x, axis, [(i, i ^ step) for i in range(count)])
     return x
+
+
+def upper_pieces():
+    n = KEEP // PIECE
+    return [(i, j) for i in range(n) for j in range(i, n)]
+
+
+def pack_symmetric(g):
+    blocks = [g[i * PIECE : (i + 1) * PIECE, j * PIECE : (j + 1) * PIECE] for i, j in upper_pieces()]
+    return jnp.stack(blocks).reshape(-1, BLK)
+
+
+def unpack_symmetric(flat):
+    n = KEEP // PIECE
+    blocks = dict(zip(upper_pieces(), flat.reshape(-1, PIECE, PIECE)))
+    rows = [
+        jnp.concatenate([blocks[(i, j)] if i <= j else blocks[(j, i)].T for j in range(n)], axis=1)
+        for i in range(n)
+    ]
+    return jnp.concatenate(rows, axis=0)
 
 
 def with_halo(cells, sides, width, closed):
@@ -46,8 +74,10 @@
     elements = rows_r * rows_a
     total_rows = elements * BLK * lax.axis_size("rad") * lax.axis_size("azi")
     kept_flat = kept.reshape(elements, KEEP, BLK)
+    steps = rounds()
+    ahead = 2
 
-    kept_gram = all_sum(mm("epi,eqi->pq", kept_flat, kept_flat))
+    kept_gram = all_sum(pack_symmetric(mm("epi,eqi->pq", kept_flat, kept_flat)), steps[:ahead])
 
     widened = with_halo(new_block, (("azi", 1),), 1, True)
     padded = with_halo(widened, (("rad", 0),), 1, False)
@@ -63,10 +93,15 @@
     image = jnp.einsum("rakij,rakvj->ravi", jacobian, picked, preferred_element_type=jnp.float32)
     image = image.reshape(elements, NEW, BLK)
 
-    moments = all_sum(
-        jnp.concatenate([mm("epi,evi->pv", kept_flat, image), mm("evi,ewi->vw", image, image)], axis=0)
-    )
+    moments = jnp.concatenate(
+        [mm("epi,evi->pv", kept_flat, image), mm("evi,ewi->vw", image, image)], axis=0
+    ).reshape(-1, BLK)
+    split = kept_gram.shape[0]
+    joint = all_sum(jnp.concatenate([kept_gram, moments], axis=0), steps[ahead:])
+    kept_gram = unpack_symmetric(joint[:split])
+    moments = all_sum(joint[split:], steps[:ahead]).reshape(KEEP + NEW, NEW)
     first, image_gram = moments[:KEEP], moments[KEEP:]
+
     second = first - mm("pq,qv->pv", kept_gram, first)
     coefficients = first + second
     twice = image - mm("epi,pv->evi", kept_flat, coefficients)
@@ -76,11 +111,12 @@
         image_gram - cross - cross.T
         + mm("pv,pw->vw", coefficients, mm("pq,qw->pw", kept_gram, coefficients))
     ) / total_rows
-    kept_share = jnp.diagonal(expanded) * 16.0 >= jnp.diagonal(image_gram) / total_rows
+    eye = jnp.eye(NEW, dtype=jnp.float32)
+    kept_share = jnp.sum(expanded * eye, axis=1) * 16.0 >= jnp.sum(image_gram * eye, axis=1) / total_rows
     gram = lax.cond(
         jnp.all(kept_share),
         lambda: expanded,
-        lambda: all_sum(mm("evi,ewi->vw", twice, twice)) / total_rows,
+        lambda: all_sum(mm("evi,ewi->vw", twice, twice), steps) / total_rows,
     )
     lower = jnp.linalg.cholesky(gram)
     flat = jnp.moveaxis(twice, 1, 0).reshape(NEW, elements * BLK)

time: 123 us -> 109 us (0.89)
  the two profiles are of different devices: /device:TPU:2 before, /device:TPU:1 now
where the time goes in v3:
time: 109 us; the launch traced here: 108 us
  waiting for transfers between devices  32.4 us (30%)
  starting transfers between devices  29.2 us (27%)
  matrix products  18.9 us (17%)
  other arithmetic  15.2 us (14%)
  local copies, waits for them, and re-layouts  11.1 us (10%)
  between operations  1.66 us (2%)
    ppermute x10, waiting for transfers between devices, all_sum(): x = x + lax.ppermute(x, axis, [(i, i ^ step) for i in range(count)])  32.4 us
    ppermute x10, starting transfers between devices, all_sum(): x = x + lax.ppermute(x, axis, [(i, i ^ step) for i in range(count)])  17.8 us
    dot_general x8, matrix products, mm(): jnp.einsum(spec, a, b, precision=lax.Precision.HIGHEST, preferred_element...  12 us
    ppermute x2, starting transfers between devices, with_halo(): lax.ppermute(tail, axis, [(i, (i + 1) % count) for i in range(ends)])  5.77 us
    ppermute x2, starting transfers between devices, with_halo(): lax.ppermute(head, axis, [((i + 1) % count, i) for i in range(ends)])  5.66 us
    unnamed x20, local copies, waits for them, and re-layouts  4.78 us
    dot_general x1, matrix products, on_device(): jnp.einsum('rakij,rakvj->ravi', jacobian, picked, preferred_element_type=...  4.38 us
    another operation x3, other arithmetic, on_device(): lower = jnp.linalg.cholesky(gram)  3.59 us
  transfers between devices with their start and end apart: 14, of which 8 were waited for; matrix products, arithmetic and copies ran while one was open for 22% of the time, Pallas kernels for 0%

profile of v3, /device:TPU:1, one launch (start us, length us, event | category | flops | bytes accessed | tf_op | source)
XLA Modules:
  0.0 108.4 jit_solution(16085767791896608656)
XLA Ops:
  1.6 2.1 %collective-permute-start.10 = (bf16[4,1,32,128]{3,2,1,0:T(8,128)(2,1)S(1)}, bf16[4,1,32,128]{3,2,1,0:T(8,128)(2,1)S(1)}, u32[]{:S(2)}, u32[]{:S(2)}) collective-permute-start(bf16[4,1,32,128]{3,2,1,0:T(8,128)(2,1)S(1)} %get-tuple-element.25), channel_id=1, source_target_pairs={{0,1},{1,2},{2,3},{3,4},{4,5},{5,6},{6,7},{7,8},{8,9},{9,10},{10,1... | collective-permute-start | bytes 98312 | tf_op jit(solution)/shard_map/ppermute | solution.py:57
  3.7 3.7 %collective-permute-start.11 = (bf16[4,1,32,128]{3,2,1,0:T(8,128)(2,1)S(1)}, bf16[4,1,32,128]{3,2,1,0:T(8,128)(2,1)S(1)}, u32[]{:S(2)}, u32[]{:S(2)}) collective-permute-start(bf16[4,1,32,128]{3,2,1,0:T(8,128)(2,1)S(1)} %get-tuple-element.26), channel_id=1, source_target_pairs={{1,0},{2,1},{3,2},{4,3},{5,4},{6,5},{7,6},{8,7},{9,8},{10,9},{11,1... | collective-permute-start | bytes 98312 | tf_op jit(solution)/shard_map/ppermute | solution.py:59
  7.5 2.7 %convolution_bitcast_fusion.2 = f32[192,192]{1,0:T(8,128)S(1)} fusion(f32[4,8,192,128]{3,2,1,0:T(8,128)S(1)} %copy-done), kind=kOutput, calls=%fused_computation.4 | convolution fusion | flops 1811939328 | bytes 3293184 | tf_op jit(solution)/shard_map/epi,eqi->pq/dot_general | solution.py:67
  14.0 1.6 %reshape.411 = f32[192,128]{1,0:T(8,128)} reshape(f32[6,64,64]{2,1,0:T(8,128)} %fusion.11) | data formatting | bytes 196608 | tf_op jit(solution)/shard_map/reshape | solution.py:36
  15.6 2.7 %collective-permute-start.8 = (f32[192,128]{1,0:T(8,128)}, f32[192,128]{1,0:T(8,128)S(1)}, u32[]{:S(2)}, u32[]{:S(2)}) collective-permute-start(f32[192,128]{1,0:T(8,128)} %reshape.411), channel_id=1, source_target_pairs={{0,16},{16,0},{32,48},{48,32},{64,80},{80,64},{96,112},{112,96},{1... | collective-permute-start | bytes 294920 | tf_op jit(solution)/shard_map/ppermute | solution.py:25
  18.5 1.9 %collective-permute-start.12 = (bf16[1,10,32,128]{3,2,1,0:T(8,128)(2,1)S(1)}, bf16[1,10,32,128]{3,2,1,0:T(8,128)(2,1)S(1)}, u32[]{:S(2)}, u32[]{:S(2)}) collective-permute-start(bf16[1,10,32,128]{3,2,1,0:T(8,128)(2,1)S(1)} %get-tuple-element.23), channel_id=1, source_target_pairs={{16,0},{32,16},{48,32},{64,48},{80,64},{96,80},{112,96},{128,112},... | collective-permute-start | bytes 245768 | tf_op jit(solution)/shard_map/ppermute | solution.py:59
  20.5 3.6 %collective-permute-start.13 = (bf16[1,10,32,128]{3,2,1,0:T(8,128)(2,1)S(1)}, bf16[1,10,32,128]{3,2,1,0:T(8,128)(2,1)S(1)}, u32[]{:S(2)}, u32[]{:S(2)}) collective-permute-start(bf16[1,10,32,128]{3,2,1,0:T(8,128)(2,1)S(1)} %get-tuple-element.24), channel_id=1, source_target_pairs={{0,16},{16,32},{32,48},{48,64},{64,80},{80,96},{96,112},{112,128},... | collective-permute-start | bytes 245768 | tf_op jit(solution)/shard_map/ppermute | solution.py:57
  24.1 1.5 %add.71 = f32[192,128]{1,0:T(8,128)} add(f32[192,128]{1,0:T(8,128)} %reshape.411, f32[192,128]{1,0:T(8,128)S(1)} %collective-permute-done.8) | non-fusion elementwise | flops 24576 | bytes 294912 | tf_op jit(solution)/shard_map/add | solution.py:25
  30.0 4.4 %fusion.33 = f32[4,8,32,128,1]{3,2,4,1,0:T(8,128)S(1)} fusion(bf16[4,8,5,32,128]{4,3,2,1,0:T(8,128)(2,1)S(1)} %bitcast_dynamic-update-slice_fusion.4, bf16[4,8,5,128,128]{4,3,2,1,0:T(8,128)(2,1)} %param.6), kind=kOutput, calls=%fused_computation.117 | convolution fusion | flops 167772160 | bytes 7077888 | tf_op jit(solution)/shard_map/rakij,rakvj->ravi/dot_general | solution.py:93
  34.3 3.0 %convolution_bitcast_fusion.3 = f32[192,32]{0,1:T(8,128)S(1)} fusion(f32[4,8,192,128]{3,2,1,0:T(8,128)S(1)} %copy-done, f32[4,8,32,128,1]{3,2,4,1,0:T(8,128)S(1)} %fusion.33), kind=kOutput, calls=%fused_computation.5 | convolution fusion | flops 301989888 | bytes 3694592 | tf_op jit(solution)/shard_map/epi,evi->pv/dot_general | solution.py:67
  39.2 4.3 %collective-permute-start.14 = (f32[248,128]{1,0:T(8,128)S(1)}, f32[248,128]{1,0:T(8,128)S(1)}, u32[]{:S(2)}, u32[]{:S(2)}) collective-permute-start(f32[248,128]{1,0:T(8,128)S(1)} %pad_maximum_fusion.4), channel_id=1, source_target_pairs={{0,64},{16,80},{32,96},{48,112},{64,0},{80,16},{96,32},{112,48},{1... | collective-permute-start | bytes 380936 | tf_op jit(solution)/shard_map/ppermute | solution.py:25
  43.5 5.5 %collective-permute-done.14 = f32[248,128]{1,0:T(8,128)S(1)} collective-permute-done((f32[248,128]{1,0:T(8,128)S(1)}, f32[248,128]{1,0:T(8,128)S(1)}, u32[]{:S(2)}, u32[]{:S(2)}) %collective-permute-start.14) | collective-permute-done | bytes 127008 | tf_op jit(solution)/shard_map/ppermute | solution.py:25
  49.0 4.8 %collective-permute-start.15 = (f32[248,128]{1,0:T(8,128)S(1)}, f32[248,128]{1,0:T(8,128)S(1)}, u32[]{:S(2)}, u32[]{:S(2)}) collective-permute-start(f32[248,128]{1,0:T(8,128)S(1)} %fusion.23), channel_id=1, source_target_pairs={{0,128},{16,144},{32,160},{48,176},{64,192},{80,208},{96,224},{112... | collective-permute-start | bytes 380936 | tf_op jit(solution)/shard_map/ppermute | solution.py:25
  53.8 6.8 %collective-permute-done.15 = f32[248,128]{1,0:T(8,128)S(1)} collective-permute-done((f32[248,128]{1,0:T(8,128)S(1)}, f32[248,128]{1,0:T(8,128)S(1)}, u32[]{:S(2)}, u32[]{:S(2)}) %collective-permute-start.15) | collective-permute-done | bytes 127008 | tf_op jit(solution)/shard_map/ppermute | solution.py:25
  60.8 3.8 %collective-permute-done.16 = f32[248,128]{1,0:T(8,128)S(1)} collective-permute-done((f32[248,128]{1,0:T(8,128)S(1)}, f32[248,128]{1,0:T(8,128)S(1)}, u32[]{:S(2)}, u32[]{:S(2)}) %collective-permute-start.16) | collective-permute-done | bytes 127008 | tf_op jit(solution)/shard_map/ppermute | solution.py:25
  64.7 5.3 %collective-permute-done.17 = f32[248,128]{1,0:T(8,128)S(1)} collective-permute-done((f32[248,128]{1,0:T(8,128)S(1)}, f32[248,128]{1,0:T(8,128)S(1)}, u32[]{:S(2)}, u32[]{:S(2)}) %collective-permute-start.17) | collective-permute-done | bytes 127008 | tf_op jit(solution)/shard_map/ppermute | solution.py:25
  70.1 3.8 %collective-permute-done.18 = f32[248,128]{1,0:T(8,128)S(1)} collective-permute-done((f32[248,128]{1,0:T(8,128)S(1)}, f32[248,128]{1,0:T(8,128)S(1)}, u32[]{:S(2)}, u32[]{:S(2)}) %collective-permute-start.18) | collective-permute-done | bytes 127008 | tf_op jit(solution)/shard_map/ppermute | solution.py:25
  73.9 5.5 %collective-permute-done.19 = f32[248,128]{1,0:T(8,128)S(1)} collective-permute-done((f32[248,128]{1,0:T(8,128)S(1)}, f32[248,128]{1,0:T(8,128)S(1)}, u32[]{:S(2)}, u32[]{:S(2)}) %collective-permute-start.19) | collective-permute-done | bytes 127008 | tf_op jit(solution)/shard_map/ppermute | solution.py:25
  79.4 5.5 %collective-permute-start.20 = (f32[56,128]{1,0:T(8,128)S(1)}, f32[56,128]{1,0:T(8,128)S(1)}, u32[]{:S(2)}, u32[]{:S(2)}) collective-permute-start(f32[56,128]{1,0:T(8,128)S(1)} %slice.159), channel_id=1, source_target_pairs={{0,16},{16,0},{32,48},{48,32},{64,80},{80,64},{96,112},{112,96},{1... | collective-permute-start | bytes 86024 | tf_op jit(solution)/shard_map/ppermute | solution.py:25
  90.2 1.2 %fusion.1 = f32[192,32]{0,1:T(8,128)S(1)} fusion(f32[192,32]{0,1:T(8,128)} %copy.28, f32[192,32]{1,0:T(8,128)S(1)} %slice.142, f32[64,64]{1,0:T(8,128)S(1)} %unstack.47, f32[64,64]{1,0:T(8,128)} %copy.26, f32[64,64]{1,0:T(8,128)} %copy.25, f32[64,64]{1,0:T(8,128)S(1)} %unstack.45, f32[64,64]{1,0:T(8,128)S(1)} %unstack.43, f32[64,64]{1,0:T(8,128)S(1)} %bitcast.217, ...), kind=kOutput, calls=%fused_computation.7 | convolution fusion | flops 14462976 | bytes 221184 | tf_op jit(solution)/shard_map/pq,qv->pv/dot_general | solution.py:67
  94.6 3.0 %fusion = f32[32,32,128]{2,1,0:T(8,128)S(1)} fusion(f32[32,32,128]{2,1,0:T(8,128)} %bitcast.213, f32[32,192,128]{2,1,0:T(8,128)S(1)} %bitcast.212, f32[192,32]{0,1:T(8,128)S(1)} %fusion.1), kind=kOutput, calls=%fused_computation.3 | convolution fusion | flops 302120960 | bytes 4218880 | tf_op jit(solution)/shard_map/epi,pv->evi/dot_general | solution.py:67
  98.5 2.9 %cholesky.17 = f32[32,32]{1,0:T(8,128)S(1)} custom-call(f32[32,32]{1,0:T(8,128)S(1)} %fusion.19), custom_call_target="Cholesky" | custom-call | tf_op jit(solution)/shard_map/jit(cholesky)/cholesky | solution.py:121
  102.8 2.4 %custom-call.6 = f32[1,32,32]{1,2,0:T(8,128)S(1)} custom-call(f32[1,32,32]{2,1,0:T(8,128)S(1)} %get-tuple-element.34), custom_call_target="InvertDiagBlocksLowerTriangular" | custom-call | tf_op jit(solution)/shard_map/triangular_solve | solution.py:123
  105.2 2.5 %fusion.2 = f32[32,32,128]{2,0,1:T(8,128)} fusion(f32[1,32,32]{1,2,0:T(8,128)S(1)} %custom-call.6, f32[32,32,128]{2,1,0:T(8,128)} %copy-done.3), kind=kOutput, calls=%fused_computation.14 | convolution fusion | flops 50331648 | bytes 1052672 | tf_op jit(solution)/shard_map/triangular_solve | solution.py:123
  (88 shorter events, 22.0 us)
Async XLA Ops:
  0.6 6.8 %copy-start = (f32[4,8,192,128]{3,2,1,0:T(8,128)S(1)}, f32[4,8,192,128]{3,2,1,0:T(8,128)}, u32[]{:S(2)}) copy-start(f32[4,8,192,128]{3,2,1,0:T(8,128)} %param.8) | copy-start | bytes 9437188
  1.6 16.8 %collective-permute-start.10 = (bf16[4,1,32,128]{3,2,1,0:T(8,128)(2,1)S(1)}, bf16[4,1,32,128]{3,2,1,0:T(8,128)(2,1)S(1)}, u32[]{:S(2)}, u32[]{:S(2)}) collective-permute-start(bf16[4,1,32,128]{3,2,1,0:T(8,128)(2,1)S(1)} %get-tuple-element.25), channel_id=1, source_target_pairs={{0,1},{1,2},{2,3},{3,4},{4,5},{5,6},{6,7},{7,8},{8,9},{9,10},{10,1... | collective-permute-start | bytes 98312 | tf_op jit(solution)/shard_map/ppermute | solution.py:57
  3.7 14.7 %copy-start.5 = (s32[4,8,5]{1,0,2:T(4,128)S(1)}, s32[4,8,5]{1,0,2:T(4,128)}, u32[]{:S(2)}) copy-start(s32[4,8,5]{1,0,2:T(4,128)} %param.9) | copy-start | bytes 1924
  3.7 14.7 %copy-start.1 = (bf16[4,8,32,128]{3,2,1,0:T(8,128)(2,1)S(1)}, bf16[4,8,32,128]{3,2,1,0:T(8,128)(2,1)}, u32[]{:S(2)}) copy-start(bf16[4,8,32,128]{3,2,1,0:T(8,128)(2,1)} %param.7) | copy-start | bytes 786436
  3.7 14.8 %collective-permute-start.11 = (bf16[4,1,32,128]{3,2,1,0:T(8,128)(2,1)S(1)}, bf16[4,1,32,128]{3,2,1,0:T(8,128)(2,1)S(1)}, u32[]{:S(2)}, u32[]{:S(2)}) collective-permute-start(bf16[4,1,32,128]{3,2,1,0:T(8,128)(2,1)S(1)} %get-tuple-element.26), channel_id=1, source_target_pairs={{1,0},{2,1},{3,2},{4,3},{5,4},{6,5},{7,6},{8,7},{9,8},{10,9},{11,1... | collective-permute-start | bytes 98312 | tf_op jit(solution)/shard_map/ppermute | solution.py:59
  15.6 8.5 %collective-permute-start.8 = (f32[192,128]{1,0:T(8,128)}, f32[192,128]{1,0:T(8,128)S(1)}, u32[]{:S(2)}, u32[]{:S(2)}) collective-permute-start(f32[192,128]{1,0:T(8,128)} %reshape.411), channel_id=1, source_target_pairs={{0,16},{16,0},{32,48},{48,32},{64,80},{80,64},{96,112},{112,96},{1... | collective-permute-start | bytes 294920 | tf_op jit(solution)/shard_map/ppermute | solution.py:25
  18.5 7.1 %collective-permute-start.12 = (bf16[1,10,32,128]{3,2,1,0:T(8,128)(2,1)S(1)}, bf16[1,10,32,128]{3,2,1,0:T(8,128)(2,1)S(1)}, u32[]{:S(2)}, u32[]{:S(2)}) collective-permute-start(bf16[1,10,32,128]{3,2,1,0:T(8,128)(2,1)S(1)} %get-tuple-element.23), channel_id=1, source_target_pairs={{16,0},{32,16},{48,32},{64,48},{80,64},{96,80},{112,96},{128,112},... | collective-permute-start | bytes 245768 | tf_op jit(solution)/shard_map/ppermute | solution.py:59
  20.5 5.2 %collective-permute-start.13 = (bf16[1,10,32,128]{3,2,1,0:T(8,128)(2,1)S(1)}, bf16[1,10,32,128]{3,2,1,0:T(8,128)(2,1)S(1)}, u32[]{:S(2)}, u32[]{:S(2)}) collective-permute-start(bf16[1,10,32,128]{3,2,1,0:T(8,128)(2,1)S(1)} %get-tuple-element.24), channel_id=1, source_target_pairs={{0,16},{16,32},{32,48},{48,64},{64,80},{80,96},{96,112},{112,128},... | collective-permute-start | bytes 245768 | tf_op jit(solution)/shard_map/ppermute | solution.py:57
  25.7 12.5 %collective-permute-start.9 = (f32[192,128]{1,0:T(8,128)}, f32[192,128]{1,0:T(8,128)}, u32[]{:S(2)}, u32[]{:S(2)}) collective-permute-start(f32[192,128]{1,0:T(8,128)} %add.71), channel_id=1, source_target_pairs={{0,32},{16,48},{32,0},{48,16},{64,96},{80,112},{96,64},{112,80},{1... | collective-permute-start | bytes 294920 | tf_op jit(solution)/shard_map/ppermute | solution.py:25
  34.3 3.0 %copy-start.2 = (f32[4,8,32,128,1]{3,2,4,1,0:T(8,128)}, f32[4,8,32,128,1]{3,2,4,1,0:T(8,128)S(1)}, u32[]{:S(2)}) copy-start(f32[4,8,32,128,1]{3,2,4,1,0:T(8,128)S(1)} %fusion.33) | copy-start | bytes 1572868
  39.2 9.8 %collective-permute-start.14 = (f32[248,128]{1,0:T(8,128)S(1)}, f32[248,128]{1,0:T(8,128)S(1)}, u32[]{:S(2)}, u32[]{:S(2)}) collective-permute-start(f32[248,128]{1,0:T(8,128)S(1)} %pad_maximum_fusion.4), channel_id=1, source_target_pairs={{0,64},{16,80},{32,96},{48,112},{64,0},{80,16},{96,32},{112,48},{1... | collective-permute-start | bytes 380936 | tf_op jit(solution)/shard_map/ppermute | solution.py:25
  49.0 11.7 %collective-permute-start.15 = (f32[248,128]{1,0:T(8,128)S(1)}, f32[248,128]{1,0:T(8,128)S(1)}, u32[]{:S(2)}, u32[]{:S(2)}) collective-permute-start(f32[248,128]{1,0:T(8,128)S(1)} %fusion.23), channel_id=1, source_target_pairs={{0,128},{16,144},{32,160},{48,176},{64,192},{80,208},{96,224},{112... | collective-permute-start | bytes 380936 | tf_op jit(solution)/shard_map/ppermute | solution.py:25
  60.7 3.9 %collective-permute-start.16 = (f32[248,128]{1,0:T(8,128)S(1)}, f32[248,128]{1,0:T(8,128)S(1)}, u32[]{:S(2)}, u32[]{:S(2)}) collective-permute-start(f32[248,128]{1,0:T(8,128)S(1)} %add.74), channel_id=1, source_target_pairs={{0,1},{1,0},{2,3},{3,2},{4,5},{5,4},{6,7},{7,6},{8,9},{9,8},{10,11... | collective-permute-start | bytes 380936 | tf_op jit(solution)/shard_map/ppermute | solution.py:25
  64.6 5.4 %collective-permute-start.17 = (f32[248,128]{1,0:T(8,128)S(1)}, f32[248,128]{1,0:T(8,128)S(1)}, u32[]{:S(2)}, u32[]{:S(2)}) collective-permute-start(f32[248,128]{1,0:T(8,128)S(1)} %add.75), channel_id=1, source_target_pairs={{0,2},{1,3},{2,0},{3,1},{4,6},{5,7},{6,4},{7,5},{8,10},{9,11},{10,... | collective-permute-start | bytes 380936 | tf_op jit(solution)/shard_map/ppermute | solution.py:25
  70.0 3.9 %collective-permute-start.18 = (f32[248,128]{1,0:T(8,128)S(1)}, f32[248,128]{1,0:T(8,128)S(1)}, u32[]{:S(2)}, u32[]{:S(2)}) collective-permute-start(f32[248,128]{1,0:T(8,128)S(1)} %add.76), channel_id=1, source_target_pairs={{0,4},{1,5},{2,6},{3,7},{4,0},{5,1},{6,2},{7,3},{8,12},{9,13},{10,... | collective-permute-start | bytes 380936 | tf_op jit(solution)/shard_map/ppermute | solution.py:25
  73.8 5.6 %collective-permute-start.19 = (f32[248,128]{1,0:T(8,128)S(1)}, f32[248,128]{1,0:T(8,128)S(1)}, u32[]{:S(2)}, u32[]{:S(2)}) collective-permute-start(f32[248,128]{1,0:T(8,128)S(1)} %add.77), channel_id=1, source_target_pairs={{0,8},{1,9},{2,10},{3,11},{4,12},{5,13},{6,14},{7,15},{8,0},{9,1},... | collective-permute-start | bytes 380936 | tf_op jit(solution)/shard_map/ppermute | solution.py:25
  79.4 6.4 %collective-permute-start.20 = (f32[56,128]{1,0:T(8,128)S(1)}, f32[56,128]{1,0:T(8,128)S(1)}, u32[]{:S(2)}, u32[]{:S(2)}) collective-permute-start(f32[56,128]{1,0:T(8,128)S(1)} %slice.159), channel_id=1, source_target_pairs={{0,16},{16,0},{32,48},{48,32},{64,80},{80,64},{96,112},{112,96},{1... | collective-permute-start | bytes 86024 | tf_op jit(solution)/shard_map/ppermute | solution.py:25
  85.8 2.8 %collective-permute-start.21 = (f32[56,128]{1,0:T(8,128)S(1)}, f32[56,128]{1,0:T(8,128)}, u32[]{:S(2)}, u32[]{:S(2)}) collective-permute-start(f32[56,128]{1,0:T(8,128)S(1)} %slice_add_fusion), channel_id=1, source_target_pairs={{0,32},{16,48},{32,0},{48,16},{64,96},{80,112},{96,64},{112,80},{1... | collective-permute-start | bytes 86024 | tf_op jit(solution)/shard_map/ppermute | solution.py:25
  91.4 6.2 %copy-start.4 = (f32[192,32]{0,1:T(8,128)}, f32[192,32]{0,1:T(8,128)S(1)}, u32[]{:S(2)}) copy-start(f32[192,32]{0,1:T(8,128)S(1)} %fusion.1) | copy-start | bytes 73732
  97.6 0.8 copy-start.3

commit v4 on v3

--- a/solution.py
+++ b/solution.py
@@ -6,7 +6,6 @@
 BLK = 128
 NEW = 32
 KEEP = 192
-PIECE = 64
 
 
 def rounds():
@@ -26,24 +25,20 @@
     return x
 
 
-def upper_pieces():
-    n = KEEP // PIECE
-    return [(i, j) for i in range(n) for j in range(i, n)]
+def pack_symmetric(g):
+    return jnp.concatenate([g[:, :BLK], g[BLK:, BLK:].reshape(-1, BLK)], axis=0)
 
 
-def pack_symmetric(g):
-    blocks = [g[i * PIECE : (i + 1) * PIECE, j * PIECE : (j + 1) * PIECE] for i, j in upper_pieces()]
-    return jnp.stack(blocks).reshape(-1, BLK)
-
-
-def unpack_symmetric(flat):
-    n = KEEP // PIECE
-    blocks = dict(zip(upper_pieces(), flat.reshape(-1, PIECE, PIECE)))
-    rows = [
-        jnp.concatenate([blocks[(i, j)] if i <= j else blocks[(j, i)].T for j in range(n)], axis=1)
-        for i in range(n)
-    ]
-    return jnp.concatenate(rows, axis=0)
+def apply_symmetric(packed, x):
+    tail = KEEP - BLK
+    upper, lower = packed[:BLK], packed[BLK:KEEP]
+    corner = packed[KEEP:].reshape(tail, tail)
+    head, rest = x[:BLK], x[BLK:]
+    return jnp.concatenate(
+        [mm("pq,qv->pv", upper, head) + mm("qp,qv->pv", lower, rest),
+         mm("pq,qv->pv", lower, head) + mm("pq,qv->pv", corner, rest)],
+        axis=0,
+    )
 
 
 def with_halo(cells, sides, width, closed):
@@ -75,7 +70,7 @@
     total_rows = elements * BLK * lax.axis_size("rad") * lax.axis_size("azi")
     kept_flat = kept.reshape(elements, KEEP, BLK)
     steps = rounds()
-    ahead = 2
+    ahead = 4
 
     kept_gram = all_sum(pack_symmetric(mm("epi,eqi->pq", kept_flat, kept_flat)), steps[:ahead])
 
@@ -98,18 +93,18 @@
     ).reshape(-1, BLK)
     split = kept_gram.shape[0]
     joint = all_sum(jnp.concatenate([kept_gram, moments], axis=0), steps[ahead:])
-    kept_gram = unpack_symmetric(joint[:split])
+    kept_gram = joint[:split]
     moments = all_sum(joint[split:], steps[:ahead]).reshape(KEEP + NEW, NEW)
     first, image_gram = moments[:KEEP], moments[KEEP:]
 
-    second = first - mm("pq,qv->pv", kept_gram, first)
+    second = first - apply_symmetric(kept_gram, first)
     coefficients = first + second
     twice = image - mm("epi,pv->evi", kept_flat, coefficients)
 
     cross = mm("pv,pw->vw", coefficients, first)
     expanded = (
         image_gram - cross - cross.T
-        + mm("pv,pw->vw", coefficients, mm("pq,qw->pw", kept_gram, coefficients))
+        + mm("pv,pw->vw", coefficients, apply_symmetric(kept_gram, coefficients))
     ) / total_rows
     eye = jnp.eye(NEW, dtype=jnp.float32)
     kept_share = jnp.sum(expanded * eye, axis=1) * 16.0 >= jnp.sum(image_gram * eye, axis=1) / total_rows

time: 109 us -> 116 us (1.064)
  the two profiles are of different devices: /device:TPU:1 before, /device:TPU:32 now
where the time goes in v4:
time: 116 us
  waiting for transfers between devices  43.5 us (38%)
  starting transfers between devices  28.2 us (24%)
  matrix products  22.1 us (19%)
  other arithmetic  13.7 us (12%)
  local copies, waits for them, and re-layouts  6.45 us (6%)
  between operations  1.74 us (2%)
    ppermute x12, waiting for transfers between devices, all_sum(): x = x + lax.ppermute(x, axis, [(i, i ^ step) for i in range(count)])  40 us
    ppermute x12, starting transfers between devices, all_sum(): x = x + lax.ppermute(x, axis, [(i, i ^ step) for i in range(count)])  17.1 us
    dot_general x14, matrix products, mm(): jnp.einsum(spec, a, b, precision=lax.Precision.HIGHEST, preferred_element...  15.2 us
    ppermute x2, starting transfers between devices, with_halo(): lax.ppermute(head, axis, [((i + 1) % count, i) for i in range(ends)])  7.61 us
    dot_general x1, matrix products, on_device(): jnp.einsum('rakij,rakvj->ravi', jacobian, picked, preferred_element_type=...  4.39 us
    another operation x3, other arithmetic, on_device(): lower = jnp.linalg.cholesky(gram)  3.59 us
    ppermute x2, starting transfers between devices, with_halo(): lax.ppermute(tail, axis, [(i, (i + 1) % count) for i in range(ends)])  3.5 us
    ppermute x2, waiting for transfers between devices, with_halo(): lax.ppermute(tail, axis, [(i, (i + 1) % count) for i in range(ends)])  3.47 us
  transfers between devices with their start and end apart: 16, of which 11 were waited for; matrix products, arithmetic and copies ran while one was open for 15% of the time, Pallas kernels for 0%

profile of v4, /device:TPU:32, one launch (start us, length us, event | category | flops | bytes accessed | tf_op | source)
XLA Modules:
  0.0 115.7 jit_solution(12787625981442717886)
XLA Ops:
  3.8 3.8 %collective-permute-start.13 = (bf16[4,1,32,128]{3,2,1,0:T(8,128)(2,1)}, bf16[4,1,32,128]{3,2,1,0:T(8,128)(2,1)S(1)}, u32[]{:S(2)}, u32[]{:S(2)}) collective-permute-start(bf16[4,1,32,128]{3,2,1,0:T(8,128)(2,1)} %get-tuple-element.29), channel_id=1, source_target_pairs={{1,0},{2,1},{3,2},{4,3},{5,4},{6,5},{7,6},{8,7},{9,8},{10,9},{11,1... | collective-permute-start | bytes 98312 | tf_op jit(solution)/shard_map/ppermute | solution.py:54
  7.6 2.7 %convolution_bitcast_fusion.2 = f32[192,192]{1,0:T(8,128)S(1)} fusion(f32[4,8,192,128]{3,2,1,0:T(8,128)S(1)} %copy-done), kind=kOutput, calls=%fused_computation.4 | convolution fusion | flops 1811939328 | bytes 3293184 | tf_op jit(solution)/shard_map/epi,eqi->pq/dot_general | solution.py:62
  12.2 3.8 %collective-permute-start.14 = (bf16[1,10,32,128]{3,2,1,0:T(8,128)(2,1)S(1)}, bf16[1,10,32,128]{3,2,1,0:T(8,128)(2,1)S(1)}, u32[]{:S(2)}, u32[]{:S(2)}) collective-permute-start(bf16[1,10,32,128]{3,2,1,0:T(8,128)(2,1)S(1)} %get-tuple-element.26), channel_id=1, source_target_pairs={{16,0},{32,16},{48,32},{64,48},{80,64},{96,80},{112,96},{128,112},... | collective-permute-start | bytes 245768 | tf_op jit(solution)/shard_map/ppermute | solution.py:54
  16.0 1.9 %collective-permute-start.15 = (bf16[1,10,32,128]{3,2,1,0:T(8,128)(2,1)S(1)}, bf16[1,10,32,128]{3,2,1,0:T(8,128)(2,1)S(1)}, u32[]{:S(2)}, u32[]{:S(2)}) collective-permute-start(bf16[1,10,32,128]{3,2,1,0:T(8,128)(2,1)S(1)} %get-tuple-element.27), channel_id=1, source_target_pairs={{0,16},{16,32},{32,48},{48,64},{64,80},{80,96},{96,112},{112,128},... | collective-permute-start | bytes 245768 | tf_op jit(solution)/shard_map/ppermute | solution.py:52
  18.5 3.5 %collective-permute-done.15 = bf16[1,10,32,128]{3,2,1,0:T(8,128)(2,1)S(1)} collective-permute-done((bf16[1,10,32,128]{3,2,1,0:T(8,128)(2,1)S(1)}, bf16[1,10,32,128]{3,2,1,0:T(8,128)(2,1)S(1)}, u32[]{:S(2)}, u32[]{:S(2)}) %collective-permute-start.15) | collective-permute-done | bytes 81952 | tf_op jit(solution)/shard_map/ppermute | solution.py:52
  26.2 4.4 %fusion.43 = f32[4,8,32,128,1]{3,2,4,1,0:T(8,128)S(1)} fusion(bf16[4,8,5,32,128]{4,3,2,1,0:T(8,128)(2,1)S(1)} %bitcast_dynamic-update-slice_fusion.4, bf16[4,8,5,128,128]{4,3,2,1,0:T(8,128)(2,1)} %param.6), kind=kOutput, calls=%fused_computation.127 | convolution fusion | flops 167772160 | bytes 7077888 | tf_op jit(solution)/shard_map/rakij,rakvj->ravi/dot_general | solution.py:88
  32.1 2.9 %convolution_bitcast_fusion.3 = f32[192,32]{0,1:T(8,128)S(1)} fusion(f32[4,8,192,128]{3,2,1,0:T(8,128)S(1)} %copy-done, f32[4,8,32,128,1]{3,2,4,1,0:T(8,128)S(1)} %fusion.43), kind=kOutput, calls=%fused_computation.5 | convolution fusion | flops 301989888 | bytes 3694592 | tf_op jit(solution)/shard_map/epi,evi->pv/dot_general | solution.py:62
  35.0 2.6 %collective-permute-done.10 = f32[224,128]{1,0:T(8,128)S(1)} collective-permute-done((f32[224,128]{1,0:T(8,128)S(1)}, f32[224,128]{1,0:T(8,128)S(1)}, u32[]{:S(2)}, u32[]{:S(2)}) %collective-permute-start.10) | collective-permute-done | bytes 114720 | tf_op jit(solution)/shard_map/ppermute | solution.py:24
  37.6 4.6 %collective-permute-start.11 = (f32[224,128]{1,0:T(8,128)S(1)}, f32[224,128]{1,0:T(8,128)S(1)}, u32[]{:S(2)}, u32[]{:S(2)}) collective-permute-start(f32[224,128]{1,0:T(8,128)S(1)} %add.97), channel_id=1, source_target_pairs={{0,128},{16,144},{32,160},{48,176},{64,192},{80,208},{96,224},{112... | collective-permute-start | bytes 344072 | tf_op jit(solution)/shard_map/ppermute | solution.py:24
  43.1 4.0 %collective-permute-done.11 = f32[224,128]{1,0:T(8,128)S(1)} collective-permute-done((f32[224,128]{1,0:T(8,128)S(1)}, f32[224,128]{1,0:T(8,128)S(1)}, u32[]{:S(2)}, u32[]{:S(2)}) %collective-permute-start.11) | collective-permute-done | bytes 114720 | tf_op jit(solution)/shard_map/ppermute | solution.py:24
  47.2 5.1 %collective-permute-done.16 = f32[280,128]{1,0:T(8,128)S(1)} collective-permute-done((f32[280,128]{1,0:T(8,128)S(1)}, f32[280,128]{1,0:T(8,128)S(1)}, u32[]{:S(2)}, u32[]{:S(2)}) %collective-permute-start.16) | collective-permute-done | bytes 143392 | tf_op jit(solution)/shard_map/ppermute | solution.py:24
  52.4 6.6 %collective-permute-done.17 = f32[280,128]{1,0:T(8,128)S(1)} collective-permute-done((f32[280,128]{1,0:T(8,128)S(1)}, f32[280,128]{1,0:T(8,128)S(1)}, u32[]{:S(2)}, u32[]{:S(2)}) %collective-permute-start.17) | collective-permute-done | bytes 143392 | tf_op jit(solution)/shard_map/ppermute | solution.py:24
  59.3 6.1 %collective-permute-done.18 = f32[280,128]{1,0:T(8,128)S(1)} collective-permute-done((f32[280,128]{1,0:T(8,128)S(1)}, f32[280,128]{1,0:T(8,128)S(1)}, u32[]{:S(2)}, u32[]{:S(2)}) %collective-permute-start.18) | collective-permute-done | bytes 143392 | tf_op jit(solution)/shard_map/ppermute | solution.py:24
  65.4 1.7 %collective-permute-start.19 = (f32[280,128]{1,0:T(8,128)S(1)}, f32[280,128]{1,0:T(8,128)S(1)}, u32[]{:S(2)}, u32[]{:S(2)}) collective-permute-start(f32[280,128]{1,0:T(8,128)S(1)} %add.101), channel_id=1, source_target_pairs={{0,8},{1,9},{2,10},{3,11},{4,12},{5,13},{6,14},{7,15},{8,0},{9,1},... | collective-permute-start | bytes 430088 | tf_op jit(solution)/shard_map/ppermute | solution.py:24
  67.1 5.0 %collective-permute-done.19 = f32[280,128]{1,0:T(8,128)S(1)} collective-permute-done((f32[280,128]{1,0:T(8,128)S(1)}, f32[280,128]{1,0:T(8,128)S(1)}, u32[]{:S(2)}, u32[]{:S(2)}) %collective-permute-start.19) | collective-permute-done | bytes 143392 | tf_op jit(solution)/shard_map/ppermute | solution.py:24
  74.3 3.0 %collective-permute-done.21 = f32[56,128]{1,0:T(8,128)S(1)} collective-permute-done((f32[56,128]{1,0:T(8,128)S(1)}, f32[56,128]{1,0:T(8,128)S(1)}, u32[]{:S(2)}, u32[]{:S(2)}) %collective-permute-start.21) | collective-permute-done | bytes 28704 | tf_op jit(solution)/shard_map/ppermute | solution.py:24
  77.3 4.4 %collective-permute-start.22 = (f32[56,128]{1,0:T(8,128)S(1)}, f32[56,128]{1,0:T(8,128)S(1)}, u32[]{:S(2)}, u32[]{:S(2)}) collective-permute-start(f32[56,128]{1,0:T(8,128)S(1)} %add.104), channel_id=1, source_target_pairs={{0,64},{16,80},{32,96},{48,112},{64,0},{80,16},{96,32},{112,48},{1... | collective-permute-start | bytes 86024 | tf_op jit(solution)/shard_map/ppermute | solution.py:24
  81.7 1.8 %collective-permute-done.22 = f32[56,128]{1,0:T(8,128)S(1)} collective-permute-done((f32[56,128]{1,0:T(8,128)S(1)}, f32[56,128]{1,0:T(8,128)S(1)}, u32[]{:S(2)}, u32[]{:S(2)}) %collective-permute-start.22) | collective-permute-done | bytes 28704 | tf_op jit(solution)/shard_map/ppermute | solution.py:24
  83.5 3.1 %collective-permute-start.23 = (f32[56,128]{1,0:T(8,128)S(1)}, f32[56,128]{1,0:T(8,128)S(1)}, u32[]{:S(2)}, u32[]{:S(2)}) collective-permute-start(f32[56,128]{1,0:T(8,128)S(1)} %add.105), channel_id=1, source_target_pairs={{0,128},{16,144},{32,160},{48,176},{64,192},{80,208},{96,224},{112... | collective-permute-start | bytes 86024 | tf_op jit(solution)/shard_map/ppermute | solution.py:24
  86.7 4.6 %collective-permute-done.23 = f32[56,128]{1,0:T(8,128)S(1)} collective-permute-done((f32[56,128]{1,0:T(8,128)S(1)}, f32[56,128]{1,0:T(8,128)S(1)}, u32[]{:S(2)}, u32[]{:S(2)}) %collective-permute-start.23) | collective-permute-done | bytes 28704 | tf_op jit(solution)/shard_map/ppermute | solution.py:24
  101.9 3.1 %fusion = f32[32,32,128]{2,1,0:T(8,128)S(1)} fusion(f32[32,32,128]{2,1,0:T(8,128)} %bitcast.189, f32[32,192,128]{2,1,0:T(8,128)S(1)} %bitcast.188, f32[192,32]{1,0:T(8,128)S(1)} %add.110), kind=kOutput, calls=%fused_computation.3 | convolution fusion | flops 302120960 | bytes 4218880 | tf_op jit(solution)/shard_map/epi,pv->evi/dot_general | solution.py:62
  105.9 2.9 %cholesky.17 = f32[32,32]{1,0:T(8,128)S(1)} custom-call(f32[32,32]{1,0:T(8,128)S(1)} %fusion.24), custom_call_target="Cholesky" | custom-call | tf_op jit(solution)/shard_map/jit(cholesky)/cholesky | solution.py:116
  110.1 2.4 %custom-call.6 = f32[1,32,32]{1,2,0:T(8,128)S(1)} custom-call(f32[1,32,32]{2,1,0:T(8,128)S(1)} %get-tuple-element.33), custom_call_target="InvertDiagBlocksLowerTriangular" | custom-call | tf_op jit(solution)/shard_map/triangular_solve | solution.py:118
  112.6 2.5 %fusion.1 = f32[32,32,128]{2,0,1:T(8,128)} fusion(f32[1,32,32]{1,2,0:T(8,128)S(1)} %custom-call.6, f32[32,32,128]{2,1,0:T(8,128)} %copy-done.3), kind=kOutput, calls=%fused_computation.16 | convolution fusion | flops 50331648 | bytes 1052672 | tf_op jit(solution)/shard_map/triangular_solve | solution.py:118
  (100 shorter events, 27.5 us)
Async XLA Ops:
  0.6 6.9 %copy-start = (f32[4,8,192,128]{3,2,1,0:T(8,128)S(1)}, f32[4,8,192,128]{3,2,1,0:T(8,128)}, u32[]{:S(2)}) copy-start(f32[4,8,192,128]{3,2,1,0:T(8,128)} %param.8) | copy-start | bytes 9437188
  2.2 9.8 %collective-permute-start.12 = (bf16[4,1,32,128]{3,2,1,0:T(8,128)(2,1)}, bf16[4,1,32,128]{3,2,1,0:T(8,128)(2,1)S(1)}, u32[]{:S(2)}, u32[]{:S(2)}) collective-permute-start(bf16[4,1,32,128]{3,2,1,0:T(8,128)(2,1)} %get-tuple-element.28), channel_id=1, source_target_pairs={{0,1},{1,2},{2,3},{3,4},{4,5},{5,6},{6,7},{7,8},{8,9},{9,10},{10,1... | collective-permute-start | bytes 98312 | tf_op jit(solution)/shard_map/ppermute | solution.py:52
  3.8 8.2 %copy-start.6 = (s32[4,8,5]{1,0,2:T(4,128)S(1)}, s32[4,8,5]{1,0,2:T(4,128)}, u32[]{:S(2)}) copy-start(s32[4,8,5]{1,0,2:T(4,128)} %param.9) | copy-start | bytes 1924
  3.8 8.3 %copy-start.1 = (bf16[4,8,32,128]{3,2,1,0:T(8,128)(2,1)S(1)}, bf16[4,8,32,128]{3,2,1,0:T(8,128)(2,1)}, u32[]{:S(2)}) copy-start(bf16[4,8,32,128]{3,2,1,0:T(8,128)(2,1)} %param.7) | copy-start | bytes 786436
  3.8 8.3 %collective-permute-start.13 = (bf16[4,1,32,128]{3,2,1,0:T(8,128)(2,1)}, bf16[4,1,32,128]{3,2,1,0:T(8,128)(2,1)S(1)}, u32[]{:S(2)}, u32[]{:S(2)}) collective-permute-start(bf16[4,1,32,128]{3,2,1,0:T(8,128)(2,1)} %get-tuple-element.29), channel_id=1, source_target_pairs={{1,0},{2,1},{3,2},{4,3},{5,4},{6,5},{7,6},{8,7},{9,8},{10,9},{11,1... | collective-permute-start | bytes 98312 | tf_op jit(solution)/shard_map/ppermute | solution.py:54
  11.0 7.0 %copy-start.4 = (f32[192,128]{1,0:T(8,128)S(1)}, f32[192,128]{1,0:T(8,128)}, u32[]{:S(2)}) copy-start(f32[192,128]{1,0:T(8,128)} %slice.159) | copy-start | bytes 294916
  11.9 6.0 %collective-permute-start.8 = (f32[224,128]{1,0:T(8,128)S(1)}, f32[224,128]{1,0:T(8,128)S(1)}, u32[]{:S(2)}, u32[]{:S(2)}) collective-permute-start(f32[224,128]{1,0:T(8,128)S(1)} %pad_maximum_fusion.5), channel_id=1, source_target_pairs={{0,16},{16,0},{32,48},{48,32},{64,80},{80,64},{96,112},{112,96},{1... | collective-permute-start | bytes 344072 | tf_op jit(solution)/shard_map/ppermute | solution.py:24
  12.2 6.3 %collective-permute-start.14 = (bf16[1,10,32,128]{3,2,1,0:T(8,128)(2,1)S(1)}, bf16[1,10,32,128]{3,2,1,0:T(8,128)(2,1)S(1)}, u32[]{:S(2)}, u32[]{:S(2)}) collective-permute-start(bf16[1,10,32,128]{3,2,1,0:T(8,128)(2,1)S(1)} %get-tuple-element.26), channel_id=1, source_target_pairs={{16,0},{32,16},{48,32},{64,48},{80,64},{96,80},{112,96},{128,112},... | collective-permute-start | bytes 245768 | tf_op jit(solution)/shard_map/ppermute | solution.py:54
  16.0 5.9 %collective-permute-start.15 = (bf16[1,10,32,128]{3,2,1,0:T(8,128)(2,1)S(1)}, bf16[1,10,32,128]{3,2,1,0:T(8,128)(2,1)S(1)}, u32[]{:S(2)}, u32[]{:S(2)}) collective-permute-start(bf16[1,10,32,128]{3,2,1,0:T(8,128)(2,1)S(1)} %get-tuple-element.27), channel_id=1, source_target_pairs={{0,16},{16,32},{32,48},{48,64},{64,80},{80,96},{96,112},{112,128},... | collective-permute-start | bytes 245768 | tf_op jit(solution)/shard_map/ppermute | solution.py:52
  18.0 12.6 %collective-permute-start.9 = (f32[224,128]{1,0:T(8,128)S(1)}, f32[224,128]{1,0:T(8,128)S(1)}, u32[]{:S(2)}, u32[]{:S(2)}) collective-permute-start(f32[224,128]{1,0:T(8,128)S(1)} %fusion.34), channel_id=1, source_target_pairs={{0,32},{16,48},{32,0},{48,16},{64,96},{80,112},{96,64},{112,80},{1... | collective-permute-start | bytes 344072 | tf_op jit(solution)/shard_map/ppermute | solution.py:24
  30.6 11.7 %copy-start.2 = (f32[4,8,32,128,1]{3,2,4,1,0:T(8,128)}, f32[4,8,32,128,1]{3,2,4,1,0:T(8,128)S(1)}, u32[]{:S(2)}) copy-start(f32[4,8,32,128,1]{3,2,4,1,0:T(8,128)S(1)} %fusion.43) | copy-start | bytes 1572868
  30.6 7.0 %collective-permute-start.10 = (f32[224,128]{1,0:T(8,128)S(1)}, f32[224,128]{1,0:T(8,128)S(1)}, u32[]{:S(2)}, u32[]{:S(2)}) collective-permute-start(f32[224,128]{1,0:T(8,128)S(1)} %add.96), channel_id=1, source_target_pairs={{0,64},{16,80},{32,96},{48,112},{64,0},{80,16},{96,32},{112,48},{1... | collective-permute-start | bytes 344072 | tf_op jit(solution)/shard_map/ppermute | solution.py:24
  37.6 9.4 %collective-permute-start.11 = (f32[224,128]{1,0:T(8,128)S(1)}, f32[224,128]{1,0:T(8,128)S(1)}, u32[]{:S(2)}, u32[]{:S(2)}) collective-permute-start(f32[224,128]{1,0:T(8,128)S(1)} %add.97), channel_id=1, source_target_pairs={{0,128},{16,144},{32,160},{48,176},{64,192},{80,208},{96,224},{112... | collective-permute-start | bytes 344072 | tf_op jit(solution)/shard_map/ppermute | solution.py:24
  47.1 5.2 %collective-permute-start.16 = (f32[280,128]{1,0:T(8,128)S(1)}, f32[280,128]{1,0:T(8,128)S(1)}, u32[]{:S(2)}, u32[]{:S(2)}) collective-permute-start(f32[280,128]{1,0:T(8,128)S(1)} %pad_maximum_fusion.4), channel_id=1, source_target_pairs={{0,1},{1,0},{2,3},{3,2},{4,5},{5,4},{6,7},{7,6},{8,9},{9,8},{10,11... | collective-permute-start | bytes 430088 | tf_op jit(solution)/shard_map/ppermute | solution.py:24
  52.3 6.7 %collective-permute-start.17 = (f32[280,128]{1,0:T(8,128)S(1)}, f32[280,128]{1,0:T(8,128)S(1)}, u32[]{:S(2)}, u32[]{:S(2)}) collective-permute-start(f32[280,128]{1,0:T(8,128)S(1)} %fusion.35), channel_id=1, source_target_pairs={{0,2},{1,3},{2,0},{3,1},{4,6},{5,7},{6,4},{7,5},{8,10},{9,11},{10,... | collective-permute-start | bytes 430088 | tf_op jit(solution)/shard_map/ppermute | solution.py:24
  59.0 6.4 %collective-permute-start.18 = (f32[280,128]{1,0:T(8,128)S(1)}, f32[280,128]{1,0:T(8,128)S(1)}, u32[]{:S(2)}, u32[]{:S(2)}) collective-permute-start(f32[280,128]{1,0:T(8,128)S(1)} %add.100), channel_id=1, source_target_pairs={{0,4},{1,5},{2,6},{3,7},{4,0},{5,1},{6,2},{7,3},{8,12},{9,13},{10,... | collective-permute-start | bytes 430088 | tf_op jit(solution)/shard_map/ppermute | solution.py:24
  65.4 6.7 %collective-permute-start.19 = (f32[280,128]{1,0:T(8,128)S(1)}, f32[280,128]{1,0:T(8,128)S(1)}, u32[]{:S(2)}, u32[]{:S(2)}) collective-permute-start(f32[280,128]{1,0:T(8,128)S(1)} %add.101), channel_id=1, source_target_pairs={{0,8},{1,9},{2,10},{3,11},{4,12},{5,13},{6,14},{7,15},{8,0},{9,1},... | collective-permute-start | bytes 430088 | tf_op jit(solution)/shard_map/ppermute | solution.py:24
  72.1 1.3 %collective-permute-start.20 = (f32[56,128]{1,0:T(8,128)S(1)}, f32[56,128]{1,0:T(8,128)S(1)}, u32[]{:S(2)}, u32[]{:S(2)}) collective-permute-start(f32[56,128]{1,0:T(8,128)S(1)} %slice.171), channel_id=1, source_target_pairs={{0,16},{16,0},{32,48},{48,32},{64,80},{80,64},{96,112},{112,96},{1... | collective-permute-start | bytes 86024 | tf_op jit(solution)/shard_map/ppermute | solution.py:24
  73.4 3.9 %collective-permute-start.21 = (f32[56,128]{1,0:T(8,128)S(1)}, f32[56,128]{1,0:T(8,128)S(1)}, u32[]{:S(2)}, u32[]{:S(2)}) collective-permute-start(f32[56,128]{1,0:T(8,128)S(1)} %slice_add_fusion), channel_id=1, source_target_pairs={{0,32},{16,48},{32,0},{48,16},{64,96},{80,112},{96,64},{112,80},{1... | collective-permute-start | bytes 86024 | tf_op jit(solution)/shard_map/ppermute | solution.py:24
  77.3 6.2 %collective-permute-start.22 = (f32[56,128]{1,0:T(8,128)S(1)}, f32[56,128]{1,0:T(8,128)S(1)}, u32[]{:S(2)}, u32[]{:S(2)}) collective-permute-start(f32[56,128]{1,0:T(8,128)S(1)} %add.104), channel_id=1, source_target_pairs={{0,64},{16,80},{32,96},{48,112},{64,0},{80,16},{96,32},{112,48},{1... | collective-permute-start | bytes 86024 | tf_op jit(solution)/shard_map/ppermute | solution.py:24
  83.5 7.8 %collective-permute-start.23 = (f32[56,128]{1,0:T(8,128)S(1)}, f32[56,128]{1,0:T(8,128)S(1)}, u32[]{:S(2)}, u32[]{:S(2)}) collective-permute-start(f32[56,128]{1,0:T(8,128)S(1)} %add.105), channel_id=1, source_target_pairs={{0,128},{16,144},{32,160},{48,176},{64,192},{80,208},{96,224},{112... | collective-permute-start | bytes 86024 | tf_op jit(solution)/shard_map/ppermute | solution.py:24
  94.6 10.4 %copy-start.5 = (f32[192,32]{0,1:T(8,128)}, f32[192,32]{0,1:T(8,128)S(1)}, u32[]{:S(2)}) copy-start(f32[192,32]{0,1:T(8,128)S(1)} %get-tuple-element.30) | copy-start | bytes 73732
  105.0 0.8 copy-start.3

commit v5 on v4

--- a/solution.py
+++ b/solution.py
@@ -25,19 +25,40 @@
     return x
 
 
+def exchange(x, axis, step):
+    count = lax.axis_size(axis)
+    return lax.ppermute(x, axis, [(i, i ^ step) for i in range(count)])
+
+
+def upper_bit(axis, step):
+    return (lax.axis_index(axis) // step) % 2 == 1
+
+
+def halve(x, axis, step):
+    half = x.shape[0] // 2
+    lo, hi = x[:half], x[half:]
+    bit = upper_bit(axis, step)
+    return jnp.where(bit, hi, lo) + exchange(jnp.where(bit, lo, hi), axis, step)
+
+
+def join(mine, other, axis, step):
+    return jnp.where(
+        upper_bit(axis, step),
+        jnp.concatenate([other, mine], axis=0),
+        jnp.concatenate([mine, other], axis=0),
+    )
+
+
 def pack_symmetric(g):
     return jnp.concatenate([g[:, :BLK], g[BLK:, BLK:].reshape(-1, BLK)], axis=0)
 
 
-def apply_symmetric(packed, x):
+def unpack_symmetric(packed):
     tail = KEEP - BLK
     upper, lower = packed[:BLK], packed[BLK:KEEP]
     corner = packed[KEEP:].reshape(tail, tail)
-    head, rest = x[:BLK], x[BLK:]
     return jnp.concatenate(
-        [mm("pq,qv->pv", upper, head) + mm("qp,qv->pv", lower, rest),
-         mm("pq,qv->pv", lower, head) + mm("pq,qv->pv", corner, rest)],
-        axis=0,
+        [jnp.concatenate([upper, lower.T], axis=1), jnp.concatenate([lower, corner], axis=1)], axis=0
     )
 
 
@@ -70,9 +91,12 @@
     total_rows = elements * BLK * lax.axis_size("rad") * lax.axis_size("azi")
     kept_flat = kept.reshape(elements, KEEP, BLK)
     steps = rounds()
-    ahead = 4
+    radial = [step for axis, step in steps if axis == "rad"]
+    around = [("azi", step) for axis, step in steps if axis == "azi"]
 
-    kept_gram = all_sum(pack_symmetric(mm("epi,eqi->pq", kept_flat, kept_flat)), steps[:ahead])
+    kept_gram = pack_symmetric(mm("epi,eqi->pq", kept_flat, kept_flat))
+    for step in radial:
+        kept_gram = halve(kept_gram, "rad", step)
 
     widened = with_halo(new_block, (("azi", 1),), 1, True)
     padded = with_halo(widened, (("rad", 0),), 1, False)
@@ -92,19 +116,24 @@
         [mm("epi,evi->pv", kept_flat, image), mm("evi,ewi->vw", image, image)], axis=0
     ).reshape(-1, BLK)
     split = kept_gram.shape[0]
-    joint = all_sum(jnp.concatenate([kept_gram, moments], axis=0), steps[ahead:])
-    kept_gram = joint[:split]
-    moments = all_sum(joint[split:], steps[:ahead]).reshape(KEEP + NEW, NEW)
+    joint = all_sum(jnp.concatenate([kept_gram, moments], axis=0), around)
+    kept_gram, moments = joint[:split], joint[split:]
+    for step in reversed(radial):
+        other = exchange(jnp.concatenate([kept_gram, moments], axis=0), "rad", step)
+        moments = moments + other[kept_gram.shape[0]:]
+        kept_gram = join(kept_gram, other[: kept_gram.shape[0]], "rad", step)
+    kept_gram = unpack_symmetric(kept_gram)
+    moments = moments.reshape(KEEP + NEW, NEW)
     first, image_gram = moments[:KEEP], moments[KEEP:]
 
-    second = first - apply_symmetric(kept_gram, first)
+    second = first - mm("pq,qv->pv", kept_gram, first)
     coefficients = first + second
     twice = image - mm("epi,pv->evi", kept_flat, coefficients)
 
     cross = mm("pv,pw->vw", coefficients, first)
     expanded = (
         image_gram - cross - cross.T
-        + mm("pv,pw->vw", coefficients, apply_symmetric(kept_gram, coefficients))
+        + mm("pv,pw->vw", coefficients, mm("pq,qw->pw", kept_gram, coefficients))
     ) / total_rows
     eye = jnp.eye(NEW, dtype=jnp.float32)
     kept_share = jnp.sum(expanded * eye, axis=1) * 16.0 >= jnp.sum(image_gram * eye, axis=1) / total_rows

time: 116 us -> 112 us (0.966)
  the two profiles are of different devices: /device:TPU:32 before, /device:TPU:1 now
where the time goes in v5:
time: 112 us; the launch traced here: 111 us
  starting transfers between devices  33.9 us (30%)
  waiting for transfers between devices  33.1 us (30%)
  matrix products  18.8 us (17%)
  other arithmetic  17.7 us (16%)
  local copies, waits for them, and re-layouts  5.4 us (5%)
  between operations  2.27 us (2%)
    ppermute x8, starting transfers between devices, exchange(): return lax.ppermute(x, axis, [(i, i ^ step) for i in range(count)])  17.9 us
    ppermute x8, waiting for transfers between devices, exchange(): return lax.ppermute(x, axis, [(i, i ^ step) for i in range(count)])  17.5 us
    ppermute x4, waiting for transfers between devices, all_sum(): x = x + lax.ppermute(x, axis, [(i, i ^ step) for i in range(count)])  12 us
    dot_general x8, matrix products, mm(): jnp.einsum(spec, a, b, precision=lax.Precision.HIGHEST, preferred_element...  11.9 us
    ppermute x2, starting transfers between devices, with_halo(): lax.ppermute(head, axis, [((i + 1) % count, i) for i in range(ends)])  7.86 us
    ppermute x2, starting transfers between devices, with_halo(): lax.ppermute(tail, axis, [(i, (i + 1) % count) for i in range(ends)])  5.13 us
    dot_general x1, matrix products, on_device(): jnp.einsum('rakij,rakvj->ravi', jacobian, picked, preferred_element_type=...  4.38 us
    eq x3, other arithmetic, on_device(): pick = jnp.where(code == c, shifted[c], pick)  4.06 us
  transfers between devices with their start and end apart: 16, of which 11 were waited for; matrix products, arithmetic and copies ran while one was open for 8% of the time, Pallas kernels for 0%

profile of v5, /device:TPU:1, one launch (start us, length us, event | category | flops | bytes accessed | tf_op | source)
XLA Modules:
  0.0 111.1 jit_solution(14382081012778229318)
XLA Ops:
  0.6 1.6 %fusion.26 = (bf16[4,1,32,128]{3,2,1,0:T(8,128)(2,1)}, bf16[4,1,32,128]{3,2,1,0:T(8,128)(2,1)}) fusion(bf16[4,8,32,128]{3,2,1,0:T(8,128)(2,1)} %param.7), kind=kLoop, calls=%fused_computation.126 | loop fusion | bytes 131072 | tf_op jit(solution)/shard_map/slice | solution.py:70
  2.2 5.8 %collective-permute-start.13 = (bf16[4,1,32,128]{3,2,1,0:T(8,128)(2,1)}, bf16[4,1,32,128]{3,2,1,0:T(8,128)(2,1)S(1)}, u32[]{:S(2)}, u32[]{:S(2)}) collective-permute-start(bf16[4,1,32,128]{3,2,1,0:T(8,128)(2,1)} %get-tuple-element.24), channel_id=1, source_target_pairs={{1,0},{2,1},{3,2},{4,3},{5,4},{6,5},{7,6},{8,7},{9,8},{10,9},{11,1... | collective-permute-start | bytes 98312 | tf_op jit(solution)/shard_map/ppermute | solution.py:75
  8.0 2.7 %convolution_bitcast_fusion.2 = f32[192,192]{1,0:T(8,128)S(1)} fusion(f32[4,8,192,128]{3,2,1,0:T(8,128)S(1)} %copy-done), kind=kOutput, calls=%fused_computation.4 | convolution fusion | flops 1811939328 | bytes 3293184 | tf_op jit(solution)/shard_map/epi,eqi->pq/dot_general | solution.py:83
  18.9 1.7 %collective-permute-start.9 = (f32[56,128]{1,0:T(8,128)S(1)}, f32[56,128]{1,0:T(8,128)S(1)}, u32[]{:S(2)}, u32[]{:S(2)}) collective-permute-start(f32[56,128]{1,0:T(8,128)S(1)} %slice_select_fusion.1), channel_id=1, source_target_pairs={{0,32},{16,48},{32,0},{48,16},{64,96},{80,112},{96,64},{112,80},{1... | collective-permute-start | bytes 86024 | tf_op jit(solution)/shard_map/ppermute | solution.py:30
  21.9 3.1 %collective-permute-start.10 = (f32[28,128]{1,0:T(8,128)S(1)}, f32[28,128]{1,0:T(8,128)S(1)}, u32[]{:S(2)}, u32[]{:S(2)}) collective-permute-start(f32[28,128]{1,0:T(8,128)S(1)} %slice_select_fusion.2), channel_id=1, source_target_pairs={{0,64},{16,80},{32,96},{48,112},{64,0},{80,16},{96,32},{112,48},{1... | collective-permute-start | bytes 43016 | tf_op jit(solution)/shard_map/ppermute | solution.py:30
  26.2 6.2 %collective-permute-start.11 = (f32[14,128]{1,0:T(8,128)S(1)}, f32[14,128]{1,0:T(8,128)S(1)}, u32[]{:S(2)}, u32[]{:S(2)}) collective-permute-start(f32[14,128]{1,0:T(8,128)S(1)} %slice_select_fusion.3), channel_id=1, source_target_pairs={{0,128},{16,144},{32,160},{48,176},{64,192},{80,208},{96,224},{112... | collective-permute-start | bytes 21512 | tf_op jit(solution)/shard_map/ppermute | solution.py:30
  32.4 5.1 %collective-permute-start.15 = (bf16[1,10,32,128]{3,2,1,0:T(8,128)(2,1)S(1)}, bf16[1,10,32,128]{3,2,1,0:T(8,128)(2,1)S(1)}, u32[]{:S(2)}, u32[]{:S(2)}) collective-permute-start(bf16[1,10,32,128]{3,2,1,0:T(8,128)(2,1)S(1)} %get-tuple-element.22), channel_id=1, source_target_pairs={{0,16},{16,32},{32,48},{48,64},{64,80},{80,96},{96,112},{112,128},... | collective-permute-start | bytes 245768 | tf_op jit(solution)/shard_map/ppermute | solution.py:73
  37.5 2.1 %collective-permute-start.14 = (bf16[1,10,32,128]{3,2,1,0:T(8,128)(2,1)S(1)}, bf16[1,10,32,128]{3,2,1,0:T(8,128)(2,1)S(1)}, u32[]{:S(2)}, u32[]{:S(2)}) collective-permute-start(bf16[1,10,32,128]{3,2,1,0:T(8,128)(2,1)S(1)} %get-tuple-element.21), channel_id=1, source_target_pairs={{16,0},{32,16},{48,32},{64,48},{80,64},{96,80},{112,96},{128,112},... | collective-permute-start | bytes 245768 | tf_op jit(solution)/shard_map/ppermute | solution.py:75
  39.6 3.6 %collective-permute-done.14 = bf16[1,10,32,128]{3,2,1,0:T(8,128)(2,1)S(1)} collective-permute-done((bf16[1,10,32,128]{3,2,1,0:T(8,128)(2,1)S(1)}, bf16[1,10,32,128]{3,2,1,0:T(8,128)(2,1)S(1)}, u32[]{:S(2)}, u32[]{:S(2)}) %collective-permute-start.14) | collective-permute-done | bytes 81952 | tf_op jit(solution)/shard_map/ppermute | solution.py:75
  48.2 4.4 %fusion.28 = f32[4,8,32,128,1]{3,2,4,1,0:T(8,128)S(1)} fusion(bf16[4,8,5,32,128]{4,3,2,1,0:T(8,128)(2,1)S(1)} %bitcast_dynamic-update-slice_fusion.4, bf16[4,8,5,128,128]{4,3,2,1,0:T(8,128)(2,1)} %param.6), kind=kOutput, calls=%fused_computation.128 | convolution fusion | flops 167772160 | bytes 7077888 | tf_op jit(solution)/shard_map/rakij,rakvj->ravi/dot_general | solution.py:112
  53.2 2.9 %convolution_bitcast_fusion.3 = f32[192,32]{0,1:T(8,128)S(1)} fusion(f32[4,8,192,128]{3,2,1,0:T(8,128)S(1)} %copy-done, f32[4,8,32,128,1]{3,2,4,1,0:T(8,128)S(1)} %fusion.28), kind=kOutput, calls=%fused_computation.5 | convolution fusion | flops 301989888 | bytes 3694592 | tf_op jit(solution)/shard_map/epi,evi->pv/dot_general | solution.py:83
  56.5 2.8 %collective-permute-done.16 = f32[70,128]{1,0:T(8,128)S(1)} collective-permute-done((f32[70,128]{1,0:T(8,128)S(1)}, f32[70,128]{1,0:T(8,128)S(1)}, u32[]{:S(2)}, u32[]{:S(2)}) %collective-permute-start.16) | collective-permute-done | bytes 35872 | tf_op jit(solution)/shard_map/ppermute | solution.py:24
  59.3 1.5 %collective-permute-start.17 = (f32[70,128]{1,0:T(8,128)S(1)}, f32[70,128]{1,0:T(8,128)S(1)}, u32[]{:S(2)}, u32[]{:S(2)}) collective-permute-start(f32[70,128]{1,0:T(8,128)S(1)} %fusion.20), channel_id=1, source_target_pairs={{0,2},{1,3},{2,0},{3,1},{4,6},{5,7},{6,4},{7,5},{8,10},{9,11},{10,... | collective-permute-start | bytes 107528 | tf_op jit(solution)/shard_map/ppermute | solution.py:24
  60.8 2.9 %collective-permute-done.17 = f32[70,128]{1,0:T(8,128)S(1)} collective-permute-done((f32[70,128]{1,0:T(8,128)S(1)}, f32[70,128]{1,0:T(8,128)S(1)}, u32[]{:S(2)}, u32[]{:S(2)}) %collective-permute-start.17) | collective-permute-done | bytes 35872 | tf_op jit(solution)/shard_map/ppermute | solution.py:24
  63.7 3.3 %collective-permute-done.18 = f32[70,128]{1,0:T(8,128)S(1)} collective-permute-done((f32[70,128]{1,0:T(8,128)S(1)}, f32[70,128]{1,0:T(8,128)S(1)}, u32[]{:S(2)}, u32[]{:S(2)}) %collective-permute-start.18) | collective-permute-done | bytes 35872 | tf_op jit(solution)/shard_map/ppermute | solution.py:24
  68.4 2.9 %collective-permute-done.19 = f32[70,128]{1,0:T(8,128)S(1)} collective-permute-done((f32[70,128]{1,0:T(8,128)S(1)}, f32[70,128]{1,0:T(8,128)S(1)}, u32[]{:S(2)}, u32[]{:S(2)}) %collective-permute-start.19) | collective-permute-done | bytes 35872 | tf_op jit(solution)/shard_map/ppermute | solution.py:24
  71.4 7.1 %collective-permute-done.20 = f32[70,128]{1,0:T(8,128)S(1)} collective-permute-done((f32[70,128]{1,0:T(8,128)S(1)}, f32[70,128]{1,0:T(8,128)S(1)}, u32[]{:S(2)}, u32[]{:S(2)}) %collective-permute-start.20) | collective-permute-done | bytes 35872 | tf_op jit(solution)/shard_map/ppermute | solution.py:30
  79.1 3.9 %collective-permute-done.21 = f32[84,128]{1,0:T(8,128)S(1)} collective-permute-done((f32[84,128]{1,0:T(8,128)S(1)}, f32[84,128]{1,0:T(8,128)S(1)}, u32[]{:S(2)}, u32[]{:S(2)}) %collective-permute-start.21) | collective-permute-done | bytes 43040 | tf_op jit(solution)/shard_map/ppermute | solution.py:30
  83.2 3.2 %collective-permute-done.22 = f32[112,128]{1,0:T(8,128)S(1)} collective-permute-done((f32[112,128]{1,0:T(8,128)S(1)}, f32[112,128]{1,0:T(8,128)S(1)}, u32[]{:S(2)}, u32[]{:S(2)}) %collective-permute-start.22) | collective-permute-done | bytes 57376 | tf_op jit(solution)/shard_map/ppermute | solution.py:30
  86.4 5.2 %collective-permute-start.23 = (f32[168,128]{1,0:T(8,128)S(1)}, f32[168,128]{1,0:T(8,128)S(1)}, u32[]{:S(2)}, u32[]{:S(2)}) collective-permute-start(f32[168,128]{1,0:T(8,128)S(1)} %pad_maximum_fusion.4), channel_id=1, source_target_pairs={{0,16},{16,0},{32,48},{48,32},{64,80},{80,64},{96,112},{112,96},{1... | collective-permute-start | bytes 258056 | tf_op jit(solution)/shard_map/ppermute | solution.py:30
  97.3 3.0 %fusion = f32[32,32,128]{2,1,0:T(8,128)S(1)} fusion(f32[32,32,128]{2,1,0:T(8,128)} %bitcast.185, f32[32,192,128]{2,1,0:T(8,128)S(1)} %bitcast.184, f32[192,32]{0,1:T(8,128)S(1)} %fusion.1), kind=kOutput, calls=%fused_computation.3 | convolution fusion | flops 302120960 | bytes 4218880 | tf_op jit(solution)/shard_map/epi,pv->evi/dot_general | solution.py:83
  101.2 2.9 %cholesky.17 = f32[32,32]{1,0:T(8,128)S(1)} custom-call(f32[32,32]{1,0:T(8,128)S(1)} %fusion.16), custom_call_target="Cholesky" | custom-call | tf_op jit(solution)/shard_map/jit(cholesky)/cholesky | solution.py:145
  105.5 2.4 %custom-call.6 = f32[1,32,32]{1,2,0:T(8,128)S(1)} custom-call(f32[1,32,32]{2,1,0:T(8,128)S(1)} %get-tuple-element.30), custom_call_target="InvertDiagBlocksLowerTriangular" | custom-call | tf_op jit(solution)/shard_map/triangular_solve | solution.py:147
  107.9 2.5 %fusion.3 = f32[32,32,128]{2,0,1:T(8,128)} fusion(f32[1,32,32]{1,2,0:T(8,128)S(1)} %custom-call.6, f32[32,32,128]{2,1,0:T(8,128)} %copy-done.3), kind=kOutput, calls=%fused_computation.16 | convolution fusion | flops 50331648 | bytes 1052672 | tf_op jit(solution)/shard_map/triangular_solve | solution.py:147
  (174 shorter events, 25.9 us)
Async XLA Ops:
  2.2 22.8 %collective-permute-start.13 = (bf16[4,1,32,128]{3,2,1,0:T(8,128)(2,1)}, bf16[4,1,32,128]{3,2,1,0:T(8,128)(2,1)S(1)}, u32[]{:S(2)}, u32[]{:S(2)}) collective-permute-start(bf16[4,1,32,128]{3,2,1,0:T(8,128)(2,1)} %get-tuple-element.24), channel_id=1, source_target_pairs={{1,0},{2,1},{3,2},{4,3},{5,4},{6,5},{7,6},{8,7},{9,8},{10,9},{11,1... | collective-permute-start | bytes 98312 | tf_op jit(solution)/shard_map/ppermute | solution.py:75
  8.0 10.1 %collective-permute-start.12 = (bf16[4,1,32,128]{3,2,1,0:T(8,128)(2,1)}, bf16[4,1,32,128]{3,2,1,0:T(8,128)(2,1)S(1)}, u32[]{:S(2)}, u32[]{:S(2)}) collective-permute-start(bf16[4,1,32,128]{3,2,1,0:T(8,128)(2,1)} %get-tuple-element.23), channel_id=1, source_target_pairs={{0,1},{1,2},{2,3},{3,4},{4,5},{5,6},{6,7},{7,8},{8,9},{9,10},{10,1... | collective-permute-start | bytes 98312 | tf_op jit(solution)/shard_map/ppermute | solution.py:73
  12.9 5.2 %collective-permute-start.8 = (f32[112,128]{1,0:T(8,128)S(1)}, f32[112,128]{1,0:T(8,128)}, u32[]{:S(2)}, u32[]{:S(2)}) collective-permute-start(f32[112,128]{1,0:T(8,128)S(1)} %slice_select_fusion), channel_id=1, source_target_pairs={{0,16},{16,0},{32,48},{48,32},{64,80},{80,64},{96,112},{112,96},{1... | collective-permute-start | bytes 172040 | tf_op jit(solution)/shard_map/ppermute | solution.py:30
  18.0 25.3 %copy-start.34 = (pred[4,8]{1,0:T(4,128)(4,1)S(1)}, pred[4,8]{1,0:T(4,128)(4,1)}, u32[]{:S(2)}) copy-start(pred[4,8]{1,0:T(4,128)(4,1)} %get-tuple-element.32) | copy-start | bytes 100
  18.0 25.3 %copy-start.35 = (pred[4,8]{1,0:T(4,128)(4,1)S(1)}, pred[4,8]{1,0:T(4,128)(4,1)}, u32[]{:S(2)}) copy-start(pred[4,8]{1,0:T(4,128)(4,1)} %get-tuple-element.33) | copy-start | bytes 100
  18.0 25.3 %copy-start.36 = (pred[4,8]{1,0:T(4,128)(4,1)S(1)}, pred[4,8]{1,0:T(4,128)(4,1)}, u32[]{:S(2)}) copy-start(pred[4,8]{1,0:T(4,128)(4,1)} %get-tuple-element.34) | copy-start | bytes 100
  18.0 25.3 %copy-start.37 = (pred[4,8]{1,0:T(4,128)(4,1)S(1)}, pred[4,8]{1,0:T(4,128)(4,1)}, u32[]{:S(2)}) copy-start(pred[4,8]{1,0:T(4,128)(4,1)} %get-tuple-element.35) | copy-start | bytes 100
  18.0 25.3 %copy-start.38 = (pred[4,8]{1,0:T(4,128)(4,1)S(1)}, pred[4,8]{1,0:T(4,128)(4,1)}, u32[]{:S(2)}) copy-start(pred[4,8]{1,0:T(4,128)(4,1)} %get-tuple-element.36) | copy-start | bytes 100
  18.0 25.3 %copy-start.39 = (pred[4,8]{1,0:T(4,128)(4,1)S(1)}, pred[4,8]{1,0:T(4,128)(4,1)}, u32[]{:S(2)}) copy-start(pred[4,8]{1,0:T(4,128)(4,1)} %get-tuple-element.37) | copy-start | bytes 100
  18.0 25.3 %copy-start.40 = (pred[4,8]{1,0:T(4,128)(4,1)S(1)}, pred[4,8]{1,0:T(4,128)(4,1)}, u32[]{:S(2)}) copy-start(pred[4,8]{1,0:T(4,128)(4,1)} %get-tuple-element.38) | copy-start | bytes 100
  18.0 25.3 %copy-start.43 = (pred[4,8]{1,0:T(4,128)(4,1)S(1)}, pred[4,8]{1,0:T(4,128)(4,1)}, u32[]{:S(2)}) copy-start(pred[4,8]{1,0:T(4,128)(4,1)} %get-tuple-element.70) | copy-start | bytes 100
  18.9 3.0 %collective-permute-start.9 = (f32[56,128]{1,0:T(8,128)S(1)}, f32[56,128]{1,0:T(8,128)S(1)}, u32[]{:S(2)}, u32[]{:S(2)}) collective-permute-start(f32[56,128]{1,0:T(8,128)S(1)} %slice_select_fusion.1), channel_id=1, source_target_pairs={{0,32},{16,48},{32,0},{48,16},{64,96},{80,112},{96,64},{112,80},{1... | collective-permute-start | bytes 86024 | tf_op jit(solution)/shard_map/ppermute | solution.py:30
  21.9 4.2 %collective-permute-start.10 = (f32[28,128]{1,0:T(8,128)S(1)}, f32[28,128]{1,0:T(8,128)S(1)}, u32[]{:S(2)}, u32[]{:S(2)}) collective-permute-start(f32[28,128]{1,0:T(8,128)S(1)} %slice_select_fusion.2), channel_id=1, source_target_pairs={{0,64},{16,80},{32,96},{48,112},{64,0},{80,16},{96,32},{112,48},{1... | collective-permute-start | bytes 43016 | tf_op jit(solution)/shard_map/ppermute | solution.py:30
  26.2 13.5 %collective-permute-start.11 = (f32[14,128]{1,0:T(8,128)S(1)}, f32[14,128]{1,0:T(8,128)S(1)}, u32[]{:S(2)}, u32[]{:S(2)}) collective-permute-start(f32[14,128]{1,0:T(8,128)S(1)} %slice_select_fusion.3), channel_id=1, source_target_pairs={{0,128},{16,144},{32,160},{48,176},{64,192},{80,208},{96,224},{112... | collective-permute-start | bytes 21512 | tf_op jit(solution)/shard_map/ppermute | solution.py:30
  32.4 7.3 %collective-permute-start.15 = (bf16[1,10,32,128]{3,2,1,0:T(8,128)(2,1)S(1)}, bf16[1,10,32,128]{3,2,1,0:T(8,128)(2,1)S(1)}, u32[]{:S(2)}, u32[]{:S(2)}) collective-permute-start(bf16[1,10,32,128]{3,2,1,0:T(8,128)(2,1)S(1)} %get-tuple-element.22), channel_id=1, source_target_pairs={{0,16},{16,32},{32,48},{48,64},{64,80},{80,96},{96,112},{112,128},... | collective-permute-start | bytes 245768 | tf_op jit(solution)/shard_map/ppermute | solution.py:73
  37.5 5.8 %collective-permute-start.14 = (bf16[1,10,32,128]{3,2,1,0:T(8,128)(2,1)S(1)}, bf16[1,10,32,128]{3,2,1,0:T(8,128)(2,1)S(1)}, u32[]{:S(2)}, u32[]{:S(2)}) collective-permute-start(bf16[1,10,32,128]{3,2,1,0:T(8,128)(2,1)S(1)} %get-tuple-element.21), channel_id=1, source_target_pairs={{16,0},{32,16},{48,32},{64,48},{80,64},{96,80},{112,96},{128,112},... | collective-permute-start | bytes 245768 | tf_op jit(solution)/shard_map/ppermute | solution.py:75
  56.4 2.9 %collective-permute-start.16 = (f32[70,128]{1,0:T(8,128)S(1)}, f32[70,128]{1,0:T(8,128)S(1)}, u32[]{:S(2)}, u32[]{:S(2)}) collective-permute-start(f32[70,128]{1,0:T(8,128)S(1)} %pad_maximum_fusion.9), channel_id=1, source_target_pairs={{0,1},{1,0},{2,3},{3,2},{4,5},{5,4},{6,7},{7,6},{8,9},{9,8},{10,11... | collective-permute-start | bytes 107528 | tf_op jit(solution)/shard_map/ppermute | solution.py:24
  59.3 4.4 %collective-permute-start.17 = (f32[70,128]{1,0:T(8,128)S(1)}, f32[70,128]{1,0:T(8,128)S(1)}, u32[]{:S(2)}, u32[]{:S(2)}) collective-permute-start(f32[70,128]{1,0:T(8,128)S(1)} %fusion.20), channel_id=1, source_target_pairs={{0,2},{1,3},{2,0},{3,1},{4,6},{5,7},{6,4},{7,5},{8,10},{9,11},{10,... | collective-permute-start | bytes 107528 | tf_op jit(solution)/shard_map/ppermute | solution.py:24
  63.7 3.3 %collective-permute-start.18 = (f32[70,128]{1,0:T(8,128)S(1)}, f32[70,128]{1,0:T(8,128)S(1)}, u32[]{:S(2)}, u32[]{:S(2)}) collective-permute-start(f32[70,128]{1,0:T(8,128)S(1)} %add.107), channel_id=1, source_target_pairs={{0,4},{1,5},{2,6},{3,7},{4,0},{5,1},{6,2},{7,3},{8,12},{9,13},{10,... | collective-permute-start | bytes 107528 | tf_op jit(solution)/shard_map/ppermute | solution.py:24
  67.0 4.3 %collective-permute-start.19 = (f32[70,128]{1,0:T(8,128)S(1)}, f32[70,128]{1,0:T(8,128)S(1)}, u32[]{:S(2)}, u32[]{:S(2)}) collective-permute-start(f32[70,128]{1,0:T(8,128)S(1)} %add.108), channel_id=1, source_target_pairs={{0,8},{1,9},{2,10},{3,11},{4,12},{5,13},{6,14},{7,15},{8,0},{9,1},... | collective-permute-start | bytes 107528 | tf_op jit(solution)/shard_map/ppermute | solution.py:24
  71.4 7.1 %collective-permute-start.20 = (f32[70,128]{1,0:T(8,128)S(1)}, f32[70,128]{1,0:T(8,128)S(1)}, u32[]{:S(2)}, u32[]{:S(2)}) collective-permute-start(f32[70,128]{1,0:T(8,128)S(1)} %add.109), channel_id=1, source_target_pairs={{0,128},{16,144},{32,160},{48,176},{64,192},{80,208},{96,224},{112... | collective-permute-start | bytes 107528 | tf_op jit(solution)/shard_map/ppermute | solution.py:30
  78.5 4.6 %collective-permute-start.21 = (f32[84,128]{1,0:T(8,128)S(1)}, f32[84,128]{1,0:T(8,128)S(1)}, u32[]{:S(2)}, u32[]{:S(2)}) collective-permute-start(f32[84,128]{1,0:T(8,128)S(1)} %pad_maximum_fusion.8), channel_id=1, source_target_pairs={{0,64},{16,80},{32,96},{48,112},{64,0},{80,16},{96,32},{112,48},{1... | collective-permute-start | bytes 129032 | tf_op jit(solution)/shard_map/ppermute | solution.py:30
  83.1 3.3 %collective-permute-start.22 = (f32[112,128]{1,0:T(8,128)S(1)}, f32[112,128]{1,0:T(8,128)S(1)}, u32[]{:S(2)}, u32[]{:S(2)}) collective-permute-start(f32[112,128]{1,0:T(8,128)S(1)} %pad_maximum_fusion.6), channel_id=1, source_target_pairs={{0,32},{16,48},{32,0},{48,16},{64,96},{80,112},{96,64},{112,80},{1... | collective-permute-start | bytes 172040 | tf_op jit(solution)/shard_map/ppermute | solution.py:30
  86.4 6.1 %collective-permute-start.23 = (f32[168,128]{1,0:T(8,128)S(1)}, f32[168,128]{1,0:T(8,128)S(1)}, u32[]{:S(2)}, u32[]{:S(2)}) collective-permute-start(f32[168,128]{1,0:T(8,128)S(1)} %pad_maximum_fusion.4), channel_id=1, source_target_pairs={{0,16},{16,0},{32,48},{48,32},{64,80},{80,64},{96,112},{112,96},{1... | collective-permute-start | bytes 258056 | tf_op jit(solution)/shard_map/ppermute | solution.py:30
  (36 other events, 60.8 us)

commit v6 on v5

--- a/solution.py
+++ b/solution.py
@@ -94,12 +94,12 @@
     radial = [step for axis, step in steps if axis == "rad"]
     around = [("azi", step) for axis, step in steps if axis == "azi"]
 
-    kept_gram = pack_symmetric(mm("epi,eqi->pq", kept_flat, kept_flat))
-    for step in radial:
-        kept_gram = halve(kept_gram, "rad", step)
+    kept_gram = halve(pack_symmetric(mm("epi,eqi->pq", kept_flat, kept_flat)), "rad", radial[0])
 
     widened = with_halo(new_block, (("azi", 1),), 1, True)
     padded = with_halo(widened, (("rad", 0),), 1, False)
+    kept_gram, padded = lax.optimization_barrier((kept_gram, padded))
+    kept_gram = halve(kept_gram, "rad", radial[1])
     shifted = [padded[c // 3 : c // 3 + rows_r, c % 3 : c % 3 + rows_a] for c in range(9)]
     slots = []
     for k in range(5):
@@ -109,8 +109,12 @@
             pick = jnp.where(code == c, shifted[c], pick)
         slots.append(pick)
     picked = jnp.stack(slots, axis=2)
+    kept_gram, picked = lax.optimization_barrier((kept_gram, picked))
+    kept_gram = halve(kept_gram, "rad", radial[2])
     image = jnp.einsum("rakij,rakvj->ravi", jacobian, picked, preferred_element_type=jnp.float32)
     image = image.reshape(elements, NEW, BLK)
+    kept_gram, image = lax.optimization_barrier((kept_gram, image))
+    kept_gram = halve(kept_gram, "rad", radial[3])
 
     moments = jnp.concatenate(
         [mm("epi,evi->pv", kept_flat, image), mm("evi,ewi->vw", image, image)], axis=0

time: 112 us -> 105 us (0.938)
  other arithmetic: 17.7 us -> 14.3 us
  matrix products: 18.8 us -> 16.2 us
  waiting for transfers between devices: 33.1 us -> 31.6 us
    ppermute x8, waiting for transfers between devices: 17.5 us -> 13.6 us  [exchange(): return lax.ppermute(x, axis, [(i, i ^ step) for i in range(count)])]
    ppermute x8, starting transfers between devices: 17.9 us -> 21.1 us  [exchange(): return lax.ppermute(x, axis, [(i, i ^ step) for i in range(count)])]
    ppermute x4, starting transfers between devices: 2.94 us -> 0.19 us  [all_sum(): x = x + lax.ppermute(x, axis, [(i, i ^ step) for i in range(count)])]
    dot_general x1, matrix products: 4.38 us -> 1.89 us  [on_device(): jnp.einsum('rakij,rakvj->ravi', jacobian, picked, preferred_element_type=...]
    ppermute x4, waiting for transfers between devices: 12 us -> 14.4 us  [all_sum(): x = x + lax.ppermute(x, axis, [(i, i ^ step) for i in range(count)])]
    eq x3, other arithmetic: 4.06 us -> 1.88 us  [on_device(): pick = jnp.where(code == c, shifted[c], pick)]
    slice x1, local copies, waits for them, and re-layouts: 0.01 us -> 1.56 us  [with_halo(): head = lax.slice_in_dim(cells, 0, width, axis=dim)]
    slice x1, local copies, waits for them, and re-layouts: 1.55 us -> 0.01 us  [with_halo(): lax.slice_in_dim(cells, cells.shape[dim] - width, cells.shape[dim], axis=...]
  transfers between devices with their start and end apart: 16 -> 16, of which waited for: 11 -> 11; matrix products, arithmetic and copies ran while one was open for 8% -> 16% of each run, Pallas kernels for 0% -> 0%
where the time goes in v6:
time: 105 us
  starting transfers between devices  34.5 us (33%)
  waiting for transfers between devices  31.6 us (30%)
  matrix products  16.2 us (15%)
  other arithmetic  14.3 us (14%)
  local copies, waits for them, and re-layouts  5.85 us (6%)
  between operations  2.21 us (2%)
    ppermute x8, starting transfers between devices, exchange(): return lax.ppermute(x, axis, [(i, i ^ step) for i in range(count)])  21.1 us
    ppermute x4, waiting for transfers between devices, all_sum(): x = x + lax.ppermute(x, axis, [(i, i ^ step) for i in range(count)])  14.4 us
    ppermute x8, waiting for transfers between devices, exchange(): return lax.ppermute(x, axis, [(i, i ^ step) for i in range(count)])  13.6 us
    dot_general x8, matrix products, mm(): jnp.einsum(spec, a, b, precision=lax.Precision.HIGHEST, preferred_element...  11.9 us
    ppermute x2, starting transfers between devices, with_halo(): lax.ppermute(head, axis, [((i + 1) % count, i) for i in range(ends)])  7.68 us
    ppermute x2, starting transfers between devices, with_halo(): lax.ppermute(tail, axis, [(i, (i + 1) % count) for i in range(ends)])  5.54 us
    another operation x3, other arithmetic, on_device(): lower = jnp.linalg.cholesky(gram)  3.6 us
    unnamed x4, other arithmetic  2.98 us
  transfers between devices with their start and end apart: 16, of which 11 were waited for; matrix products, arithmetic and copies ran while one was open for 16% of the time, Pallas kernels for 0%

profile of v6, /device:TPU:1, one launch (start us, length us, event | category | flops | bytes accessed | tf_op | source)
XLA Modules:
  0.0 104.6 jit_solution(8919888873131531234)
XLA Ops:
  0.6 1.6 %fusion.19 = (bf16[4,1,32,128]{3,2,1,0:T(8,128)(2,1)}, bf16[4,1,32,128]{3,2,1,0:T(8,128)(2,1)}) fusion(bf16[4,8,32,128]{3,2,1,0:T(8,128)(2,1)} %param.7), kind=kLoop, calls=%fused_computation.112 | loop fusion | bytes 131072 | tf_op jit(solution)/shard_map/slice | solution.py:69
  2.2 5.8 %collective-permute-start.10 = (bf16[4,1,32,128]{3,2,1,0:T(8,128)(2,1)}, bf16[4,1,32,128]{3,2,1,0:T(8,128)(2,1)}, u32[]{:S(2)}, u32[]{:S(2)}) collective-permute-start(bf16[4,1,32,128]{3,2,1,0:T(8,128)(2,1)} %get-tuple-element.28), channel_id=1, source_target_pairs={{1,0},{2,1},{3,2},{4,3},{5,4},{6,5},{7,6},{8,7},{9,8},{10,9},{11,1... | collective-permute-start | bytes 98312 | tf_op jit(solution)/shard_map/ppermute | solution.py:75
  8.0 2.7 %convolution_bitcast_fusion.2 = f32[192,192]{1,0:T(8,128)S(1)} fusion(f32[4,8,192,128]{3,2,1,0:T(8,128)S(1)} %copy-done), kind=kOutput, calls=%fused_computation.7 | convolution fusion | flops 1811939328 | bytes 3293184 | tf_op jit(solution)/shard_map/epi,eqi->pq/dot_general | solution.py:83
  16.9 5.5 %collective-permute-start.11 = (bf16[1,10,32,128]{3,2,1,0:T(8,128)(2,1)S(1)}, bf16[1,10,32,128]{3,2,1,0:T(8,128)(2,1)S(1)}, u32[]{:S(2)}, u32[]{:S(2)}) collective-permute-start(bf16[1,10,32,128]{3,2,1,0:T(8,128)(2,1)S(1)} %get-tuple-element.26), channel_id=1, source_target_pairs={{0,16},{16,32},{32,48},{48,64},{64,80},{80,96},{96,112},{112,128},... | collective-permute-start | bytes 245768 | tf_op jit(solution)/shard_map/ppermute | solution.py:73
  22.5 1.9 %collective-permute-start.12 = (bf16[1,10,32,128]{3,2,1,0:T(8,128)(2,1)S(1)}, bf16[1,10,32,128]{3,2,1,0:T(8,128)(2,1)S(1)}, u32[]{:S(2)}, u32[]{:S(2)}) collective-permute-start(bf16[1,10,32,128]{3,2,1,0:T(8,128)(2,1)S(1)} %get-tuple-element.27), channel_id=1, source_target_pairs={{16,0},{32,16},{48,32},{64,48},{80,64},{96,80},{112,96},{128,112},... | collective-permute-start | bytes 245768 | tf_op jit(solution)/shard_map/ppermute | solution.py:75
  25.2 3.0 %collective-permute-done.12 = bf16[1,10,32,128]{3,2,1,0:T(8,128)(2,1)S(1)} collective-permute-done((bf16[1,10,32,128]{3,2,1,0:T(8,128)(2,1)S(1)}, bf16[1,10,32,128]{3,2,1,0:T(8,128)(2,1)S(1)}, u32[]{:S(2)}, u32[]{:S(2)}) %collective-permute-start.12) | collective-permute-done | bytes 81952 | tf_op jit(solution)/shard_map/ppermute | solution.py:75
  28.3 1.7 %collective-permute-start.13 = (f32[56,128]{1,0:T(8,128)S(1)}, f32[56,128]{1,0:T(8,128)S(1)}, u32[]{:S(2)}, u32[]{:S(2)}) collective-permute-start(f32[56,128]{1,0:T(8,128)S(1)} %slice_select_fusion.1), channel_id=1, source_target_pairs={{0,32},{16,48},{32,0},{48,16},{64,96},{80,112},{96,64},{112,80},{1... | collective-permute-start | bytes 86024 | tf_op jit(solution)/shard_map/ppermute | solution.py:30
  34.4 5.5 %collective-permute-start.14 = (f32[28,128]{1,0:T(8,128)S(1)}, f32[28,128]{1,0:T(8,128)S(1)}, u32[]{:S(2)}, u32[]{:S(2)}) collective-permute-start(f32[28,128]{1,0:T(8,128)S(1)} %slice_select_fusion.2), channel_id=1, source_target_pairs={{0,64},{16,80},{32,96},{48,112},{64,0},{80,16},{96,32},{112,48},{1... | collective-permute-start | bytes 43016 | tf_op jit(solution)/shard_map/ppermute | solution.py:30
  39.9 1.9 %fusion = f32[4,8,32,128,1]{3,2,0,1,4:T(8,128)S(1)} fusion(bf16[4,8,5,128,128]{4,3,2,1,0:T(8,128)(2,1)S(1)} %copy-done.38, bf16[4,8,5,32,128]{4,3,1,0,2:T(8,128)(2,1)S(1)} %bitcast_dynamic-update-slice_fusion), kind=kOutput, calls=%fused_computation.2 | convolution fusion | flops 167772160 | bytes 7077888 | tf_op jit(solution)/shard_map/rakij,rakvj->ravi/dot_general | solution.py:114
  44.0 2.9 %convolution_bitcast_fusion.3 = f32[192,32]{0,1:T(8,128)S(1)} fusion(f32[32,32,128]{2,1,0:T(8,128)S(1)} %bitcast.171, f32[32,192,128]{2,1,0:T(8,128)S(1)} %bitcast.168), kind=kOutput, calls=%fused_computation.8 | convolution fusion | flops 301989888 | bytes 3694592 | tf_op jit(solution)/shard_map/epi,evi->pv/dot_general | solution.py:83
  47.2 2.0 %collective-permute-done.15 = f32[14,128]{1,0:T(8,128)S(1)} collective-permute-done((f32[14,128]{1,0:T(8,128)S(1)}, f32[14,128]{1,0:T(8,128)S(1)}, u32[]{:S(2)}, u32[]{:S(2)}) %collective-permute-start.15) | collective-permute-done | bytes 7200 | tf_op jit(solution)/shard_map/ppermute | solution.py:30
  49.3 3.0 %collective-permute-done.16 = f32[70,128]{1,0:T(8,128)S(1)} collective-permute-done((f32[70,128]{1,0:T(8,128)S(1)}, f32[70,128]{1,0:T(8,128)S(1)}, u32[]{:S(2)}, u32[]{:S(2)}) %collective-permute-start.16) | collective-permute-done | bytes 35872 | tf_op jit(solution)/shard_map/ppermute | solution.py:24
  52.4 4.3 %collective-permute-done.17 = f32[70,128]{1,0:T(8,128)S(1)} collective-permute-done((f32[70,128]{1,0:T(8,128)S(1)}, f32[70,128]{1,0:T(8,128)S(1)}, u32[]{:S(2)}, u32[]{:S(2)}) %collective-permute-start.17) | collective-permute-done | bytes 35872 | tf_op jit(solution)/shard_map/ppermute | solution.py:24
  56.8 2.8 %collective-permute-done.18 = f32[70,128]{1,0:T(8,128)S(1)} collective-permute-done((f32[70,128]{1,0:T(8,128)S(1)}, f32[70,128]{1,0:T(8,128)S(1)}, u32[]{:S(2)}, u32[]{:S(2)}) %collective-permute-start.18) | collective-permute-done | bytes 35872 | tf_op jit(solution)/shard_map/ppermute | solution.py:24
  59.6 4.3 %collective-permute-done.19 = f32[70,128]{1,0:T(8,128)S(1)} collective-permute-done((f32[70,128]{1,0:T(8,128)S(1)}, f32[70,128]{1,0:T(8,128)S(1)}, u32[]{:S(2)}, u32[]{:S(2)}) %collective-permute-start.19) | collective-permute-done | bytes 35872 | tf_op jit(solution)/shard_map/ppermute | solution.py:24
  63.9 2.3 %collective-permute-start.20 = (f32[70,128]{1,0:T(8,128)S(1)}, f32[70,128]{1,0:T(8,128)S(1)}, u32[]{:S(2)}, u32[]{:S(2)}) collective-permute-start(f32[70,128]{1,0:T(8,128)S(1)} %add.109), channel_id=1, source_target_pairs={{0,128},{16,144},{32,160},{48,176},{64,192},{80,208},{96,224},{112... | collective-permute-start | bytes 107528 | tf_op jit(solution)/shard_map/ppermute | solution.py:30
  66.2 4.4 %collective-permute-done.20 = f32[70,128]{1,0:T(8,128)S(1)} collective-permute-done((f32[70,128]{1,0:T(8,128)S(1)}, f32[70,128]{1,0:T(8,128)S(1)}, u32[]{:S(2)}, u32[]{:S(2)}) %collective-permute-start.20) | collective-permute-done | bytes 35872 | tf_op jit(solution)/shard_map/ppermute | solution.py:30
  72.0 3.3 %collective-permute-done.21 = f32[84,128]{1,0:T(8,128)S(1)} collective-permute-done((f32[84,128]{1,0:T(8,128)S(1)}, f32[84,128]{1,0:T(8,128)S(1)}, u32[]{:S(2)}, u32[]{:S(2)}) %collective-permute-start.21) | collective-permute-done | bytes 43040 | tf_op jit(solution)/shard_map/ppermute | solution.py:30
  75.5 3.0 %collective-permute-done.22 = f32[112,128]{1,0:T(8,128)S(1)} collective-permute-done((f32[112,128]{1,0:T(8,128)S(1)}, f32[112,128]{1,0:T(8,128)S(1)}, u32[]{:S(2)}, u32[]{:S(2)}) %collective-permute-start.22) | collective-permute-done | bytes 57376 | tf_op jit(solution)/shard_map/ppermute | solution.py:30
  78.5 7.6 %collective-permute-start.23 = (f32[168,128]{1,0:T(8,128)S(1)}, f32[168,128]{1,0:T(8,128)S(1)}, u32[]{:S(2)}, u32[]{:S(2)}) collective-permute-start(f32[168,128]{1,0:T(8,128)S(1)} %pad_maximum_fusion.1), channel_id=1, source_target_pairs={{0,16},{16,0},{32,48},{48,32},{64,80},{80,64},{96,112},{112,96},{1... | collective-permute-start | bytes 258056 | tf_op jit(solution)/shard_map/ppermute | solution.py:30
  88.9 3.9 %fusion.3 = f32[32,32,128]{2,1,0:T(8,128)} fusion(f32[32,32,128]{2,1,0:T(8,128)} %bitcast.172, f32[32,192,128]{2,1,0:T(8,128)S(1)} %bitcast.169, f32[192,32]{0,1:T(8,128)S(1)} %fusion.4), kind=kOutput, calls=%fused_computation.6 | convolution fusion | flops 302120960 | bytes 4218880 | tf_op jit(solution)/shard_map/epi,pv->evi/dot_general | solution.py:83
  94.8 2.9 %cholesky.17 = f32[32,32]{1,0:T(8,128)S(1)} custom-call(f32[32,32]{1,0:T(8,128)S(1)} %fusion.13), custom_call_target="Cholesky" | custom-call | tf_op jit(solution)/shard_map/jit(cholesky)/cholesky | solution.py:149
  99.7 2.4 %custom-call.6 = f32[1,32,32]{1,2,0:T(8,128)S(1)} custom-call(f32[1,32,32]{2,1,0:T(8,128)S(1)} %get-tuple-element.35), custom_call_target="InvertDiagBlocksLowerTriangular" | custom-call | tf_op jit(solution)/shard_map/triangular_solve | solution.py:151
  102.2 2.5 %fusion.6 = f32[32,32,128]{2,0,1:T(8,128)} fusion(f32[1,32,32]{1,2,0:T(8,128)S(1)} %custom-call.6, f32[32,32,128]{2,1,0:T(8,128)} %fusion.3), kind=kOutput, calls=%fused_computation.15 | convolution fusion | flops 50331648 | bytes 1052672 | tf_op jit(solution)/shard_map/triangular_solve | solution.py:151
  (166 shorter events, 21.3 us)
Async XLA Ops:
  2.2 13.9 %collective-permute-start.10 = (bf16[4,1,32,128]{3,2,1,0:T(8,128)(2,1)}, bf16[4,1,32,128]{3,2,1,0:T(8,128)(2,1)}, u32[]{:S(2)}, u32[]{:S(2)}) collective-permute-start(bf16[4,1,32,128]{3,2,1,0:T(8,128)(2,1)} %get-tuple-element.28), channel_id=1, source_target_pairs={{1,0},{2,1},{3,2},{4,3},{5,4},{6,5},{7,6},{8,7},{9,8},{10,9},{11,1... | collective-permute-start | bytes 98312 | tf_op jit(solution)/shard_map/ppermute | solution.py:75
  8.0 6.4 %collective-permute-start.9 = (bf16[4,1,32,128]{3,2,1,0:T(8,128)(2,1)}, bf16[4,1,32,128]{3,2,1,0:T(8,128)(2,1)}, u32[]{:S(2)}, u32[]{:S(2)}) collective-permute-start(bf16[4,1,32,128]{3,2,1,0:T(8,128)(2,1)} %get-tuple-element.29), channel_id=1, source_target_pairs={{0,1},{1,2},{2,3},{3,4},{4,5},{5,6},{6,7},{7,8},{8,9},{9,10},{10,1... | collective-permute-start | bytes 98312 | tf_op jit(solution)/shard_map/ppermute | solution.py:73
  10.8 13.6 %collective-permute-start.8 = (f32[112,128]{1,0:T(8,128)S(1)}, f32[112,128]{1,0:T(8,128)}, u32[]{:S(2)}, u32[]{:S(2)}) collective-permute-start(f32[112,128]{1,0:T(8,128)S(1)} %slice_select_fusion), channel_id=1, source_target_pairs={{0,16},{16,0},{32,48},{48,32},{64,80},{80,64},{96,112},{112,96},{1... | collective-permute-start | bytes 172040 | tf_op jit(solution)/shard_map/ppermute | solution.py:30
  13.7 16.3 %copy-start.30 = (pred[4,8]{1,0:T(4,128)(4,1)S(1)}, pred[4,8]{1,0:T(4,128)(4,1)}, u32[]{:S(2)}) copy-start(pred[4,8]{1,0:T(4,128)(4,1)} %get-tuple-element.37) | copy-start | bytes 100
  13.7 16.3 %copy-start.31 = (pred[4,8]{1,0:T(4,128)(4,1)S(1)}, pred[4,8]{1,0:T(4,128)(4,1)}, u32[]{:S(2)}) copy-start(pred[4,8]{1,0:T(4,128)(4,1)} %get-tuple-element.38) | copy-start | bytes 100
  13.7 16.3 %copy-start.32 = (pred[4,8]{1,0:T(4,128)(4,1)S(1)}, pred[4,8]{1,0:T(4,128)(4,1)}, u32[]{:S(2)}) copy-start(pred[4,8]{1,0:T(4,128)(4,1)} %get-tuple-element.39) | copy-start | bytes 100
  13.7 16.3 %copy-start.33 = (pred[4,8]{1,0:T(4,128)(4,1)S(1)}, pred[4,8]{1,0:T(4,128)(4,1)}, u32[]{:S(2)}) copy-start(pred[4,8]{1,0:T(4,128)(4,1)} %get-tuple-element.40) | copy-start | bytes 100
  13.7 16.3 %copy-start.34 = (pred[4,8]{1,0:T(4,128)(4,1)S(1)}, pred[4,8]{1,0:T(4,128)(4,1)}, u32[]{:S(2)}) copy-start(pred[4,8]{1,0:T(4,128)(4,1)} %get-tuple-element.41) | copy-start | bytes 100
  13.7 16.3 %copy-start.35 = (pred[4,8]{1,0:T(4,128)(4,1)S(1)}, pred[4,8]{1,0:T(4,128)(4,1)}, u32[]{:S(2)}) copy-start(pred[4,8]{1,0:T(4,128)(4,1)} %get-tuple-element.42) | copy-start | bytes 100
  13.7 16.3 %copy-start.36 = (pred[4,8]{1,0:T(4,128)(4,1)S(1)}, pred[4,8]{1,0:T(4,128)(4,1)}, u32[]{:S(2)}) copy-start(pred[4,8]{1,0:T(4,128)(4,1)} %get-tuple-element.43) | copy-start | bytes 100
  13.7 16.3 %copy-start.37 = (pred[4,8]{1,0:T(4,128)(4,1)S(1)}, pred[4,8]{1,0:T(4,128)(4,1)}, u32[]{:S(2)}) copy-start(pred[4,8]{1,0:T(4,128)(4,1)} %get-tuple-element.75) | copy-start | bytes 100
  16.9 8.3 %collective-permute-start.11 = (bf16[1,10,32,128]{3,2,1,0:T(8,128)(2,1)S(1)}, bf16[1,10,32,128]{3,2,1,0:T(8,128)(2,1)S(1)}, u32[]{:S(2)}, u32[]{:S(2)}) collective-permute-start(bf16[1,10,32,128]{3,2,1,0:T(8,128)(2,1)S(1)} %get-tuple-element.26), channel_id=1, source_target_pairs={{0,16},{16,32},{32,48},{48,64},{64,80},{80,96},{96,112},{112,128},... | collective-permute-start | bytes 245768 | tf_op jit(solution)/shard_map/ppermute | solution.py:73
  22.5 5.8 %collective-permute-start.12 = (bf16[1,10,32,128]{3,2,1,0:T(8,128)(2,1)S(1)}, bf16[1,10,32,128]{3,2,1,0:T(8,128)(2,1)S(1)}, u32[]{:S(2)}, u32[]{:S(2)}) collective-permute-start(bf16[1,10,32,128]{3,2,1,0:T(8,128)(2,1)S(1)} %get-tuple-element.27), channel_id=1, source_target_pairs={{16,0},{32,16},{48,32},{64,48},{80,64},{96,80},{112,96},{128,112},... | collective-permute-start | bytes 245768 | tf_op jit(solution)/shard_map/ppermute | solution.py:75
  28.3 6.1 %collective-permute-start.13 = (f32[56,128]{1,0:T(8,128)S(1)}, f32[56,128]{1,0:T(8,128)S(1)}, u32[]{:S(2)}, u32[]{:S(2)}) collective-permute-start(f32[56,128]{1,0:T(8,128)S(1)} %slice_select_fusion.1), channel_id=1, source_target_pairs={{0,32},{16,48},{32,0},{48,16},{64,96},{80,112},{96,64},{112,80},{1... | collective-permute-start | bytes 86024 | tf_op jit(solution)/shard_map/ppermute | solution.py:30
  34.4 7.5 %collective-permute-start.14 = (f32[28,128]{1,0:T(8,128)S(1)}, f32[28,128]{1,0:T(8,128)S(1)}, u32[]{:S(2)}, u32[]{:S(2)}) collective-permute-start(f32[28,128]{1,0:T(8,128)S(1)} %slice_select_fusion.2), channel_id=1, source_target_pairs={{0,64},{16,80},{32,96},{48,112},{64,0},{80,16},{96,32},{112,48},{1... | collective-permute-start | bytes 43016 | tf_op jit(solution)/shard_map/ppermute | solution.py:30
  42.5 6.7 %collective-permute-start.15 = (f32[14,128]{1,0:T(8,128)S(1)}, f32[14,128]{1,0:T(8,128)S(1)}, u32[]{:S(2)}, u32[]{:S(2)}) collective-permute-start(f32[14,128]{1,0:T(8,128)S(1)} %slice_select_fusion.3), channel_id=1, source_target_pairs={{0,128},{16,144},{32,160},{48,176},{64,192},{80,208},{96,224},{112... | collective-permute-start | bytes 21512 | tf_op jit(solution)/shard_map/ppermute | solution.py:30
  49.2 3.1 %collective-permute-start.16 = (f32[70,128]{1,0:T(8,128)S(1)}, f32[70,128]{1,0:T(8,128)S(1)}, u32[]{:S(2)}, u32[]{:S(2)}) collective-permute-start(f32[70,128]{1,0:T(8,128)S(1)} %pad_maximum_fusion.6), channel_id=1, source_target_pairs={{0,1},{1,0},{2,3},{3,2},{4,5},{5,4},{6,7},{7,6},{8,9},{9,8},{10,11... | collective-permute-start | bytes 107528 | tf_op jit(solution)/shard_map/ppermute | solution.py:24
  52.3 4.4 %collective-permute-start.17 = (f32[70,128]{1,0:T(8,128)S(1)}, f32[70,128]{1,0:T(8,128)S(1)}, u32[]{:S(2)}, u32[]{:S(2)}) collective-permute-start(f32[70,128]{1,0:T(8,128)S(1)} %fusion.17), channel_id=1, source_target_pairs={{0,2},{1,3},{2,0},{3,1},{4,6},{5,7},{6,4},{7,5},{8,10},{9,11},{10,... | collective-permute-start | bytes 107528 | tf_op jit(solution)/shard_map/ppermute | solution.py:24
  56.7 2.8 %collective-permute-start.18 = (f32[70,128]{1,0:T(8,128)S(1)}, f32[70,128]{1,0:T(8,128)S(1)}, u32[]{:S(2)}, u32[]{:S(2)}) collective-permute-start(f32[70,128]{1,0:T(8,128)S(1)} %add.107), channel_id=1, source_target_pairs={{0,4},{1,5},{2,6},{3,7},{4,0},{5,1},{6,2},{7,3},{8,12},{9,13},{10,... | collective-permute-start | bytes 107528 | tf_op jit(solution)/shard_map/ppermute | solution.py:24
  59.6 4.3 %collective-permute-start.19 = (f32[70,128]{1,0:T(8,128)S(1)}, f32[70,128]{1,0:T(8,128)S(1)}, u32[]{:S(2)}, u32[]{:S(2)}) collective-permute-start(f32[70,128]{1,0:T(8,128)S(1)} %add.108), channel_id=1, source_target_pairs={{0,8},{1,9},{2,10},{3,11},{4,12},{5,13},{6,14},{7,15},{8,0},{9,1},... | collective-permute-start | bytes 107528 | tf_op jit(solution)/shard_map/ppermute | solution.py:24
  63.9 6.7 %collective-permute-start.20 = (f32[70,128]{1,0:T(8,128)S(1)}, f32[70,128]{1,0:T(8,128)S(1)}, u32[]{:S(2)}, u32[]{:S(2)}) collective-permute-start(f32[70,128]{1,0:T(8,128)S(1)} %add.109), channel_id=1, source_target_pairs={{0,128},{16,144},{32,160},{48,176},{64,192},{80,208},{96,224},{112... | collective-permute-start | bytes 107528 | tf_op jit(solution)/shard_map/ppermute | solution.py:30
  70.6 4.7 %collective-permute-start.21 = (f32[84,128]{1,0:T(8,128)S(1)}, f32[84,128]{1,0:T(8,128)S(1)}, u32[]{:S(2)}, u32[]{:S(2)}) collective-permute-start(f32[84,128]{1,0:T(8,128)S(1)} %pad_maximum_fusion.5), channel_id=1, source_target_pairs={{0,64},{16,80},{32,96},{48,112},{64,0},{80,16},{96,32},{112,48},{1... | collective-permute-start | bytes 129032 | tf_op jit(solution)/shard_map/ppermute | solution.py:30
  75.3 3.1 %collective-permute-start.22 = (f32[112,128]{1,0:T(8,128)S(1)}, f32[112,128]{1,0:T(8,128)S(1)}, u32[]{:S(2)}, u32[]{:S(2)}) collective-permute-start(f32[112,128]{1,0:T(8,128)S(1)} %pad_maximum_fusion.3), channel_id=1, source_target_pairs={{0,32},{16,48},{32,0},{48,16},{64,96},{80,112},{96,64},{112,80},{1... | collective-permute-start | bytes 172040 | tf_op jit(solution)/shard_map/ppermute | solution.py:30
  78.5 8.5 %collective-permute-start.23 = (f32[168,128]{1,0:T(8,128)S(1)}, f32[168,128]{1,0:T(8,128)S(1)}, u32[]{:S(2)}, u32[]{:S(2)}) collective-permute-start(f32[168,128]{1,0:T(8,128)S(1)} %pad_maximum_fusion.1), channel_id=1, source_target_pairs={{0,16},{16,0},{32,48},{48,32},{64,80},{80,64},{96,112},{112,96},{1... | collective-permute-start | bytes 258056 | tf_op jit(solution)/shard_map/ppermute | solution.py:30
  (31 other events, 53.3 us)

commit v7 on v6

--- a/solution.py
+++ b/solution.py
@@ -101,8 +101,8 @@
     kept_gram, padded = lax.optimization_barrier((kept_gram, padded))
     kept_gram = halve(kept_gram, "rad", radial[1])
     shifted = [padded[c // 3 : c // 3 + rows_r, c % 3 : c % 3 + rows_a] for c in range(9)]
-    slots = []
-    for k in range(5):
+    slots = [new_block]
+    for k in range(1, 5):
         code = columns[:, :, k][:, :, None, None]
         pick = shifted[0]
         for c in range(1, 9):
@@ -132,7 +132,6 @@
 
     second = first - mm("pq,qv->pv", kept_gram, first)
     coefficients = first + second
-    twice = image - mm("epi,pv->evi", kept_flat, coefficients)
 
     cross = mm("pv,pw->vw", coefficients, first)
     expanded = (
@@ -141,15 +140,26 @@
     ) / total_rows
     eye = jnp.eye(NEW, dtype=jnp.float32)
     kept_share = jnp.sum(expanded * eye, axis=1) * 16.0 >= jnp.sum(image_gram * eye, axis=1) / total_rows
-    gram = lax.cond(
-        jnp.all(kept_share),
-        lambda: expanded,
-        lambda: all_sum(mm("evi,ewi->vw", twice, twice), steps) / total_rows,
-    )
-    lower = jnp.linalg.cholesky(gram)
-    flat = jnp.moveaxis(twice, 1, 0).reshape(NEW, elements * BLK)
-    solved = lax.linalg.triangular_solve(lower, flat, left_side=True, lower=True)
-    basis = jnp.moveaxis(solved.reshape(NEW, elements, BLK), 0, 1).reshape(rows_r, rows_a, NEW, BLK)
+
+    def factor_of(gram):
+        lower = jnp.linalg.cholesky(gram)
+        inverse = lax.linalg.triangular_solve(lower, eye, left_side=True, lower=True)
+        return lower, inverse
+
+    def expanded_path():
+        lower, inverse = factor_of(expanded)
+        basis = mm("evi,wv->ewi", image, inverse) - mm(
+            "epi,pw->ewi", kept_flat, mm("pv,wv->pw", coefficients, inverse)
+        )
+        return basis, lower
+
+    def direct_path():
+        twice = image - mm("epi,pv->evi", kept_flat, coefficients)
+        lower, inverse = factor_of(all_sum(mm("evi,ewi->vw", twice, twice), steps) / total_rows)
+        return mm("evi,wv->ewi", twice, inverse), lower
+
+    basis, lower = lax.cond(jnp.all(kept_share), expanded_path, direct_path)
+    basis = basis.reshape(rows_r, rows_a, NEW, BLK)
     return (basis, coefficients, lower.T)
 
 

time: 105 us -> 106 us (level)
  matrix products: 16.2 us -> 22.7 us
  other arithmetic: 14.3 us -> 10.9 us
  starting transfers between devices: 34.5 us -> 37.5 us
  local copies, waits for them, and re-layouts: 5.85 us -> 3.03 us
  waiting for transfers between devices: 31.6 us -> 29.5 us
    dot_general x8 -> x10, matrix products: 11.9 us -> 19.2 us  [mm(): jnp.einsum(spec, a, b, precision=lax.Precision.HIGHEST, preferred_element...]
    ppermute x4, starting transfers between devices: 0.19 us -> 4.65 us  [all_sum(): x = x + lax.ppermute(x, axis, [(i, i ^ step) for i in range(count)])]
    ppermute x4, waiting for transfers between devices: 14.4 us -> 10.2 us  [all_sum(): x = x + lax.ppermute(x, axis, [(i, i ^ step) for i in range(count)])]
    ppermute x8, waiting for transfers between devices: 13.6 us -> 16.8 us  [exchange(): return lax.ppermute(x, axis, [(i, i ^ step) for i in range(count)])]
    ppermute x2, starting transfers between devices: 5.54 us -> 2.56 us  [with_halo(): lax.ppermute(tail, axis, [(i, (i + 1) % count) for i in range(ends)])]
    ppermute x2, waiting for transfers between devices: 2.98 us -> 0.15 us  [with_halo(): lax.ppermute(head, axis, [((i + 1) % count, i) for i in range(ends)])]
    another operation x1, matrix products: 2.49 us -> 0.22 us  [factor_of(): lax.linalg.triangular_solve(lower, eye, left_side=True, lower=True)]
    eq x3 -> x2, other arithmetic: 1.88 us -> 0.03 us  [on_device(): pick = jnp.where(code == c, shifted[c], pick)]
  transfers between devices with their start and end apart: 16 -> 16, of which waited for: 11 -> 12; matrix products, arithmetic and copies ran while one was open for 16% -> 6% of each run, Pallas kernels for 0% -> 0%
where the time goes in v7:
time: 106 us
  starting transfers between devices  37.5 us (35%)
  waiting for transfers between devices  29.5 us (28%)
  matrix products  22.7 us (21%)
  other arithmetic  10.9 us (10%)
  local copies, waits for them, and re-layouts  3.03 us (3%)
  between operations  1.8 us (2%)
    ppermute x8, starting transfers between devices, exchange(): return lax.ppermute(x, axis, [(i, i ^ step) for i in range(count)])  22.5 us
    dot_general x10, matrix products, mm(): jnp.einsum(spec, a, b, precision=lax.Precision.HIGHEST, preferred_element...  19.2 us
    ppermute x8, waiting for transfers between devices, exchange(): return lax.ppermute(x, axis, [(i, i ^ step) for i in range(count)])  16.8 us
    ppermute x4, waiting for transfers between devices, all_sum(): x = x + lax.ppermute(x, axis, [(i, i ^ step) for i in range(count)])  10.2 us
    ppermute x2, starting transfers between devices, with_halo(): lax.ppermute(head, axis, [((i + 1) % count, i) for i in range(ends)])  7.86 us
    ppermute x4, starting transfers between devices, all_sum(): x = x + lax.ppermute(x, axis, [(i, i ^ step) for i in range(count)])  4.65 us
    another operation x3, other arithmetic, factor_of(): lower = jnp.linalg.cholesky(gram)  3.6 us
    dot_general x1, matrix products, on_device(): jnp.einsum('rakij,rakvj->ravi', jacobian, picked, preferred_element_type=...  3.23 us
  transfers between devices with their start and end apart: 16, of which 12 were waited for; matrix products, arithmetic and copies ran while one was open for 6% of the time, Pallas kernels for 0%

profile of v7, /device:TPU:1, one launch (start us, length us, event | category | flops | bytes accessed | tf_op | source)
XLA Modules:
  0.0 105.7 jit_solution(5388142322189313233)
XLA Ops:
  0.7 5.5 %convolution_bitcast_fusion.4 = f32[192,192]{1,0:T(8,128)S(1)} fusion(f32[4,8,192,128]{3,2,1,0:T(8,128)} %param.11), kind=kOutput, calls=%fused_computation.32 | convolution fusion | flops 1811939328 | bytes 3293184 | tf_op jit(solution)/shard_map/epi,eqi->pq/dot_general | solution.py:83
  6.3 3.3 %collective-permute-start.8 = (f32[112,128]{1,0:T(8,128)S(1)}, f32[112,128]{1,0:T(8,128)S(1)}, u32[]{:S(2)}, u32[]{:S(2)}) collective-permute-start(f32[112,128]{1,0:T(8,128)S(1)} %slice_select_fusion), channel_id=1, source_target_pairs={{0,16},{16,0},{32,48},{48,32},{64,80},{80,64},{96,112},{112,96},{1... | collective-permute-start | bytes 172040 | tf_op jit(solution)/shard_map/ppermute | solution.py:30
  9.8 4.8 %collective-permute-start.10 = (bf16[4,1,32,128]{3,2,1,0:T(8,128)(2,1)S(1)}, bf16[4,1,32,128]{3,2,1,0:T(8,128)(2,1)S(1)}, u32[]{:S(2)}, u32[]{:S(2)}) collective-permute-start(bf16[4,1,32,128]{3,2,1,0:T(8,128)(2,1)S(1)} %get-tuple-element.73), channel_id=1, source_target_pairs={{1,0},{2,1},{3,2},{4,3},{5,4},{6,5},{7,6},{8,7},{9,8},{10,9},{11,1... | collective-permute-start | bytes 98312 | tf_op jit(solution)/shard_map/ppermute | solution.py:75
  15.9 3.1 %collective-permute-start.12 = (bf16[1,10,32,128]{3,2,1,0:T(8,128)(2,1)S(1)}, bf16[1,10,32,128]{3,2,1,0:T(8,128)(2,1)S(1)}, u32[]{:S(2)}, u32[]{:S(2)}) collective-permute-start(bf16[1,10,32,128]{3,2,1,0:T(8,128)(2,1)S(1)} %get-tuple-element.72), channel_id=1, source_target_pairs={{16,0},{32,16},{48,32},{64,48},{80,64},{96,80},{112,96},{128,112},... | collective-permute-start | bytes 245768 | tf_op jit(solution)/shard_map/ppermute | solution.py:75
  19.0 2.5 %collective-permute-start.11 = (bf16[1,10,32,128]{3,2,1,0:T(8,128)(2,1)S(1)}, bf16[1,10,32,128]{3,2,1,0:T(8,128)(2,1)S(1)}, u32[]{:S(2)}, u32[]{:S(2)}) collective-permute-start(bf16[1,10,32,128]{3,2,1,0:T(8,128)(2,1)S(1)} %get-tuple-element.71), channel_id=1, source_target_pairs={{0,16},{16,32},{32,48},{48,64},{64,80},{80,96},{96,112},{112,128},... | collective-permute-start | bytes 245768 | tf_op jit(solution)/shard_map/ppermute | solution.py:73
  28.3 4.2 %collective-permute-start.14 = (f32[28,128]{1,0:T(8,128)S(1)}, f32[28,128]{1,0:T(8,128)S(1)}, u32[]{:S(2)}, u32[]{:S(2)}) collective-permute-start(f32[28,128]{1,0:T(8,128)S(1)} %slice_select_fusion.2), channel_id=1, source_target_pairs={{0,64},{16,80},{32,96},{48,112},{64,0},{80,16},{96,32},{112,48},{1... | collective-permute-start | bytes 43016 | tf_op jit(solution)/shard_map/ppermute | solution.py:30
  32.5 3.2 %fusion.9 = f32[4,8,32,128,1]{3,2,0,1,4:T(8,128)S(1)} fusion(bf16[4,8,5,128,128]{4,3,2,1,0:T(8,128)(2,1)S(1)} %bitcast.170, bf16[4,8,5,32,128]{4,3,1,0,2:T(8,128)(2,1)} %copy-done.4), kind=kOutput, calls=%fused_computation.29 | convolution fusion | flops 167772160 | bytes 7077888 | tf_op jit(solution)/shard_map/rakij,rakvj->ravi/dot_general | solution.py:114
  36.6 2.9 %convolution_bitcast_fusion.5 = f32[192,32]{0,1:T(8,128)S(1)} fusion(f32[32,32,128]{2,1,0:T(8,128)S(1)} %bitcast.165, f32[32,192,128]{2,1,0:T(8,128)S(1)} %bitcast.161), kind=kOutput, calls=%fused_computation.33 | convolution fusion | flops 301989888 | bytes 3694592 | tf_op jit(solution)/shard_map/epi,evi->pv/dot_general | solution.py:83
  39.6 2.3 %collective-permute-start.15 = (f32[14,128]{1,0:T(8,128)S(1)}, f32[14,128]{1,0:T(8,128)S(1)}, u32[]{:S(2)}, u32[]{:S(2)}) collective-permute-start(f32[14,128]{1,0:T(8,128)S(1)} %slice_select_fusion.3), channel_id=1, source_target_pairs={{0,128},{16,144},{32,160},{48,176},{64,192},{80,208},{96,224},{112... | collective-permute-start | bytes 21512 | tf_op jit(solution)/shard_map/ppermute | solution.py:30
  42.1 4.1 %collective-permute-done.15 = f32[14,128]{1,0:T(8,128)S(1)} collective-permute-done((f32[14,128]{1,0:T(8,128)S(1)}, f32[14,128]{1,0:T(8,128)S(1)}, u32[]{:S(2)}, u32[]{:S(2)}) %collective-permute-start.15) | collective-permute-done | bytes 7200 | tf_op jit(solution)/shard_map/ppermute | solution.py:30
  46.4 2.8 %collective-permute-done.16 = f32[70,128]{1,0:T(8,128)S(1)} collective-permute-done((f32[70,128]{1,0:T(8,128)S(1)}, f32[70,128]{1,0:T(8,128)S(1)}, u32[]{:S(2)}, u32[]{:S(2)}) %collective-permute-start.16) | collective-permute-done | bytes 35872 | tf_op jit(solution)/shard_map/ppermute | solution.py:24
  49.2 2.4 %collective-permute-start.17 = (f32[70,128]{1,0:T(8,128)S(1)}, f32[70,128]{1,0:T(8,128)S(1)}, u32[]{:S(2)}, u32[]{:S(2)}) collective-permute-start(f32[70,128]{1,0:T(8,128)S(1)} %fusion.19), channel_id=1, source_target_pairs={{0,2},{1,3},{2,0},{3,1},{4,6},{5,7},{6,4},{7,5},{8,10},{9,11},{10,... | collective-permute-start | bytes 107528 | tf_op jit(solution)/shard_map/ppermute | solution.py:24
  51.6 2.1 %collective-permute-done.17 = f32[70,128]{1,0:T(8,128)S(1)} collective-permute-done((f32[70,128]{1,0:T(8,128)S(1)}, f32[70,128]{1,0:T(8,128)S(1)}, u32[]{:S(2)}, u32[]{:S(2)}) %collective-permute-start.17) | collective-permute-done | bytes 35872 | tf_op jit(solution)/shard_map/ppermute | solution.py:24
  54.3 2.5 %collective-permute-done.18 = f32[70,128]{1,0:T(8,128)S(1)} collective-permute-done((f32[70,128]{1,0:T(8,128)S(1)}, f32[70,128]{1,0:T(8,128)S(1)}, u32[]{:S(2)}, u32[]{:S(2)}) %collective-permute-start.18) | collective-permute-done | bytes 35872 | tf_op jit(solution)/shard_map/ppermute | solution.py:24
  58.4 2.8 %collective-permute-done.19 = f32[70,128]{1,0:T(8,128)S(1)} collective-permute-done((f32[70,128]{1,0:T(8,128)S(1)}, f32[70,128]{1,0:T(8,128)S(1)}, u32[]{:S(2)}, u32[]{:S(2)}) %collective-permute-start.19) | collective-permute-done | bytes 35872 | tf_op jit(solution)/shard_map/ppermute | solution.py:24
  61.1 1.9 %collective-permute-start.20 = (f32[70,128]{1,0:T(8,128)S(1)}, f32[70,128]{1,0:T(8,128)S(1)}, u32[]{:S(2)}, u32[]{:S(2)}) collective-permute-start(f32[70,128]{1,0:T(8,128)S(1)} %add.106), channel_id=1, source_target_pairs={{0,128},{16,144},{32,160},{48,176},{64,192},{80,208},{96,224},{112... | collective-permute-start | bytes 107528 | tf_op jit(solution)/shard_map/ppermute | solution.py:30
  63.1 4.8 %collective-permute-done.20 = f32[70,128]{1,0:T(8,128)S(1)} collective-permute-done((f32[70,128]{1,0:T(8,128)S(1)}, f32[70,128]{1,0:T(8,128)S(1)}, u32[]{:S(2)}, u32[]{:S(2)}) %collective-permute-start.20) | collective-permute-done | bytes 35872 | tf_op jit(solution)/shard_map/ppermute | solution.py:30
  68.2 3.9 %collective-permute-done.21 = f32[84,128]{1,0:T(8,128)S(1)} collective-permute-done((f32[84,128]{1,0:T(8,128)S(1)}, f32[84,128]{1,0:T(8,128)S(1)}, u32[]{:S(2)}, u32[]{:S(2)}) %collective-permute-start.21) | collective-permute-done | bytes 43040 | tf_op jit(solution)/shard_map/ppermute | solution.py:30
  72.2 3.0 %collective-permute-done.22 = f32[112,128]{1,0:T(8,128)S(1)} collective-permute-done((f32[112,128]{1,0:T(8,128)S(1)}, f32[112,128]{1,0:T(8,128)S(1)}, u32[]{:S(2)}, u32[]{:S(2)}) %collective-permute-start.22) | collective-permute-done | bytes 57376 | tf_op jit(solution)/shard_map/ppermute | solution.py:30
  75.3 9.3 %collective-permute-start.23 = (f32[168,128]{1,0:T(8,128)S(1)}, f32[168,128]{1,0:T(8,128)S(1)}, u32[]{:S(2)}, u32[]{:S(2)}) collective-permute-start(f32[168,128]{1,0:T(8,128)S(1)} %pad_maximum_fusion.1), channel_id=1, source_target_pairs={{0,16},{16,0},{32,48},{48,32},{64,80},{80,64},{96,112},{112,96},{1... | collective-permute-start | bytes 258056 | tf_op jit(solution)/shard_map/ppermute | solution.py:30
  92.4 12.6 %conditional.1 = (f32[32,32]{1,0:T(8,128)S(1)}, f32[4,8,32,128]{3,2,1,0:T(8,128)}) conditional(s32[]{:T(128)} %convert_element_type.8, (f32[192,32]{0,1:T(8,128)}, f32[32,192,128]{2,1,0:T(8,128)S(1)}, f32[32,32,128]{2,1,0:T(8,128)}, f32[32,32]{0,1:T(8,128)S(1)}) %tuple.75, (f32[32,32]{0,1:T(8,128)S(1)}, f32[32,32]{0,1:T(8,128)S(1)}, ...), branch_computations={%region_3.8_spmd, %region_6.9_spmd} | conditional | flops 403195936 | bytes 8176238 | solution.py:161
  92.7 2.9 %cholesky.55 = f32[32,32]{1,0:T(8,128)S(1)} custom-call(f32[32,32]{1,0:T(8,128)S(1)} %fusion.8), custom_call_target="Cholesky" | custom-call | tf_op jit(solution)/shard_map/cond/branch_1_fun/jit(cholesky)/cholesky | solution.py:145
  97.0 2.4 %custom-call.7 = f32[1,32,32]{1,2,0:T(8,128)S(1)} custom-call(f32[1,32,32]{2,1,0:T(8,128)S(1)} %get-tuple-element.69), custom_call_target="InvertDiagBlocksLowerTriangular" | custom-call | tf_op jit(solution)/shard_map/cond/branch_1_fun/triangular_solve/custom-call.0 | solution.py:146
  102.2 2.8 %convolution_subtract_fusion = f32[32,32,128]{2,0,1:T(8,128)} fusion(f32[32,32,128]{2,0,1:T(8,128)S(1)} %fusion.4, f32[32,192,1]{1,0,2:T(8,128)S(1)} %convolution_bitcast_fusion.3, f32[32,192,128]{2,1,0:T(8,128)S(1)} %get-tuple-element.29), kind=kOutput, calls=%fused_computation.15 | convolution fusion | flops 302120960 | bytes 4218880 | tf_op jit(solution)/shard_map/cond/branch_1_fun/epi,pw->ewi/dot_general | solution.py:83
  (106 shorter events, 23.9 us)
Async XLA Ops:
  0.6 9.0 %copy-start.3 = (bf16[4,8,32,128]{3,2,1,0:T(8,128)(2,1)S(1)}, bf16[4,8,32,128]{3,2,1,0:T(8,128)(2,1)}, u32[]{:S(2)}) copy-start(bf16[4,8,32,128]{3,2,1,0:T(8,128)(2,1)} %param.10) | copy-start | bytes 786436
  0.6 13.9 %copy-start.5 = (s32[4,8,5]{1,0,2:T(4,128)S(1)}, s32[4,8,5]{1,0,2:T(4,128)}, u32[]{:S(2)}) copy-start(s32[4,8,5]{1,0,2:T(4,128)} %param.12) | copy-start | bytes 1924
  6.3 15.2 %collective-permute-start.8 = (f32[112,128]{1,0:T(8,128)S(1)}, f32[112,128]{1,0:T(8,128)S(1)}, u32[]{:S(2)}, u32[]{:S(2)}) collective-permute-start(f32[112,128]{1,0:T(8,128)S(1)} %slice_select_fusion), channel_id=1, source_target_pairs={{0,16},{16,0},{32,48},{48,32},{64,80},{80,64},{96,112},{112,96},{1... | collective-permute-start | bytes 172040 | tf_op jit(solution)/shard_map/ppermute | solution.py:30
  9.7 6.2 %collective-permute-start.9 = (bf16[4,1,32,128]{3,2,1,0:T(8,128)(2,1)S(1)}, bf16[4,1,32,128]{3,2,1,0:T(8,128)(2,1)S(1)}, u32[]{:S(2)}, u32[]{:S(2)}) collective-permute-start(bf16[4,1,32,128]{3,2,1,0:T(8,128)(2,1)S(1)} %get-tuple-element.74), channel_id=1, source_target_pairs={{0,1},{1,2},{2,3},{3,4},{4,5},{5,6},{6,7},{7,8},{8,9},{9,10},{10,1... | collective-permute-start | bytes 98312 | tf_op jit(solution)/shard_map/ppermute | solution.py:73
  9.8 6.1 %collective-permute-start.10 = (bf16[4,1,32,128]{3,2,1,0:T(8,128)(2,1)S(1)}, bf16[4,1,32,128]{3,2,1,0:T(8,128)(2,1)S(1)}, u32[]{:S(2)}, u32[]{:S(2)}) collective-permute-start(bf16[4,1,32,128]{3,2,1,0:T(8,128)(2,1)S(1)} %get-tuple-element.73), channel_id=1, source_target_pairs={{1,0},{2,1},{3,2},{4,3},{5,4},{6,5},{7,6},{8,7},{9,8},{10,9},{11,1... | collective-permute-start | bytes 98312 | tf_op jit(solution)/shard_map/ppermute | solution.py:75
  15.9 5.8 %collective-permute-start.12 = (bf16[1,10,32,128]{3,2,1,0:T(8,128)(2,1)S(1)}, bf16[1,10,32,128]{3,2,1,0:T(8,128)(2,1)S(1)}, u32[]{:S(2)}, u32[]{:S(2)}) collective-permute-start(bf16[1,10,32,128]{3,2,1,0:T(8,128)(2,1)S(1)} %get-tuple-element.72), channel_id=1, source_target_pairs={{16,0},{32,16},{48,32},{64,48},{80,64},{96,80},{112,96},{128,112},... | collective-permute-start | bytes 245768 | tf_op jit(solution)/shard_map/ppermute | solution.py:75
  19.0 3.9 %collective-permute-start.11 = (bf16[1,10,32,128]{3,2,1,0:T(8,128)(2,1)S(1)}, bf16[1,10,32,128]{3,2,1,0:T(8,128)(2,1)S(1)}, u32[]{:S(2)}, u32[]{:S(2)}) collective-permute-start(bf16[1,10,32,128]{3,2,1,0:T(8,128)(2,1)S(1)} %get-tuple-element.71), channel_id=1, source_target_pairs={{0,16},{16,32},{32,48},{48,64},{64,80},{80,96},{96,112},{112,128},... | collective-permute-start | bytes 245768 | tf_op jit(solution)/shard_map/ppermute | solution.py:73
  23.0 9.5 %slice-start = ((s8[5242880]{0:T(1024)(128)(4,1)}), s8[4194304]{0:T(1024)(128)(4,1)S(1)}, s32[]{:S(2)}) async-start(s8[5242880]{0:T(1024)(128)(4,1)} %bitcast.169), calls=%async_computation | async-start | bytes 8388608
  23.1 4.2 %collective-permute-start.13 = (f32[56,128]{1,0:T(8,128)S(1)}, f32[56,128]{1,0:T(8,128)S(1)}, u32[]{:S(2)}, u32[]{:S(2)}) collective-permute-start(f32[56,128]{1,0:T(8,128)S(1)} %slice_select_fusion.1), channel_id=1, source_target_pairs={{0,32},{16,48},{32,0},{48,16},{64,96},{80,112},{96,64},{112,80},{1... | collective-permute-start | bytes 86024 | tf_op jit(solution)/shard_map/ppermute | solution.py:30
  24.8 7.7 %slice-start.1 = ((s8[5242880]{0:T(1024)(128)(4,1)}), s8[1048576]{0:T(1024)(128)(4,1)S(1)}, s32[]{:S(2)}) async-start(s8[5242880]{0:T(1024)(128)(4,1)} %bitcast.169), calls=%async_computation.1 | async-start | bytes 2097152
  27.2 1.1 %copy-start.4 = (bf16[4,8,5,32,128]{4,3,1,0,2:T(8,128)(2,1)}, bf16[4,8,5,32,128]{4,3,1,0,2:T(8,128)(2,1)S(1)}, u32[]{:S(2)}) copy-start(bf16[4,8,5,32,128]{4,3,1,0,2:T(8,128)(2,1)S(1)} %bitcast_dynamic-update-slice_fusion) | copy-start | bytes 3932164
  28.3 8.3 %copy-start = (f32[4,8,192,128]{3,2,1,0:T(8,128)S(1)}, f32[4,8,192,128]{3,2,1,0:T(8,128)}, u32[]{:S(2)}) copy-start(f32[4,8,192,128]{3,2,1,0:T(8,128)} %param.11) | copy-start | bytes 9437188
  28.3 7.5 %collective-permute-start.14 = (f32[28,128]{1,0:T(8,128)S(1)}, f32[28,128]{1,0:T(8,128)S(1)}, u32[]{:S(2)}, u32[]{:S(2)}) collective-permute-start(f32[28,128]{1,0:T(8,128)S(1)} %slice_select_fusion.2), channel_id=1, source_target_pairs={{0,64},{16,80},{32,96},{48,112},{64,0},{80,16},{96,32},{112,48},{1... | collective-permute-start | bytes 43016 | tf_op jit(solution)/shard_map/ppermute | solution.py:30
  35.8 0.8 copy-start.1
  39.6 6.7 %collective-permute-start.15 = (f32[14,128]{1,0:T(8,128)S(1)}, f32[14,128]{1,0:T(8,128)S(1)}, u32[]{:S(2)}, u32[]{:S(2)}) collective-permute-start(f32[14,128]{1,0:T(8,128)S(1)} %slice_select_fusion.3), channel_id=1, source_target_pairs={{0,128},{16,144},{32,160},{48,176},{64,192},{80,208},{96,224},{112... | collective-permute-start | bytes 21512 | tf_op jit(solution)/shard_map/ppermute | solution.py:30
  46.3 2.9 %collective-permute-start.16 = (f32[70,128]{1,0:T(8,128)S(1)}, f32[70,128]{1,0:T(8,128)S(1)}, u32[]{:S(2)}, u32[]{:S(2)}) collective-permute-start(f32[70,128]{1,0:T(8,128)S(1)} %pad_maximum_fusion.6), channel_id=1, source_target_pairs={{0,1},{1,0},{2,3},{3,2},{4,5},{5,4},{6,7},{7,6},{8,9},{9,8},{10,11... | collective-permute-start | bytes 107528 | tf_op jit(solution)/shard_map/ppermute | solution.py:24
  49.2 4.5 %collective-permute-start.17 = (f32[70,128]{1,0:T(8,128)S(1)}, f32[70,128]{1,0:T(8,128)S(1)}, u32[]{:S(2)}, u32[]{:S(2)}) collective-permute-start(f32[70,128]{1,0:T(8,128)S(1)} %fusion.19), channel_id=1, source_target_pairs={{0,2},{1,3},{2,0},{3,1},{4,6},{5,7},{6,4},{7,5},{8,10},{9,11},{10,... | collective-permute-start | bytes 107528 | tf_op jit(solution)/shard_map/ppermute | solution.py:24
  53.7 3.1 %collective-permute-start.18 = (f32[70,128]{1,0:T(8,128)S(1)}, f32[70,128]{1,0:T(8,128)S(1)}, u32[]{:S(2)}, u32[]{:S(2)}) collective-permute-start(f32[70,128]{1,0:T(8,128)S(1)} %add.104), channel_id=1, source_target_pairs={{0,4},{1,5},{2,6},{3,7},{4,0},{5,1},{6,2},{7,3},{8,12},{9,13},{10,... | collective-permute-start | bytes 107528 | tf_op jit(solution)/shard_map/ppermute | solution.py:24
  56.8 4.3 %collective-permute-start.19 = (f32[70,128]{1,0:T(8,128)S(1)}, f32[70,128]{1,0:T(8,128)S(1)}, u32[]{:S(2)}, u32[]{:S(2)}) collective-permute-start(f32[70,128]{1,0:T(8,128)S(1)} %add.105), channel_id=1, source_target_pairs={{0,8},{1,9},{2,10},{3,11},{4,12},{5,13},{6,14},{7,15},{8,0},{9,1},... | collective-permute-start | bytes 107528 | tf_op jit(solution)/shard_map/ppermute | solution.py:24
  61.1 6.7 %collective-permute-start.20 = (f32[70,128]{1,0:T(8,128)S(1)}, f32[70,128]{1,0:T(8,128)S(1)}, u32[]{:S(2)}, u32[]{:S(2)}) collective-permute-start(f32[70,128]{1,0:T(8,128)S(1)} %add.106), channel_id=1, source_target_pairs={{0,128},{16,144},{32,160},{48,176},{64,192},{80,208},{96,224},{112... | collective-permute-start | bytes 107528 | tf_op jit(solution)/shard_map/ppermute | solution.py:30
  67.9 4.2 %collective-permute-start.21 = (f32[84,128]{1,0:T(8,128)S(1)}, f32[84,128]{1,0:T(8,128)S(1)}, u32[]{:S(2)}, u32[]{:S(2)}) collective-permute-start(f32[84,128]{1,0:T(8,128)S(1)} %pad_maximum_fusion.5), channel_id=1, source_target_pairs={{0,64},{16,80},{32,96},{48,112},{64,0},{80,16},{96,32},{112,48},{1... | collective-permute-start | bytes 129032 | tf_op jit(solution)/shard_map/ppermute | solution.py:30
  72.1 3.1 %collective-permute-start.22 = (f32[112,128]{1,0:T(8,128)S(1)}, f32[112,128]{1,0:T(8,128)S(1)}, u32[]{:S(2)}, u32[]{:S(2)}) collective-permute-start(f32[112,128]{1,0:T(8,128)S(1)} %pad_maximum_fusion.3), channel_id=1, source_target_pairs={{0,32},{16,48},{32,0},{48,16},{64,96},{80,112},{96,64},{112,80},{1... | collective-permute-start | bytes 172040 | tf_op jit(solution)/shard_map/ppermute | solution.py:30
  75.3 10.3 %collective-permute-start.23 = (f32[168,128]{1,0:T(8,128)S(1)}, f32[168,128]{1,0:T(8,128)S(1)}, u32[]{:S(2)}, u32[]{:S(2)}) collective-permute-start(f32[168,128]{1,0:T(8,128)S(1)} %pad_maximum_fusion.1), channel_id=1, source_target_pairs={{0,16},{16,0},{32,48},{48,32},{64,80},{80,64},{96,112},{112,96},{1... | collective-permute-start | bytes 258056 | tf_op jit(solution)/shard_map/ppermute | solution.py:30

commit v8 on v7

--- a/solution.py
+++ b/solution.py
@@ -96,10 +96,20 @@
 
     kept_gram = halve(pack_symmetric(mm("epi,eqi->pq", kept_flat, kept_flat)), "rad", radial[0])
 
-    widened = with_halo(new_block, (("azi", 1),), 1, True)
-    padded = with_halo(widened, (("rad", 0),), 1, False)
-    kept_gram, padded = lax.optimization_barrier((kept_gram, padded))
+    n_a, n_r = lax.axis_size("azi"), lax.axis_size("rad")
+    west = lax.ppermute(new_block[:, rows_a - 1 :], "azi", [(i, (i + 1) % n_a) for i in range(n_a)])
+    east = lax.ppermute(new_block[:, :1], "azi", [((i + 1) % n_a, i) for i in range(n_a)])
+    kept_gram, west, east = lax.optimization_barrier((kept_gram, west, east))
     kept_gram = halve(kept_gram, "rad", radial[1])
+
+    def row(r):
+        return jnp.concatenate([west[r : r + 1], new_block[r : r + 1], east[r : r + 1]], axis=1)
+
+    north = lax.ppermute(row(rows_r - 1), "rad", [(i, i + 1) for i in range(n_r - 1)])
+    south = lax.ppermute(row(0), "rad", [(i + 1, i) for i in range(n_r - 1)])
+    padded = jnp.concatenate(
+        [north, jnp.concatenate([west, new_block, east], axis=1), south], axis=0
+    )
     shifted = [padded[c // 3 : c // 3 + rows_r, c % 3 : c % 3 + rows_a] for c in range(9)]
     slots = [new_block]
     for k in range(1, 5):
@@ -109,20 +119,20 @@
             pick = jnp.where(code == c, shifted[c], pick)
         slots.append(pick)
     picked = jnp.stack(slots, axis=2)
-    kept_gram, picked = lax.optimization_barrier((kept_gram, picked))
-    kept_gram = halve(kept_gram, "rad", radial[2])
     image = jnp.einsum("rakij,rakvj->ravi", jacobian, picked, preferred_element_type=jnp.float32)
     image = image.reshape(elements, NEW, BLK)
-    kept_gram, image = lax.optimization_barrier((kept_gram, image))
-    kept_gram = halve(kept_gram, "rad", radial[3])
 
     moments = jnp.concatenate(
         [mm("epi,evi->pv", kept_flat, image), mm("evi,ewi->vw", image, image)], axis=0
     ).reshape(-1, BLK)
     split = kept_gram.shape[0]
-    joint = all_sum(jnp.concatenate([kept_gram, moments], axis=0), around)
+    ahead = 2
+    joint = all_sum(
+        jnp.concatenate([kept_gram, moments], axis=0),
+        [("rad", step) for step in radial[ahead:]] + around,
+    )
     kept_gram, moments = joint[:split], joint[split:]
-    for step in reversed(radial):
+    for step in reversed(radial[:ahead]):
         other = exchange(jnp.concatenate([kept_gram, moments], axis=0), "rad", step)
         moments = moments + other[kept_gram.shape[0]:]
         kept_gram = join(kept_gram, other[: kept_gram.shape[0]], "rad", step)

time: 106 us -> 101 us (0.953)
  waiting for transfers between devices: 29.5 us -> 19.9 us
  other arithmetic: 10.9 us -> 13.4 us
  local copies, waits for them, and re-layouts: 3.03 us -> 4.77 us
    ppermute x8 -> x4, waiting for transfers between devices: 16.8 us -> 2.5 us  [exchange(): return lax.ppermute(x, axis, [(i, i ^ step) for i in range(count)])]
    ppermute x8 -> x4, starting transfers between devices: 22.5 us -> 14.6 us  [exchange(): return lax.ppermute(x, axis, [(i, i ^ step) for i in range(count)])]
    ppermute x4 -> x6, starting transfers between devices: 4.65 us -> 12.3 us  [all_sum(): x = x + lax.ppermute(x, axis, [(i, i ^ step) for i in range(count)])]
    ppermute x4 -> x6, waiting for transfers between devices: 10.2 us -> 16 us  [all_sum(): x = x + lax.ppermute(x, axis, [(i, i ^ step) for i in range(count)])]
    unnamed x4 -> x3, other arithmetic: 2.35 us -> 4.33 us
    slice x6, local copies, waits for them, and re-layouts: 0.31 us -> 1.59 us  [on_device(): first, image_gram = (moments[:KEEP], moments[KEEP:])]
    ppermute x4, waiting for transfers between devices: 2.57 us -> 1.38 us  [the longest x1 1.3 us: on_device(): lax.ppermute(row(rows_r - 1), 'rad', [(i, i + 1) for i in range(n_r - 1)])]
  transfers between devices with their start and end apart: 16 -> 14, of which waited for: 12 -> 10; matrix products, arithmetic and copies ran while one was open for 6% -> 7% of each run, Pallas kernels for 0% -> 0%
where the time goes in v8:
time: 101 us; the launch traced here: 100 us
  starting transfers between devices  38.2 us (38%)
  matrix products  22 us (22%)
  waiting for transfers between devices  19.9 us (20%)
  other arithmetic  13.4 us (13%)
  local copies, waits for them, and re-layouts  4.77 us (5%)
  between operations  1.65 us (2%)
    dot_general x10, matrix products, mm(): jnp.einsum(spec, a, b, precision=lax.Precision.HIGHEST, preferred_element...  18.5 us
    ppermute x6, waiting for transfers between devices, all_sum(): x = x + lax.ppermute(x, axis, [(i, i ^ step) for i in range(count)])  16 us
    ppermute x4, starting transfers between devices, exchange(): return lax.ppermute(x, axis, [(i, i ^ step) for i in range(count)])  14.6 us
    ppermute x6, starting transfers between devices, all_sum(): x = x + lax.ppermute(x, axis, [(i, i ^ step) for i in range(count)])  12.3 us
    ppermute x1, starting transfers between devices, on_device(): lax.ppermute(new_block[:, :1], 'azi', [((i + 1) % n_a, i) for i in range(...  5.76 us
    unnamed x3, other arithmetic  4.33 us
    another operation x3, other arithmetic, factor_of(): lower = jnp.linalg.cholesky(gram)  3.6 us
    dot_general x1, matrix products, on_device(): jnp.einsum('rakij,rakvj->ravi', jacobian, picked, preferred_element_type=...  3.36 us
  transfers between devices with their start and end apart: 14, of which 10 were waited for; matrix products, arithmetic and copies ran while one was open for 7% of the time, Pallas kernels for 0%

profile of v8, /device:TPU:1, one launch (start us, length us, event | category | flops | bytes accessed | tf_op | source)
XLA Modules:
  0.0 100.3 jit_solution(515991534495793412)
XLA Ops:
  1.4 5.8 %collective-permute-start.10 = (bf16[4,1,32,128]{3,2,1,0:T(8,128)(2,1)S(1)}, bf16[4,1,32,128]{3,2,1,0:T(8,128)(2,1)S(1)}, u32[]{:S(2)}, u32[]{:S(2)}) collective-permute-start(bf16[4,1,32,128]{3,2,1,0:T(8,128)(2,1)S(1)} %get-tuple-element.72), channel_id=1, source_target_pairs={{1,0},{2,1},{3,2},{4,3},{5,4},{6,5},{7,6},{8,7},{9,8},{10,9},{11,1... | collective-permute-start | bytes 98312 | tf_op jit(solution)/shard_map/ppermute | solution.py:101
  7.2 5.5 %convolution_bitcast_fusion.4 = f32[192,192]{1,0:T(8,128)S(1)} fusion(f32[4,8,192,128]{3,2,1,0:T(8,128)} %param.11), kind=kOutput, calls=%fused_computation.29 | convolution fusion | flops 1811939328 | bytes 3293184 | tf_op jit(solution)/shard_map/epi,eqi->pq/dot_general | solution.py:83
  14.9 1.7 %collective-permute-start.11 = (f32[56,128]{1,0:T(8,128)S(1)}, f32[56,128]{1,0:T(8,128)S(1)}, u32[]{:S(2)}, u32[]{:S(2)}) collective-permute-start(f32[56,128]{1,0:T(8,128)S(1)} %slice_select_fusion.1), channel_id=1, source_target_pairs={{0,32},{16,48},{32,0},{48,16},{64,96},{80,112},{96,64},{112,80},{1... | collective-permute-start | bytes 86024 | tf_op jit(solution)/shard_map/ppermute | solution.py:30
  16.6 2.7 %collective-permute-start.12 = (bf16[1,10,32,128]{3,2,1,0:T(8,128)(2,1)S(1)}, bf16[1,10,32,128]{3,2,1,0:T(8,128)(2,1)S(1)}, u32[]{:S(2)}, u32[]{:S(2)}) collective-permute-start(bf16[1,10,32,128]{3,2,1,0:T(8,128)(2,1)S(1)} %pad_maximum_fusion.5), channel_id=1, source_target_pairs={{16,0},{32,16},{48,32},{64,48},{80,64},{96,80},{112,96},{128,112},... | collective-permute-start | bytes 245768 | tf_op jit(solution)/shard_map/ppermute | solution.py:109
  19.3 2.9 %collective-permute-start.13 = (bf16[1,10,32,128]{3,2,1,0:T(8,128)(2,1)S(1)}, bf16[1,10,32,128]{3,2,1,0:T(8,128)(2,1)S(1)}, u32[]{:S(2)}, u32[]{:S(2)}) collective-permute-start(bf16[1,10,32,128]{3,2,1,0:T(8,128)(2,1)S(1)} %pad_maximum_fusion.6), channel_id=1, source_target_pairs={{0,16},{16,32},{32,48},{48,64},{64,80},{80,96},{96,112},{112,128},... | collective-permute-start | bytes 245768 | tf_op jit(solution)/shard_map/ppermute | solution.py:108
  29.5 3.4 %fusion.32 = f32[4,8,32,128,1]{3,2,4,1,0:T(8,128)S(1)} fusion(bf16[4,8,5,32,128]{4,3,2,1,0:T(8,128)(2,1)} %bitcast_dynamic-update-slice_fusion.3, bf16[4,8,5,128,128]{4,3,2,1,0:T(8,128)(2,1)S(1)} %copy-done.4), kind=kOutput, calls=%fused_computation.126 | convolution fusion | flops 167772160 | bytes 7077888 | tf_op jit(solution)/shard_map/rakij,rakvj->ravi/dot_general | solution.py:122
  33.7 2.9 %convolution_bitcast_fusion.5 = f32[192,32]{0,1:T(8,128)S(1)} fusion(f32[4,8,192,128]{3,2,1,0:T(8,128)S(1)} %copy-done, f32[4,8,32,128,1]{3,2,4,1,0:T(8,128)S(1)} %fusion.32), kind=kOutput, calls=%fused_computation.30 | convolution fusion | flops 301989888 | bytes 3694592 | tf_op jit(solution)/shard_map/epi,evi->pv/dot_general | solution.py:83
  36.9 3.1 %collective-permute-start.14 = (f32[112,128]{1,0:T(8,128)S(1)}, f32[112,128]{1,0:T(8,128)S(1)}, u32[]{:S(2)}, u32[]{:S(2)}) collective-permute-start(f32[112,128]{1,0:T(8,128)S(1)} %pad_maximum_fusion.8), channel_id=1, source_target_pairs={{0,64},{16,80},{32,96},{48,112},{64,0},{80,16},{96,32},{112,48},{1... | collective-permute-start | bytes 172040 | tf_op jit(solution)/shard_map/ppermute | solution.py:24
  40.0 1.6 %collective-permute-done.14 = f32[112,128]{1,0:T(8,128)S(1)} collective-permute-done((f32[112,128]{1,0:T(8,128)S(1)}, f32[112,128]{1,0:T(8,128)S(1)}, u32[]{:S(2)}, u32[]{:S(2)}) %collective-permute-start.14) | collective-permute-done | bytes 57376 | tf_op jit(solution)/shard_map/ppermute | solution.py:24
  41.5 6.3 %collective-permute-start.15 = (f32[112,128]{1,0:T(8,128)S(1)}, f32[112,128]{1,0:T(8,128)S(1)}, u32[]{:S(2)}, u32[]{:S(2)}) collective-permute-start(f32[112,128]{1,0:T(8,128)S(1)} %fusion.21), channel_id=1, source_target_pairs={{0,128},{16,144},{32,160},{48,176},{64,192},{80,208},{96,224},{112... | collective-permute-start | bytes 172040 | tf_op jit(solution)/shard_map/ppermute | solution.py:24
  47.8 1.7 %collective-permute-done.15 = f32[112,128]{1,0:T(8,128)S(1)} collective-permute-done((f32[112,128]{1,0:T(8,128)S(1)}, f32[112,128]{1,0:T(8,128)S(1)}, u32[]{:S(2)}, u32[]{:S(2)}) %collective-permute-start.15) | collective-permute-done | bytes 57376 | tf_op jit(solution)/shard_map/ppermute | solution.py:24
  49.6 3.3 %collective-permute-done.16 = f32[112,128]{1,0:T(8,128)S(1)} collective-permute-done((f32[112,128]{1,0:T(8,128)S(1)}, f32[112,128]{1,0:T(8,128)S(1)}, u32[]{:S(2)}, u32[]{:S(2)}) %collective-permute-start.16) | collective-permute-done | bytes 57376 | tf_op jit(solution)/shard_map/ppermute | solution.py:24
  54.1 3.4 %collective-permute-done.17 = f32[112,128]{1,0:T(8,128)S(1)} collective-permute-done((f32[112,128]{1,0:T(8,128)S(1)}, f32[112,128]{1,0:T(8,128)S(1)}, u32[]{:S(2)}, u32[]{:S(2)}) %collective-permute-start.17) | collective-permute-done | bytes 57376 | tf_op jit(solution)/shard_map/ppermute | solution.py:24
  57.6 3.0 %collective-permute-done.18 = f32[112,128]{1,0:T(8,128)S(1)} collective-permute-done((f32[112,128]{1,0:T(8,128)S(1)}, f32[112,128]{1,0:T(8,128)S(1)}, u32[]{:S(2)}, u32[]{:S(2)}) %collective-permute-start.18) | collective-permute-done | bytes 57376 | tf_op jit(solution)/shard_map/ppermute | solution.py:24
  60.7 1.6 %collective-permute-start.19 = (f32[112,128]{1,0:T(8,128)S(1)}, f32[112,128]{1,0:T(8,128)S(1)}, u32[]{:S(2)}, u32[]{:S(2)}) collective-permute-start(f32[112,128]{1,0:T(8,128)S(1)} %add.87), channel_id=1, source_target_pairs={{0,8},{1,9},{2,10},{3,11},{4,12},{5,13},{6,14},{7,15},{8,0},{9,1},... | collective-permute-start | bytes 172040 | tf_op jit(solution)/shard_map/ppermute | solution.py:24
  62.3 3.0 %collective-permute-done.19 = f32[112,128]{1,0:T(8,128)S(1)} collective-permute-done((f32[112,128]{1,0:T(8,128)S(1)}, f32[112,128]{1,0:T(8,128)S(1)}, u32[]{:S(2)}, u32[]{:S(2)}) %collective-permute-start.19) | collective-permute-done | bytes 57376 | tf_op jit(solution)/shard_map/ppermute | solution.py:24
  65.3 2.6 %collective-permute-start.20 = (f32[112,128]{1,0:T(8,128)S(1)}, f32[112,128]{1,0:T(8,128)S(1)}, u32[]{:S(2)}, u32[]{:S(2)}) collective-permute-start(f32[112,128]{1,0:T(8,128)S(1)} %add.88), channel_id=1, source_target_pairs={{0,32},{16,48},{32,0},{48,16},{64,96},{80,112},{96,64},{112,80},{1... | collective-permute-start | bytes 172040 | tf_op jit(solution)/shard_map/ppermute | solution.py:30
  67.9 1.6 %collective-permute-done.20 = f32[112,128]{1,0:T(8,128)S(1)} collective-permute-done((f32[112,128]{1,0:T(8,128)S(1)}, f32[112,128]{1,0:T(8,128)S(1)}, u32[]{:S(2)}, u32[]{:S(2)}) %collective-permute-start.20) | collective-permute-done | bytes 57376 | tf_op jit(solution)/shard_map/ppermute | solution.py:30
  69.5 9.2 %collective-permute-start.21 = (f32[168,128]{1,0:T(8,128)S(1)}, f32[168,128]{1,0:T(8,128)S(1)}, u32[]{:S(2)}, u32[]{:S(2)}) collective-permute-start(f32[168,128]{1,0:T(8,128)S(1)} %pad_maximum_fusion.4), channel_id=1, source_target_pairs={{0,16},{16,0},{32,48},{48,32},{64,80},{80,64},{96,112},{112,96},{1... | collective-permute-start | bytes 258056 | tf_op jit(solution)/shard_map/ppermute | solution.py:30
  87.0 12.6 %conditional.1 = (f32[32,32]{1,0:T(8,128)S(1)}, f32[4,8,32,128]{3,2,1,0:T(8,128)}) conditional(s32[]{:T(128)} %convert_element_type.8, (f32[192,32]{0,1:T(8,128)}, f32[32,192,128]{2,1,0:T(8,128)S(1)}, f32[32,32,128]{2,1,0:T(8,128)}, f32[32,32]{0,1:T(8,128)S(1)}) %tuple.79, (f32[32,32]{0,1:T(8,128)S(1)}, f32[32,32]{0,1:T(8,128)S(1)}, ...), branch_computations={%region_3.8_spmd, %region_6.9_spmd} | conditional | flops 403195936 | bytes 8176238 | solution.py:171
  87.3 2.9 %cholesky.55 = f32[32,32]{1,0:T(8,128)S(1)} custom-call(f32[32,32]{1,0:T(8,128)S(1)} %fusion.8), custom_call_target="Cholesky" | custom-call | tf_op jit(solution)/shard_map/cond/branch_1_fun/jit(cholesky)/cholesky | solution.py:155
  91.6 2.4 %custom-call.7 = f32[1,32,32]{1,2,0:T(8,128)S(1)} custom-call(f32[1,32,32]{2,1,0:T(8,128)S(1)} %get-tuple-element.63), custom_call_target="InvertDiagBlocksLowerTriangular" | custom-call | tf_op jit(solution)/shard_map/cond/branch_1_fun/triangular_solve/custom-call.0 | solution.py:156
  95.2 1.6 %fusion.4 = f32[32,32,128]{2,0,1:T(8,128)S(1)} fusion(f32[32,32,128]{2,1,0:T(8,128)} %get-tuple-element.27, f32[32,32]{1,0:T(8,128)S(1)} %fusion.6), kind=kOutput, calls=%fused_computation.17 | convolution fusion | flops 50331648 | bytes 1052672 | tf_op jit(solution)/shard_map/cond/branch_1_fun/evi,wv->ewi/dot_general | solution.py:83
  96.8 2.8 %convolution_subtract_fusion = f32[32,32,128]{2,0,1:T(8,128)} fusion(f32[32,32,128]{2,0,1:T(8,128)S(1)} %fusion.4, f32[32,192,1]{1,0,2:T(8,128)S(1)} %convolution_bitcast_fusion.3, f32[32,192,128]{2,1,0:T(8,128)S(1)} %get-tuple-element.29), kind=kOutput, calls=%fused_computation.15 | convolution fusion | flops 302120960 | bytes 4218880 | tf_op jit(solution)/shard_map/cond/branch_1_fun/epi,pw->ewi/dot_general | solution.py:83
  (88 shorter events, 23.3 us)
Async XLA Ops:
  1.4 13.4 %collective-permute-start.10 = (bf16[4,1,32,128]{3,2,1,0:T(8,128)(2,1)S(1)}, bf16[4,1,32,128]{3,2,1,0:T(8,128)(2,1)S(1)}, u32[]{:S(2)}, u32[]{:S(2)}) collective-permute-start(bf16[4,1,32,128]{3,2,1,0:T(8,128)(2,1)S(1)} %get-tuple-element.72), channel_id=1, source_target_pairs={{1,0},{2,1},{3,2},{4,3},{5,4},{6,5},{7,6},{8,7},{9,8},{10,9},{11,1... | collective-permute-start | bytes 98312 | tf_op jit(solution)/shard_map/ppermute | solution.py:101
  7.2 7.7 %collective-permute-start.9 = (bf16[4,1,32,128]{3,2,1,0:T(8,128)(2,1)S(1)}, bf16[4,1,32,128]{3,2,1,0:T(8,128)(2,1)S(1)}, u32[]{:S(2)}, u32[]{:S(2)}) collective-permute-start(bf16[4,1,32,128]{3,2,1,0:T(8,128)(2,1)S(1)} %get-tuple-element.73), channel_id=1, source_target_pairs={{0,1},{1,2},{2,3},{3,4},{4,5},{5,6},{6,7},{7,8},{8,9},{9,10},{10,1... | collective-permute-start | bytes 98312 | tf_op jit(solution)/shard_map/ppermute | solution.py:100
  7.2 6.7 %copy-start.2 = (bf16[4,8,32,128]{3,2,1,0:T(8,128)(2,1)S(1)}, bf16[4,8,32,128]{3,2,1,0:T(8,128)(2,1)}, u32[]{:S(2)}) copy-start(bf16[4,8,32,128]{3,2,1,0:T(8,128)(2,1)} %param.10) | copy-start | bytes 786436
  7.2 7.5 %copy-start.5 = (s32[4,8,5]{1,0,2:T(4,128)S(1)}, s32[4,8,5]{1,0,2:T(4,128)}, u32[]{:S(2)}) copy-start(s32[4,8,5]{1,0,2:T(4,128)} %param.12) | copy-start | bytes 1924
  12.9 1.9 %collective-permute-start.8 = (f32[112,128]{1,0:T(8,128)S(1)}, f32[112,128]{1,0:T(8,128)S(1)}, u32[]{:S(2)}, u32[]{:S(2)}) collective-permute-start(f32[112,128]{1,0:T(8,128)S(1)} %slice_select_fusion), channel_id=1, source_target_pairs={{0,16},{16,0},{32,48},{48,32},{64,80},{80,64},{96,112},{112,96},{1... | collective-permute-start | bytes 172040 | tf_op jit(solution)/shard_map/ppermute | solution.py:30
  14.9 7.4 %collective-permute-start.11 = (f32[56,128]{1,0:T(8,128)S(1)}, f32[56,128]{1,0:T(8,128)S(1)}, u32[]{:S(2)}, u32[]{:S(2)}) collective-permute-start(f32[56,128]{1,0:T(8,128)S(1)} %slice_select_fusion.1), channel_id=1, source_target_pairs={{0,32},{16,48},{32,0},{48,16},{64,96},{80,112},{96,64},{112,80},{1... | collective-permute-start | bytes 86024 | tf_op jit(solution)/shard_map/ppermute | solution.py:30
  16.6 5.8 %collective-permute-start.12 = (bf16[1,10,32,128]{3,2,1,0:T(8,128)(2,1)S(1)}, bf16[1,10,32,128]{3,2,1,0:T(8,128)(2,1)S(1)}, u32[]{:S(2)}, u32[]{:S(2)}) collective-permute-start(bf16[1,10,32,128]{3,2,1,0:T(8,128)(2,1)S(1)} %pad_maximum_fusion.5), channel_id=1, source_target_pairs={{16,0},{32,16},{48,32},{64,48},{80,64},{96,80},{112,96},{128,112},... | collective-permute-start | bytes 245768 | tf_op jit(solution)/shard_map/ppermute | solution.py:109
  19.3 4.4 %collective-permute-start.13 = (bf16[1,10,32,128]{3,2,1,0:T(8,128)(2,1)S(1)}, bf16[1,10,32,128]{3,2,1,0:T(8,128)(2,1)S(1)}, u32[]{:S(2)}, u32[]{:S(2)}) collective-permute-start(bf16[1,10,32,128]{3,2,1,0:T(8,128)(2,1)S(1)} %pad_maximum_fusion.6), channel_id=1, source_target_pairs={{0,16},{16,32},{32,48},{48,64},{64,80},{80,96},{96,112},{112,128},... | collective-permute-start | bytes 245768 | tf_op jit(solution)/shard_map/ppermute | solution.py:108
  25.2 4.2 %copy-start.4 = (bf16[4,8,5,128,128]{4,3,2,1,0:T(8,128)(2,1)S(1)}, bf16[4,8,5,128,128]{4,3,2,1,0:T(8,128)(2,1)}, u32[]{:S(2)}) copy-start(bf16[4,8,5,128,128]{4,3,2,1,0:T(8,128)(2,1)} %param.9) | copy-start | bytes 15728644
  29.5 4.2 %copy-start = (f32[4,8,192,128]{3,2,1,0:T(8,128)S(1)}, f32[4,8,192,128]{3,2,1,0:T(8,128)}, u32[]{:S(2)}) copy-start(f32[4,8,192,128]{3,2,1,0:T(8,128)} %param.11) | copy-start | bytes 9437188
  32.8 0.8 copy-start.1
  36.9 4.6 %collective-permute-start.14 = (f32[112,128]{1,0:T(8,128)S(1)}, f32[112,128]{1,0:T(8,128)S(1)}, u32[]{:S(2)}, u32[]{:S(2)}) collective-permute-start(f32[112,128]{1,0:T(8,128)S(1)} %pad_maximum_fusion.8), channel_id=1, source_target_pairs={{0,64},{16,80},{32,96},{48,112},{64,0},{80,16},{96,32},{112,48},{1... | collective-permute-start | bytes 172040 | tf_op jit(solution)/shard_map/ppermute | solution.py:24
  41.5 7.9 %collective-permute-start.15 = (f32[112,128]{1,0:T(8,128)S(1)}, f32[112,128]{1,0:T(8,128)S(1)}, u32[]{:S(2)}, u32[]{:S(2)}) collective-permute-start(f32[112,128]{1,0:T(8,128)S(1)} %fusion.21), channel_id=1, source_target_pairs={{0,128},{16,144},{32,160},{48,176},{64,192},{80,208},{96,224},{112... | collective-permute-start | bytes 172040 | tf_op jit(solution)/shard_map/ppermute | solution.py:24
  49.5 3.4 %collective-permute-start.16 = (f32[112,128]{1,0:T(8,128)S(1)}, f32[112,128]{1,0:T(8,128)S(1)}, u32[]{:S(2)}, u32[]{:S(2)}) collective-permute-start(f32[112,128]{1,0:T(8,128)S(1)} %add.84), channel_id=1, source_target_pairs={{0,1},{1,0},{2,3},{3,2},{4,5},{5,4},{6,7},{7,6},{8,9},{9,8},{10,11... | collective-permute-start | bytes 172040 | tf_op jit(solution)/shard_map/ppermute | solution.py:24
  52.9 4.6 %collective-permute-start.17 = (f32[112,128]{1,0:T(8,128)S(1)}, f32[112,128]{1,0:T(8,128)S(1)}, u32[]{:S(2)}, u32[]{:S(2)}) collective-permute-start(f32[112,128]{1,0:T(8,128)S(1)} %add.85), channel_id=1, source_target_pairs={{0,2},{1,3},{2,0},{3,1},{4,6},{5,7},{6,4},{7,5},{8,10},{9,11},{10,... | collective-permute-start | bytes 172040 | tf_op jit(solution)/shard_map/ppermute | solution.py:24
  57.5 3.1 %collective-permute-start.18 = (f32[112,128]{1,0:T(8,128)S(1)}, f32[112,128]{1,0:T(8,128)S(1)}, u32[]{:S(2)}, u32[]{:S(2)}) collective-permute-start(f32[112,128]{1,0:T(8,128)S(1)} %add.86), channel_id=1, source_target_pairs={{0,4},{1,5},{2,6},{3,7},{4,0},{5,1},{6,2},{7,3},{8,12},{9,13},{10,... | collective-permute-start | bytes 172040 | tf_op jit(solution)/shard_map/ppermute | solution.py:24
  60.7 4.6 %collective-permute-start.19 = (f32[112,128]{1,0:T(8,128)S(1)}, f32[112,128]{1,0:T(8,128)S(1)}, u32[]{:S(2)}, u32[]{:S(2)}) collective-permute-start(f32[112,128]{1,0:T(8,128)S(1)} %add.87), channel_id=1, source_target_pairs={{0,8},{1,9},{2,10},{3,11},{4,12},{5,13},{6,14},{7,15},{8,0},{9,1},... | collective-permute-start | bytes 172040 | tf_op jit(solution)/shard_map/ppermute | solution.py:24
  65.3 4.2 %collective-permute-start.20 = (f32[112,128]{1,0:T(8,128)S(1)}, f32[112,128]{1,0:T(8,128)S(1)}, u32[]{:S(2)}, u32[]{:S(2)}) collective-permute-start(f32[112,128]{1,0:T(8,128)S(1)} %add.88), channel_id=1, source_target_pairs={{0,32},{16,48},{32,0},{48,16},{64,96},{80,112},{96,64},{112,80},{1... | collective-permute-start | bytes 172040 | tf_op jit(solution)/shard_map/ppermute | solution.py:30
  69.5 10.1 %collective-permute-start.21 = (f32[168,128]{1,0:T(8,128)S(1)}, f32[168,128]{1,0:T(8,128)S(1)}, u32[]{:S(2)}, u32[]{:S(2)}) collective-permute-start(f32[168,128]{1,0:T(8,128)S(1)} %pad_maximum_fusion.4), channel_id=1, source_target_pairs={{0,16},{16,0},{32,48},{48,32},{64,80},{80,64},{96,112},{112,96},{1... | collective-permute-start | bytes 258056 | tf_op jit(solution)/shard_map/ppermute | solution.py:30

commit v9 on v8

--- a/solution.py
+++ b/solution.py
@@ -94,7 +94,9 @@
     radial = [step for axis, step in steps if axis == "rad"]
     around = [("azi", step) for axis, step in steps if axis == "azi"]
 
-    kept_gram = halve(pack_symmetric(mm("epi,eqi->pq", kept_flat, kept_flat)), "rad", radial[0])
+    kept_gram = halve(pack_symmetric(jnp.einsum(
+        "epi,eqi->pq", kept_flat, kept_flat, precision=lax.Precision.HIGH,
+        preferred_element_type=jnp.float32)), "rad", radial[0])
 
     n_a, n_r = lax.axis_size("azi"), lax.axis_size("rad")
     west = lax.ppermute(new_block[:, rows_a - 1 :], "azi", [(i, (i + 1) % n_a) for i in range(n_a)])

time: 101 us -> 101 us (level)
  waiting for transfers between devices: 19.9 us -> 21.3 us
  matrix products: 22 us -> 20.9 us
    dot_general x10 -> x9, matrix products: 18.5 us -> 12.9 us  [mm(): jnp.einsum(spec, a, b, precision=lax.Precision.HIGHEST, preferred_element...]
    dot_general x0 -> x1, matrix products: none -> 4.36 us  [on_device(): jnp.einsum('epi,eqi->pq', kept_flat, kept_flat, precision=lax.Precision.H...]
    ppermute x6, waiting for transfers between devices: 16 us -> 17.4 us  [all_sum(): x = x + lax.ppermute(x, axis, [(i, i ^ step) for i in range(count)])]
    ppermute x1, starting transfers between devices: 2.68 us -> 3.88 us  [on_device(): south = lax.ppermute(row(0), 'rad', [(i + 1, i) for i in range(n_r - 1)])]
  transfers between devices with their start and end apart: 14 -> 14, of which waited for: 10 -> 9; matrix products, arithmetic and copies ran while one was open for 7% -> 5% of each run, Pallas kernels for 0% -> 0%
where the time goes in v9:
time: 101 us; the launch traced here: 100 us
  starting transfers between devices  37.7 us (37%)
  waiting for transfers between devices  21.3 us (21%)
  matrix products  20.9 us (21%)
  other arithmetic  13.4 us (13%)
  local copies, waits for them, and re-layouts  4.77 us (5%)
  between operations  1.65 us (2%)
    ppermute x6, waiting for transfers between devices, all_sum(): x = x + lax.ppermute(x, axis, [(i, i ^ step) for i in range(count)])  17.4 us
    ppermute x4, starting transfers between devices, exchange(): return lax.ppermute(x, axis, [(i, i ^ step) for i in range(count)])  14.7 us
    dot_general x9, matrix products, mm(): jnp.einsum(spec, a, b, precision=lax.Precision.HIGHEST, preferred_element...  12.9 us
    ppermute x6, starting transfers between devices, all_sum(): x = x + lax.ppermute(x, axis, [(i, i ^ step) for i in range(count)])  11.4 us
    ppermute x1, starting transfers between devices, on_device(): lax.ppermute(new_block[:, :1], 'azi', [((i + 1) % n_a, i) for i in range(...  5.76 us
    dot_general x1, matrix products, on_device(): jnp.einsum('epi,eqi->pq', kept_flat, kept_flat, precision=lax.Precision.H...  4.36 us
    unnamed x3, other arithmetic  4.33 us
    ppermute x1, starting transfers between devices, on_device(): south = lax.ppermute(row(0), 'rad', [(i + 1, i) for i in range(n_r - 1)])  3.88 us
  transfers between devices with their start and end apart: 14, of which 9 were waited for; matrix products, arithmetic and copies ran while one was open for 5% of the time, Pallas kernels for 0%

profile of v9, /device:TPU:1, one launch (start us, length us, event | category | flops | bytes accessed | tf_op | source)
XLA Modules:
  0.0 100.0 jit_solution(12737437662845763885)
XLA Ops:
  1.4 5.8 %collective-permute-start.10 = (bf16[4,1,32,128]{3,2,1,0:T(8,128)(2,1)S(1)}, bf16[4,1,32,128]{3,2,1,0:T(8,128)(2,1)S(1)}, u32[]{:S(2)}, u32[]{:S(2)}) collective-permute-start(bf16[4,1,32,128]{3,2,1,0:T(8,128)(2,1)S(1)} %get-tuple-element.72), channel_id=1, source_target_pairs={{1,0},{2,1},{3,2},{4,3},{5,4},{6,5},{7,6},{8,7},{9,8},{10,9},{11,1... | collective-permute-start | bytes 98312 | tf_op jit(solution)/shard_map/ppermute | solution.py:103
  7.2 4.4 %convolution_bitcast_fusion.4 = f32[192,192]{1,0:T(8,128)S(1)} fusion(f32[4,8,192,128]{3,2,1,0:T(8,128)} %param.11), kind=kOutput, calls=%fused_computation.29 | convolution fusion | flops 905969664 | bytes 3293184 | tf_op jit(solution)/shard_map/epi,eqi->pq/dot_general | solution.py:97
  13.7 1.7 %collective-permute-start.11 = (f32[56,128]{1,0:T(8,128)S(1)}, f32[56,128]{1,0:T(8,128)S(1)}, u32[]{:S(2)}, u32[]{:S(2)}) collective-permute-start(f32[56,128]{1,0:T(8,128)S(1)} %slice_select_fusion.1), channel_id=1, source_target_pairs={{0,32},{16,48},{32,0},{48,16},{64,96},{80,112},{96,64},{112,80},{1... | collective-permute-start | bytes 86024 | tf_op jit(solution)/shard_map/ppermute | solution.py:30
  15.4 3.9 %collective-permute-start.12 = (bf16[1,10,32,128]{3,2,1,0:T(8,128)(2,1)S(1)}, bf16[1,10,32,128]{3,2,1,0:T(8,128)(2,1)S(1)}, u32[]{:S(2)}, u32[]{:S(2)}) collective-permute-start(bf16[1,10,32,128]{3,2,1,0:T(8,128)(2,1)S(1)} %pad_maximum_fusion.5), channel_id=1, source_target_pairs={{16,0},{32,16},{48,32},{64,48},{80,64},{96,80},{112,96},{128,112},... | collective-permute-start | bytes 245768 | tf_op jit(solution)/shard_map/ppermute | solution.py:111
  19.3 1.9 %collective-permute-start.13 = (bf16[1,10,32,128]{3,2,1,0:T(8,128)(2,1)S(1)}, bf16[1,10,32,128]{3,2,1,0:T(8,128)(2,1)S(1)}, u32[]{:S(2)}, u32[]{:S(2)}) collective-permute-start(bf16[1,10,32,128]{3,2,1,0:T(8,128)(2,1)S(1)} %pad_maximum_fusion.6), channel_id=1, source_target_pairs={{0,16},{16,32},{32,48},{48,64},{64,80},{80,96},{96,112},{112,128},... | collective-permute-start | bytes 245768 | tf_op jit(solution)/shard_map/ppermute | solution.py:110
  22.7 1.5 %bitcast_dynamic-update-slice_fusion.2 = (bf16[4,8,5,32,128]{4,3,2,1,0:T(8,128)(2,1)}, bf16[4,8,32,128]{3,2,1,0:T(8,128)(2,1)S(1)}, bf16[4,8,32,128]{3,2,1,0:T(8...) fusion(bf16[4,8,5,32,128]{4,3,2,1,0:T(8,128)(2,1)} %bitcast_dynamic-update-slice_fusion.4, ...), kind=kLoop, calls=%fused_computation.56 | loop fusion | flops 5242880 | bytes 2130176
  28.5 3.4 %fusion.32 = f32[4,8,32,128,1]{3,2,4,1,0:T(8,128)S(1)} fusion(bf16[4,8,5,32,128]{4,3,2,1,0:T(8,128)(2,1)} %bitcast_dynamic-update-slice_fusion.3, bf16[4,8,5,128,128]{4,3,2,1,0:T(8,128)(2,1)S(1)} %copy-done.4), kind=kOutput, calls=%fused_computation.126 | convolution fusion | flops 167772160 | bytes 7077888 | tf_op jit(solution)/shard_map/rakij,rakvj->ravi/dot_general | solution.py:124
  32.7 2.9 %convolution_bitcast_fusion.5 = f32[192,32]{0,1:T(8,128)S(1)} fusion(f32[4,8,192,128]{3,2,1,0:T(8,128)S(1)} %copy-done, f32[4,8,32,128,1]{3,2,4,1,0:T(8,128)S(1)} %fusion.32), kind=kOutput, calls=%fused_computation.30 | convolution fusion | flops 301989888 | bytes 3694592 | tf_op jit(solution)/shard_map/epi,evi->pv/dot_general | solution.py:83
  35.9 3.1 %collective-permute-start.14 = (f32[112,128]{1,0:T(8,128)S(1)}, f32[112,128]{1,0:T(8,128)S(1)}, u32[]{:S(2)}, u32[]{:S(2)}) collective-permute-start(f32[112,128]{1,0:T(8,128)S(1)} %pad_maximum_fusion.8), channel_id=1, source_target_pairs={{0,64},{16,80},{32,96},{48,112},{64,0},{80,16},{96,32},{112,48},{1... | collective-permute-start | bytes 172040 | tf_op jit(solution)/shard_map/ppermute | solution.py:24
  39.0 1.6 %collective-permute-done.14 = f32[112,128]{1,0:T(8,128)S(1)} collective-permute-done((f32[112,128]{1,0:T(8,128)S(1)}, f32[112,128]{1,0:T(8,128)S(1)}, u32[]{:S(2)}, u32[]{:S(2)}) %collective-permute-start.14) | collective-permute-done | bytes 57376 | tf_op jit(solution)/shard_map/ppermute | solution.py:24
  40.6 6.7 %collective-permute-start.15 = (f32[112,128]{1,0:T(8,128)S(1)}, f32[112,128]{1,0:T(8,128)S(1)}, u32[]{:S(2)}, u32[]{:S(2)}) collective-permute-start(f32[112,128]{1,0:T(8,128)S(1)} %fusion.21), channel_id=1, source_target_pairs={{0,128},{16,144},{32,160},{48,176},{64,192},{80,208},{96,224},{112... | collective-permute-start | bytes 172040 | tf_op jit(solution)/shard_map/ppermute | solution.py:24
  47.3 1.6 %collective-permute-done.15 = f32[112,128]{1,0:T(8,128)S(1)} collective-permute-done((f32[112,128]{1,0:T(8,128)S(1)}, f32[112,128]{1,0:T(8,128)S(1)}, u32[]{:S(2)}, u32[]{:S(2)}) %collective-permute-start.15) | collective-permute-done | bytes 57376 | tf_op jit(solution)/shard_map/ppermute | solution.py:24
  49.0 3.3 %collective-permute-done.16 = f32[112,128]{1,0:T(8,128)S(1)} collective-permute-done((f32[112,128]{1,0:T(8,128)S(1)}, f32[112,128]{1,0:T(8,128)S(1)}, u32[]{:S(2)}, u32[]{:S(2)}) %collective-permute-start.16) | collective-permute-done | bytes 57376 | tf_op jit(solution)/shard_map/ppermute | solution.py:24
  52.9 4.2 %collective-permute-done.17 = f32[112,128]{1,0:T(8,128)S(1)} collective-permute-done((f32[112,128]{1,0:T(8,128)S(1)}, f32[112,128]{1,0:T(8,128)S(1)}, u32[]{:S(2)}, u32[]{:S(2)}) %collective-permute-start.17) | collective-permute-done | bytes 57376 | tf_op jit(solution)/shard_map/ppermute | solution.py:24
  57.2 3.0 %collective-permute-done.18 = f32[112,128]{1,0:T(8,128)S(1)} collective-permute-done((f32[112,128]{1,0:T(8,128)S(1)}, f32[112,128]{1,0:T(8,128)S(1)}, u32[]{:S(2)}, u32[]{:S(2)}) %collective-permute-start.18) | collective-permute-done | bytes 57376 | tf_op jit(solution)/shard_map/ppermute | solution.py:24
  61.1 3.7 %collective-permute-done.19 = f32[112,128]{1,0:T(8,128)S(1)} collective-permute-done((f32[112,128]{1,0:T(8,128)S(1)}, f32[112,128]{1,0:T(8,128)S(1)}, u32[]{:S(2)}, u32[]{:S(2)}) %collective-permute-start.19) | collective-permute-done | bytes 57376 | tf_op jit(solution)/shard_map/ppermute | solution.py:24
  64.9 2.7 %collective-permute-start.20 = (f32[112,128]{1,0:T(8,128)S(1)}, f32[112,128]{1,0:T(8,128)S(1)}, u32[]{:S(2)}, u32[]{:S(2)}) collective-permute-start(f32[112,128]{1,0:T(8,128)S(1)} %add.88), channel_id=1, source_target_pairs={{0,32},{16,48},{32,0},{48,16},{64,96},{80,112},{96,64},{112,80},{1... | collective-permute-start | bytes 172040 | tf_op jit(solution)/shard_map/ppermute | solution.py:30
  67.6 1.6 %collective-permute-done.20 = f32[112,128]{1,0:T(8,128)S(1)} collective-permute-done((f32[112,128]{1,0:T(8,128)S(1)}, f32[112,128]{1,0:T(8,128)S(1)}, u32[]{:S(2)}, u32[]{:S(2)}) %collective-permute-start.20) | collective-permute-done | bytes 57376 | tf_op jit(solution)/shard_map/ppermute | solution.py:30
  69.2 9.2 %collective-permute-start.21 = (f32[168,128]{1,0:T(8,128)S(1)}, f32[168,128]{1,0:T(8,128)S(1)}, u32[]{:S(2)}, u32[]{:S(2)}) collective-permute-start(f32[168,128]{1,0:T(8,128)S(1)} %pad_maximum_fusion.4), channel_id=1, source_target_pairs={{0,16},{16,0},{32,48},{48,32},{64,80},{80,64},{96,112},{112,96},{1... | collective-permute-start | bytes 258056 | tf_op jit(solution)/shard_map/ppermute | solution.py:30
  86.7 12.6 %conditional.1 = (f32[32,32]{1,0:T(8,128)S(1)}, f32[4,8,32,128]{3,2,1,0:T(8,128)}) conditional(s32[]{:T(128)} %convert_element_type.8, (f32[192,32]{0,1:T(8,128)}, f32[32,192,128]{2,1,0:T(8,128)S(1)}, f32[32,32,128]{2,1,0:T(8,128)}, f32[32,32]{0,1:T(8,128)S(1)}) %tuple.79, (f32[32,32]{0,1:T(8,128)S(1)}, f32[32,32]{0,1:T(8,128)S(1)}, ...), branch_computations={%region_3.8_spmd, %region_6.9_spmd} | conditional | flops 403195936 | bytes 8176238 | solution.py:173
  87.0 2.9 %cholesky.55 = f32[32,32]{1,0:T(8,128)S(1)} custom-call(f32[32,32]{1,0:T(8,128)S(1)} %fusion.8), custom_call_target="Cholesky" | custom-call | tf_op jit(solution)/shard_map/cond/branch_1_fun/jit(cholesky)/cholesky | solution.py:157
  91.3 2.4 %custom-call.7 = f32[1,32,32]{1,2,0:T(8,128)S(1)} custom-call(f32[1,32,32]{2,1,0:T(8,128)S(1)} %get-tuple-element.63), custom_call_target="InvertDiagBlocksLowerTriangular" | custom-call | tf_op jit(solution)/shard_map/cond/branch_1_fun/triangular_solve/custom-call.0 | solution.py:158
  94.9 1.6 %fusion.4 = f32[32,32,128]{2,0,1:T(8,128)S(1)} fusion(f32[32,32,128]{2,1,0:T(8,128)} %get-tuple-element.27, f32[32,32]{1,0:T(8,128)S(1)} %fusion.6), kind=kOutput, calls=%fused_computation.17 | convolution fusion | flops 50331648 | bytes 1052672 | tf_op jit(solution)/shard_map/cond/branch_1_fun/evi,wv->ewi/dot_general | solution.py:83
  96.5 2.8 %convolution_subtract_fusion = f32[32,32,128]{2,0,1:T(8,128)} fusion(f32[32,32,128]{2,0,1:T(8,128)S(1)} %fusion.4, f32[32,192,1]{1,0,2:T(8,128)S(1)} %convolution_bitcast_fusion.3, f32[32,192,128]{2,1,0:T(8,128)S(1)} %get-tuple-element.29), kind=kOutput, calls=%fused_computation.15 | convolution fusion | flops 302120960 | bytes 4218880 | tf_op jit(solution)/shard_map/cond/branch_1_fun/epi,pw->ewi/dot_general | solution.py:83
  (88 shorter events, 22.1 us)
Async XLA Ops:
  1.4 12.2 %collective-permute-start.10 = (bf16[4,1,32,128]{3,2,1,0:T(8,128)(2,1)S(1)}, bf16[4,1,32,128]{3,2,1,0:T(8,128)(2,1)S(1)}, u32[]{:S(2)}, u32[]{:S(2)}) collective-permute-start(bf16[4,1,32,128]{3,2,1,0:T(8,128)(2,1)S(1)} %get-tuple-element.72), channel_id=1, source_target_pairs={{1,0},{2,1},{3,2},{4,3},{5,4},{6,5},{7,6},{8,7},{9,8},{10,9},{11,1... | collective-permute-start | bytes 98312 | tf_op jit(solution)/shard_map/ppermute | solution.py:103
  7.2 6.5 %collective-permute-start.9 = (bf16[4,1,32,128]{3,2,1,0:T(8,128)(2,1)S(1)}, bf16[4,1,32,128]{3,2,1,0:T(8,128)(2,1)S(1)}, u32[]{:S(2)}, u32[]{:S(2)}) collective-permute-start(bf16[4,1,32,128]{3,2,1,0:T(8,128)(2,1)S(1)} %get-tuple-element.73), channel_id=1, source_target_pairs={{0,1},{1,2},{2,3},{3,4},{4,5},{5,6},{6,7},{7,8},{8,9},{9,10},{10,1... | collective-permute-start | bytes 98312 | tf_op jit(solution)/shard_map/ppermute | solution.py:102
  7.2 5.5 %copy-start.2 = (bf16[4,8,32,128]{3,2,1,0:T(8,128)(2,1)S(1)}, bf16[4,8,32,128]{3,2,1,0:T(8,128)(2,1)}, u32[]{:S(2)}) copy-start(bf16[4,8,32,128]{3,2,1,0:T(8,128)(2,1)} %param.10) | copy-start | bytes 786436
  7.2 6.3 %copy-start.5 = (s32[4,8,5]{1,0,2:T(4,128)S(1)}, s32[4,8,5]{1,0,2:T(4,128)}, u32[]{:S(2)}) copy-start(s32[4,8,5]{1,0,2:T(4,128)} %param.12) | copy-start | bytes 1924
  11.7 1.9 %collective-permute-start.8 = (f32[112,128]{1,0:T(8,128)S(1)}, f32[112,128]{1,0:T(8,128)S(1)}, u32[]{:S(2)}, u32[]{:S(2)}) collective-permute-start(f32[112,128]{1,0:T(8,128)S(1)} %slice_select_fusion), channel_id=1, source_target_pairs={{0,16},{16,0},{32,48},{48,32},{64,80},{80,64},{96,112},{112,96},{1... | collective-permute-start | bytes 172040 | tf_op jit(solution)/shard_map/ppermute | solution.py:30
  13.7 7.6 %collective-permute-start.11 = (f32[56,128]{1,0:T(8,128)S(1)}, f32[56,128]{1,0:T(8,128)S(1)}, u32[]{:S(2)}, u32[]{:S(2)}) collective-permute-start(f32[56,128]{1,0:T(8,128)S(1)} %slice_select_fusion.1), channel_id=1, source_target_pairs={{0,32},{16,48},{32,0},{48,16},{64,96},{80,112},{96,64},{112,80},{1... | collective-permute-start | bytes 86024 | tf_op jit(solution)/shard_map/ppermute | solution.py:30
  15.4 5.9 %collective-permute-start.12 = (bf16[1,10,32,128]{3,2,1,0:T(8,128)(2,1)S(1)}, bf16[1,10,32,128]{3,2,1,0:T(8,128)(2,1)S(1)}, u32[]{:S(2)}, u32[]{:S(2)}) collective-permute-start(bf16[1,10,32,128]{3,2,1,0:T(8,128)(2,1)S(1)} %pad_maximum_fusion.5), channel_id=1, source_target_pairs={{16,0},{32,16},{48,32},{64,48},{80,64},{96,80},{112,96},{128,112},... | collective-permute-start | bytes 245768 | tf_op jit(solution)/shard_map/ppermute | solution.py:111
  19.3 3.4 %collective-permute-start.13 = (bf16[1,10,32,128]{3,2,1,0:T(8,128)(2,1)S(1)}, bf16[1,10,32,128]{3,2,1,0:T(8,128)(2,1)S(1)}, u32[]{:S(2)}, u32[]{:S(2)}) collective-permute-start(bf16[1,10,32,128]{3,2,1,0:T(8,128)(2,1)S(1)} %pad_maximum_fusion.6), channel_id=1, source_target_pairs={{0,16},{16,32},{32,48},{48,64},{64,80},{80,96},{96,112},{112,128},... | collective-permute-start | bytes 245768 | tf_op jit(solution)/shard_map/ppermute | solution.py:110
  24.3 4.2 %copy-start.4 = (bf16[4,8,5,128,128]{4,3,2,1,0:T(8,128)(2,1)S(1)}, bf16[4,8,5,128,128]{4,3,2,1,0:T(8,128)(2,1)}, u32[]{:S(2)}) copy-start(bf16[4,8,5,128,128]{4,3,2,1,0:T(8,128)(2,1)} %param.9) | copy-start | bytes 15728644
  28.5 4.2 %copy-start = (f32[4,8,192,128]{3,2,1,0:T(8,128)S(1)}, f32[4,8,192,128]{3,2,1,0:T(8,128)}, u32[]{:S(2)}) copy-start(f32[4,8,192,128]{3,2,1,0:T(8,128)} %param.11) | copy-start | bytes 9437188
  31.9 0.8 copy-start.1
  35.9 4.6 %collective-permute-start.14 = (f32[112,128]{1,0:T(8,128)S(1)}, f32[112,128]{1,0:T(8,128)S(1)}, u32[]{:S(2)}, u32[]{:S(2)}) collective-permute-start(f32[112,128]{1,0:T(8,128)S(1)} %pad_maximum_fusion.8), channel_id=1, source_target_pairs={{0,64},{16,80},{32,96},{48,112},{64,0},{80,16},{96,32},{112,48},{1... | collective-permute-start | bytes 172040 | tf_op jit(solution)/shard_map/ppermute | solution.py:24
  40.6 8.3 %collective-permute-start.15 = (f32[112,128]{1,0:T(8,128)S(1)}, f32[112,128]{1,0:T(8,128)S(1)}, u32[]{:S(2)}, u32[]{:S(2)}) collective-permute-start(f32[112,128]{1,0:T(8,128)S(1)} %fusion.21), channel_id=1, source_target_pairs={{0,128},{16,144},{32,160},{48,176},{64,192},{80,208},{96,224},{112... | collective-permute-start | bytes 172040 | tf_op jit(solution)/shard_map/ppermute | solution.py:24
  48.9 3.4 %collective-permute-start.16 = (f32[112,128]{1,0:T(8,128)S(1)}, f32[112,128]{1,0:T(8,128)S(1)}, u32[]{:S(2)}, u32[]{:S(2)}) collective-permute-start(f32[112,128]{1,0:T(8,128)S(1)} %add.84), channel_id=1, source_target_pairs={{0,1},{1,0},{2,3},{3,2},{4,5},{5,4},{6,7},{7,6},{8,9},{9,8},{10,11... | collective-permute-start | bytes 172040 | tf_op jit(solution)/shard_map/ppermute | solution.py:24
  52.3 4.8 %collective-permute-start.17 = (f32[112,128]{1,0:T(8,128)S(1)}, f32[112,128]{1,0:T(8,128)S(1)}, u32[]{:S(2)}, u32[]{:S(2)}) collective-permute-start(f32[112,128]{1,0:T(8,128)S(1)} %add.85), channel_id=1, source_target_pairs={{0,2},{1,3},{2,0},{3,1},{4,6},{5,7},{6,4},{7,5},{8,10},{9,11},{10,... | collective-permute-start | bytes 172040 | tf_op jit(solution)/shard_map/ppermute | solution.py:24
  57.1 3.1 %collective-permute-start.18 = (f32[112,128]{1,0:T(8,128)S(1)}, f32[112,128]{1,0:T(8,128)S(1)}, u32[]{:S(2)}, u32[]{:S(2)}) collective-permute-start(f32[112,128]{1,0:T(8,128)S(1)} %add.86), channel_id=1, source_target_pairs={{0,4},{1,5},{2,6},{3,7},{4,0},{5,1},{6,2},{7,3},{8,12},{9,13},{10,... | collective-permute-start | bytes 172040 | tf_op jit(solution)/shard_map/ppermute | solution.py:24
  60.2 4.6 %collective-permute-start.19 = (f32[112,128]{1,0:T(8,128)S(1)}, f32[112,128]{1,0:T(8,128)S(1)}, u32[]{:S(2)}, u32[]{:S(2)}) collective-permute-start(f32[112,128]{1,0:T(8,128)S(1)} %add.87), channel_id=1, source_target_pairs={{0,8},{1,9},{2,10},{3,11},{4,12},{5,13},{6,14},{7,15},{8,0},{9,1},... | collective-permute-start | bytes 172040 | tf_op jit(solution)/shard_map/ppermute | solution.py:24
  64.9 4.3 %collective-permute-start.20 = (f32[112,128]{1,0:T(8,128)S(1)}, f32[112,128]{1,0:T(8,128)S(1)}, u32[]{:S(2)}, u32[]{:S(2)}) collective-permute-start(f32[112,128]{1,0:T(8,128)S(1)} %add.88), channel_id=1, source_target_pairs={{0,32},{16,48},{32,0},{48,16},{64,96},{80,112},{96,64},{112,80},{1... | collective-permute-start | bytes 172040 | tf_op jit(solution)/shard_map/ppermute | solution.py:30
  69.2 10.2 %collective-permute-start.21 = (f32[168,128]{1,0:T(8,128)S(1)}, f32[168,128]{1,0:T(8,128)S(1)}, u32[]{:S(2)}, u32[]{:S(2)}) collective-permute-start(f32[168,128]{1,0:T(8,128)S(1)} %pad_maximum_fusion.4), channel_id=1, source_target_pairs={{0,16},{16,0},{32,48},{48,32},{64,80},{80,64},{96,112},{112,96},{1... | collective-permute-start | bytes 258056 | tf_op jit(solution)/shard_map/ppermute | solution.py:30

commit v10 on v8

--- a/solution.py
+++ b/solution.py
@@ -20,14 +20,21 @@
 
 def all_sum(x, steps):
     for axis, step in steps:
-        count = lax.axis_size(axis)
-        x = x + lax.ppermute(x, axis, [(i, i ^ step) for i in range(count)])
+        x = x + exchange(x, axis, step)
     return x
+
+
+def partner(axis, step, i):
+    if axis == "azi" and step in (2, 8):
+        unit = step // 2
+        digit = (i // unit) % 4
+        return i + (3 - digit - digit) * unit
+    return i ^ step
 
 
 def exchange(x, axis, step):
     count = lax.axis_size(axis)
-    return lax.ppermute(x, axis, [(i, i ^ step) for i in range(count)])
+    return lax.ppermute(x, axis, [(i, partner(axis, step, i)) for i in range(count)])
 
 
 def upper_bit(axis, step):
@@ -111,15 +118,15 @@
         [north, jnp.concatenate([west, new_block, east], axis=1), south], axis=0
     )
     shifted = [padded[c // 3 : c // 3 + rows_r, c % 3 : c % 3 + rows_a] for c in range(9)]
-    slots = [new_block]
+    image = jnp.einsum("raij,ravj->ravi", jacobian[:, :, 0], new_block, preferred_element_type=jnp.float32)
     for k in range(1, 5):
         code = columns[:, :, k][:, :, None, None]
         pick = shifted[0]
         for c in range(1, 9):
             pick = jnp.where(code == c, shifted[c], pick)
-        slots.append(pick)
-    picked = jnp.stack(slots, axis=2)
-    image = jnp.einsum("rakij,rakvj->ravi", jacobian, picked, preferred_element_type=jnp.float32)
+        image = image + jnp.einsum(
+            "raij,ravj->ravi", jacobian[:, :, k], pick, preferred_element_type=jnp.float32
+        )
     image = image.reshape(elements, NEW, BLK)
 
     moments = jnp.concatenate(

time: 101 us -> 101 us (level)
  waiting for transfers between devices: 19.9 us -> 25.8 us
  other arithmetic: 13.4 us -> 7.72 us
  matrix products: 22 us -> 24.9 us
  starting transfers between devices: 38.2 us -> 36.1 us
    unnamed x3 -> x0, other arithmetic: 4.33 us -> none
    ppermute x1, waiting for transfers between devices: 0.01 us -> 4.05 us  [on_device(): lax.ppermute(new_block[:, rows_a - 1:], 'azi', [(i, (i + 1) % n_a) for i...]
    dot_general x1 -> x5, matrix products: 3.36 us -> 6.19 us  [the longest x4 4.31 us: on_device(): jnp.einsum('raij,ravj->ravi', jacobian[:, :, k], pick, preferred_element_...]
    ppermute x1, starting transfers between devices: 5.76 us -> 3.27 us  [on_device(): lax.ppermute(new_block[:, :1], 'azi', [((i + 1) % n_a, i) for i in range(...]
    ppermute x10, waiting for transfers between devices: 18.5 us -> 20.4 us  [exchange(): lax.ppermute(x, axis, [(i, partner(axis, step, i)) for i in range(count)])]
    another operation x1 -> x0, other arithmetic: 1.43 us -> none  [on_device(): picked = jnp.stack(slots, axis=2)]
  transfers between devices with their start and end apart: 14 -> 14, of which waited for: 10 -> 11; matrix products, arithmetic and copies ran while one was open for 7% -> 2% of each run, Pallas kernels for 0% -> 0%
where the time goes in v10:
time: 101 us
  starting transfers between devices  36.1 us (36%)
  waiting for transfers between devices  25.8 us (26%)
  matrix products  24.9 us (25%)
  other arithmetic  7.72 us (8%)
  local copies, waits for them, and re-layouts  4.15 us (4%)
  between operations  1.69 us (2%)
    ppermute x10, starting transfers between devices, exchange(): lax.ppermute(x, axis, [(i, partner(axis, step, i)) for i in range(count)])  27.3 us
    ppermute x10, waiting for transfers between devices, exchange(): lax.ppermute(x, axis, [(i, partner(axis, step, i)) for i in range(count)])  20.4 us
    dot_general x10, matrix products, mm(): jnp.einsum(spec, a, b, precision=lax.Precision.HIGHEST, preferred_element...  18.4 us
    dot_general x4, matrix products, on_device(): jnp.einsum('raij,ravj->ravi', jacobian[:, :, k], pick, preferred_element_...  4.31 us
    ppermute x1, waiting for transfers between devices, on_device(): lax.ppermute(new_block[:, rows_a - 1:], 'azi', [(i, (i + 1) % n_a) for i...  4.05 us
    ppermute x1, starting transfers between devices, on_device(): south = lax.ppermute(row(0), 'rad', [(i + 1, i) for i in range(n_r - 1)])  3.64 us
    another operation x3, other arithmetic, factor_of(): lower = jnp.linalg.cholesky(gram)  3.6 us
    ppermute x1, starting transfers between devices, on_device(): lax.ppermute(new_block[:, :1], 'azi', [((i + 1) % n_a, i) for i in range(...  3.27 us
  transfers between devices with their start and end apart: 14, of which 11 were waited for; matrix products, arithmetic and copies ran while one was open for 2% of the time, Pallas kernels for 0%

profile of v10, /device:TPU:1, one launch (start us, length us, event | category | flops | bytes accessed | tf_op | source)
XLA Modules:
  0.0 100.6 jit_solution(10632350410782565385)
XLA Ops:
  0.7 5.5 %convolution_bitcast_fusion.4 = f32[192,192]{1,0:T(8,128)S(1)} fusion(f32[4,8,192,128]{3,2,1,0:T(8,128)} %param.11), kind=kOutput, calls=%fused_computation.33 | convolution fusion | flops 1811939328 | bytes 3293184 | tf_op jit(solution)/shard_map/epi,eqi->pq/dot_general | solution.py:90
  6.3 3.3 %collective-permute-start.8 = (f32[112,128]{1,0:T(8,128)S(1)}, f32[112,128]{1,0:T(8,128)S(1)}, u32[]{:S(2)}, u32[]{:S(2)}) collective-permute-start(f32[112,128]{1,0:T(8,128)S(1)} %slice_select_fusion), channel_id=1, source_target_pairs={{0,16},{16,0},{32,48},{48,32},{64,80},{80,64},{96,112},{112,96},{1... | collective-permute-start | bytes 172040 | tf_op jit(solution)/shard_map/ppermute | solution.py:37
  9.7 3.3 %collective-permute-start.10 = (bf16[4,1,32,128]{3,2,1,0:T(8,128)(2,1)S(1)}, bf16[4,1,32,128]{3,2,1,0:T(8,128)(2,1)S(1)}, u32[]{:S(2)}, u32[]{:S(2)}) collective-permute-start(bf16[4,1,32,128]{3,2,1,0:T(8,128)(2,1)S(1)} %get-tuple-element.73), channel_id=1, source_target_pairs={{1,0},{2,1},{3,2},{4,3},{5,4},{6,5},{7,6},{8,7},{9,8},{10,9},{11,1... | collective-permute-start | bytes 98312 | tf_op jit(solution)/shard_map/ppermute | solution.py:108
  13.0 1.9 %fusion.15 = f32[4,8,32,128]{3,2,1,0:T(8,128)S(1)} fusion(bf16[4,8,32,128]{3,2,1,0:T(8,128)(2,1)S(1)} %copy-done.3, bf16[4,8,5,128,128]{4,3,2,1,0:T(8,128)(2,1)} %param.9), kind=kOutput, calls=%fused_computation.44 | convolution fusion | flops 33554432 | bytes 1835008 | tf_op jit(solution)/shard_map/raij,ravj->ravi/dot_general | solution.py:121
  15.0 4.0 %collective-permute-done.9 = bf16[4,1,32,128]{3,2,1,0:T(8,128)(2,1)S(1)} collective-permute-done((bf16[4,1,32,128]{3,2,1,0:T(8,128)(2,1)S(1)}, bf16[4,1,32,128]{3,2,1,0:T(8,128)(2,1)S(1)}, u32[]{:S(2)}, u32[]{:S(2)}) %collective-permute-start.9) | collective-permute-done | bytes 32800 | tf_op jit(solution)/shard_map/ppermute | solution.py:107
  19.0 1.6 %collective-permute-start.11 = (f32[56,128]{1,0:T(8,128)S(1)}, f32[56,128]{1,0:T(8,128)S(1)}, u32[]{:S(2)}, u32[]{:S(2)}) collective-permute-start(f32[56,128]{1,0:T(8,128)S(1)} %slice_select_fusion.1), channel_id=1, source_target_pairs={{0,32},{16,48},{32,0},{48,16},{64,96},{80,112},{96,64},{112,80},{1... | collective-permute-start | bytes 86024 | tf_op jit(solution)/shard_map/ppermute | solution.py:37
  20.7 3.6 %collective-permute-start.12 = (bf16[1,10,32,128]{3,2,1,0:T(8,128)(2,1)S(1)}, bf16[1,10,32,128]{3,2,1,0:T(8,128)(2,1)S(1)}, u32[]{:S(2)}, u32[]{:S(2)}) collective-permute-start(bf16[1,10,32,128]{3,2,1,0:T(8,128)(2,1)S(1)} %pad_maximum_fusion.5), channel_id=1, source_target_pairs={{16,0},{32,16},{48,32},{64,48},{80,64},{96,80},{112,96},{128,112},... | collective-permute-start | bytes 245768 | tf_op jit(solution)/shard_map/ppermute | solution.py:116
  24.4 1.9 %collective-permute-start.13 = (bf16[1,10,32,128]{3,2,1,0:T(8,128)(2,1)S(1)}, bf16[1,10,32,128]{3,2,1,0:T(8,128)(2,1)S(1)}, u32[]{:S(2)}, u32[]{:S(2)}) collective-permute-start(bf16[1,10,32,128]{3,2,1,0:T(8,128)(2,1)S(1)} %pad_maximum_fusion.6), channel_id=1, source_target_pairs={{0,16},{16,32},{32,48},{48,64},{64,80},{80,96},{96,112},{112,128},... | collective-permute-start | bytes 245768 | tf_op jit(solution)/shard_map/ppermute | solution.py:115
  27.8 2.1 %convolution_add_fusion.3 = f32[4,8,32,128]{3,2,1,0:T(8,128)S(1)} fusion(f32[4,8,32,128]{3,2,1,0:T(8,128)S(1)} %fusion.15, bf16[4,8,5,128,128]{4,3,2,1,0:T(8,128)(2,1)} %param.9, bf16[4,8,32,128]{3,2,1,0:T(8,128)(2,1)S(1)} %get-tuple-element.69, bf16[4,8,32,128]{3,2,1,0:T(8,128)(2,1)S(1)} %get-tuple-element.70, bf16[4,8,32,128]{3,2,1,0:T(8,128)(2,1)S(1)} %copy-done.3, ...), kind=kOutput, calls=%fused_computation.32 | convolution fusion | flops 35258368 | bytes 3965184 | tf_op jit(solution)/shard_map/raij,ravj->ravi/dot_general | solution.py:127
  33.4 2.9 %convolution_bitcast_fusion.5 = f32[192,32]{0,1:T(8,128)S(1)} fusion(f32[4,8,32,128]{3,2,1,0:T(8,128)S(1)} %convolution_add_fusion, f32[4,8,192,128]{3,2,1,0:T(8,128)S(1)} %copy-done), kind=kOutput, calls=%fused_computation.34 | convolution fusion | flops 301989888 | bytes 3694592 | tf_op jit(solution)/shard_map/epi,evi->pv/dot_general | solution.py:90
  37.2 3.1 %collective-permute-start.14 = (f32[112,128]{1,0:T(8,128)S(1)}, f32[112,128]{1,0:T(8,128)S(1)}, u32[]{:S(2)}, u32[]{:S(2)}) collective-permute-start(f32[112,128]{1,0:T(8,128)S(1)} %pad_maximum_fusion.8), channel_id=1, source_target_pairs={{0,64},{16,80},{32,96},{48,112},{64,0},{80,16},{96,32},{112,48},{1... | collective-permute-start | bytes 172040 | tf_op jit(solution)/shard_map/ppermute | solution.py:37
  40.2 1.6 %collective-permute-done.14 = f32[112,128]{1,0:T(8,128)S(1)} collective-permute-done((f32[112,128]{1,0:T(8,128)S(1)}, f32[112,128]{1,0:T(8,128)S(1)}, u32[]{:S(2)}, u32[]{:S(2)}) %collective-permute-start.14) | collective-permute-done | bytes 57376 | tf_op jit(solution)/shard_map/ppermute | solution.py:37
  41.8 6.9 %collective-permute-start.15 = (f32[112,128]{1,0:T(8,128)S(1)}, f32[112,128]{1,0:T(8,128)S(1)}, u32[]{:S(2)}, u32[]{:S(2)}) collective-permute-start(f32[112,128]{1,0:T(8,128)S(1)} %fusion.94), channel_id=1, source_target_pairs={{0,128},{16,144},{32,160},{48,176},{64,192},{80,208},{96,224},{112... | collective-permute-start | bytes 172040 | tf_op jit(solution)/shard_map/ppermute | solution.py:37
  50.4 3.3 %collective-permute-done.16 = f32[112,128]{1,0:T(8,128)S(1)} collective-permute-done((f32[112,128]{1,0:T(8,128)S(1)}, f32[112,128]{1,0:T(8,128)S(1)}, u32[]{:S(2)}, u32[]{:S(2)}) %collective-permute-start.16) | collective-permute-done | bytes 57376 | tf_op jit(solution)/shard_map/ppermute | solution.py:37
  53.8 4.2 %collective-permute-done.17 = f32[112,128]{1,0:T(8,128)S(1)} collective-permute-done((f32[112,128]{1,0:T(8,128)S(1)}, f32[112,128]{1,0:T(8,128)S(1)}, u32[]{:S(2)}, u32[]{:S(2)}) %collective-permute-start.17) | collective-permute-done | bytes 57376 | tf_op jit(solution)/shard_map/ppermute | solution.py:37
  58.1 3.0 %collective-permute-done.18 = f32[112,128]{1,0:T(8,128)S(1)} collective-permute-done((f32[112,128]{1,0:T(8,128)S(1)}, f32[112,128]{1,0:T(8,128)S(1)}, u32[]{:S(2)}, u32[]{:S(2)}) %collective-permute-start.18) | collective-permute-done | bytes 57376 | tf_op jit(solution)/shard_map/ppermute | solution.py:37
  61.3 4.2 %collective-permute-done.19 = f32[112,128]{1,0:T(8,128)S(1)} collective-permute-done((f32[112,128]{1,0:T(8,128)S(1)}, f32[112,128]{1,0:T(8,128)S(1)}, u32[]{:S(2)}, u32[]{:S(2)}) %collective-permute-start.19) | collective-permute-done | bytes 57376 | tf_op jit(solution)/shard_map/ppermute | solution.py:37
  65.5 2.3 %collective-permute-start.20 = (f32[112,128]{1,0:T(8,128)S(1)}, f32[112,128]{1,0:T(8,128)S(1)}, u32[]{:S(2)}, u32[]{:S(2)}) collective-permute-start(f32[112,128]{1,0:T(8,128)S(1)} %add.104), channel_id=1, source_target_pairs={{0,32},{16,48},{32,0},{48,16},{64,96},{80,112},{96,64},{112,80},{1... | collective-permute-start | bytes 172040 | tf_op jit(solution)/shard_map/ppermute | solution.py:37
  69.4 9.6 %collective-permute-start.21 = (f32[168,128]{1,0:T(8,128)S(1)}, f32[168,128]{1,0:T(8,128)S(1)}, u32[]{:S(2)}, u32[]{:S(2)}) collective-permute-start(f32[168,128]{1,0:T(8,128)S(1)} %pad_maximum_fusion.4), channel_id=1, source_target_pairs={{0,16},{16,0},{32,48},{48,32},{64,80},{80,64},{96,112},{112,96},{1... | collective-permute-start | bytes 258056 | tf_op jit(solution)/shard_map/ppermute | solution.py:37
  87.3 12.6 %conditional.1 = (f32[32,32]{1,0:T(8,128)S(1)}, f32[4,8,32,128]{3,2,1,0:T(8,128)}) conditional(s32[]{:T(128)} %convert_element_type.8, (f32[192,32]{0,1:T(8,128)}, f32[32,192,128]{2,1,0:T(8,128)S(1)}, f32[32,32,128]{2,1,0:T(8,128)}, f32[32,32]{0,1:T(8,128)S(1)}) %tuple.79, (f32[32,32]{0,1:T(8,128)S(1)}, f32[32,32]{0,1:T(8,128)S(1)}, ...), branch_computations={%region_3.8_spmd, %region_6.9_spmd} | conditional | flops 403195936 | bytes 8176238 | solution.py:178
  87.7 2.9 %cholesky.55 = f32[32,32]{1,0:T(8,128)S(1)} custom-call(f32[32,32]{1,0:T(8,128)S(1)} %fusion.8), custom_call_target="Cholesky" | custom-call | tf_op jit(solution)/shard_map/cond/branch_1_fun/jit(cholesky)/cholesky | solution.py:162
  91.9 2.4 %custom-call.7 = f32[1,32,32]{1,2,0:T(8,128)S(1)} custom-call(f32[1,32,32]{2,1,0:T(8,128)S(1)} %get-tuple-element.63), custom_call_target="InvertDiagBlocksLowerTriangular" | custom-call | tf_op jit(solution)/shard_map/cond/branch_1_fun/triangular_solve/custom-call.0 | solution.py:163
  94.6 1.6 %fusion.4 = f32[32,32,128]{2,0,1:T(8,128)S(1)} fusion(f32[32,32,128]{2,1,0:T(8,128)} %get-tuple-element.27, f32[32,32]{1,0:T(8,128)S(1)} %fusion.6), kind=kOutput, calls=%fused_computation.17 | convolution fusion | flops 50331648 | bytes 1052672 | tf_op jit(solution)/shard_map/cond/branch_1_fun/evi,wv->ewi/dot_general | solution.py:90
  97.1 2.8 %convolution_subtract_fusion = f32[32,32,128]{2,0,1:T(8,128)} fusion(f32[32,32,128]{2,0,1:T(8,128)S(1)} %fusion.4, f32[32,192,1]{1,0,2:T(8,128)S(1)} %convolution_bitcast_fusion.3, f32[32,192,128]{2,1,0:T(8,128)S(1)} %get-tuple-element.29), kind=kOutput, calls=%fused_computation.15 | convolution fusion | flops 302120960 | bytes 4218880 | tf_op jit(solution)/shard_map/cond/branch_1_fun/epi,pw->ewi/dot_general | solution.py:90
  (90 shorter events, 20.3 us)
Async XLA Ops:
  0.6 9.0 %copy-start.3 = (bf16[4,8,32,128]{3,2,1,0:T(8,128)(2,1)S(1)}, bf16[4,8,32,128]{3,2,1,0:T(8,128)(2,1)}, u32[]{:S(2)}) copy-start(bf16[4,8,32,128]{3,2,1,0:T(8,128)(2,1)} %param.10) | copy-start | bytes 786436
  0.6 12.3 %copy-start.6 = (s32[4,8,5]{1,0,2:T(4,128)S(1)}, s32[4,8,5]{1,0,2:T(4,128)}, u32[]{:S(2)}) copy-start(s32[4,8,5]{1,0,2:T(4,128)} %param.12) | copy-start | bytes 1924
  6.3 8.6 %collective-permute-start.8 = (f32[112,128]{1,0:T(8,128)S(1)}, f32[112,128]{1,0:T(8,128)S(1)}, u32[]{:S(2)}, u32[]{:S(2)}) collective-permute-start(f32[112,128]{1,0:T(8,128)S(1)} %slice_select_fusion), channel_id=1, source_target_pairs={{0,16},{16,0},{32,48},{48,32},{64,80},{80,64},{96,112},{112,96},{1... | collective-permute-start | bytes 172040 | tf_op jit(solution)/shard_map/ppermute | solution.py:37
  9.7 5.3 %collective-permute-start.10 = (bf16[4,1,32,128]{3,2,1,0:T(8,128)(2,1)S(1)}, bf16[4,1,32,128]{3,2,1,0:T(8,128)(2,1)S(1)}, u32[]{:S(2)}, u32[]{:S(2)}) collective-permute-start(bf16[4,1,32,128]{3,2,1,0:T(8,128)(2,1)S(1)} %get-tuple-element.73), channel_id=1, source_target_pairs={{1,0},{2,1},{3,2},{4,3},{5,4},{6,5},{7,6},{8,7},{9,8},{10,9},{11,1... | collective-permute-start | bytes 98312 | tf_op jit(solution)/shard_map/ppermute | solution.py:108
  12.9 6.1 %collective-permute-start.9 = (bf16[4,1,32,128]{3,2,1,0:T(8,128)(2,1)S(1)}, bf16[4,1,32,128]{3,2,1,0:T(8,128)(2,1)S(1)}, u32[]{:S(2)}, u32[]{:S(2)}) collective-permute-start(bf16[4,1,32,128]{3,2,1,0:T(8,128)(2,1)S(1)} %get-tuple-element.74), channel_id=1, source_target_pairs={{0,1},{1,2},{2,3},{3,4},{4,5},{5,6},{6,7},{7,8},{8,9},{9,10},{10,1... | collective-permute-start | bytes 98312 | tf_op jit(solution)/shard_map/ppermute | solution.py:107
  19.0 7.3 %collective-permute-start.11 = (f32[56,128]{1,0:T(8,128)S(1)}, f32[56,128]{1,0:T(8,128)S(1)}, u32[]{:S(2)}, u32[]{:S(2)}) collective-permute-start(f32[56,128]{1,0:T(8,128)S(1)} %slice_select_fusion.1), channel_id=1, source_target_pairs={{0,32},{16,48},{32,0},{48,16},{64,96},{80,112},{96,64},{112,80},{1... | collective-permute-start | bytes 86024 | tf_op jit(solution)/shard_map/ppermute | solution.py:37
  20.7 5.8 %collective-permute-start.12 = (bf16[1,10,32,128]{3,2,1,0:T(8,128)(2,1)S(1)}, bf16[1,10,32,128]{3,2,1,0:T(8,128)(2,1)S(1)}, u32[]{:S(2)}, u32[]{:S(2)}) collective-permute-start(bf16[1,10,32,128]{3,2,1,0:T(8,128)(2,1)S(1)} %pad_maximum_fusion.5), channel_id=1, source_target_pairs={{16,0},{32,16},{48,32},{64,48},{80,64},{96,80},{112,96},{128,112},... | collective-permute-start | bytes 245768 | tf_op jit(solution)/shard_map/ppermute | solution.py:116
  24.4 3.4 %collective-permute-start.13 = (bf16[1,10,32,128]{3,2,1,0:T(8,128)(2,1)S(1)}, bf16[1,10,32,128]{3,2,1,0:T(8,128)(2,1)S(1)}, u32[]{:S(2)}, u32[]{:S(2)}) collective-permute-start(bf16[1,10,32,128]{3,2,1,0:T(8,128)(2,1)S(1)} %pad_maximum_fusion.6), channel_id=1, source_target_pairs={{0,16},{16,32},{32,48},{48,64},{64,80},{80,96},{96,112},{112,128},... | collective-permute-start | bytes 245768 | tf_op jit(solution)/shard_map/ppermute | solution.py:115
  26.4 3.6 %copy-start.4 = (bf16[4,8,5,128,128]{4,3,2,1,0:T(8,128)(2,1)S(1)}, bf16[4,8,5,128,128]{4,3,2,1,0:T(8,128)(2,1)}, u32[]{:S(2)}) copy-start(bf16[4,8,5,128,128]{4,3,2,1,0:T(8,128)(2,1)} %param.9) | copy-start | bytes 15728644
  31.4 1.9 %copy-start = (f32[4,8,192,128]{3,2,1,0:T(8,128)S(1)}, f32[4,8,192,128]{3,2,1,0:T(8,128)}, u32[]{:S(2)}) copy-start(f32[4,8,192,128]{3,2,1,0:T(8,128)} %param.11) | copy-start | bytes 9437188
  33.4 2.9 %copy-start.1 = (f32[4,8,32,128]{3,2,1,0:T(8,128)}, f32[4,8,32,128]{3,2,1,0:T(8,128)S(1)}, u32[]{:S(2)}) copy-start(f32[4,8,32,128]{3,2,1,0:T(8,128)S(1)} %convolution_add_fusion) | copy-start | bytes 1572868
  37.2 4.6 %collective-permute-start.14 = (f32[112,128]{1,0:T(8,128)S(1)}, f32[112,128]{1,0:T(8,128)S(1)}, u32[]{:S(2)}, u32[]{:S(2)}) collective-permute-start(f32[112,128]{1,0:T(8,128)S(1)} %pad_maximum_fusion.8), channel_id=1, source_target_pairs={{0,64},{16,80},{32,96},{48,112},{64,0},{80,16},{96,32},{112,48},{1... | collective-permute-start | bytes 172040 | tf_op jit(solution)/shard_map/ppermute | solution.py:37
  41.8 8.4 %collective-permute-start.15 = (f32[112,128]{1,0:T(8,128)S(1)}, f32[112,128]{1,0:T(8,128)S(1)}, u32[]{:S(2)}, u32[]{:S(2)}) collective-permute-start(f32[112,128]{1,0:T(8,128)S(1)} %fusion.94), channel_id=1, source_target_pairs={{0,128},{16,144},{32,160},{48,176},{64,192},{80,208},{96,224},{112... | collective-permute-start | bytes 172040 | tf_op jit(solution)/shard_map/ppermute | solution.py:37
  50.3 3.4 %collective-permute-start.16 = (f32[112,128]{1,0:T(8,128)S(1)}, f32[112,128]{1,0:T(8,128)S(1)}, u32[]{:S(2)}, u32[]{:S(2)}) collective-permute-start(f32[112,128]{1,0:T(8,128)S(1)} %add.100), channel_id=1, source_target_pairs={{0,1},{1,0},{2,3},{3,2},{4,5},{5,4},{6,7},{7,6},{8,9},{9,8},{10,11... | collective-permute-start | bytes 172040 | tf_op jit(solution)/shard_map/ppermute | solution.py:37
  53.7 4.3 %collective-permute-start.17 = (f32[112,128]{1,0:T(8,128)S(1)}, f32[112,128]{1,0:T(8,128)S(1)}, u32[]{:S(2)}, u32[]{:S(2)}) collective-permute-start(f32[112,128]{1,0:T(8,128)S(1)} %add.101), channel_id=1, source_target_pairs={{0,3},{1,2},{2,1},{3,0},{4,7},{5,6},{6,5},{7,4},{8,11},{9,10},{10,... | collective-permute-start | bytes 172040 | tf_op jit(solution)/shard_map/ppermute | solution.py:37
  58.0 3.1 %collective-permute-start.18 = (f32[112,128]{1,0:T(8,128)S(1)}, f32[112,128]{1,0:T(8,128)S(1)}, u32[]{:S(2)}, u32[]{:S(2)}) collective-permute-start(f32[112,128]{1,0:T(8,128)S(1)} %add.102), channel_id=1, source_target_pairs={{0,4},{1,5},{2,6},{3,7},{4,0},{5,1},{6,2},{7,3},{8,12},{9,13},{10,... | collective-permute-start | bytes 172040 | tf_op jit(solution)/shard_map/ppermute | solution.py:37
  61.2 4.3 %collective-permute-start.19 = (f32[112,128]{1,0:T(8,128)S(1)}, f32[112,128]{1,0:T(8,128)S(1)}, u32[]{:S(2)}, u32[]{:S(2)}) collective-permute-start(f32[112,128]{1,0:T(8,128)S(1)} %add.103), channel_id=1, source_target_pairs={{0,12},{1,13},{2,14},{3,15},{4,8},{5,9},{6,10},{7,11},{8,4},{9,5},... | collective-permute-start | bytes 172040 | tf_op jit(solution)/shard_map/ppermute | solution.py:37
  65.5 3.9 %collective-permute-start.20 = (f32[112,128]{1,0:T(8,128)S(1)}, f32[112,128]{1,0:T(8,128)S(1)}, u32[]{:S(2)}, u32[]{:S(2)}) collective-permute-start(f32[112,128]{1,0:T(8,128)S(1)} %add.104), channel_id=1, source_target_pairs={{0,32},{16,48},{32,0},{48,16},{64,96},{80,112},{96,64},{112,80},{1... | collective-permute-start | bytes 172040 | tf_op jit(solution)/shard_map/ppermute | solution.py:37
  69.4 10.6 %collective-permute-start.21 = (f32[168,128]{1,0:T(8,128)S(1)}, f32[168,128]{1,0:T(8,128)S(1)}, u32[]{:S(2)}, u32[]{:S(2)}) collective-permute-start(f32[168,128]{1,0:T(8,128)S(1)} %pad_maximum_fusion.4), channel_id=1, source_target_pairs={{0,16},{16,0},{32,48},{48,32},{64,80},{80,64},{96,112},{112,96},{1... | collective-permute-start | bytes 258056 | tf_op jit(solution)/shard_map/ppermute | solution.py:37
  80.2 0.6 copy-start.5

commit v11 on v10

--- a/solution.py
+++ b/solution.py
@@ -101,13 +101,12 @@
     radial = [step for axis, step in steps if axis == "rad"]
     around = [("azi", step) for axis, step in steps if axis == "azi"]
 
-    kept_gram = halve(pack_symmetric(mm("epi,eqi->pq", kept_flat, kept_flat)), "rad", radial[0])
-
     n_a, n_r = lax.axis_size("azi"), lax.axis_size("rad")
     west = lax.ppermute(new_block[:, rows_a - 1 :], "azi", [(i, (i + 1) % n_a) for i in range(n_a)])
     east = lax.ppermute(new_block[:, :1], "azi", [((i + 1) % n_a, i) for i in range(n_a)])
+    kept_gram = pack_symmetric(mm("epi,eqi->pq", kept_flat, kept_flat))
     kept_gram, west, east = lax.optimization_barrier((kept_gram, west, east))
-    kept_gram = halve(kept_gram, "rad", radial[1])
+    kept_gram = halve(halve(kept_gram, "rad", radial[0]), "rad", radial[1])
 
     def row(r):
         return jnp.concatenate([west[r : r + 1], new_block[r : r + 1], east[r : r + 1]], axis=1)
@@ -117,6 +116,7 @@
     padded = jnp.concatenate(
         [north, jnp.concatenate([west, new_block, east], axis=1), south], axis=0
     )
+    kept_gram, padded = lax.optimization_barrier((kept_gram, padded))
     shifted = [padded[c // 3 : c // 3 + rows_r, c % 3 : c % 3 + rows_a] for c in range(9)]
     image = jnp.einsum("raij,ravj->ravi", jacobian[:, :, 0], new_block, preferred_element_type=jnp.float32)
     for k in range(1, 5):

time: 101 us -> 101 us (level)
  waiting for transfers between devices: 25.8 us -> 21.1 us
  matrix products: 24.9 us -> 28.6 us
  other arithmetic: 7.72 us -> 9.2 us
    ppermute x1, waiting for transfers between devices: 4.05 us -> 0.01 us  [on_device(): lax.ppermute(new_block[:, rows_a - 1:], 'azi', [(i, (i + 1) % n_a) for i...]
    dot_general x4, matrix products: 4.31 us -> 8 us  [on_device(): jnp.einsum('raij,ravj->ravi', jacobian[:, :, k], pick, preferred_element_...]
    ppermute x10, starting transfers between devices: 27.3 us -> 23.9 us  [exchange(): lax.ppermute(x, axis, [(i, partner(axis, step, i)) for i in range(count)])]
    ppermute x1, starting transfers between devices: 3.27 us -> 5.76 us  [on_device(): lax.ppermute(new_block[:, :1], 'azi', [((i + 1) % n_a, i) for i in range(...]
    ppermute x1, starting transfers between devices: 3.64 us -> 1.93 us  [on_device(): south = lax.ppermute(row(0), 'rad', [(i + 1, i) for i in range(n_r - 1)])]
    ppermute x1, starting transfers between devices: 1.92 us -> 3.63 us  [on_device(): lax.ppermute(row(rows_r - 1), 'rad', [(i, i + 1) for i in range(n_r - 1)])]
    unnamed x14 -> x7, local copies, waits for them, and re-layouts: 1.84 us -> 0.26 us
    eq x2, other arithmetic: 0.04 us -> 1.49 us  [on_device(): pick = jnp.where(code == c, shifted[c], pick)]
  transfers between devices with their start and end apart: 14 -> 14, of which waited for: 11 -> 9; matrix products, arithmetic and copies ran while one was open for 2% -> 10% of each run, Pallas kernels for 0% -> 0%
where the time goes in v11:
time: 101 us
  starting transfers between devices  35.2 us (35%)
  matrix products  28.6 us (28%)
  waiting for transfers between devices  21.1 us (21%)
  other arithmetic  9.2 us (9%)
  local copies, waits for them, and re-layouts  4.81 us (5%)
  between operations  1.61 us (2%)
    ppermute x10, starting transfers between devices, exchange(): lax.ppermute(x, axis, [(i, partner(axis, step, i)) for i in range(count)])  23.9 us
    ppermute x10, waiting for transfers between devices, exchange(): lax.ppermute(x, axis, [(i, partner(axis, step, i)) for i in range(count)])  21.1 us
    dot_general x10, matrix products, mm(): jnp.einsum(spec, a, b, precision=lax.Precision.HIGHEST, preferred_element...  18.5 us
    dot_general x4, matrix products, on_device(): jnp.einsum('raij,ravj->ravi', jacobian[:, :, k], pick, preferred_element_...  8 us
    ppermute x1, starting transfers between devices, on_device(): lax.ppermute(new_block[:, :1], 'azi', [((i + 1) % n_a, i) for i in range(...  5.76 us
    ppermute x1, starting transfers between devices, on_device(): lax.ppermute(row(rows_r - 1), 'rad', [(i, i + 1) for i in range(n_r - 1)])  3.63 us
    another operation x3, other arithmetic, factor_of(): lower = jnp.linalg.cholesky(gram)  3.6 us
    another operation x2, other arithmetic, factor_of(): lax.linalg.triangular_solve(lower, eye, left_side=True, lower=True)  3.09 us
  transfers between devices with their start and end apart: 14, of which 9 were waited for; matrix products, arithmetic and copies ran while one was open for 10% of the time, Pallas kernels for 0%

profile of v11, /device:TPU:1, one launch (start us, length us, event | category | flops | bytes accessed | tf_op | source)
XLA Modules:
  0.0 100.7 jit_solution(14134089452053538704)
XLA Ops:
  1.4 5.8 %collective-permute-start.9 = (bf16[4,1,32,128]{3,2,1,0:T(8,128)(2,1)S(1)}, bf16[4,1,32,128]{3,2,1,0:T(8,128)(2,1)S(1)}, u32[]{:S(2)}, u32[]{:S(2)}) collective-permute-start(bf16[4,1,32,128]{3,2,1,0:T(8,128)(2,1)S(1)} %get-tuple-element.71), channel_id=1, source_target_pairs={{1,0},{2,1},{3,2},{4,3},{5,4},{6,5},{7,6},{8,7},{9,8},{10,9},{11,1... | collective-permute-start | bytes 98312 | tf_op jit(solution)/shard_map/ppermute | solution.py:106
  9.6 5.5 %convolution_bitcast_fusion.4 = f32[192,192]{1,0:T(8,128)S(1)} fusion(f32[4,8,192,128]{3,2,1,0:T(8,128)} %param.11), kind=kOutput, calls=%fused_computation.33 | convolution fusion | flops 1811939328 | bytes 3293184 | tf_op jit(solution)/shard_map/epi,eqi->pq/dot_general | solution.py:90
  15.2 1.9 %fusion.15 = f32[4,8,32,128]{3,2,1,0:T(8,128)S(1)} fusion(bf16[4,8,32,128]{3,2,1,0:T(8,128)(2,1)S(1)} %copy-done.3, bf16[4,8,5,128,128]{4,3,2,1,0:T(8,128)(2,1)} %param.9), kind=kOutput, calls=%fused_computation.44 | convolution fusion | flops 33554432 | bytes 1835008 | tf_op jit(solution)/shard_map/raij,ravj->ravi/dot_general | solution.py:121
  18.3 1.9 %collective-permute-start.13 = (bf16[1,10,32,128]{3,2,1,0:T(8,128)(2,1)S(1)}, bf16[1,10,32,128]{3,2,1,0:T(8,128)(2,1)S(1)}, u32[]{:S(2)}, u32[]{:S(2)}) collective-permute-start(bf16[1,10,32,128]{3,2,1,0:T(8,128)(2,1)S(1)} %pad_maximum_fusion.4), channel_id=1, source_target_pairs={{16,0},{32,16},{48,32},{64,48},{80,64},{96,80},{112,96},{128,112},... | collective-permute-start | bytes 245768 | tf_op jit(solution)/shard_map/ppermute | solution.py:115
  20.2 3.6 %collective-permute-start.12 = (bf16[1,10,32,128]{3,2,1,0:T(8,128)(2,1)S(1)}, bf16[1,10,32,128]{3,2,1,0:T(8,128)(2,1)S(1)}, u32[]{:S(2)}, u32[]{:S(2)}) collective-permute-start(bf16[1,10,32,128]{3,2,1,0:T(8,128)(2,1)S(1)} %pad_maximum_fusion.3), channel_id=1, source_target_pairs={{0,16},{16,32},{32,48},{48,64},{64,80},{80,96},{96,112},{112,128},... | collective-permute-start | bytes 245768 | tf_op jit(solution)/shard_map/ppermute | solution.py:114
  26.9 2.0 %convolution_add_fusion.3 = f32[4,8,32,128]{3,2,1,0:T(8,128)S(1)} fusion(f32[4,8,32,128]{3,2,1,0:T(8,128)S(1)} %fusion.15, bf16[4,8,5,128,128]{4,3,2,1,0:T(8,128)(2,1)} %param.9, pred[4,8]{1,0:T(4,128)(4,1)S(1)} %get-tuple-element.89, pred[4,8]{1,0:T(4,128)(4,1)S(1)} %get-tuple-element.88, pred[4,8]{1,0:T(4,128)(4,1)S(1)} %get-tuple-element.87, ...), kind=kOutput, calls=%fused_computation.32 | convolution fusion | flops 34734080 | bytes 4460544 | tf_op jit(solution)/shard_map/raij,ravj->ravi/dot_general | solution.py:127
  28.9 2.0 %convolution_add_fusion.2 = f32[4,8,32,128]{3,2,1,0:T(8,128)S(1)} fusion(f32[4,8,32,128]{3,2,1,0:T(8,128)S(1)} %convolution_add_fusion.3, bf16[4,8,5,128,128]{4,3,2,1,0:T(8,128)(2,1)} %param.9, pred[4,8]{1,0:T(4,128)(4,1)S(1)} %get-tuple-element.96, pred[4,8]{1,0:T(4,128)(4,1)S(1)} %get-tuple-element.95, pred[4,8]{1,0:T(4,128)(4,1)S(1)} %get-tuple-element.94, ...), kind=kOutput, calls=%fused_computation.31 | convolution fusion | flops 34734080 | bytes 4460544 | tf_op jit(solution)/shard_map/raij,ravj->ravi/dot_general | solution.py:127
  30.8 2.0 %convolution_add_fusion.1 = f32[4,8,32,128]{3,2,1,0:T(8,128)S(1)} fusion(f32[4,8,32,128]{3,2,1,0:T(8,128)S(1)} %convolution_add_fusion.2, bf16[4,8,5,128,128]{4,3,2,1,0:T(8,128)(2,1)} %param.9, pred[4,8]{1,0:T(4,128)(4,1)S(1)} %get-tuple-element.104, pred[4,8]{1,0:T(4,128)(4,1)S(1)} %get-tuple-element.103, pred[4,8]{1,0:T(4,128)(4,1)S(1)} %get-tuple-element.102, ...), kind=kOutput, calls=%fused_computation.30 | convolution fusion | flops 34734080 | bytes 4460544 | tf_op jit(solution)/shard_map/raij,ravj->ravi/dot_general | solution.py:127
  32.8 2.1 %convolution_add_fusion = f32[4,8,32,128]{3,2,1,0:T(8,128)S(1)} fusion(f32[4,8,32,128]{3,2,1,0:T(8,128)S(1)} %convolution_add_fusion.1, bf16[4,8,5,128,128]{4,3,2,1,0:T(8,128)(2,1)} %param.9, pred[4,8]{1,0:T(4,128)(4,1)S(1)} %get-tuple-element.110, pred[4,8]{1,0:T(4,128)(4,1)S(1)} %get-tuple-element.109, pred[4,8]{1,0:T(4,128)(4,1)S(1)} %get-tuple-element.108, ...), kind=kOutput, calls=%fused_computation.29 | convolution fusion | flops 34734080 | bytes 4460544 | tf_op jit(solution)/shard_map/raij,ravj->ravi/dot_general | solution.py:127
  35.8 2.9 %convolution_bitcast_fusion.5 = f32[192,32]{0,1:T(8,128)S(1)} fusion(f32[4,8,32,128]{3,2,1,0:T(8,128)S(1)} %convolution_add_fusion, f32[4,8,192,128]{3,2,1,0:T(8,128)S(1)} %copy-done), kind=kOutput, calls=%fused_computation.34 | convolution fusion | flops 301989888 | bytes 3694592 | tf_op jit(solution)/shard_map/epi,evi->pv/dot_general | solution.py:90
  39.0 4.3 %collective-permute-start.14 = (f32[112,128]{1,0:T(8,128)S(1)}, f32[112,128]{1,0:T(8,128)S(1)}, u32[]{:S(2)}, u32[]{:S(2)}) collective-permute-start(f32[112,128]{1,0:T(8,128)S(1)} %constant_dynamic-update-slice_fusion), channel_id=1, source_target_pairs={{0,64},{16,80},{32,96},{48,112},{64,0},{80,16},{96,32},{112,48},{1... | collective-permute-start | bytes 172040 | tf_op jit(solution)/shard_map/ppermute | solution.py:37
  43.3 2.8 %collective-permute-done.14 = f32[112,128]{1,0:T(8,128)S(1)} collective-permute-done((f32[112,128]{1,0:T(8,128)S(1)}, f32[112,128]{1,0:T(8,128)S(1)}, u32[]{:S(2)}, u32[]{:S(2)}) %collective-permute-start.14) | collective-permute-done | bytes 57376 | tf_op jit(solution)/shard_map/ppermute | solution.py:37
  46.1 4.0 %collective-permute-start.15 = (f32[112,128]{1,0:T(8,128)S(1)}, f32[112,128]{1,0:T(8,128)S(1)}, u32[]{:S(2)}, u32[]{:S(2)}) collective-permute-start(f32[112,128]{1,0:T(8,128)S(1)} %add.99), channel_id=1, source_target_pairs={{0,128},{16,144},{32,160},{48,176},{64,192},{80,208},{96,224},{112... | collective-permute-start | bytes 172040 | tf_op jit(solution)/shard_map/ppermute | solution.py:37
  50.1 3.1 %collective-permute-done.15 = f32[112,128]{1,0:T(8,128)S(1)} collective-permute-done((f32[112,128]{1,0:T(8,128)S(1)}, f32[112,128]{1,0:T(8,128)S(1)}, u32[]{:S(2)}, u32[]{:S(2)}) %collective-permute-start.15) | collective-permute-done | bytes 57376 | tf_op jit(solution)/shard_map/ppermute | solution.py:37
  53.5 3.0 %collective-permute-done.16 = f32[112,128]{1,0:T(8,128)S(1)} collective-permute-done((f32[112,128]{1,0:T(8,128)S(1)}, f32[112,128]{1,0:T(8,128)S(1)}, u32[]{:S(2)}, u32[]{:S(2)}) %collective-permute-start.16) | collective-permute-done | bytes 57376 | tf_op jit(solution)/shard_map/ppermute | solution.py:37
  58.3 2.6 %collective-permute-done.17 = f32[112,128]{1,0:T(8,128)S(1)} collective-permute-done((f32[112,128]{1,0:T(8,128)S(1)}, f32[112,128]{1,0:T(8,128)S(1)}, u32[]{:S(2)}, u32[]{:S(2)}) %collective-permute-start.17) | collective-permute-done | bytes 57376 | tf_op jit(solution)/shard_map/ppermute | solution.py:37
  61.2 3.1 %collective-permute-done.18 = f32[112,128]{1,0:T(8,128)S(1)} collective-permute-done((f32[112,128]{1,0:T(8,128)S(1)}, f32[112,128]{1,0:T(8,128)S(1)}, u32[]{:S(2)}, u32[]{:S(2)}) %collective-permute-start.18) | collective-permute-done | bytes 57376 | tf_op jit(solution)/shard_map/ppermute | solution.py:37
  64.3 2.8 %collective-permute-start.19 = (f32[112,128]{1,0:T(8,128)S(1)}, f32[112,128]{1,0:T(8,128)S(1)}, u32[]{:S(2)}, u32[]{:S(2)}) collective-permute-start(f32[112,128]{1,0:T(8,128)S(1)} %add.103), channel_id=1, source_target_pairs={{0,12},{1,13},{2,14},{3,15},{4,8},{5,9},{6,10},{7,11},{8,4},{9,5},... | collective-permute-start | bytes 172040 | tf_op jit(solution)/shard_map/ppermute | solution.py:37
  68.9 2.8 %collective-permute-done.20 = f32[112,128]{1,0:T(8,128)S(1)} collective-permute-done((f32[112,128]{1,0:T(8,128)S(1)}, f32[112,128]{1,0:T(8,128)S(1)}, u32[]{:S(2)}, u32[]{:S(2)}) %collective-permute-start.20) | collective-permute-done | bytes 57376 | tf_op jit(solution)/shard_map/ppermute | solution.py:37
  71.8 7.4 %collective-permute-start.21 = (f32[168,128]{1,0:T(8,128)S(1)}, f32[168,128]{1,0:T(8,128)S(1)}, u32[]{:S(2)}, u32[]{:S(2)}) collective-permute-start(f32[168,128]{1,0:T(8,128)S(1)} %pad_maximum_fusion.2), channel_id=1, source_target_pairs={{0,16},{16,0},{32,48},{48,32},{64,80},{80,64},{96,112},{112,96},{1... | collective-permute-start | bytes 258056 | tf_op jit(solution)/shard_map/ppermute | solution.py:37
  87.5 12.6 %conditional.1 = (f32[32,32]{1,0:T(8,128)S(1)}, f32[4,8,32,128]{3,2,1,0:T(8,128)}) conditional(s32[]{:T(128)} %convert_element_type.8, (f32[192,32]{0,1:T(8,128)}, f32[32,192,128]{2,1,0:T(8,128)S(1)}, f32[32,32,128]{2,1,0:T(8,128)}, f32[32,32]{0,1:T(8,128)S(1)}) %tuple.77, (f32[32,32]{0,1:T(8,128)S(1)}, f32[32,32]{0,1:T(8,128)S(1)}, ...), branch_computations={%region_3.8_spmd, %region_6.9_spmd} | conditional | flops 403195936 | bytes 8176238 | solution.py:178
  87.8 2.9 %cholesky.55 = f32[32,32]{1,0:T(8,128)S(1)} custom-call(f32[32,32]{1,0:T(8,128)S(1)} %fusion.8), custom_call_target="Cholesky" | custom-call | tf_op jit(solution)/shard_map/cond/branch_1_fun/jit(cholesky)/cholesky | solution.py:162
  92.0 2.4 %custom-call.7 = f32[1,32,32]{1,2,0:T(8,128)S(1)} custom-call(f32[1,32,32]{2,1,0:T(8,128)S(1)} %get-tuple-element.67), custom_call_target="InvertDiagBlocksLowerTriangular" | custom-call | tf_op jit(solution)/shard_map/cond/branch_1_fun/triangular_solve/custom-call.0 | solution.py:163
  97.3 2.8 %convolution_subtract_fusion = f32[32,32,128]{2,0,1:T(8,128)} fusion(f32[32,32,128]{2,0,1:T(8,128)S(1)} %fusion.4, f32[32,192,1]{1,0,2:T(8,128)S(1)} %convolution_bitcast_fusion.3, f32[32,192,128]{2,1,0:T(8,128)S(1)} %get-tuple-element.29), kind=kOutput, calls=%fused_computation.15 | convolution fusion | flops 302120960 | bytes 4218880 | tf_op jit(solution)/shard_map/cond/branch_1_fun/epi,pw->ewi/dot_general | solution.py:90
  (83 shorter events, 25.1 us)
Async XLA Ops:
  1.4 15.8 %collective-permute-start.9 = (bf16[4,1,32,128]{3,2,1,0:T(8,128)(2,1)S(1)}, bf16[4,1,32,128]{3,2,1,0:T(8,128)(2,1)S(1)}, u32[]{:S(2)}, u32[]{:S(2)}) collective-permute-start(bf16[4,1,32,128]{3,2,1,0:T(8,128)(2,1)S(1)} %get-tuple-element.71), channel_id=1, source_target_pairs={{1,0},{2,1},{3,2},{4,3},{5,4},{6,5},{7,6},{8,7},{9,8},{10,9},{11,1... | collective-permute-start | bytes 98312 | tf_op jit(solution)/shard_map/ppermute | solution.py:106
  7.2 10.0 %collective-permute-start.8 = (bf16[4,1,32,128]{3,2,1,0:T(8,128)(2,1)S(1)}, bf16[4,1,32,128]{3,2,1,0:T(8,128)(2,1)S(1)}, u32[]{:S(2)}, u32[]{:S(2)}) collective-permute-start(bf16[4,1,32,128]{3,2,1,0:T(8,128)(2,1)S(1)} %get-tuple-element.72), channel_id=1, source_target_pairs={{0,1},{1,2},{2,3},{3,4},{4,5},{5,6},{6,7},{7,8},{8,9},{9,10},{10,1... | collective-permute-start | bytes 98312 | tf_op jit(solution)/shard_map/ppermute | solution.py:105
  9.6 5.7 %copy-start.3 = (bf16[4,8,32,128]{3,2,1,0:T(8,128)(2,1)S(1)}, bf16[4,8,32,128]{3,2,1,0:T(8,128)(2,1)}, u32[]{:S(2)}) copy-start(bf16[4,8,32,128]{3,2,1,0:T(8,128)(2,1)} %param.10) | copy-start | bytes 786436
  17.2 6.7 %collective-permute-start.10 = (f32[112,128]{1,0:T(8,128)S(1)}, f32[112,128]{1,0:T(8,128)S(1)}, u32[]{:S(2)}, u32[]{:S(2)}) collective-permute-start(f32[112,128]{1,0:T(8,128)S(1)} %slice_select_fusion), channel_id=1, source_target_pairs={{0,16},{16,0},{32,48},{48,32},{64,80},{80,64},{96,112},{112,96},{1... | collective-permute-start | bytes 172040 | tf_op jit(solution)/shard_map/ppermute | solution.py:37
  18.3 7.4 %collective-permute-start.13 = (bf16[1,10,32,128]{3,2,1,0:T(8,128)(2,1)S(1)}, bf16[1,10,32,128]{3,2,1,0:T(8,128)(2,1)S(1)}, u32[]{:S(2)}, u32[]{:S(2)}) collective-permute-start(bf16[1,10,32,128]{3,2,1,0:T(8,128)(2,1)S(1)} %pad_maximum_fusion.4), channel_id=1, source_target_pairs={{16,0},{32,16},{48,32},{64,48},{80,64},{96,80},{112,96},{128,112},... | collective-permute-start | bytes 245768 | tf_op jit(solution)/shard_map/ppermute | solution.py:115
  20.2 5.4 %collective-permute-start.12 = (bf16[1,10,32,128]{3,2,1,0:T(8,128)(2,1)S(1)}, bf16[1,10,32,128]{3,2,1,0:T(8,128)(2,1)S(1)}, u32[]{:S(2)}, u32[]{:S(2)}) collective-permute-start(bf16[1,10,32,128]{3,2,1,0:T(8,128)(2,1)S(1)} %pad_maximum_fusion.3), channel_id=1, source_target_pairs={{0,16},{16,32},{32,48},{48,64},{64,80},{80,96},{96,112},{112,128},... | collective-permute-start | bytes 245768 | tf_op jit(solution)/shard_map/ppermute | solution.py:114
  23.9 3.0 %collective-permute-start.11 = (f32[56,128]{1,0:T(8,128)S(1)}, f32[56,128]{1,0:T(8,128)S(1)}, u32[]{:S(2)}, u32[]{:S(2)}) collective-permute-start(f32[56,128]{1,0:T(8,128)S(1)} %slice_select_fusion.1), channel_id=1, source_target_pairs={{0,32},{16,48},{32,0},{48,16},{64,96},{80,112},{96,64},{112,80},{1... | collective-permute-start | bytes 86024 | tf_op jit(solution)/shard_map/ppermute | solution.py:37
  32.8 3.0 %copy-start = (f32[4,8,192,128]{3,2,1,0:T(8,128)S(1)}, f32[4,8,192,128]{3,2,1,0:T(8,128)}, u32[]{:S(2)}) copy-start(f32[4,8,192,128]{3,2,1,0:T(8,128)} %param.11) | copy-start | bytes 9437188
  34.9 0.8 copy-start.1
  39.0 7.1 %collective-permute-start.14 = (f32[112,128]{1,0:T(8,128)S(1)}, f32[112,128]{1,0:T(8,128)S(1)}, u32[]{:S(2)}, u32[]{:S(2)}) collective-permute-start(f32[112,128]{1,0:T(8,128)S(1)} %constant_dynamic-update-slice_fusion), channel_id=1, source_target_pairs={{0,64},{16,80},{32,96},{48,112},{64,0},{80,16},{96,32},{112,48},{1... | collective-permute-start | bytes 172040 | tf_op jit(solution)/shard_map/ppermute | solution.py:37
  46.1 7.1 %collective-permute-start.15 = (f32[112,128]{1,0:T(8,128)S(1)}, f32[112,128]{1,0:T(8,128)S(1)}, u32[]{:S(2)}, u32[]{:S(2)}) collective-permute-start(f32[112,128]{1,0:T(8,128)S(1)} %add.99), channel_id=1, source_target_pairs={{0,128},{16,144},{32,160},{48,176},{64,192},{80,208},{96,224},{112... | collective-permute-start | bytes 172040 | tf_op jit(solution)/shard_map/ppermute | solution.py:37
  53.2 3.3 %collective-permute-start.16 = (f32[112,128]{1,0:T(8,128)S(1)}, f32[112,128]{1,0:T(8,128)S(1)}, u32[]{:S(2)}, u32[]{:S(2)}) collective-permute-start(f32[112,128]{1,0:T(8,128)S(1)} %add.100), channel_id=1, source_target_pairs={{0,1},{1,0},{2,3},{3,2},{4,5},{5,4},{6,7},{7,6},{8,9},{9,8},{10,11... | collective-permute-start | bytes 172040 | tf_op jit(solution)/shard_map/ppermute | solution.py:37
  56.5 4.3 %collective-permute-start.17 = (f32[112,128]{1,0:T(8,128)S(1)}, f32[112,128]{1,0:T(8,128)S(1)}, u32[]{:S(2)}, u32[]{:S(2)}) collective-permute-start(f32[112,128]{1,0:T(8,128)S(1)} %add.101), channel_id=1, source_target_pairs={{0,3},{1,2},{2,1},{3,0},{4,7},{5,6},{6,5},{7,4},{8,11},{9,10},{10,... | collective-permute-start | bytes 172040 | tf_op jit(solution)/shard_map/ppermute | solution.py:37
  60.9 3.4 %collective-permute-start.18 = (f32[112,128]{1,0:T(8,128)S(1)}, f32[112,128]{1,0:T(8,128)S(1)}, u32[]{:S(2)}, u32[]{:S(2)}) collective-permute-start(f32[112,128]{1,0:T(8,128)S(1)} %add.102), channel_id=1, source_target_pairs={{0,4},{1,5},{2,6},{3,7},{4,0},{5,1},{6,2},{7,3},{8,12},{9,13},{10,... | collective-permute-start | bytes 172040 | tf_op jit(solution)/shard_map/ppermute | solution.py:37
  64.3 4.3 %collective-permute-start.19 = (f32[112,128]{1,0:T(8,128)S(1)}, f32[112,128]{1,0:T(8,128)S(1)}, u32[]{:S(2)}, u32[]{:S(2)}) collective-permute-start(f32[112,128]{1,0:T(8,128)S(1)} %add.103), channel_id=1, source_target_pairs={{0,12},{1,13},{2,14},{3,15},{4,8},{5,9},{6,10},{7,11},{8,4},{9,5},... | collective-permute-start | bytes 172040 | tf_op jit(solution)/shard_map/ppermute | solution.py:37
  68.6 3.1 %collective-permute-start.20 = (f32[112,128]{1,0:T(8,128)S(1)}, f32[112,128]{1,0:T(8,128)S(1)}, u32[]{:S(2)}, u32[]{:S(2)}) collective-permute-start(f32[112,128]{1,0:T(8,128)S(1)} %add.104), channel_id=1, source_target_pairs={{0,32},{16,48},{32,0},{48,16},{64,96},{80,112},{96,64},{112,80},{1... | collective-permute-start | bytes 172040 | tf_op jit(solution)/shard_map/ppermute | solution.py:37
  71.8 8.3 %collective-permute-start.21 = (f32[168,128]{1,0:T(8,128)S(1)}, f32[168,128]{1,0:T(8,128)S(1)}, u32[]{:S(2)}, u32[]{:S(2)}) collective-permute-start(f32[168,128]{1,0:T(8,128)S(1)} %pad_maximum_fusion.2), channel_id=1, source_target_pairs={{0,16},{16,0},{32,48},{48,32},{64,80},{80,64},{96,112},{112,96},{1... | collective-permute-start | bytes 258056 | tf_op jit(solution)/shard_map/ppermute | solution.py:37

commit v12 on v8

--- a/solution.py
+++ b/solution.py
@@ -158,8 +158,12 @@
 
     def expanded_path():
         lower, inverse = factor_of(expanded)
-        basis = mm("evi,wv->ewi", image, inverse) - mm(
-            "epi,pw->ewi", kept_flat, mm("pv,wv->pw", coefficients, inverse)
+        fast = lax.Precision.HIGH
+        basis = jnp.einsum(
+            "evi,wv->ewi", image, inverse, precision=fast, preferred_element_type=jnp.float32
+        ) - jnp.einsum(
+            "epi,pw->ewi", kept_flat, mm("pv,wv->pw", coefficients, inverse),
+            precision=fast, preferred_element_type=jnp.float32,
         )
         return basis, lower
 

time: 101 us -> 99.5 us (0.985)
  matrix products: 22 us -> 20.9 us
    dot_general x10 -> x8, matrix products: 18.5 us -> 14.1 us  [mm(): jnp.einsum(spec, a, b, precision=lax.Precision.HIGHEST, preferred_element...]
    dot_general x0 -> x2, matrix products: none -> 3.28 us  [the longest x1 1.87 us: expanded_path(): jnp.einsum('epi,pw->ewi', kept_flat, mm('pv,wv->pw', coefficients, invers...]
where the time goes in v12:
time: 99.5 us; the launch traced here: 98.9 us
  starting transfers between devices  38.2 us (38%)
  matrix products  20.9 us (21%)
  waiting for transfers between devices  19.9 us (20%)
  other arithmetic  13.4 us (13%)
  local copies, waits for them, and re-layouts  4.77 us (5%)
  between operations  1.65 us (2%)
    ppermute x6, waiting for transfers between devices, all_sum(): x = x + lax.ppermute(x, axis, [(i, i ^ step) for i in range(count)])  16 us
    ppermute x4, starting transfers between devices, exchange(): return lax.ppermute(x, axis, [(i, i ^ step) for i in range(count)])  14.6 us
    dot_general x8, matrix products, mm(): jnp.einsum(spec, a, b, precision=lax.Precision.HIGHEST, preferred_element...  14.1 us
    ppermute x6, starting transfers between devices, all_sum(): x = x + lax.ppermute(x, axis, [(i, i ^ step) for i in range(count)])  12.3 us
    ppermute x1, starting transfers between devices, on_device(): lax.ppermute(new_block[:, :1], 'azi', [((i + 1) % n_a, i) for i in range(...  5.76 us
    unnamed x3, other arithmetic  4.33 us
    another operation x3, other arithmetic, factor_of(): lower = jnp.linalg.cholesky(gram)  3.6 us
    dot_general x1, matrix products, on_device(): jnp.einsum('rakij,rakvj->ravi', jacobian, picked, preferred_element_type=...  3.36 us
  transfers between devices with their start and end apart: 14, of which 10 were waited for; matrix products, arithmetic and copies ran while one was open for 7% of the time, Pallas kernels for 0%

profile of v12, /device:TPU:1, one launch (start us, length us, event | category | flops | bytes accessed | tf_op | source)
XLA Modules:
  0.0 98.9 jit_solution(7591287249779011431)
XLA Ops:
  1.4 5.8 %collective-permute-start.10 = (bf16[4,1,32,128]{3,2,1,0:T(8,128)(2,1)S(1)}, bf16[4,1,32,128]{3,2,1,0:T(8,128)(2,1)S(1)}, u32[]{:S(2)}, u32[]{:S(2)}) collective-permute-start(bf16[4,1,32,128]{3,2,1,0:T(8,128)(2,1)S(1)} %get-tuple-element.72), channel_id=1, source_target_pairs={{1,0},{2,1},{3,2},{4,3},{5,4},{6,5},{7,6},{8,7},{9,8},{10,9},{11,1... | collective-permute-start | bytes 98312 | tf_op jit(solution)/shard_map/ppermute | solution.py:101
  7.2 5.5 %convolution_bitcast_fusion.4 = f32[192,192]{1,0:T(8,128)S(1)} fusion(f32[4,8,192,128]{3,2,1,0:T(8,128)} %param.11), kind=kOutput, calls=%fused_computation.29 | convolution fusion | flops 1811939328 | bytes 3293184 | tf_op jit(solution)/shard_map/epi,eqi->pq/dot_general | solution.py:83
  14.9 1.7 %collective-permute-start.11 = (f32[56,128]{1,0:T(8,128)S(1)}, f32[56,128]{1,0:T(8,128)S(1)}, u32[]{:S(2)}, u32[]{:S(2)}) collective-permute-start(f32[56,128]{1,0:T(8,128)S(1)} %slice_select_fusion.1), channel_id=1, source_target_pairs={{0,32},{16,48},{32,0},{48,16},{64,96},{80,112},{96,64},{112,80},{1... | collective-permute-start | bytes 86024 | tf_op jit(solution)/shard_map/ppermute | solution.py:30
  16.6 2.7 %collective-permute-start.12 = (bf16[1,10,32,128]{3,2,1,0:T(8,128)(2,1)S(1)}, bf16[1,10,32,128]{3,2,1,0:T(8,128)(2,1)S(1)}, u32[]{:S(2)}, u32[]{:S(2)}) collective-permute-start(bf16[1,10,32,128]{3,2,1,0:T(8,128)(2,1)S(1)} %pad_maximum_fusion.5), channel_id=1, source_target_pairs={{16,0},{32,16},{48,32},{64,48},{80,64},{96,80},{112,96},{128,112},... | collective-permute-start | bytes 245768 | tf_op jit(solution)/shard_map/ppermute | solution.py:109
  19.3 2.9 %collective-permute-start.13 = (bf16[1,10,32,128]{3,2,1,0:T(8,128)(2,1)S(1)}, bf16[1,10,32,128]{3,2,1,0:T(8,128)(2,1)S(1)}, u32[]{:S(2)}, u32[]{:S(2)}) collective-permute-start(bf16[1,10,32,128]{3,2,1,0:T(8,128)(2,1)S(1)} %pad_maximum_fusion.6), channel_id=1, source_target_pairs={{0,16},{16,32},{32,48},{48,64},{64,80},{80,96},{96,112},{112,128},... | collective-permute-start | bytes 245768 | tf_op jit(solution)/shard_map/ppermute | solution.py:108
  23.7 1.5 %bitcast_dynamic-update-slice_fusion.2 = (bf16[4,8,5,32,128]{4,3,2,1,0:T(8,128)(2,1)}, bf16[4,8,32,128]{3,2,1,0:T(8,128)(2,1)S(1)}, bf16[4,8,32,128]{3,2,1,0:T(8...) fusion(bf16[4,8,5,32,128]{4,3,2,1,0:T(8,128)(2,1)} %bitcast_dynamic-update-slice_fusion.4, ...), kind=kLoop, calls=%fused_computation.56 | loop fusion | flops 5242880 | bytes 2130176
  29.5 3.4 %fusion.32 = f32[4,8,32,128,1]{3,2,4,1,0:T(8,128)S(1)} fusion(bf16[4,8,5,32,128]{4,3,2,1,0:T(8,128)(2,1)} %bitcast_dynamic-update-slice_fusion.3, bf16[4,8,5,128,128]{4,3,2,1,0:T(8,128)(2,1)S(1)} %copy-done.4), kind=kOutput, calls=%fused_computation.126 | convolution fusion | flops 167772160 | bytes 7077888 | tf_op jit(solution)/shard_map/rakij,rakvj->ravi/dot_general | solution.py:122
  33.7 2.9 %convolution_bitcast_fusion.5 = f32[192,32]{0,1:T(8,128)S(1)} fusion(f32[4,8,192,128]{3,2,1,0:T(8,128)S(1)} %copy-done, f32[4,8,32,128,1]{3,2,4,1,0:T(8,128)S(1)} %fusion.32), kind=kOutput, calls=%fused_computation.30 | convolution fusion | flops 301989888 | bytes 3694592 | tf_op jit(solution)/shard_map/epi,evi->pv/dot_general | solution.py:83
  36.9 3.1 %collective-permute-start.14 = (f32[112,128]{1,0:T(8,128)S(1)}, f32[112,128]{1,0:T(8,128)S(1)}, u32[]{:S(2)}, u32[]{:S(2)}) collective-permute-start(f32[112,128]{1,0:T(8,128)S(1)} %pad_maximum_fusion.8), channel_id=1, source_target_pairs={{0,64},{16,80},{32,96},{48,112},{64,0},{80,16},{96,32},{112,48},{1... | collective-permute-start | bytes 172040 | tf_op jit(solution)/shard_map/ppermute | solution.py:24
  40.0 1.6 %collective-permute-done.14 = f32[112,128]{1,0:T(8,128)S(1)} collective-permute-done((f32[112,128]{1,0:T(8,128)S(1)}, f32[112,128]{1,0:T(8,128)S(1)}, u32[]{:S(2)}, u32[]{:S(2)}) %collective-permute-start.14) | collective-permute-done | bytes 57376 | tf_op jit(solution)/shard_map/ppermute | solution.py:24
  41.5 6.3 %collective-permute-start.15 = (f32[112,128]{1,0:T(8,128)S(1)}, f32[112,128]{1,0:T(8,128)S(1)}, u32[]{:S(2)}, u32[]{:S(2)}) collective-permute-start(f32[112,128]{1,0:T(8,128)S(1)} %fusion.21), channel_id=1, source_target_pairs={{0,128},{16,144},{32,160},{48,176},{64,192},{80,208},{96,224},{112... | collective-permute-start | bytes 172040 | tf_op jit(solution)/shard_map/ppermute | solution.py:24
  47.8 1.7 %collective-permute-done.15 = f32[112,128]{1,0:T(8,128)S(1)} collective-permute-done((f32[112,128]{1,0:T(8,128)S(1)}, f32[112,128]{1,0:T(8,128)S(1)}, u32[]{:S(2)}, u32[]{:S(2)}) %collective-permute-start.15) | collective-permute-done | bytes 57376 | tf_op jit(solution)/shard_map/ppermute | solution.py:24
  49.6 3.3 %collective-permute-done.16 = f32[112,128]{1,0:T(8,128)S(1)} collective-permute-done((f32[112,128]{1,0:T(8,128)S(1)}, f32[112,128]{1,0:T(8,128)S(1)}, u32[]{:S(2)}, u32[]{:S(2)}) %collective-permute-start.16) | collective-permute-done | bytes 57376 | tf_op jit(solution)/shard_map/ppermute | solution.py:24
  54.1 3.4 %collective-permute-done.17 = f32[112,128]{1,0:T(8,128)S(1)} collective-permute-done((f32[112,128]{1,0:T(8,128)S(1)}, f32[112,128]{1,0:T(8,128)S(1)}, u32[]{:S(2)}, u32[]{:S(2)}) %collective-permute-start.17) | collective-permute-done | bytes 57376 | tf_op jit(solution)/shard_map/ppermute | solution.py:24
  57.6 3.0 %collective-permute-done.18 = f32[112,128]{1,0:T(8,128)S(1)} collective-permute-done((f32[112,128]{1,0:T(8,128)S(1)}, f32[112,128]{1,0:T(8,128)S(1)}, u32[]{:S(2)}, u32[]{:S(2)}) %collective-permute-start.18) | collective-permute-done | bytes 57376 | tf_op jit(solution)/shard_map/ppermute | solution.py:24
  60.7 1.6 %collective-permute-start.19 = (f32[112,128]{1,0:T(8,128)S(1)}, f32[112,128]{1,0:T(8,128)S(1)}, u32[]{:S(2)}, u32[]{:S(2)}) collective-permute-start(f32[112,128]{1,0:T(8,128)S(1)} %add.87), channel_id=1, source_target_pairs={{0,8},{1,9},{2,10},{3,11},{4,12},{5,13},{6,14},{7,15},{8,0},{9,1},... | collective-permute-start | bytes 172040 | tf_op jit(solution)/shard_map/ppermute | solution.py:24
  62.3 3.0 %collective-permute-done.19 = f32[112,128]{1,0:T(8,128)S(1)} collective-permute-done((f32[112,128]{1,0:T(8,128)S(1)}, f32[112,128]{1,0:T(8,128)S(1)}, u32[]{:S(2)}, u32[]{:S(2)}) %collective-permute-start.19) | collective-permute-done | bytes 57376 | tf_op jit(solution)/shard_map/ppermute | solution.py:24
  65.3 2.6 %collective-permute-start.20 = (f32[112,128]{1,0:T(8,128)S(1)}, f32[112,128]{1,0:T(8,128)S(1)}, u32[]{:S(2)}, u32[]{:S(2)}) collective-permute-start(f32[112,128]{1,0:T(8,128)S(1)} %add.88), channel_id=1, source_target_pairs={{0,32},{16,48},{32,0},{48,16},{64,96},{80,112},{96,64},{112,80},{1... | collective-permute-start | bytes 172040 | tf_op jit(solution)/shard_map/ppermute | solution.py:30
  67.9 1.6 %collective-permute-done.20 = f32[112,128]{1,0:T(8,128)S(1)} collective-permute-done((f32[112,128]{1,0:T(8,128)S(1)}, f32[112,128]{1,0:T(8,128)S(1)}, u32[]{:S(2)}, u32[]{:S(2)}) %collective-permute-start.20) | collective-permute-done | bytes 57376 | tf_op jit(solution)/shard_map/ppermute | solution.py:30
  69.5 9.2 %collective-permute-start.21 = (f32[168,128]{1,0:T(8,128)S(1)}, f32[168,128]{1,0:T(8,128)S(1)}, u32[]{:S(2)}, u32[]{:S(2)}) collective-permute-start(f32[168,128]{1,0:T(8,128)S(1)} %pad_maximum_fusion.4), channel_id=1, source_target_pairs={{0,16},{16,0},{32,48},{48,32},{64,80},{80,64},{96,112},{112,96},{1... | collective-permute-start | bytes 258056 | tf_op jit(solution)/shard_map/ppermute | solution.py:30
  87.0 11.2 %conditional.1 = (f32[32,32]{1,0:T(8,128)S(1)}, f32[4,8,32,128]{3,2,1,0:T(8,128)}) conditional(s32[]{:T(128)} %convert_element_type.8, (f32[192,32]{0,1:T(8,128)}, f32[32,192,128]{2,1,0:T(8,128)S(1)}, f32[32,32,128]{2,1,0:T(8,128)}, f32[32,32]{0,1:T(8,128)S(1)}) %tuple.79, (f32[32,32]{0,1:T(8,128)S(1)}, f32[32,32]{0,1:T(8,128)S(1)}, ...), branch_computations={%region_3.8_spmd, %region_6.9_spmd} | conditional | flops 403195936 | bytes 8176238 | solution.py:175
  87.1 2.9 %cholesky.55 = f32[32,32]{1,0:T(8,128)S(1)} custom-call(f32[32,32]{1,0:T(8,128)S(1)} %fusion.8), custom_call_target="Cholesky" | custom-call | tf_op jit(solution)/shard_map/cond/branch_1_fun/jit(cholesky)/cholesky | solution.py:155
  91.4 2.4 %custom-call.7 = f32[1,32,32]{1,2,0:T(8,128)S(1)} custom-call(f32[1,32,32]{2,1,0:T(8,128)S(1)} %get-tuple-element.63), custom_call_target="InvertDiagBlocksLowerTriangular" | custom-call | tf_op jit(solution)/shard_map/cond/branch_1_fun/triangular_solve/custom-call.0 | solution.py:156
  96.4 1.9 %convolution_subtract_fusion = f32[32,32,128]{2,0,1:T(8,128)} fusion(f32[32,32,128]{2,0,1:T(8,128)S(1)} %fusion.4, f32[32,192,1]{1,0,2:T(8,128)S(1)} %convolution_bitcast_fusion.3, f32[32,192,128]{2,1,0:T(8,128)S(1)} %get-tuple-element.29), kind=kOutput, calls=%fused_computation.15 | convolution fusion | flops 151126016 | bytes 4218880 | tf_op jit(solution)/shard_map/cond/branch_1_fun/epi,pw->ewi/dot_general | solution.py:164
  (88 shorter events, 23.2 us)
Async XLA Ops:
  1.4 13.4 %collective-permute-start.10 = (bf16[4,1,32,128]{3,2,1,0:T(8,128)(2,1)S(1)}, bf16[4,1,32,128]{3,2,1,0:T(8,128)(2,1)S(1)}, u32[]{:S(2)}, u32[]{:S(2)}) collective-permute-start(bf16[4,1,32,128]{3,2,1,0:T(8,128)(2,1)S(1)} %get-tuple-element.72), channel_id=1, source_target_pairs={{1,0},{2,1},{3,2},{4,3},{5,4},{6,5},{7,6},{8,7},{9,8},{10,9},{11,1... | collective-permute-start | bytes 98312 | tf_op jit(solution)/shard_map/ppermute | solution.py:101
  7.2 7.7 %collective-permute-start.9 = (bf16[4,1,32,128]{3,2,1,0:T(8,128)(2,1)S(1)}, bf16[4,1,32,128]{3,2,1,0:T(8,128)(2,1)S(1)}, u32[]{:S(2)}, u32[]{:S(2)}) collective-permute-start(bf16[4,1,32,128]{3,2,1,0:T(8,128)(2,1)S(1)} %get-tuple-element.73), channel_id=1, source_target_pairs={{0,1},{1,2},{2,3},{3,4},{4,5},{5,6},{6,7},{7,8},{8,9},{9,10},{10,1... | collective-permute-start | bytes 98312 | tf_op jit(solution)/shard_map/ppermute | solution.py:100
  7.2 6.7 %copy-start.2 = (bf16[4,8,32,128]{3,2,1,0:T(8,128)(2,1)S(1)}, bf16[4,8,32,128]{3,2,1,0:T(8,128)(2,1)}, u32[]{:S(2)}) copy-start(bf16[4,8,32,128]{3,2,1,0:T(8,128)(2,1)} %param.10) | copy-start | bytes 786436
  7.2 7.5 %copy-start.5 = (s32[4,8,5]{1,0,2:T(4,128)S(1)}, s32[4,8,5]{1,0,2:T(4,128)}, u32[]{:S(2)}) copy-start(s32[4,8,5]{1,0,2:T(4,128)} %param.12) | copy-start | bytes 1924
  12.9 1.9 %collective-permute-start.8 = (f32[112,128]{1,0:T(8,128)S(1)}, f32[112,128]{1,0:T(8,128)S(1)}, u32[]{:S(2)}, u32[]{:S(2)}) collective-permute-start(f32[112,128]{1,0:T(8,128)S(1)} %slice_select_fusion), channel_id=1, source_target_pairs={{0,16},{16,0},{32,48},{48,32},{64,80},{80,64},{96,112},{112,96},{1... | collective-permute-start | bytes 172040 | tf_op jit(solution)/shard_map/ppermute | solution.py:30
  14.9 7.4 %collective-permute-start.11 = (f32[56,128]{1,0:T(8,128)S(1)}, f32[56,128]{1,0:T(8,128)S(1)}, u32[]{:S(2)}, u32[]{:S(2)}) collective-permute-start(f32[56,128]{1,0:T(8,128)S(1)} %slice_select_fusion.1), channel_id=1, source_target_pairs={{0,32},{16,48},{32,0},{48,16},{64,96},{80,112},{96,64},{112,80},{1... | collective-permute-start | bytes 86024 | tf_op jit(solution)/shard_map/ppermute | solution.py:30
  16.6 5.8 %collective-permute-start.12 = (bf16[1,10,32,128]{3,2,1,0:T(8,128)(2,1)S(1)}, bf16[1,10,32,128]{3,2,1,0:T(8,128)(2,1)S(1)}, u32[]{:S(2)}, u32[]{:S(2)}) collective-permute-start(bf16[1,10,32,128]{3,2,1,0:T(8,128)(2,1)S(1)} %pad_maximum_fusion.5), channel_id=1, source_target_pairs={{16,0},{32,16},{48,32},{64,48},{80,64},{96,80},{112,96},{128,112},... | collective-permute-start | bytes 245768 | tf_op jit(solution)/shard_map/ppermute | solution.py:109
  19.3 4.4 %collective-permute-start.13 = (bf16[1,10,32,128]{3,2,1,0:T(8,128)(2,1)S(1)}, bf16[1,10,32,128]{3,2,1,0:T(8,128)(2,1)S(1)}, u32[]{:S(2)}, u32[]{:S(2)}) collective-permute-start(bf16[1,10,32,128]{3,2,1,0:T(8,128)(2,1)S(1)} %pad_maximum_fusion.6), channel_id=1, source_target_pairs={{0,16},{16,32},{32,48},{48,64},{64,80},{80,96},{96,112},{112,128},... | collective-permute-start | bytes 245768 | tf_op jit(solution)/shard_map/ppermute | solution.py:108
  25.2 4.2 %copy-start.4 = (bf16[4,8,5,128,128]{4,3,2,1,0:T(8,128)(2,1)S(1)}, bf16[4,8,5,128,128]{4,3,2,1,0:T(8,128)(2,1)}, u32[]{:S(2)}) copy-start(bf16[4,8,5,128,128]{4,3,2,1,0:T(8,128)(2,1)} %param.9) | copy-start | bytes 15728644
  29.5 4.2 %copy-start = (f32[4,8,192,128]{3,2,1,0:T(8,128)S(1)}, f32[4,8,192,128]{3,2,1,0:T(8,128)}, u32[]{:S(2)}) copy-start(f32[4,8,192,128]{3,2,1,0:T(8,128)} %param.11) | copy-start | bytes 9437188
  32.8 0.8 copy-start.1
  36.9 4.6 %collective-permute-start.14 = (f32[112,128]{1,0:T(8,128)S(1)}, f32[112,128]{1,0:T(8,128)S(1)}, u32[]{:S(2)}, u32[]{:S(2)}) collective-permute-start(f32[112,128]{1,0:T(8,128)S(1)} %pad_maximum_fusion.8), channel_id=1, source_target_pairs={{0,64},{16,80},{32,96},{48,112},{64,0},{80,16},{96,32},{112,48},{1... | collective-permute-start | bytes 172040 | tf_op jit(solution)/shard_map/ppermute | solution.py:24
  41.5 7.9 %collective-permute-start.15 = (f32[112,128]{1,0:T(8,128)S(1)}, f32[112,128]{1,0:T(8,128)S(1)}, u32[]{:S(2)}, u32[]{:S(2)}) collective-permute-start(f32[112,128]{1,0:T(8,128)S(1)} %fusion.21), channel_id=1, source_target_pairs={{0,128},{16,144},{32,160},{48,176},{64,192},{80,208},{96,224},{112... | collective-permute-start | bytes 172040 | tf_op jit(solution)/shard_map/ppermute | solution.py:24
  49.5 3.4 %collective-permute-start.16 = (f32[112,128]{1,0:T(8,128)S(1)}, f32[112,128]{1,0:T(8,128)S(1)}, u32[]{:S(2)}, u32[]{:S(2)}) collective-permute-start(f32[112,128]{1,0:T(8,128)S(1)} %add.84), channel_id=1, source_target_pairs={{0,1},{1,0},{2,3},{3,2},{4,5},{5,4},{6,7},{7,6},{8,9},{9,8},{10,11... | collective-permute-start | bytes 172040 | tf_op jit(solution)/shard_map/ppermute | solution.py:24
  52.9 4.6 %collective-permute-start.17 = (f32[112,128]{1,0:T(8,128)S(1)}, f32[112,128]{1,0:T(8,128)S(1)}, u32[]{:S(2)}, u32[]{:S(2)}) collective-permute-start(f32[112,128]{1,0:T(8,128)S(1)} %add.85), channel_id=1, source_target_pairs={{0,2},{1,3},{2,0},{3,1},{4,6},{5,7},{6,4},{7,5},{8,10},{9,11},{10,... | collective-permute-start | bytes 172040 | tf_op jit(solution)/shard_map/ppermute | solution.py:24
  57.5 3.1 %collective-permute-start.18 = (f32[112,128]{1,0:T(8,128)S(1)}, f32[112,128]{1,0:T(8,128)S(1)}, u32[]{:S(2)}, u32[]{:S(2)}) collective-permute-start(f32[112,128]{1,0:T(8,128)S(1)} %add.86), channel_id=1, source_target_pairs={{0,4},{1,5},{2,6},{3,7},{4,0},{5,1},{6,2},{7,3},{8,12},{9,13},{10,... | collective-permute-start | bytes 172040 | tf_op jit(solution)/shard_map/ppermute | solution.py:24
  60.7 4.6 %collective-permute-start.19 = (f32[112,128]{1,0:T(8,128)S(1)}, f32[112,128]{1,0:T(8,128)S(1)}, u32[]{:S(2)}, u32[]{:S(2)}) collective-permute-start(f32[112,128]{1,0:T(8,128)S(1)} %add.87), channel_id=1, source_target_pairs={{0,8},{1,9},{2,10},{3,11},{4,12},{5,13},{6,14},{7,15},{8,0},{9,1},... | collective-permute-start | bytes 172040 | tf_op jit(solution)/shard_map/ppermute | solution.py:24
  65.3 4.2 %collective-permute-start.20 = (f32[112,128]{1,0:T(8,128)S(1)}, f32[112,128]{1,0:T(8,128)S(1)}, u32[]{:S(2)}, u32[]{:S(2)}) collective-permute-start(f32[112,128]{1,0:T(8,128)S(1)} %add.88), channel_id=1, source_target_pairs={{0,32},{16,48},{32,0},{48,16},{64,96},{80,112},{96,64},{112,80},{1... | collective-permute-start | bytes 172040 | tf_op jit(solution)/shard_map/ppermute | solution.py:30
  69.5 10.1 %collective-permute-start.21 = (f32[168,128]{1,0:T(8,128)S(1)}, f32[168,128]{1,0:T(8,128)S(1)}, u32[]{:S(2)}, u32[]{:S(2)}) collective-permute-start(f32[168,128]{1,0:T(8,128)S(1)} %pad_maximum_fusion.4), channel_id=1, source_target_pairs={{0,16},{16,0},{32,48},{48,32},{64,80},{80,64},{96,112},{112,96},{1... | collective-permute-start | bytes 258056 | tf_op jit(solution)/shard_map/ppermute | solution.py:30

commit v13 on v12

--- a/solution.py
+++ b/solution.py
@@ -149,7 +149,7 @@
         + mm("pv,pw->vw", coefficients, mm("pq,qw->pw", kept_gram, coefficients))
     ) / total_rows
     eye = jnp.eye(NEW, dtype=jnp.float32)
-    kept_share = jnp.sum(expanded * eye, axis=1) * 16.0 >= jnp.sum(image_gram * eye, axis=1) / total_rows
+    kept_share = jnp.min(jnp.sum(expanded * 16.0 - image_gram / total_rows, axis=1, where=eye > 0)) >= 0.0
 
     def factor_of(gram):
         lower = jnp.linalg.cholesky(gram)
@@ -172,7 +172,7 @@
         lower, inverse = factor_of(all_sum(mm("evi,ewi->vw", twice, twice), steps) / total_rows)
         return mm("evi,wv->ewi", twice, inverse), lower
 
-    basis, lower = lax.cond(jnp.all(kept_share), expanded_path, direct_path)
+    basis, lower = lax.cond(kept_share, expanded_path, direct_path)
     basis = basis.reshape(rows_r, rows_a, NEW, BLK)
     return (basis, coefficients, lower.T)
 

time: 99.5 us -> 99.5 us (level)
  no operation moved by 1% of the time
where the time goes in v13:
time: 99.5 us; the launch traced here: 98.9 us
  starting transfers between devices  38.2 us (38%)
  matrix products  21 us (21%)
  waiting for transfers between devices  19.9 us (20%)
  other arithmetic  13.4 us (13%)
  local copies, waits for them, and re-layouts  4.75 us (5%)
  between operations  1.63 us (2%)
    ppermute x6, waiting for transfers between devices, all_sum(): x = x + lax.ppermute(x, axis, [(i, i ^ step) for i in range(count)])  16 us
    ppermute x4, starting transfers between devices, exchange(): return lax.ppermute(x, axis, [(i, i ^ step) for i in range(count)])  14.6 us
    dot_general x8, matrix products, mm(): jnp.einsum(spec, a, b, precision=lax.Precision.HIGHEST, preferred_element...  14.1 us
    ppermute x6, starting transfers between devices, all_sum(): x = x + lax.ppermute(x, axis, [(i, i ^ step) for i in range(count)])  12.3 us
    ppermute x1, starting transfers between devices, on_device(): lax.ppermute(new_block[:, :1], 'azi', [((i + 1) % n_a, i) for i in range(...  5.76 us
    unnamed x3, other arithmetic  4.39 us
    another operation x3, other arithmetic, factor_of(): lower = jnp.linalg.cholesky(gram)  3.6 us
    dot_general x1, matrix products, on_device(): jnp.einsum('rakij,rakvj->ravi', jacobian, picked, preferred_element_type=...  3.36 us
  transfers between devices with their start and end apart: 14, of which 10 were waited for; matrix products, arithmetic and copies ran while one was open for 7% of the time, Pallas kernels for 0%

profile of v13, /device:TPU:1, one launch (start us, length us, event | category | flops | bytes accessed | tf_op | source)
XLA Modules:
  0.0 98.9 jit_solution(7770955572098770904)
XLA Ops:
  1.4 5.8 %collective-permute-start.10 = (bf16[4,1,32,128]{3,2,1,0:T(8,128)(2,1)S(1)}, bf16[4,1,32,128]{3,2,1,0:T(8,128)(2,1)S(1)}, u32[]{:S(2)}, u32[]{:S(2)}) collective-permute-start(bf16[4,1,32,128]{3,2,1,0:T(8,128)(2,1)S(1)} %get-tuple-element.75), channel_id=1, source_target_pairs={{1,0},{2,1},{3,2},{4,3},{5,4},{6,5},{7,6},{8,7},{9,8},{10,9},{11,1... | collective-permute-start | bytes 98312 | tf_op jit(solution)/shard_map/ppermute | solution.py:101
  7.2 5.5 %convolution_bitcast_fusion.4 = f32[192,192]{1,0:T(8,128)S(1)} fusion(f32[4,8,192,128]{3,2,1,0:T(8,128)} %param.11), kind=kOutput, calls=%fused_computation.30 | convolution fusion | flops 1811939328 | bytes 3293184 | tf_op jit(solution)/shard_map/epi,eqi->pq/dot_general | solution.py:83
  14.9 1.7 %collective-permute-start.11 = (f32[56,128]{1,0:T(8,128)S(1)}, f32[56,128]{1,0:T(8,128)S(1)}, u32[]{:S(2)}, u32[]{:S(2)}) collective-permute-start(f32[56,128]{1,0:T(8,128)S(1)} %slice_select_fusion.1), channel_id=1, source_target_pairs={{0,32},{16,48},{32,0},{48,16},{64,96},{80,112},{96,64},{112,80},{1... | collective-permute-start | bytes 86024 | tf_op jit(solution)/shard_map/ppermute | solution.py:30
  16.6 2.7 %collective-permute-start.12 = (bf16[1,10,32,128]{3,2,1,0:T(8,128)(2,1)S(1)}, bf16[1,10,32,128]{3,2,1,0:T(8,128)(2,1)S(1)}, u32[]{:S(2)}, u32[]{:S(2)}) collective-permute-start(bf16[1,10,32,128]{3,2,1,0:T(8,128)(2,1)S(1)} %pad_maximum_fusion.5), channel_id=1, source_target_pairs={{16,0},{32,16},{48,32},{64,48},{80,64},{96,80},{112,96},{128,112},... | collective-permute-start | bytes 245768 | tf_op jit(solution)/shard_map/ppermute | solution.py:109
  19.3 2.9 %collective-permute-start.13 = (bf16[1,10,32,128]{3,2,1,0:T(8,128)(2,1)S(1)}, bf16[1,10,32,128]{3,2,1,0:T(8,128)(2,1)S(1)}, u32[]{:S(2)}, u32[]{:S(2)}) collective-permute-start(bf16[1,10,32,128]{3,2,1,0:T(8,128)(2,1)S(1)} %pad_maximum_fusion.6), channel_id=1, source_target_pairs={{0,16},{16,32},{32,48},{48,64},{64,80},{80,96},{96,112},{112,128},... | collective-permute-start | bytes 245768 | tf_op jit(solution)/shard_map/ppermute | solution.py:108
  23.7 1.6 %bitcast_dynamic-update-slice_fusion.2 = (bf16[4,8,5,32,128]{4,3,2,1,0:T(8,128)(2,1)}, bf16[4,8,32,128]{3,2,1,0:T(8,128)(2,1)S(1)}, bf16[4,8,32,128]{3,2,1,0:T(8...) fusion(bf16[4,8,5,32,128]{4,3,2,1,0:T(8,128)(2,1)} %bitcast_dynamic-update-slice_fusion.4, ...), kind=kLoop, calls=%fused_computation.56 | loop fusion | flops 5242880 | bytes 2130176
  29.5 3.4 %fusion.31 = f32[4,8,32,128,1]{3,2,4,1,0:T(8,128)S(1)} fusion(bf16[4,8,5,32,128]{4,3,2,1,0:T(8,128)(2,1)} %bitcast_dynamic-update-slice_fusion.3, bf16[4,8,5,128,128]{4,3,2,1,0:T(8,128)(2,1)S(1)} %copy-done.4), kind=kOutput, calls=%fused_computation.124 | convolution fusion | flops 167772160 | bytes 7077888 | tf_op jit(solution)/shard_map/rakij,rakvj->ravi/dot_general | solution.py:122
  33.7 2.9 %convolution_bitcast_fusion.5 = f32[192,32]{0,1:T(8,128)S(1)} fusion(f32[4,8,192,128]{3,2,1,0:T(8,128)S(1)} %copy-done, f32[4,8,32,128,1]{3,2,4,1,0:T(8,128)S(1)} %fusion.31), kind=kOutput, calls=%fused_computation.31 | convolution fusion | flops 301989888 | bytes 3694592 | tf_op jit(solution)/shard_map/epi,evi->pv/dot_general | solution.py:83
  36.9 3.1 %collective-permute-start.14 = (f32[112,128]{1,0:T(8,128)S(1)}, f32[112,128]{1,0:T(8,128)S(1)}, u32[]{:S(2)}, u32[]{:S(2)}) collective-permute-start(f32[112,128]{1,0:T(8,128)S(1)} %pad_maximum_fusion.8), channel_id=1, source_target_pairs={{0,64},{16,80},{32,96},{48,112},{64,0},{80,16},{96,32},{112,48},{1... | collective-permute-start | bytes 172040 | tf_op jit(solution)/shard_map/ppermute | solution.py:24
  40.0 1.6 %collective-permute-done.14 = f32[112,128]{1,0:T(8,128)S(1)} collective-permute-done((f32[112,128]{1,0:T(8,128)S(1)}, f32[112,128]{1,0:T(8,128)S(1)}, u32[]{:S(2)}, u32[]{:S(2)}) %collective-permute-start.14) | collective-permute-done | bytes 57376 | tf_op jit(solution)/shard_map/ppermute | solution.py:24
  41.6 6.3 %collective-permute-start.15 = (f32[112,128]{1,0:T(8,128)S(1)}, f32[112,128]{1,0:T(8,128)S(1)}, u32[]{:S(2)}, u32[]{:S(2)}) collective-permute-start(f32[112,128]{1,0:T(8,128)S(1)} %fusion.20), channel_id=1, source_target_pairs={{0,128},{16,144},{32,160},{48,176},{64,192},{80,208},{96,224},{112... | collective-permute-start | bytes 172040 | tf_op jit(solution)/shard_map/ppermute | solution.py:24
  47.8 1.7 %collective-permute-done.15 = f32[112,128]{1,0:T(8,128)S(1)} collective-permute-done((f32[112,128]{1,0:T(8,128)S(1)}, f32[112,128]{1,0:T(8,128)S(1)}, u32[]{:S(2)}, u32[]{:S(2)}) %collective-permute-start.15) | collective-permute-done | bytes 57376 | tf_op jit(solution)/shard_map/ppermute | solution.py:24
  49.6 3.3 %collective-permute-done.16 = f32[112,128]{1,0:T(8,128)S(1)} collective-permute-done((f32[112,128]{1,0:T(8,128)S(1)}, f32[112,128]{1,0:T(8,128)S(1)}, u32[]{:S(2)}, u32[]{:S(2)}) %collective-permute-start.16) | collective-permute-done | bytes 57376 | tf_op jit(solution)/shard_map/ppermute | solution.py:24
  54.1 3.4 %collective-permute-done.17 = f32[112,128]{1,0:T(8,128)S(1)} collective-permute-done((f32[112,128]{1,0:T(8,128)S(1)}, f32[112,128]{1,0:T(8,128)S(1)}, u32[]{:S(2)}, u32[]{:S(2)}) %collective-permute-start.17) | collective-permute-done | bytes 57376 | tf_op jit(solution)/shard_map/ppermute | solution.py:24
  57.7 3.0 %collective-permute-done.18 = f32[112,128]{1,0:T(8,128)S(1)} collective-permute-done((f32[112,128]{1,0:T(8,128)S(1)}, f32[112,128]{1,0:T(8,128)S(1)}, u32[]{:S(2)}, u32[]{:S(2)}) %collective-permute-start.18) | collective-permute-done | bytes 57376 | tf_op jit(solution)/shard_map/ppermute | solution.py:24
  60.7 1.6 %collective-permute-start.19 = (f32[112,128]{1,0:T(8,128)S(1)}, f32[112,128]{1,0:T(8,128)S(1)}, u32[]{:S(2)}, u32[]{:S(2)}) collective-permute-start(f32[112,128]{1,0:T(8,128)S(1)} %add.87), channel_id=1, source_target_pairs={{0,8},{1,9},{2,10},{3,11},{4,12},{5,13},{6,14},{7,15},{8,0},{9,1},... | collective-permute-start | bytes 172040 | tf_op jit(solution)/shard_map/ppermute | solution.py:24
  62.3 3.0 %collective-permute-done.19 = f32[112,128]{1,0:T(8,128)S(1)} collective-permute-done((f32[112,128]{1,0:T(8,128)S(1)}, f32[112,128]{1,0:T(8,128)S(1)}, u32[]{:S(2)}, u32[]{:S(2)}) %collective-permute-start.19) | collective-permute-done | bytes 57376 | tf_op jit(solution)/shard_map/ppermute | solution.py:24
  65.3 2.6 %collective-permute-start.20 = (f32[112,128]{1,0:T(8,128)S(1)}, f32[112,128]{1,0:T(8,128)S(1)}, u32[]{:S(2)}, u32[]{:S(2)}) collective-permute-start(f32[112,128]{1,0:T(8,128)S(1)} %add.88), channel_id=1, source_target_pairs={{0,32},{16,48},{32,0},{48,16},{64,96},{80,112},{96,64},{112,80},{1... | collective-permute-start | bytes 172040 | tf_op jit(solution)/shard_map/ppermute | solution.py:30
  68.0 1.6 %collective-permute-done.20 = f32[112,128]{1,0:T(8,128)S(1)} collective-permute-done((f32[112,128]{1,0:T(8,128)S(1)}, f32[112,128]{1,0:T(8,128)S(1)}, u32[]{:S(2)}, u32[]{:S(2)}) %collective-permute-start.20) | collective-permute-done | bytes 57376 | tf_op jit(solution)/shard_map/ppermute | solution.py:30
  69.6 9.2 %collective-permute-start.21 = (f32[168,128]{1,0:T(8,128)S(1)}, f32[168,128]{1,0:T(8,128)S(1)}, u32[]{:S(2)}, u32[]{:S(2)}) collective-permute-start(f32[168,128]{1,0:T(8,128)S(1)} %pad_maximum_fusion.4), channel_id=1, source_target_pairs={{0,16},{16,0},{32,48},{48,32},{64,80},{80,64},{96,112},{112,96},{1... | collective-permute-start | bytes 258056 | tf_op jit(solution)/shard_map/ppermute | solution.py:30
  87.0 11.3 %conditional.1 = (f32[32,32]{1,0:T(8,128)S(1)}, f32[4,8,32,128]{3,2,1,0:T(8,128)}) conditional(s32[]{:T(128)} %convert_element_type.11, (f32[192,32]{0,1:T(8,128)}, f32[32,192,128]{2,1,0:T(8,128)S(1)}, f32[32,32,128]{2,1,0:T(8,128)}, f32[32,32]{0,1:T(8,128)S(1)}) %tuple.79, (f32[32,32]{0,1:T(8,128)S(1)}, f32[32,32]{0,1:T(8,128)S(1)}, ...), branch_computations={%region_2.7_spmd, %region_5.8_spmd} | conditional | flops 403195936 | bytes 8176238 | solution.py:175
  87.1 2.9 %cholesky.55 = f32[32,32]{1,0:T(8,128)S(1)} custom-call(f32[32,32]{1,0:T(8,128)S(1)} %fusion.8), custom_call_target="Cholesky" | custom-call | tf_op jit(solution)/shard_map/cond/branch_1_fun/jit(cholesky)/cholesky | solution.py:155
  91.3 2.4 %custom-call.7 = f32[1,32,32]{1,2,0:T(8,128)S(1)} custom-call(f32[1,32,32]{2,1,0:T(8,128)S(1)} %get-tuple-element.66), custom_call_target="InvertDiagBlocksLowerTriangular" | custom-call | tf_op jit(solution)/shard_map/cond/branch_1_fun/triangular_solve/custom-call.0 | solution.py:156
  96.3 1.9 %convolution_subtract_fusion = f32[32,32,128]{2,0,1:T(8,128)} fusion(f32[32,32,128]{2,0,1:T(8,128)S(1)} %fusion.4, f32[32,192,1]{1,0,2:T(8,128)S(1)} %convolution_bitcast_fusion.3, f32[32,192,128]{2,1,0:T(8,128)S(1)} %get-tuple-element.32), kind=kOutput, calls=%fused_computation.15 | convolution fusion | flops 151126016 | bytes 4218880 | tf_op jit(solution)/shard_map/cond/branch_1_fun/epi,pw->ewi/dot_general | solution.py:164
  (88 shorter events, 23.2 us)
Async XLA Ops:
  1.4 13.4 %collective-permute-start.10 = (bf16[4,1,32,128]{3,2,1,0:T(8,128)(2,1)S(1)}, bf16[4,1,32,128]{3,2,1,0:T(8,128)(2,1)S(1)}, u32[]{:S(2)}, u32[]{:S(2)}) collective-permute-start(bf16[4,1,32,128]{3,2,1,0:T(8,128)(2,1)S(1)} %get-tuple-element.75), channel_id=1, source_target_pairs={{1,0},{2,1},{3,2},{4,3},{5,4},{6,5},{7,6},{8,7},{9,8},{10,9},{11,1... | collective-permute-start | bytes 98312 | tf_op jit(solution)/shard_map/ppermute | solution.py:101
  7.2 7.7 %collective-permute-start.9 = (bf16[4,1,32,128]{3,2,1,0:T(8,128)(2,1)S(1)}, bf16[4,1,32,128]{3,2,1,0:T(8,128)(2,1)S(1)}, u32[]{:S(2)}, u32[]{:S(2)}) collective-permute-start(bf16[4,1,32,128]{3,2,1,0:T(8,128)(2,1)S(1)} %get-tuple-element.76), channel_id=1, source_target_pairs={{0,1},{1,2},{2,3},{3,4},{4,5},{5,6},{6,7},{7,8},{8,9},{9,10},{10,1... | collective-permute-start | bytes 98312 | tf_op jit(solution)/shard_map/ppermute | solution.py:100
  7.2 6.7 %copy-start.2 = (bf16[4,8,32,128]{3,2,1,0:T(8,128)(2,1)S(1)}, bf16[4,8,32,128]{3,2,1,0:T(8,128)(2,1)}, u32[]{:S(2)}) copy-start(bf16[4,8,32,128]{3,2,1,0:T(8,128)(2,1)} %param.10) | copy-start | bytes 786436
  7.2 7.5 %copy-start.5 = (s32[4,8,5]{1,0,2:T(4,128)S(1)}, s32[4,8,5]{1,0,2:T(4,128)}, u32[]{:S(2)}) copy-start(s32[4,8,5]{1,0,2:T(4,128)} %param.12) | copy-start | bytes 1924
  12.9 1.9 %collective-permute-start.8 = (f32[112,128]{1,0:T(8,128)S(1)}, f32[112,128]{1,0:T(8,128)S(1)}, u32[]{:S(2)}, u32[]{:S(2)}) collective-permute-start(f32[112,128]{1,0:T(8,128)S(1)} %slice_select_fusion), channel_id=1, source_target_pairs={{0,16},{16,0},{32,48},{48,32},{64,80},{80,64},{96,112},{112,96},{1... | collective-permute-start | bytes 172040 | tf_op jit(solution)/shard_map/ppermute | solution.py:30
  14.9 7.4 %collective-permute-start.11 = (f32[56,128]{1,0:T(8,128)S(1)}, f32[56,128]{1,0:T(8,128)S(1)}, u32[]{:S(2)}, u32[]{:S(2)}) collective-permute-start(f32[56,128]{1,0:T(8,128)S(1)} %slice_select_fusion.1), channel_id=1, source_target_pairs={{0,32},{16,48},{32,0},{48,16},{64,96},{80,112},{96,64},{112,80},{1... | collective-permute-start | bytes 86024 | tf_op jit(solution)/shard_map/ppermute | solution.py:30
  16.6 5.8 %collective-permute-start.12 = (bf16[1,10,32,128]{3,2,1,0:T(8,128)(2,1)S(1)}, bf16[1,10,32,128]{3,2,1,0:T(8,128)(2,1)S(1)}, u32[]{:S(2)}, u32[]{:S(2)}) collective-permute-start(bf16[1,10,32,128]{3,2,1,0:T(8,128)(2,1)S(1)} %pad_maximum_fusion.5), channel_id=1, source_target_pairs={{16,0},{32,16},{48,32},{64,48},{80,64},{96,80},{112,96},{128,112},... | collective-permute-start | bytes 245768 | tf_op jit(solution)/shard_map/ppermute | solution.py:109
  19.3 4.3 %collective-permute-start.13 = (bf16[1,10,32,128]{3,2,1,0:T(8,128)(2,1)S(1)}, bf16[1,10,32,128]{3,2,1,0:T(8,128)(2,1)S(1)}, u32[]{:S(2)}, u32[]{:S(2)}) collective-permute-start(bf16[1,10,32,128]{3,2,1,0:T(8,128)(2,1)S(1)} %pad_maximum_fusion.6), channel_id=1, source_target_pairs={{0,16},{16,32},{32,48},{48,64},{64,80},{80,96},{96,112},{112,128},... | collective-permute-start | bytes 245768 | tf_op jit(solution)/shard_map/ppermute | solution.py:108
  25.2 4.2 %copy-start.4 = (bf16[4,8,5,128,128]{4,3,2,1,0:T(8,128)(2,1)S(1)}, bf16[4,8,5,128,128]{4,3,2,1,0:T(8,128)(2,1)}, u32[]{:S(2)}) copy-start(bf16[4,8,5,128,128]{4,3,2,1,0:T(8,128)(2,1)} %param.9) | copy-start | bytes 15728644
  29.5 4.2 %copy-start = (f32[4,8,192,128]{3,2,1,0:T(8,128)S(1)}, f32[4,8,192,128]{3,2,1,0:T(8,128)}, u32[]{:S(2)}) copy-start(f32[4,8,192,128]{3,2,1,0:T(8,128)} %param.11) | copy-start | bytes 9437188
  32.8 0.8 copy-start.1
  36.9 4.6 %collective-permute-start.14 = (f32[112,128]{1,0:T(8,128)S(1)}, f32[112,128]{1,0:T(8,128)S(1)}, u32[]{:S(2)}, u32[]{:S(2)}) collective-permute-start(f32[112,128]{1,0:T(8,128)S(1)} %pad_maximum_fusion.8), channel_id=1, source_target_pairs={{0,64},{16,80},{32,96},{48,112},{64,0},{80,16},{96,32},{112,48},{1... | collective-permute-start | bytes 172040 | tf_op jit(solution)/shard_map/ppermute | solution.py:24
  41.6 7.9 %collective-permute-start.15 = (f32[112,128]{1,0:T(8,128)S(1)}, f32[112,128]{1,0:T(8,128)S(1)}, u32[]{:S(2)}, u32[]{:S(2)}) collective-permute-start(f32[112,128]{1,0:T(8,128)S(1)} %fusion.20), channel_id=1, source_target_pairs={{0,128},{16,144},{32,160},{48,176},{64,192},{80,208},{96,224},{112... | collective-permute-start | bytes 172040 | tf_op jit(solution)/shard_map/ppermute | solution.py:24
  49.5 3.4 %collective-permute-start.16 = (f32[112,128]{1,0:T(8,128)S(1)}, f32[112,128]{1,0:T(8,128)S(1)}, u32[]{:S(2)}, u32[]{:S(2)}) collective-permute-start(f32[112,128]{1,0:T(8,128)S(1)} %add.84), channel_id=1, source_target_pairs={{0,1},{1,0},{2,3},{3,2},{4,5},{5,4},{6,7},{7,6},{8,9},{9,8},{10,11... | collective-permute-start | bytes 172040 | tf_op jit(solution)/shard_map/ppermute | solution.py:24
  52.9 4.6 %collective-permute-start.17 = (f32[112,128]{1,0:T(8,128)S(1)}, f32[112,128]{1,0:T(8,128)S(1)}, u32[]{:S(2)}, u32[]{:S(2)}) collective-permute-start(f32[112,128]{1,0:T(8,128)S(1)} %add.85), channel_id=1, source_target_pairs={{0,2},{1,3},{2,0},{3,1},{4,6},{5,7},{6,4},{7,5},{8,10},{9,11},{10,... | collective-permute-start | bytes 172040 | tf_op jit(solution)/shard_map/ppermute | solution.py:24
  57.6 3.1 %collective-permute-start.18 = (f32[112,128]{1,0:T(8,128)S(1)}, f32[112,128]{1,0:T(8,128)S(1)}, u32[]{:S(2)}, u32[]{:S(2)}) collective-permute-start(f32[112,128]{1,0:T(8,128)S(1)} %add.86), channel_id=1, source_target_pairs={{0,4},{1,5},{2,6},{3,7},{4,0},{5,1},{6,2},{7,3},{8,12},{9,13},{10,... | collective-permute-start | bytes 172040 | tf_op jit(solution)/shard_map/ppermute | solution.py:24
  60.7 4.6 %collective-permute-start.19 = (f32[112,128]{1,0:T(8,128)S(1)}, f32[112,128]{1,0:T(8,128)S(1)}, u32[]{:S(2)}, u32[]{:S(2)}) collective-permute-start(f32[112,128]{1,0:T(8,128)S(1)} %add.87), channel_id=1, source_target_pairs={{0,8},{1,9},{2,10},{3,11},{4,12},{5,13},{6,14},{7,15},{8,0},{9,1},... | collective-permute-start | bytes 172040 | tf_op jit(solution)/shard_map/ppermute | solution.py:24
  65.3 4.2 %collective-permute-start.20 = (f32[112,128]{1,0:T(8,128)S(1)}, f32[112,128]{1,0:T(8,128)S(1)}, u32[]{:S(2)}, u32[]{:S(2)}) collective-permute-start(f32[112,128]{1,0:T(8,128)S(1)} %add.88), channel_id=1, source_target_pairs={{0,32},{16,48},{32,0},{48,16},{64,96},{80,112},{96,64},{112,80},{1... | collective-permute-start | bytes 172040 | tf_op jit(solution)/shard_map/ppermute | solution.py:30
  69.6 10.1 %collective-permute-start.21 = (f32[168,128]{1,0:T(8,128)S(1)}, f32[168,128]{1,0:T(8,128)S(1)}, u32[]{:S(2)}, u32[]{:S(2)}) collective-permute-start(f32[168,128]{1,0:T(8,128)S(1)} %pad_maximum_fusion.4), channel_id=1, source_target_pairs={{0,16},{16,0},{32,48},{48,32},{64,80},{80,64},{96,112},{112,96},{1... | collective-permute-start | bytes 258056 | tf_op jit(solution)/shard_map/ppermute | solution.py:30

commit v14 on v12

--- a/solution.py
+++ b/solution.py
@@ -20,14 +20,21 @@
 
 def all_sum(x, steps):
     for axis, step in steps:
-        count = lax.axis_size(axis)
-        x = x + lax.ppermute(x, axis, [(i, i ^ step) for i in range(count)])
+        x = x + exchange(x, axis, step)
     return x
+
+
+def partner(axis, step, i):
+    if axis == "azi" and step in (2, 8):
+        unit = step // 2
+        digit = (i // unit) % 4
+        return i + (3 - digit - digit) * unit
+    return i ^ step
 
 
 def exchange(x, axis, step):
     count = lax.axis_size(axis)
-    return lax.ppermute(x, axis, [(i, i ^ step) for i in range(count)])
+    return lax.ppermute(x, axis, [(i, partner(axis, step, i)) for i in range(count)])
 
 
 def upper_bit(axis, step):

time: 99.5 us -> 98.9 us (level)
  waiting for transfers between devices: 19.9 us -> 17.4 us
  starting transfers between devices: 38.2 us -> 40.1 us
    ppermute x10, waiting for transfers between devices: 18.5 us -> 16 us  [exchange(): lax.ppermute(x, axis, [(i, partner(axis, step, i)) for i in range(count)])]
    ppermute x10, starting transfers between devices: 26.9 us -> 28.8 us  [exchange(): lax.ppermute(x, axis, [(i, partner(axis, step, i)) for i in range(count)])]
where the time goes in v14:
time: 98.9 us; the launch traced here: 98.3 us
  starting transfers between devices  40.1 us (41%)
  matrix products  20.9 us (21%)
  waiting for transfers between devices  17.4 us (18%)
  other arithmetic  13.4 us (14%)
  local copies, waits for them, and re-layouts  4.77 us (5%)
  between operations  1.64 us (2%)
    ppermute x10, starting transfers between devices, exchange(): lax.ppermute(x, axis, [(i, partner(axis, step, i)) for i in range(count)])  28.8 us
    ppermute x10, waiting for transfers between devices, exchange(): lax.ppermute(x, axis, [(i, partner(axis, step, i)) for i in range(count)])  16 us
    dot_general x8, matrix products, mm(): jnp.einsum(spec, a, b, precision=lax.Precision.HIGHEST, preferred_element...  14.1 us
    ppermute x1, starting transfers between devices, on_device(): lax.ppermute(new_block[:, :1], 'azi', [((i + 1) % n_a, i) for i in range(...  5.76 us
    unnamed x3, other arithmetic  4.33 us
    another operation x3, other arithmetic, factor_of(): lower = jnp.linalg.cholesky(gram)  3.6 us
    dot_general x1, matrix products, on_device(): jnp.einsum('rakij,rakvj->ravi', jacobian, picked, preferred_element_type=...  3.36 us
    another operation x2, other arithmetic, factor_of(): lax.linalg.triangular_solve(lower, eye, left_side=True, lower=True)  3.09 us
  transfers between devices with their start and end apart: 14, of which 10 were waited for; matrix products, arithmetic and copies ran while one was open for 7% of the time, Pallas kernels for 0%

profile of v14, /device:TPU:1, one launch (start us, length us, event | category | flops | bytes accessed | tf_op | source)
XLA Modules:
  0.0 98.3 jit_solution(3238423742987098764)
XLA Ops:
  1.4 5.8 %collective-permute-start.10 = (bf16[4,1,32,128]{3,2,1,0:T(8,128)(2,1)S(1)}, bf16[4,1,32,128]{3,2,1,0:T(8,128)(2,1)S(1)}, u32[]{:S(2)}, u32[]{:S(2)}) collective-permute-start(bf16[4,1,32,128]{3,2,1,0:T(8,128)(2,1)S(1)} %get-tuple-element.72), channel_id=1, source_target_pairs={{1,0},{2,1},{3,2},{4,3},{5,4},{6,5},{7,6},{8,7},{9,8},{10,9},{11,1... | collective-permute-start | bytes 98312 | tf_op jit(solution)/shard_map/ppermute | solution.py:108
  7.2 5.5 %convolution_bitcast_fusion.4 = f32[192,192]{1,0:T(8,128)S(1)} fusion(f32[4,8,192,128]{3,2,1,0:T(8,128)} %param.11), kind=kOutput, calls=%fused_computation.29 | convolution fusion | flops 1811939328 | bytes 3293184 | tf_op jit(solution)/shard_map/epi,eqi->pq/dot_general | solution.py:90
  14.9 1.7 %collective-permute-start.11 = (f32[56,128]{1,0:T(8,128)S(1)}, f32[56,128]{1,0:T(8,128)S(1)}, u32[]{:S(2)}, u32[]{:S(2)}) collective-permute-start(f32[56,128]{1,0:T(8,128)S(1)} %slice_select_fusion.1), channel_id=1, source_target_pairs={{0,32},{16,48},{32,0},{48,16},{64,96},{80,112},{96,64},{112,80},{1... | collective-permute-start | bytes 86024 | tf_op jit(solution)/shard_map/ppermute | solution.py:37
  16.6 2.7 %collective-permute-start.12 = (bf16[1,10,32,128]{3,2,1,0:T(8,128)(2,1)S(1)}, bf16[1,10,32,128]{3,2,1,0:T(8,128)(2,1)S(1)}, u32[]{:S(2)}, u32[]{:S(2)}) collective-permute-start(bf16[1,10,32,128]{3,2,1,0:T(8,128)(2,1)S(1)} %pad_maximum_fusion.5), channel_id=1, source_target_pairs={{16,0},{32,16},{48,32},{64,48},{80,64},{96,80},{112,96},{128,112},... | collective-permute-start | bytes 245768 | tf_op jit(solution)/shard_map/ppermute | solution.py:116
  19.3 2.9 %collective-permute-start.13 = (bf16[1,10,32,128]{3,2,1,0:T(8,128)(2,1)S(1)}, bf16[1,10,32,128]{3,2,1,0:T(8,128)(2,1)S(1)}, u32[]{:S(2)}, u32[]{:S(2)}) collective-permute-start(bf16[1,10,32,128]{3,2,1,0:T(8,128)(2,1)S(1)} %pad_maximum_fusion.6), channel_id=1, source_target_pairs={{0,16},{16,32},{32,48},{48,64},{64,80},{80,96},{96,112},{112,128},... | collective-permute-start | bytes 245768 | tf_op jit(solution)/shard_map/ppermute | solution.py:115
  29.5 3.4 %fusion.32 = f32[4,8,32,128,1]{3,2,4,1,0:T(8,128)S(1)} fusion(bf16[4,8,5,32,128]{4,3,2,1,0:T(8,128)(2,1)} %bitcast_dynamic-update-slice_fusion.3, bf16[4,8,5,128,128]{4,3,2,1,0:T(8,128)(2,1)S(1)} %copy-done.4), kind=kOutput, calls=%fused_computation.126 | convolution fusion | flops 167772160 | bytes 7077888 | tf_op jit(solution)/shard_map/rakij,rakvj->ravi/dot_general | solution.py:129
  33.7 2.9 %convolution_bitcast_fusion.5 = f32[192,32]{0,1:T(8,128)S(1)} fusion(f32[4,8,192,128]{3,2,1,0:T(8,128)S(1)} %copy-done, f32[4,8,32,128,1]{3,2,4,1,0:T(8,128)S(1)} %fusion.32), kind=kOutput, calls=%fused_computation.30 | convolution fusion | flops 301989888 | bytes 3694592 | tf_op jit(solution)/shard_map/epi,evi->pv/dot_general | solution.py:90
  36.9 3.1 %collective-permute-start.14 = (f32[112,128]{1,0:T(8,128)S(1)}, f32[112,128]{1,0:T(8,128)S(1)}, u32[]{:S(2)}, u32[]{:S(2)}) collective-permute-start(f32[112,128]{1,0:T(8,128)S(1)} %pad_maximum_fusion.8), channel_id=1, source_target_pairs={{0,64},{16,80},{32,96},{48,112},{64,0},{80,16},{96,32},{112,48},{1... | collective-permute-start | bytes 172040 | tf_op jit(solution)/shard_map/ppermute | solution.py:37
  40.0 1.6 %collective-permute-done.14 = f32[112,128]{1,0:T(8,128)S(1)} collective-permute-done((f32[112,128]{1,0:T(8,128)S(1)}, f32[112,128]{1,0:T(8,128)S(1)}, u32[]{:S(2)}, u32[]{:S(2)}) %collective-permute-start.14) | collective-permute-done | bytes 57376 | tf_op jit(solution)/shard_map/ppermute | solution.py:37
  41.5 6.3 %collective-permute-start.15 = (f32[112,128]{1,0:T(8,128)S(1)}, f32[112,128]{1,0:T(8,128)S(1)}, u32[]{:S(2)}, u32[]{:S(2)}) collective-permute-start(f32[112,128]{1,0:T(8,128)S(1)} %fusion.21), channel_id=1, source_target_pairs={{0,128},{16,144},{32,160},{48,176},{64,192},{80,208},{96,224},{112... | collective-permute-start | bytes 172040 | tf_op jit(solution)/shard_map/ppermute | solution.py:37
  47.8 1.7 %collective-permute-done.15 = f32[112,128]{1,0:T(8,128)S(1)} collective-permute-done((f32[112,128]{1,0:T(8,128)S(1)}, f32[112,128]{1,0:T(8,128)S(1)}, u32[]{:S(2)}, u32[]{:S(2)}) %collective-permute-start.15) | collective-permute-done | bytes 57376 | tf_op jit(solution)/shard_map/ppermute | solution.py:37
  49.6 3.3 %collective-permute-done.16 = f32[112,128]{1,0:T(8,128)S(1)} collective-permute-done((f32[112,128]{1,0:T(8,128)S(1)}, f32[112,128]{1,0:T(8,128)S(1)}, u32[]{:S(2)}, u32[]{:S(2)}) %collective-permute-start.16) | collective-permute-done | bytes 57376 | tf_op jit(solution)/shard_map/ppermute | solution.py:37
  52.9 1.7 %collective-permute-start.17 = (f32[112,128]{1,0:T(8,128)S(1)}, f32[112,128]{1,0:T(8,128)S(1)}, u32[]{:S(2)}, u32[]{:S(2)}) collective-permute-start(f32[112,128]{1,0:T(8,128)S(1)} %add.85), channel_id=1, source_target_pairs={{0,3},{1,2},{2,1},{3,0},{4,7},{5,6},{6,5},{7,4},{8,11},{9,10},{10,... | collective-permute-start | bytes 172040 | tf_op jit(solution)/shard_map/ppermute | solution.py:37
  54.7 2.6 %collective-permute-done.17 = f32[112,128]{1,0:T(8,128)S(1)} collective-permute-done((f32[112,128]{1,0:T(8,128)S(1)}, f32[112,128]{1,0:T(8,128)S(1)}, u32[]{:S(2)}, u32[]{:S(2)}) %collective-permute-start.17) | collective-permute-done | bytes 57376 | tf_op jit(solution)/shard_map/ppermute | solution.py:37
  57.5 2.8 %collective-permute-done.18 = f32[112,128]{1,0:T(8,128)S(1)} collective-permute-done((f32[112,128]{1,0:T(8,128)S(1)}, f32[112,128]{1,0:T(8,128)S(1)}, u32[]{:S(2)}, u32[]{:S(2)}) %collective-permute-start.18) | collective-permute-done | bytes 57376 | tf_op jit(solution)/shard_map/ppermute | solution.py:37
  60.4 2.8 %collective-permute-start.19 = (f32[112,128]{1,0:T(8,128)S(1)}, f32[112,128]{1,0:T(8,128)S(1)}, u32[]{:S(2)}, u32[]{:S(2)}) collective-permute-start(f32[112,128]{1,0:T(8,128)S(1)} %add.87), channel_id=1, source_target_pairs={{0,12},{1,13},{2,14},{3,15},{4,8},{5,9},{6,10},{7,11},{8,4},{9,5},... | collective-permute-start | bytes 172040 | tf_op jit(solution)/shard_map/ppermute | solution.py:37
  63.1 1.6 %collective-permute-done.19 = f32[112,128]{1,0:T(8,128)S(1)} collective-permute-done((f32[112,128]{1,0:T(8,128)S(1)}, f32[112,128]{1,0:T(8,128)S(1)}, u32[]{:S(2)}, u32[]{:S(2)}) %collective-permute-start.19) | collective-permute-done | bytes 57376 | tf_op jit(solution)/shard_map/ppermute | solution.py:37
  64.7 2.6 %collective-permute-start.20 = (f32[112,128]{1,0:T(8,128)S(1)}, f32[112,128]{1,0:T(8,128)S(1)}, u32[]{:S(2)}, u32[]{:S(2)}) collective-permute-start(f32[112,128]{1,0:T(8,128)S(1)} %add.88), channel_id=1, source_target_pairs={{0,32},{16,48},{32,0},{48,16},{64,96},{80,112},{96,64},{112,80},{1... | collective-permute-start | bytes 172040 | tf_op jit(solution)/shard_map/ppermute | solution.py:37
  67.3 1.6 %collective-permute-done.20 = f32[112,128]{1,0:T(8,128)S(1)} collective-permute-done((f32[112,128]{1,0:T(8,128)S(1)}, f32[112,128]{1,0:T(8,128)S(1)}, u32[]{:S(2)}, u32[]{:S(2)}) %collective-permute-start.20) | collective-permute-done | bytes 57376 | tf_op jit(solution)/shard_map/ppermute | solution.py:37
  69.0 9.2 %collective-permute-start.21 = (f32[168,128]{1,0:T(8,128)S(1)}, f32[168,128]{1,0:T(8,128)S(1)}, u32[]{:S(2)}, u32[]{:S(2)}) collective-permute-start(f32[168,128]{1,0:T(8,128)S(1)} %pad_maximum_fusion.4), channel_id=1, source_target_pairs={{0,16},{16,0},{32,48},{48,32},{64,80},{80,64},{96,112},{112,96},{1... | collective-permute-start | bytes 258056 | tf_op jit(solution)/shard_map/ppermute | solution.py:37
  86.4 11.2 %conditional.1 = (f32[32,32]{1,0:T(8,128)S(1)}, f32[4,8,32,128]{3,2,1,0:T(8,128)}) conditional(s32[]{:T(128)} %convert_element_type.8, (f32[192,32]{0,1:T(8,128)}, f32[32,192,128]{2,1,0:T(8,128)S(1)}, f32[32,32,128]{2,1,0:T(8,128)}, f32[32,32]{0,1:T(8,128)S(1)}) %tuple.79, (f32[32,32]{0,1:T(8,128)S(1)}, f32[32,32]{0,1:T(8,128)S(1)}, ...), branch_computations={%region_3.8_spmd, %region_6.9_spmd} | conditional | flops 403195936 | bytes 8176238 | solution.py:182
  86.5 2.9 %cholesky.55 = f32[32,32]{1,0:T(8,128)S(1)} custom-call(f32[32,32]{1,0:T(8,128)S(1)} %fusion.8), custom_call_target="Cholesky" | custom-call | tf_op jit(solution)/shard_map/cond/branch_1_fun/jit(cholesky)/cholesky | solution.py:162
  90.8 2.4 %custom-call.7 = f32[1,32,32]{1,2,0:T(8,128)S(1)} custom-call(f32[1,32,32]{2,1,0:T(8,128)S(1)} %get-tuple-element.63), custom_call_target="InvertDiagBlocksLowerTriangular" | custom-call | tf_op jit(solution)/shard_map/cond/branch_1_fun/triangular_solve/custom-call.0 | solution.py:163
  95.8 1.9 %convolution_subtract_fusion = f32[32,32,128]{2,0,1:T(8,128)} fusion(f32[32,32,128]{2,0,1:T(8,128)S(1)} %fusion.4, f32[32,192,1]{1,0,2:T(8,128)S(1)} %convolution_bitcast_fusion.3, f32[32,192,128]{2,1,0:T(8,128)S(1)} %get-tuple-element.29), kind=kOutput, calls=%fused_computation.15 | convolution fusion | flops 151126016 | bytes 4218880 | tf_op jit(solution)/shard_map/cond/branch_1_fun/epi,pw->ewi/dot_general | solution.py:171
  (88 shorter events, 23.8 us)
Async XLA Ops:
  1.4 13.4 %collective-permute-start.10 = (bf16[4,1,32,128]{3,2,1,0:T(8,128)(2,1)S(1)}, bf16[4,1,32,128]{3,2,1,0:T(8,128)(2,1)S(1)}, u32[]{:S(2)}, u32[]{:S(2)}) collective-permute-start(bf16[4,1,32,128]{3,2,1,0:T(8,128)(2,1)S(1)} %get-tuple-element.72), channel_id=1, source_target_pairs={{1,0},{2,1},{3,2},{4,3},{5,4},{6,5},{7,6},{8,7},{9,8},{10,9},{11,1... | collective-permute-start | bytes 98312 | tf_op jit(solution)/shard_map/ppermute | solution.py:108
  7.2 7.7 %collective-permute-start.9 = (bf16[4,1,32,128]{3,2,1,0:T(8,128)(2,1)S(1)}, bf16[4,1,32,128]{3,2,1,0:T(8,128)(2,1)S(1)}, u32[]{:S(2)}, u32[]{:S(2)}) collective-permute-start(bf16[4,1,32,128]{3,2,1,0:T(8,128)(2,1)S(1)} %get-tuple-element.73), channel_id=1, source_target_pairs={{0,1},{1,2},{2,3},{3,4},{4,5},{5,6},{6,7},{7,8},{8,9},{9,10},{10,1... | collective-permute-start | bytes 98312 | tf_op jit(solution)/shard_map/ppermute | solution.py:107
  7.2 6.7 %copy-start.2 = (bf16[4,8,32,128]{3,2,1,0:T(8,128)(2,1)S(1)}, bf16[4,8,32,128]{3,2,1,0:T(8,128)(2,1)}, u32[]{:S(2)}) copy-start(bf16[4,8,32,128]{3,2,1,0:T(8,128)(2,1)} %param.10) | copy-start | bytes 786436
  7.2 7.5 %copy-start.5 = (s32[4,8,5]{1,0,2:T(4,128)S(1)}, s32[4,8,5]{1,0,2:T(4,128)}, u32[]{:S(2)}) copy-start(s32[4,8,5]{1,0,2:T(4,128)} %param.12) | copy-start | bytes 1924
  12.9 1.9 %collective-permute-start.8 = (f32[112,128]{1,0:T(8,128)S(1)}, f32[112,128]{1,0:T(8,128)S(1)}, u32[]{:S(2)}, u32[]{:S(2)}) collective-permute-start(f32[112,128]{1,0:T(8,128)S(1)} %slice_select_fusion), channel_id=1, source_target_pairs={{0,16},{16,0},{32,48},{48,32},{64,80},{80,64},{96,112},{112,96},{1... | collective-permute-start | bytes 172040 | tf_op jit(solution)/shard_map/ppermute | solution.py:37
  14.9 7.4 %collective-permute-start.11 = (f32[56,128]{1,0:T(8,128)S(1)}, f32[56,128]{1,0:T(8,128)S(1)}, u32[]{:S(2)}, u32[]{:S(2)}) collective-permute-start(f32[56,128]{1,0:T(8,128)S(1)} %slice_select_fusion.1), channel_id=1, source_target_pairs={{0,32},{16,48},{32,0},{48,16},{64,96},{80,112},{96,64},{112,80},{1... | collective-permute-start | bytes 86024 | tf_op jit(solution)/shard_map/ppermute | solution.py:37
  16.6 5.8 %collective-permute-start.12 = (bf16[1,10,32,128]{3,2,1,0:T(8,128)(2,1)S(1)}, bf16[1,10,32,128]{3,2,1,0:T(8,128)(2,1)S(1)}, u32[]{:S(2)}, u32[]{:S(2)}) collective-permute-start(bf16[1,10,32,128]{3,2,1,0:T(8,128)(2,1)S(1)} %pad_maximum_fusion.5), channel_id=1, source_target_pairs={{16,0},{32,16},{48,32},{64,48},{80,64},{96,80},{112,96},{128,112},... | collective-permute-start | bytes 245768 | tf_op jit(solution)/shard_map/ppermute | solution.py:116
  19.3 4.4 %collective-permute-start.13 = (bf16[1,10,32,128]{3,2,1,0:T(8,128)(2,1)S(1)}, bf16[1,10,32,128]{3,2,1,0:T(8,128)(2,1)S(1)}, u32[]{:S(2)}, u32[]{:S(2)}) collective-permute-start(bf16[1,10,32,128]{3,2,1,0:T(8,128)(2,1)S(1)} %pad_maximum_fusion.6), channel_id=1, source_target_pairs={{0,16},{16,32},{32,48},{48,64},{64,80},{80,96},{96,112},{112,128},... | collective-permute-start | bytes 245768 | tf_op jit(solution)/shard_map/ppermute | solution.py:115
  25.2 4.2 %copy-start.4 = (bf16[4,8,5,128,128]{4,3,2,1,0:T(8,128)(2,1)S(1)}, bf16[4,8,5,128,128]{4,3,2,1,0:T(8,128)(2,1)}, u32[]{:S(2)}) copy-start(bf16[4,8,5,128,128]{4,3,2,1,0:T(8,128)(2,1)} %param.9) | copy-start | bytes 15728644
  29.5 4.2 %copy-start = (f32[4,8,192,128]{3,2,1,0:T(8,128)S(1)}, f32[4,8,192,128]{3,2,1,0:T(8,128)}, u32[]{:S(2)}) copy-start(f32[4,8,192,128]{3,2,1,0:T(8,128)} %param.11) | copy-start | bytes 9437188
  32.8 0.8 copy-start.1
  36.9 4.6 %collective-permute-start.14 = (f32[112,128]{1,0:T(8,128)S(1)}, f32[112,128]{1,0:T(8,128)S(1)}, u32[]{:S(2)}, u32[]{:S(2)}) collective-permute-start(f32[112,128]{1,0:T(8,128)S(1)} %pad_maximum_fusion.8), channel_id=1, source_target_pairs={{0,64},{16,80},{32,96},{48,112},{64,0},{80,16},{96,32},{112,48},{1... | collective-permute-start | bytes 172040 | tf_op jit(solution)/shard_map/ppermute | solution.py:37
  41.5 7.9 %collective-permute-start.15 = (f32[112,128]{1,0:T(8,128)S(1)}, f32[112,128]{1,0:T(8,128)S(1)}, u32[]{:S(2)}, u32[]{:S(2)}) collective-permute-start(f32[112,128]{1,0:T(8,128)S(1)} %fusion.21), channel_id=1, source_target_pairs={{0,128},{16,144},{32,160},{48,176},{64,192},{80,208},{96,224},{112... | collective-permute-start | bytes 172040 | tf_op jit(solution)/shard_map/ppermute | solution.py:37
  49.5 3.4 %collective-permute-start.16 = (f32[112,128]{1,0:T(8,128)S(1)}, f32[112,128]{1,0:T(8,128)S(1)}, u32[]{:S(2)}, u32[]{:S(2)}) collective-permute-start(f32[112,128]{1,0:T(8,128)S(1)} %add.84), channel_id=1, source_target_pairs={{0,1},{1,0},{2,3},{3,2},{4,5},{5,4},{6,7},{7,6},{8,9},{9,8},{10,11... | collective-permute-start | bytes 172040 | tf_op jit(solution)/shard_map/ppermute | solution.py:37
  52.9 4.3 %collective-permute-start.17 = (f32[112,128]{1,0:T(8,128)S(1)}, f32[112,128]{1,0:T(8,128)S(1)}, u32[]{:S(2)}, u32[]{:S(2)}) collective-permute-start(f32[112,128]{1,0:T(8,128)S(1)} %add.85), channel_id=1, source_target_pairs={{0,3},{1,2},{2,1},{3,0},{4,7},{5,6},{6,5},{7,4},{8,11},{9,10},{10,... | collective-permute-start | bytes 172040 | tf_op jit(solution)/shard_map/ppermute | solution.py:37
  57.2 3.1 %collective-permute-start.18 = (f32[112,128]{1,0:T(8,128)S(1)}, f32[112,128]{1,0:T(8,128)S(1)}, u32[]{:S(2)}, u32[]{:S(2)}) collective-permute-start(f32[112,128]{1,0:T(8,128)S(1)} %add.86), channel_id=1, source_target_pairs={{0,4},{1,5},{2,6},{3,7},{4,0},{5,1},{6,2},{7,3},{8,12},{9,13},{10,... | collective-permute-start | bytes 172040 | tf_op jit(solution)/shard_map/ppermute | solution.py:37
  60.4 4.3 %collective-permute-start.19 = (f32[112,128]{1,0:T(8,128)S(1)}, f32[112,128]{1,0:T(8,128)S(1)}, u32[]{:S(2)}, u32[]{:S(2)}) collective-permute-start(f32[112,128]{1,0:T(8,128)S(1)} %add.87), channel_id=1, source_target_pairs={{0,12},{1,13},{2,14},{3,15},{4,8},{5,9},{6,10},{7,11},{8,4},{9,5},... | collective-permute-start | bytes 172040 | tf_op jit(solution)/shard_map/ppermute | solution.py:37
  64.7 4.2 %collective-permute-start.20 = (f32[112,128]{1,0:T(8,128)S(1)}, f32[112,128]{1,0:T(8,128)S(1)}, u32[]{:S(2)}, u32[]{:S(2)}) collective-permute-start(f32[112,128]{1,0:T(8,128)S(1)} %add.88), channel_id=1, source_target_pairs={{0,32},{16,48},{32,0},{48,16},{64,96},{80,112},{96,64},{112,80},{1... | collective-permute-start | bytes 172040 | tf_op jit(solution)/shard_map/ppermute | solution.py:37
  69.0 10.1 %collective-permute-start.21 = (f32[168,128]{1,0:T(8,128)S(1)}, f32[168,128]{1,0:T(8,128)S(1)}, u32[]{:S(2)}, u32[]{:S(2)}) collective-permute-start(f32[168,128]{1,0:T(8,128)S(1)} %pad_maximum_fusion.4), channel_id=1, source_target_pairs={{0,16},{16,0},{32,48},{48,32},{64,80},{80,64},{96,112},{112,96},{1... | collective-permute-start | bytes 258056 | tf_op jit(solution)/shard_map/ppermute | solution.py:37

commit v15 on v12

--- a/solution.py
+++ b/solution.py
@@ -94,7 +94,9 @@
     radial = [step for axis, step in steps if axis == "rad"]
     around = [("azi", step) for axis, step in steps if axis == "azi"]
 
-    kept_gram = halve(pack_symmetric(mm("epi,eqi->pq", kept_flat, kept_flat)), "rad", radial[0])
+    kept_gram = halve(pack_symmetric(jnp.einsum(
+        "epi,eqi->pq", kept_flat, kept_flat, precision=lax.Precision.HIGH,
+        preferred_element_type=jnp.float32)), "rad", radial[0])
 
     n_a, n_r = lax.axis_size("azi"), lax.axis_size("rad")
     west = lax.ppermute(new_block[:, rows_a - 1 :], "azi", [(i, (i + 1) % n_a) for i in range(n_a)])
@@ -111,15 +113,15 @@
         [north, jnp.concatenate([west, new_block, east], axis=1), south], axis=0
     )
     shifted = [padded[c // 3 : c // 3 + rows_r, c % 3 : c % 3 + rows_a] for c in range(9)]
-    slots = [new_block]
+    image = jnp.einsum("raij,ravj->ravi", jacobian[:, :, 0], new_block, preferred_element_type=jnp.float32)
     for k in range(1, 5):
         code = columns[:, :, k][:, :, None, None]
         pick = shifted[0]
         for c in range(1, 9):
             pick = jnp.where(code == c, shifted[c], pick)
-        slots.append(pick)
-    picked = jnp.stack(slots, axis=2)
-    image = jnp.einsum("rakij,rakvj->ravi", jacobian, picked, preferred_element_type=jnp.float32)
+        image = image + jnp.einsum(
+            "raij,ravj->ravi", jacobian[:, :, k], pick, preferred_element_type=jnp.float32
+        )
     image = image.reshape(elements, NEW, BLK)
 
     moments = jnp.concatenate(

time: 99.5 us -> 99.3 us (level)
  waiting for transfers between devices: 19.9 us -> 26.4 us
  other arithmetic: 13.4 us -> 7.72 us
  starting transfers between devices: 38.2 us -> 36.1 us
  matrix products: 20.9 us -> 22.6 us
    dot_general x1 -> x6, matrix products: 3.36 us -> 10.5 us  [the longest x1 4.36 us: on_device(): jnp.einsum('epi,eqi->pq', kept_flat, kept_flat, precision=lax.Precision.H...]
    dot_general x8 -> x7, matrix products: 14.1 us -> 8.48 us  [mm(): jnp.einsum(spec, a, b, precision=lax.Precision.HIGHEST, preferred_element...]
    unnamed x3 -> x0, other arithmetic: 4.33 us -> none
    ppermute x1, waiting for transfers between devices: 0.01 us -> 4.05 us  [on_device(): lax.ppermute(new_block[:, rows_a - 1:], 'azi', [(i, (i + 1) % n_a) for i...]
    ppermute x6, waiting for transfers between devices: 16 us -> 18.5 us  [all_sum(): x = x + lax.ppermute(x, axis, [(i, i ^ step) for i in range(count)])]
    ppermute x1, starting transfers between devices: 5.76 us -> 3.27 us  [on_device(): lax.ppermute(new_block[:, :1], 'azi', [((i + 1) % n_a, i) for i in range(...]
    ppermute x4, starting transfers between devices: 14.6 us -> 16.9 us  [exchange(): return lax.ppermute(x, axis, [(i, i ^ step) for i in range(count)])]
    ppermute x6, starting transfers between devices: 12.3 us -> 10.3 us  [all_sum(): x = x + lax.ppermute(x, axis, [(i, i ^ step) for i in range(count)])]
  transfers between devices with their start and end apart: 14 -> 14, of which waited for: 10 -> 11; matrix products, arithmetic and copies ran while one was open for 7% -> 2% of each run, Pallas kernels for 0% -> 0%
where the time goes in v15:
time: 99.3 us; the launch traced here: 98.7 us
  starting transfers between devices  36.1 us (36%)
  waiting for transfers between devices  26.4 us (27%)
  matrix products  22.6 us (23%)
  other arithmetic  7.72 us (8%)
  local copies, waits for them, and re-layouts  4.15 us (4%)
  between operations  1.69 us (2%)
    ppermute x6, waiting for transfers between devices, all_sum(): x = x + lax.ppermute(x, axis, [(i, i ^ step) for i in range(count)])  18.5 us
    ppermute x4, starting transfers between devices, exchange(): return lax.ppermute(x, axis, [(i, i ^ step) for i in range(count)])  16.9 us
    ppermute x6, starting transfers between devices, all_sum(): x = x + lax.ppermute(x, axis, [(i, i ^ step) for i in range(count)])  10.3 us
    dot_general x7, matrix products, mm(): jnp.einsum(spec, a, b, precision=lax.Precision.HIGHEST, preferred_element...  8.48 us
    dot_general x1, matrix products, on_device(): jnp.einsum('epi,eqi->pq', kept_flat, kept_flat, precision=lax.Precision.H...  4.36 us
    dot_general x4, matrix products, on_device(): jnp.einsum('raij,ravj->ravi', jacobian[:, :, k], pick, preferred_element_...  4.31 us
    ppermute x1, waiting for transfers between devices, on_device(): lax.ppermute(new_block[:, rows_a - 1:], 'azi', [(i, (i + 1) % n_a) for i...  4.05 us
    ppermute x1, starting transfers between devices, on_device(): south = lax.ppermute(row(0), 'rad', [(i + 1, i) for i in range(n_r - 1)])  3.64 us
  transfers between devices with their start and end apart: 14, of which 11 were waited for; matrix products, arithmetic and copies ran while one was open for 2% of the time, Pallas kernels for 0%

profile of v15, /device:TPU:1, one launch (start us, length us, event | category | flops | bytes accessed | tf_op | source)
XLA Modules:
  0.0 98.7 jit_solution(2209416230696625233)
XLA Ops:
  0.7 4.4 %convolution_bitcast_fusion.4 = f32[192,192]{1,0:T(8,128)S(1)} fusion(f32[4,8,192,128]{3,2,1,0:T(8,128)} %param.11), kind=kOutput, calls=%fused_computation.33 | convolution fusion | flops 905969664 | bytes 3293184 | tf_op jit(solution)/shard_map/epi,eqi->pq/dot_general | solution.py:97
  5.2 3.3 %collective-permute-start.8 = (f32[112,128]{1,0:T(8,128)S(1)}, f32[112,128]{1,0:T(8,128)S(1)}, u32[]{:S(2)}, u32[]{:S(2)}) collective-permute-start(f32[112,128]{1,0:T(8,128)S(1)} %slice_select_fusion), channel_id=1, source_target_pairs={{0,16},{16,0},{32,48},{48,32},{64,80},{80,64},{96,112},{112,96},{1... | collective-permute-start | bytes 172040 | tf_op jit(solution)/shard_map/ppermute | solution.py:30
  8.5 3.3 %collective-permute-start.10 = (bf16[4,1,32,128]{3,2,1,0:T(8,128)(2,1)S(1)}, bf16[4,1,32,128]{3,2,1,0:T(8,128)(2,1)S(1)}, u32[]{:S(2)}, u32[]{:S(2)}) collective-permute-start(bf16[4,1,32,128]{3,2,1,0:T(8,128)(2,1)S(1)} %get-tuple-element.73), channel_id=1, source_target_pairs={{1,0},{2,1},{3,2},{4,3},{5,4},{6,5},{7,6},{8,7},{9,8},{10,9},{11,1... | collective-permute-start | bytes 98312 | tf_op jit(solution)/shard_map/ppermute | solution.py:103
  11.8 1.9 %fusion.15 = f32[4,8,32,128]{3,2,1,0:T(8,128)S(1)} fusion(bf16[4,8,32,128]{3,2,1,0:T(8,128)(2,1)S(1)} %copy-done.3, bf16[4,8,5,128,128]{4,3,2,1,0:T(8,128)(2,1)} %param.9), kind=kOutput, calls=%fused_computation.44 | convolution fusion | flops 33554432 | bytes 1835008 | tf_op jit(solution)/shard_map/raij,ravj->ravi/dot_general | solution.py:116
  13.8 4.0 %collective-permute-done.9 = bf16[4,1,32,128]{3,2,1,0:T(8,128)(2,1)S(1)} collective-permute-done((bf16[4,1,32,128]{3,2,1,0:T(8,128)(2,1)S(1)}, bf16[4,1,32,128]{3,2,1,0:T(8,128)(2,1)S(1)}, u32[]{:S(2)}, u32[]{:S(2)}) %collective-permute-start.9) | collective-permute-done | bytes 32800 | tf_op jit(solution)/shard_map/ppermute | solution.py:102
  17.9 1.6 %collective-permute-start.11 = (f32[56,128]{1,0:T(8,128)S(1)}, f32[56,128]{1,0:T(8,128)S(1)}, u32[]{:S(2)}, u32[]{:S(2)}) collective-permute-start(f32[56,128]{1,0:T(8,128)S(1)} %slice_select_fusion.1), channel_id=1, source_target_pairs={{0,32},{16,48},{32,0},{48,16},{64,96},{80,112},{96,64},{112,80},{1... | collective-permute-start | bytes 86024 | tf_op jit(solution)/shard_map/ppermute | solution.py:30
  19.5 3.6 %collective-permute-start.12 = (bf16[1,10,32,128]{3,2,1,0:T(8,128)(2,1)S(1)}, bf16[1,10,32,128]{3,2,1,0:T(8,128)(2,1)S(1)}, u32[]{:S(2)}, u32[]{:S(2)}) collective-permute-start(bf16[1,10,32,128]{3,2,1,0:T(8,128)(2,1)S(1)} %pad_maximum_fusion.5), channel_id=1, source_target_pairs={{16,0},{32,16},{48,32},{64,48},{80,64},{96,80},{112,96},{128,112},... | collective-permute-start | bytes 245768 | tf_op jit(solution)/shard_map/ppermute | solution.py:111
  23.2 1.9 %collective-permute-start.13 = (bf16[1,10,32,128]{3,2,1,0:T(8,128)(2,1)S(1)}, bf16[1,10,32,128]{3,2,1,0:T(8,128)(2,1)S(1)}, u32[]{:S(2)}, u32[]{:S(2)}) collective-permute-start(bf16[1,10,32,128]{3,2,1,0:T(8,128)(2,1)S(1)} %pad_maximum_fusion.6), channel_id=1, source_target_pairs={{0,16},{16,32},{32,48},{48,64},{64,80},{80,96},{96,112},{112,128},... | collective-permute-start | bytes 245768 | tf_op jit(solution)/shard_map/ppermute | solution.py:110
  26.7 2.1 %convolution_add_fusion.3 = f32[4,8,32,128]{3,2,1,0:T(8,128)S(1)} fusion(f32[4,8,32,128]{3,2,1,0:T(8,128)S(1)} %fusion.15, bf16[4,8,5,128,128]{4,3,2,1,0:T(8,128)(2,1)} %param.9, bf16[4,8,32,128]{3,2,1,0:T(8,128)(2,1)S(1)} %get-tuple-element.69, bf16[4,8,32,128]{3,2,1,0:T(8,128)(2,1)S(1)} %get-tuple-element.70, bf16[4,8,32,128]{3,2,1,0:T(8,128)(2,1)S(1)} %copy-done.3, ...), kind=kOutput, calls=%fused_computation.32 | convolution fusion | flops 35258368 | bytes 3965184 | tf_op jit(solution)/shard_map/raij,ravj->ravi/dot_general | solution.py:122
  32.2 2.9 %convolution_bitcast_fusion.5 = f32[192,32]{0,1:T(8,128)S(1)} fusion(f32[4,8,32,128]{3,2,1,0:T(8,128)S(1)} %convolution_add_fusion, f32[4,8,192,128]{3,2,1,0:T(8,128)S(1)} %copy-done), kind=kOutput, calls=%fused_computation.34 | convolution fusion | flops 301989888 | bytes 3694592 | tf_op jit(solution)/shard_map/epi,evi->pv/dot_general | solution.py:83
  36.0 3.1 %collective-permute-start.14 = (f32[112,128]{1,0:T(8,128)S(1)}, f32[112,128]{1,0:T(8,128)S(1)}, u32[]{:S(2)}, u32[]{:S(2)}) collective-permute-start(f32[112,128]{1,0:T(8,128)S(1)} %pad_maximum_fusion.8), channel_id=1, source_target_pairs={{0,64},{16,80},{32,96},{48,112},{64,0},{80,16},{96,32},{112,48},{1... | collective-permute-start | bytes 172040 | tf_op jit(solution)/shard_map/ppermute | solution.py:24
  40.6 6.7 %collective-permute-start.15 = (f32[112,128]{1,0:T(8,128)S(1)}, f32[112,128]{1,0:T(8,128)S(1)}, u32[]{:S(2)}, u32[]{:S(2)}) collective-permute-start(f32[112,128]{1,0:T(8,128)S(1)} %fusion.94), channel_id=1, source_target_pairs={{0,128},{16,144},{32,160},{48,176},{64,192},{80,208},{96,224},{112... | collective-permute-start | bytes 172040 | tf_op jit(solution)/shard_map/ppermute | solution.py:24
  47.3 1.6 %collective-permute-done.15 = f32[112,128]{1,0:T(8,128)S(1)} collective-permute-done((f32[112,128]{1,0:T(8,128)S(1)}, f32[112,128]{1,0:T(8,128)S(1)}, u32[]{:S(2)}, u32[]{:S(2)}) %collective-permute-start.15) | collective-permute-done | bytes 57376 | tf_op jit(solution)/shard_map/ppermute | solution.py:24
  49.0 3.3 %collective-permute-done.16 = f32[112,128]{1,0:T(8,128)S(1)} collective-permute-done((f32[112,128]{1,0:T(8,128)S(1)}, f32[112,128]{1,0:T(8,128)S(1)}, u32[]{:S(2)}, u32[]{:S(2)}) %collective-permute-start.16) | collective-permute-done | bytes 57376 | tf_op jit(solution)/shard_map/ppermute | solution.py:24
  52.6 4.5 %collective-permute-done.17 = f32[112,128]{1,0:T(8,128)S(1)} collective-permute-done((f32[112,128]{1,0:T(8,128)S(1)}, f32[112,128]{1,0:T(8,128)S(1)}, u32[]{:S(2)}, u32[]{:S(2)}) %collective-permute-start.17) | collective-permute-done | bytes 57376 | tf_op jit(solution)/shard_map/ppermute | solution.py:24
  57.2 3.0 %collective-permute-done.18 = f32[112,128]{1,0:T(8,128)S(1)} collective-permute-done((f32[112,128]{1,0:T(8,128)S(1)}, f32[112,128]{1,0:T(8,128)S(1)}, u32[]{:S(2)}, u32[]{:S(2)}) %collective-permute-start.18) | collective-permute-done | bytes 57376 | tf_op jit(solution)/shard_map/ppermute | solution.py:24
  60.4 4.5 %collective-permute-done.19 = f32[112,128]{1,0:T(8,128)S(1)} collective-permute-done((f32[112,128]{1,0:T(8,128)S(1)}, f32[112,128]{1,0:T(8,128)S(1)}, u32[]{:S(2)}, u32[]{:S(2)}) %collective-permute-start.19) | collective-permute-done | bytes 57376 | tf_op jit(solution)/shard_map/ppermute | solution.py:24
  64.9 2.3 %collective-permute-start.20 = (f32[112,128]{1,0:T(8,128)S(1)}, f32[112,128]{1,0:T(8,128)S(1)}, u32[]{:S(2)}, u32[]{:S(2)}) collective-permute-start(f32[112,128]{1,0:T(8,128)S(1)} %add.104), channel_id=1, source_target_pairs={{0,32},{16,48},{32,0},{48,16},{64,96},{80,112},{96,64},{112,80},{1... | collective-permute-start | bytes 172040 | tf_op jit(solution)/shard_map/ppermute | solution.py:30
  67.2 1.6 %collective-permute-done.20 = f32[112,128]{1,0:T(8,128)S(1)} collective-permute-done((f32[112,128]{1,0:T(8,128)S(1)}, f32[112,128]{1,0:T(8,128)S(1)}, u32[]{:S(2)}, u32[]{:S(2)}) %collective-permute-start.20) | collective-permute-done | bytes 57376 | tf_op jit(solution)/shard_map/ppermute | solution.py:30
  68.8 9.6 %collective-permute-start.21 = (f32[168,128]{1,0:T(8,128)S(1)}, f32[168,128]{1,0:T(8,128)S(1)}, u32[]{:S(2)}, u32[]{:S(2)}) collective-permute-start(f32[168,128]{1,0:T(8,128)S(1)} %pad_maximum_fusion.4), channel_id=1, source_target_pairs={{0,16},{16,0},{32,48},{48,32},{64,80},{80,64},{96,112},{112,96},{1... | collective-permute-start | bytes 258056 | tf_op jit(solution)/shard_map/ppermute | solution.py:30
  86.7 11.2 %conditional.1 = (f32[32,32]{1,0:T(8,128)S(1)}, f32[4,8,32,128]{3,2,1,0:T(8,128)}) conditional(s32[]{:T(128)} %convert_element_type.8, (f32[192,32]{0,1:T(8,128)}, f32[32,192,128]{2,1,0:T(8,128)S(1)}, f32[32,32,128]{2,1,0:T(8,128)}, f32[32,32]{0,1:T(8,128)S(1)}) %tuple.79, (f32[32,32]{0,1:T(8,128)S(1)}, f32[32,32]{0,1:T(8,128)S(1)}, ...), branch_computations={%region_3.8_spmd, %region_6.9_spmd} | conditional | flops 403195936 | bytes 8176238 | solution.py:177
  86.8 2.9 %cholesky.55 = f32[32,32]{1,0:T(8,128)S(1)} custom-call(f32[32,32]{1,0:T(8,128)S(1)} %fusion.8), custom_call_target="Cholesky" | custom-call | tf_op jit(solution)/shard_map/cond/branch_1_fun/jit(cholesky)/cholesky | solution.py:157
  91.1 2.4 %custom-call.7 = f32[1,32,32]{1,2,0:T(8,128)S(1)} custom-call(f32[1,32,32]{2,1,0:T(8,128)S(1)} %get-tuple-element.63), custom_call_target="InvertDiagBlocksLowerTriangular" | custom-call | tf_op jit(solution)/shard_map/cond/branch_1_fun/triangular_solve/custom-call.0 | solution.py:158
  96.1 1.9 %convolution_subtract_fusion = f32[32,32,128]{2,0,1:T(8,128)} fusion(f32[32,32,128]{2,0,1:T(8,128)S(1)} %fusion.4, f32[32,192,1]{1,0,2:T(8,128)S(1)} %convolution_bitcast_fusion.3, f32[32,192,128]{2,1,0:T(8,128)S(1)} %get-tuple-element.29), kind=kOutput, calls=%fused_computation.15 | convolution fusion | flops 151126016 | bytes 4218880 | tf_op jit(solution)/shard_map/cond/branch_1_fun/epi,pw->ewi/dot_general | solution.py:166
  (90 shorter events, 20.3 us)
Async XLA Ops:
  0.6 7.8 %copy-start.3 = (bf16[4,8,32,128]{3,2,1,0:T(8,128)(2,1)S(1)}, bf16[4,8,32,128]{3,2,1,0:T(8,128)(2,1)}, u32[]{:S(2)}) copy-start(bf16[4,8,32,128]{3,2,1,0:T(8,128)(2,1)} %param.10) | copy-start | bytes 786436
  0.6 11.1 %copy-start.6 = (s32[4,8,5]{1,0,2:T(4,128)S(1)}, s32[4,8,5]{1,0,2:T(4,128)}, u32[]{:S(2)}) copy-start(s32[4,8,5]{1,0,2:T(4,128)} %param.12) | copy-start | bytes 1924
  5.2 8.6 %collective-permute-start.8 = (f32[112,128]{1,0:T(8,128)S(1)}, f32[112,128]{1,0:T(8,128)S(1)}, u32[]{:S(2)}, u32[]{:S(2)}) collective-permute-start(f32[112,128]{1,0:T(8,128)S(1)} %slice_select_fusion), channel_id=1, source_target_pairs={{0,16},{16,0},{32,48},{48,32},{64,80},{80,64},{96,112},{112,96},{1... | collective-permute-start | bytes 172040 | tf_op jit(solution)/shard_map/ppermute | solution.py:30
  8.5 5.3 %collective-permute-start.10 = (bf16[4,1,32,128]{3,2,1,0:T(8,128)(2,1)S(1)}, bf16[4,1,32,128]{3,2,1,0:T(8,128)(2,1)S(1)}, u32[]{:S(2)}, u32[]{:S(2)}) collective-permute-start(bf16[4,1,32,128]{3,2,1,0:T(8,128)(2,1)S(1)} %get-tuple-element.73), channel_id=1, source_target_pairs={{1,0},{2,1},{3,2},{4,3},{5,4},{6,5},{7,6},{8,7},{9,8},{10,9},{11,1... | collective-permute-start | bytes 98312 | tf_op jit(solution)/shard_map/ppermute | solution.py:103
  11.8 6.1 %collective-permute-start.9 = (bf16[4,1,32,128]{3,2,1,0:T(8,128)(2,1)S(1)}, bf16[4,1,32,128]{3,2,1,0:T(8,128)(2,1)S(1)}, u32[]{:S(2)}, u32[]{:S(2)}) collective-permute-start(bf16[4,1,32,128]{3,2,1,0:T(8,128)(2,1)S(1)} %get-tuple-element.74), channel_id=1, source_target_pairs={{0,1},{1,2},{2,3},{3,4},{4,5},{5,6},{6,7},{7,8},{8,9},{9,10},{10,1... | collective-permute-start | bytes 98312 | tf_op jit(solution)/shard_map/ppermute | solution.py:102
  17.9 7.3 %collective-permute-start.11 = (f32[56,128]{1,0:T(8,128)S(1)}, f32[56,128]{1,0:T(8,128)S(1)}, u32[]{:S(2)}, u32[]{:S(2)}) collective-permute-start(f32[56,128]{1,0:T(8,128)S(1)} %slice_select_fusion.1), channel_id=1, source_target_pairs={{0,32},{16,48},{32,0},{48,16},{64,96},{80,112},{96,64},{112,80},{1... | collective-permute-start | bytes 86024 | tf_op jit(solution)/shard_map/ppermute | solution.py:30
  19.5 5.8 %collective-permute-start.12 = (bf16[1,10,32,128]{3,2,1,0:T(8,128)(2,1)S(1)}, bf16[1,10,32,128]{3,2,1,0:T(8,128)(2,1)S(1)}, u32[]{:S(2)}, u32[]{:S(2)}) collective-permute-start(bf16[1,10,32,128]{3,2,1,0:T(8,128)(2,1)S(1)} %pad_maximum_fusion.5), channel_id=1, source_target_pairs={{16,0},{32,16},{48,32},{64,48},{80,64},{96,80},{112,96},{128,112},... | collective-permute-start | bytes 245768 | tf_op jit(solution)/shard_map/ppermute | solution.py:111
  23.2 3.4 %collective-permute-start.13 = (bf16[1,10,32,128]{3,2,1,0:T(8,128)(2,1)S(1)}, bf16[1,10,32,128]{3,2,1,0:T(8,128)(2,1)S(1)}, u32[]{:S(2)}, u32[]{:S(2)}) collective-permute-start(bf16[1,10,32,128]{3,2,1,0:T(8,128)(2,1)S(1)} %pad_maximum_fusion.6), channel_id=1, source_target_pairs={{0,16},{16,32},{32,48},{48,64},{64,80},{80,96},{96,112},{112,128},... | collective-permute-start | bytes 245768 | tf_op jit(solution)/shard_map/ppermute | solution.py:110
  25.2 3.6 %copy-start.4 = (bf16[4,8,5,128,128]{4,3,2,1,0:T(8,128)(2,1)S(1)}, bf16[4,8,5,128,128]{4,3,2,1,0:T(8,128)(2,1)}, u32[]{:S(2)}) copy-start(bf16[4,8,5,128,128]{4,3,2,1,0:T(8,128)(2,1)} %param.9) | copy-start | bytes 15728644
  30.3 1.9 %copy-start = (f32[4,8,192,128]{3,2,1,0:T(8,128)S(1)}, f32[4,8,192,128]{3,2,1,0:T(8,128)}, u32[]{:S(2)}) copy-start(f32[4,8,192,128]{3,2,1,0:T(8,128)} %param.11) | copy-start | bytes 9437188
  32.2 2.9 %copy-start.1 = (f32[4,8,32,128]{3,2,1,0:T(8,128)}, f32[4,8,32,128]{3,2,1,0:T(8,128)S(1)}, u32[]{:S(2)}) copy-start(f32[4,8,32,128]{3,2,1,0:T(8,128)S(1)} %convolution_add_fusion) | copy-start | bytes 1572868
  36.0 4.6 %collective-permute-start.14 = (f32[112,128]{1,0:T(8,128)S(1)}, f32[112,128]{1,0:T(8,128)S(1)}, u32[]{:S(2)}, u32[]{:S(2)}) collective-permute-start(f32[112,128]{1,0:T(8,128)S(1)} %pad_maximum_fusion.8), channel_id=1, source_target_pairs={{0,64},{16,80},{32,96},{48,112},{64,0},{80,16},{96,32},{112,48},{1... | collective-permute-start | bytes 172040 | tf_op jit(solution)/shard_map/ppermute | solution.py:24
  40.6 8.3 %collective-permute-start.15 = (f32[112,128]{1,0:T(8,128)S(1)}, f32[112,128]{1,0:T(8,128)S(1)}, u32[]{:S(2)}, u32[]{:S(2)}) collective-permute-start(f32[112,128]{1,0:T(8,128)S(1)} %fusion.94), channel_id=1, source_target_pairs={{0,128},{16,144},{32,160},{48,176},{64,192},{80,208},{96,224},{112... | collective-permute-start | bytes 172040 | tf_op jit(solution)/shard_map/ppermute | solution.py:24
  48.9 3.4 %collective-permute-start.16 = (f32[112,128]{1,0:T(8,128)S(1)}, f32[112,128]{1,0:T(8,128)S(1)}, u32[]{:S(2)}, u32[]{:S(2)}) collective-permute-start(f32[112,128]{1,0:T(8,128)S(1)} %add.100), channel_id=1, source_target_pairs={{0,1},{1,0},{2,3},{3,2},{4,5},{5,4},{6,7},{7,6},{8,9},{9,8},{10,11... | collective-permute-start | bytes 172040 | tf_op jit(solution)/shard_map/ppermute | solution.py:24
  52.3 4.8 %collective-permute-start.17 = (f32[112,128]{1,0:T(8,128)S(1)}, f32[112,128]{1,0:T(8,128)S(1)}, u32[]{:S(2)}, u32[]{:S(2)}) collective-permute-start(f32[112,128]{1,0:T(8,128)S(1)} %add.101), channel_id=1, source_target_pairs={{0,2},{1,3},{2,0},{3,1},{4,6},{5,7},{6,4},{7,5},{8,10},{9,11},{10,... | collective-permute-start | bytes 172040 | tf_op jit(solution)/shard_map/ppermute | solution.py:24
  57.1 3.1 %collective-permute-start.18 = (f32[112,128]{1,0:T(8,128)S(1)}, f32[112,128]{1,0:T(8,128)S(1)}, u32[]{:S(2)}, u32[]{:S(2)}) collective-permute-start(f32[112,128]{1,0:T(8,128)S(1)} %add.102), channel_id=1, source_target_pairs={{0,4},{1,5},{2,6},{3,7},{4,0},{5,1},{6,2},{7,3},{8,12},{9,13},{10,... | collective-permute-start | bytes 172040 | tf_op jit(solution)/shard_map/ppermute | solution.py:24
  60.3 4.6 %collective-permute-start.19 = (f32[112,128]{1,0:T(8,128)S(1)}, f32[112,128]{1,0:T(8,128)S(1)}, u32[]{:S(2)}, u32[]{:S(2)}) collective-permute-start(f32[112,128]{1,0:T(8,128)S(1)} %add.103), channel_id=1, source_target_pairs={{0,8},{1,9},{2,10},{3,11},{4,12},{5,13},{6,14},{7,15},{8,0},{9,1},... | collective-permute-start | bytes 172040 | tf_op jit(solution)/shard_map/ppermute | solution.py:24
  64.9 3.9 %collective-permute-start.20 = (f32[112,128]{1,0:T(8,128)S(1)}, f32[112,128]{1,0:T(8,128)S(1)}, u32[]{:S(2)}, u32[]{:S(2)}) collective-permute-start(f32[112,128]{1,0:T(8,128)S(1)} %add.104), channel_id=1, source_target_pairs={{0,32},{16,48},{32,0},{48,16},{64,96},{80,112},{96,64},{112,80},{1... | collective-permute-start | bytes 172040 | tf_op jit(solution)/shard_map/ppermute | solution.py:30
  68.8 10.6 %collective-permute-start.21 = (f32[168,128]{1,0:T(8,128)S(1)}, f32[168,128]{1,0:T(8,128)S(1)}, u32[]{:S(2)}, u32[]{:S(2)}) collective-permute-start(f32[168,128]{1,0:T(8,128)S(1)} %pad_maximum_fusion.4), channel_id=1, source_target_pairs={{0,16},{16,0},{32,48},{48,32},{64,80},{80,64},{96,112},{112,96},{1... | collective-permute-start | bytes 258056 | tf_op jit(solution)/shard_map/ppermute | solution.py:30
  79.6 0.6 copy-start.5

commit v16 on v12

--- a/solution.py
+++ b/solution.py
@@ -152,7 +152,7 @@
     kept_share = jnp.sum(expanded * eye, axis=1) * 16.0 >= jnp.sum(image_gram * eye, axis=1) / total_rows
 
     def factor_of(gram):
-        lower = jnp.linalg.cholesky(gram)
+        lower = jnp.linalg.cholesky(gram, symmetrize_input=False)
         inverse = lax.linalg.triangular_solve(lower, eye, left_side=True, lower=True)
         return lower, inverse
 

time: 99.5 us -> 99.5 us (level)
  no operation moved by 1% of the time
where the time goes in v16:
time: 99.5 us; the launch traced here: 98.9 us
  starting transfers between devices  38.2 us (38%)
  matrix products  20.9 us (21%)
  waiting for transfers between devices  19.9 us (20%)
  other arithmetic  13.4 us (13%)
  local copies, waits for them, and re-layouts  4.77 us (5%)
  between operations  1.65 us (2%)
    ppermute x6, waiting for transfers between devices, all_sum(): x = x + lax.ppermute(x, axis, [(i, i ^ step) for i in range(count)])  16 us
    ppermute x4, starting transfers between devices, exchange(): return lax.ppermute(x, axis, [(i, i ^ step) for i in range(count)])  14.6 us
    dot_general x8, matrix products, mm(): jnp.einsum(spec, a, b, precision=lax.Precision.HIGHEST, preferred_element...  14.1 us
    ppermute x6, starting transfers between devices, all_sum(): x = x + lax.ppermute(x, axis, [(i, i ^ step) for i in range(count)])  12.3 us
    ppermute x1, starting transfers between devices, on_device(): lax.ppermute(new_block[:, :1], 'azi', [((i + 1) % n_a, i) for i in range(...  5.76 us
    unnamed x3, other arithmetic  4.33 us
    another operation x3, other arithmetic, factor_of(): lower = jnp.linalg.cholesky(gram, symmetrize_input=False)  3.6 us
    dot_general x1, matrix products, on_device(): jnp.einsum('rakij,rakvj->ravi', jacobian, picked, preferred_element_type=...  3.36 us
  transfers between devices with their start and end apart: 14, of which 10 were waited for; matrix products, arithmetic and copies ran while one was open for 7% of the time, Pallas kernels for 0%

profile of v16, /device:TPU:1, one launch (start us, length us, event | category | flops | bytes accessed | tf_op | source)
XLA Modules:
  0.0 98.9 jit_solution(1591815959056012252)
XLA Ops:
  1.4 5.8 %collective-permute-start.10 = (bf16[4,1,32,128]{3,2,1,0:T(8,128)(2,1)S(1)}, bf16[4,1,32,128]{3,2,1,0:T(8,128)(2,1)S(1)}, u32[]{:S(2)}, u32[]{:S(2)}) collective-permute-start(bf16[4,1,32,128]{3,2,1,0:T(8,128)(2,1)S(1)} %get-tuple-element.72), channel_id=1, source_target_pairs={{1,0},{2,1},{3,2},{4,3},{5,4},{6,5},{7,6},{8,7},{9,8},{10,9},{11,1... | collective-permute-start | bytes 98312 | tf_op jit(solution)/shard_map/ppermute | solution.py:101
  7.2 5.5 %convolution_bitcast_fusion.4 = f32[192,192]{1,0:T(8,128)S(1)} fusion(f32[4,8,192,128]{3,2,1,0:T(8,128)} %param.11), kind=kOutput, calls=%fused_computation.25 | convolution fusion | flops 1811939328 | bytes 3293184 | tf_op jit(solution)/shard_map/epi,eqi->pq/dot_general | solution.py:83
  14.9 1.7 %collective-permute-start.11 = (f32[56,128]{1,0:T(8,128)S(1)}, f32[56,128]{1,0:T(8,128)S(1)}, u32[]{:S(2)}, u32[]{:S(2)}) collective-permute-start(f32[56,128]{1,0:T(8,128)S(1)} %slice_select_fusion.1), channel_id=1, source_target_pairs={{0,32},{16,48},{32,0},{48,16},{64,96},{80,112},{96,64},{112,80},{1... | collective-permute-start | bytes 86024 | tf_op jit(solution)/shard_map/ppermute | solution.py:30
  16.6 2.7 %collective-permute-start.12 = (bf16[1,10,32,128]{3,2,1,0:T(8,128)(2,1)S(1)}, bf16[1,10,32,128]{3,2,1,0:T(8,128)(2,1)S(1)}, u32[]{:S(2)}, u32[]{:S(2)}) collective-permute-start(bf16[1,10,32,128]{3,2,1,0:T(8,128)(2,1)S(1)} %pad_maximum_fusion.5), channel_id=1, source_target_pairs={{16,0},{32,16},{48,32},{64,48},{80,64},{96,80},{112,96},{128,112},... | collective-permute-start | bytes 245768 | tf_op jit(solution)/shard_map/ppermute | solution.py:109
  19.3 2.9 %collective-permute-start.13 = (bf16[1,10,32,128]{3,2,1,0:T(8,128)(2,1)S(1)}, bf16[1,10,32,128]{3,2,1,0:T(8,128)(2,1)S(1)}, u32[]{:S(2)}, u32[]{:S(2)}) collective-permute-start(bf16[1,10,32,128]{3,2,1,0:T(8,128)(2,1)S(1)} %pad_maximum_fusion.6), channel_id=1, source_target_pairs={{0,16},{16,32},{32,48},{48,64},{64,80},{80,96},{96,112},{112,128},... | collective-permute-start | bytes 245768 | tf_op jit(solution)/shard_map/ppermute | solution.py:108
  23.7 1.5 %bitcast_dynamic-update-slice_fusion.2 = (bf16[4,8,5,32,128]{4,3,2,1,0:T(8,128)(2,1)}, bf16[4,8,32,128]{3,2,1,0:T(8,128)(2,1)S(1)}, bf16[4,8,32,128]{3,2,1,0:T(8...) fusion(bf16[4,8,5,32,128]{4,3,2,1,0:T(8,128)(2,1)} %bitcast_dynamic-update-slice_fusion.4, ...), kind=kLoop, calls=%fused_computation.52 | loop fusion | flops 5242880 | bytes 2130176
  29.5 3.4 %fusion.30 = f32[4,8,32,128,1]{3,2,4,1,0:T(8,128)S(1)} fusion(bf16[4,8,5,32,128]{4,3,2,1,0:T(8,128)(2,1)} %bitcast_dynamic-update-slice_fusion.3, bf16[4,8,5,128,128]{4,3,2,1,0:T(8,128)(2,1)S(1)} %copy-done.4), kind=kOutput, calls=%fused_computation.122 | convolution fusion | flops 167772160 | bytes 7077888 | tf_op jit(solution)/shard_map/rakij,rakvj->ravi/dot_general | solution.py:122
  33.7 2.9 %convolution_bitcast_fusion.5 = f32[192,32]{0,1:T(8,128)S(1)} fusion(f32[4,8,192,128]{3,2,1,0:T(8,128)S(1)} %copy-done, f32[4,8,32,128,1]{3,2,4,1,0:T(8,128)S(1)} %fusion.30), kind=kOutput, calls=%fused_computation.26 | convolution fusion | flops 301989888 | bytes 3694592 | tf_op jit(solution)/shard_map/epi,evi->pv/dot_general | solution.py:83
  36.9 3.1 %collective-permute-start.14 = (f32[112,128]{1,0:T(8,128)S(1)}, f32[112,128]{1,0:T(8,128)S(1)}, u32[]{:S(2)}, u32[]{:S(2)}) collective-permute-start(f32[112,128]{1,0:T(8,128)S(1)} %pad_maximum_fusion.8), channel_id=1, source_target_pairs={{0,64},{16,80},{32,96},{48,112},{64,0},{80,16},{96,32},{112,48},{1... | collective-permute-start | bytes 172040 | tf_op jit(solution)/shard_map/ppermute | solution.py:24
  40.0 1.6 %collective-permute-done.14 = f32[112,128]{1,0:T(8,128)S(1)} collective-permute-done((f32[112,128]{1,0:T(8,128)S(1)}, f32[112,128]{1,0:T(8,128)S(1)}, u32[]{:S(2)}, u32[]{:S(2)}) %collective-permute-start.14) | collective-permute-done | bytes 57376 | tf_op jit(solution)/shard_map/ppermute | solution.py:24
  41.5 6.3 %collective-permute-start.15 = (f32[112,128]{1,0:T(8,128)S(1)}, f32[112,128]{1,0:T(8,128)S(1)}, u32[]{:S(2)}, u32[]{:S(2)}) collective-permute-start(f32[112,128]{1,0:T(8,128)S(1)} %fusion.19), channel_id=1, source_target_pairs={{0,128},{16,144},{32,160},{48,176},{64,192},{80,208},{96,224},{112... | collective-permute-start | bytes 172040 | tf_op jit(solution)/shard_map/ppermute | solution.py:24
  47.8 1.7 %collective-permute-done.15 = f32[112,128]{1,0:T(8,128)S(1)} collective-permute-done((f32[112,128]{1,0:T(8,128)S(1)}, f32[112,128]{1,0:T(8,128)S(1)}, u32[]{:S(2)}, u32[]{:S(2)}) %collective-permute-start.15) | collective-permute-done | bytes 57376 | tf_op jit(solution)/shard_map/ppermute | solution.py:24
  49.6 3.3 %collective-permute-done.16 = f32[112,128]{1,0:T(8,128)S(1)} collective-permute-done((f32[112,128]{1,0:T(8,128)S(1)}, f32[112,128]{1,0:T(8,128)S(1)}, u32[]{:S(2)}, u32[]{:S(2)}) %collective-permute-start.16) | collective-permute-done | bytes 57376 | tf_op jit(solution)/shard_map/ppermute | solution.py:24
  54.1 3.4 %collective-permute-done.17 = f32[112,128]{1,0:T(8,128)S(1)} collective-permute-done((f32[112,128]{1,0:T(8,128)S(1)}, f32[112,128]{1,0:T(8,128)S(1)}, u32[]{:S(2)}, u32[]{:S(2)}) %collective-permute-start.17) | collective-permute-done | bytes 57376 | tf_op jit(solution)/shard_map/ppermute | solution.py:24
  57.6 3.0 %collective-permute-done.18 = f32[112,128]{1,0:T(8,128)S(1)} collective-permute-done((f32[112,128]{1,0:T(8,128)S(1)}, f32[112,128]{1,0:T(8,128)S(1)}, u32[]{:S(2)}, u32[]{:S(2)}) %collective-permute-start.18) | collective-permute-done | bytes 57376 | tf_op jit(solution)/shard_map/ppermute | solution.py:24
  60.7 1.6 %collective-permute-start.19 = (f32[112,128]{1,0:T(8,128)S(1)}, f32[112,128]{1,0:T(8,128)S(1)}, u32[]{:S(2)}, u32[]{:S(2)}) collective-permute-start(f32[112,128]{1,0:T(8,128)S(1)} %add.84), channel_id=1, source_target_pairs={{0,8},{1,9},{2,10},{3,11},{4,12},{5,13},{6,14},{7,15},{8,0},{9,1},... | collective-permute-start | bytes 172040 | tf_op jit(solution)/shard_map/ppermute | solution.py:24
  62.3 3.0 %collective-permute-done.19 = f32[112,128]{1,0:T(8,128)S(1)} collective-permute-done((f32[112,128]{1,0:T(8,128)S(1)}, f32[112,128]{1,0:T(8,128)S(1)}, u32[]{:S(2)}, u32[]{:S(2)}) %collective-permute-start.19) | collective-permute-done | bytes 57376 | tf_op jit(solution)/shard_map/ppermute | solution.py:24
  65.3 2.6 %collective-permute-start.20 = (f32[112,128]{1,0:T(8,128)S(1)}, f32[112,128]{1,0:T(8,128)S(1)}, u32[]{:S(2)}, u32[]{:S(2)}) collective-permute-start(f32[112,128]{1,0:T(8,128)S(1)} %add.85), channel_id=1, source_target_pairs={{0,32},{16,48},{32,0},{48,16},{64,96},{80,112},{96,64},{112,80},{1... | collective-permute-start | bytes 172040 | tf_op jit(solution)/shard_map/ppermute | solution.py:30
  67.9 1.6 %collective-permute-done.20 = f32[112,128]{1,0:T(8,128)S(1)} collective-permute-done((f32[112,128]{1,0:T(8,128)S(1)}, f32[112,128]{1,0:T(8,128)S(1)}, u32[]{:S(2)}, u32[]{:S(2)}) %collective-permute-start.20) | collective-permute-done | bytes 57376 | tf_op jit(solution)/shard_map/ppermute | solution.py:30
  69.5 9.2 %collective-permute-start.21 = (f32[168,128]{1,0:T(8,128)S(1)}, f32[168,128]{1,0:T(8,128)S(1)}, u32[]{:S(2)}, u32[]{:S(2)}) collective-permute-start(f32[168,128]{1,0:T(8,128)S(1)} %pad_maximum_fusion.4), channel_id=1, source_target_pairs={{0,16},{16,0},{32,48},{48,32},{64,80},{80,64},{96,112},{112,96},{1... | collective-permute-start | bytes 258056 | tf_op jit(solution)/shard_map/ppermute | solution.py:30
  87.0 11.2 %conditional.1 = (f32[32,32]{1,0:T(8,128)S(1)}, f32[4,8,32,128]{3,2,1,0:T(8,128)}) conditional(s32[]{:T(128)} %convert_element_type.8, (f32[192,32]{0,1:T(8,128)}, f32[32,192,128]{2,1,0:T(8,128)S(1)}, f32[32,32,128]{2,1,0:T(8,128)}, f32[32,32]{0,1:T(8,128)S(1)}) %tuple.79, (f32[32,32]{0,1:T(8,128)S(1)}, f32[32,32]{0,1:T(8,128)S(1)}, ...), branch_computations={%region_3.8_spmd, %region_6.9_spmd} | conditional | flops 403193888 | bytes 8155758 | solution.py:175
  87.1 2.9 %cholesky.56 = f32[32,32]{1,0:T(8,128)S(1)} custom-call(f32[32,32]{1,0:T(8,128)S(1)} %copy.33), custom_call_target="Cholesky" | custom-call | tf_op jit(solution)/shard_map/cond/branch_1_fun/jit(cholesky)/cholesky | solution.py:155
  91.3 2.4 %custom-call.7 = f32[1,32,32]{1,2,0:T(8,128)S(1)} custom-call(f32[1,32,32]{2,1,0:T(8,128)S(1)} %get-tuple-element.63), custom_call_target="InvertDiagBlocksLowerTriangular" | custom-call | tf_op jit(solution)/shard_map/cond/branch_1_fun/triangular_solve/custom-call.0 | solution.py:156
  96.4 1.9 %convolution_subtract_fusion = f32[32,32,128]{2,0,1:T(8,128)} fusion(f32[32,32,128]{2,0,1:T(8,128)S(1)} %fusion.3, f32[32,192,1]{1,0,2:T(8,128)S(1)} %convolution_bitcast_fusion.3, f32[32,192,128]{2,1,0:T(8,128)S(1)} %get-tuple-element.29), kind=kOutput, calls=%fused_computation.13 | convolution fusion | flops 151126016 | bytes 4218880 | tf_op jit(solution)/shard_map/cond/branch_1_fun/epi,pw->ewi/dot_general | solution.py:164
  (87 shorter events, 23.2 us)
Async XLA Ops:
  1.4 13.4 %collective-permute-start.10 = (bf16[4,1,32,128]{3,2,1,0:T(8,128)(2,1)S(1)}, bf16[4,1,32,128]{3,2,1,0:T(8,128)(2,1)S(1)}, u32[]{:S(2)}, u32[]{:S(2)}) collective-permute-start(bf16[4,1,32,128]{3,2,1,0:T(8,128)(2,1)S(1)} %get-tuple-element.72), channel_id=1, source_target_pairs={{1,0},{2,1},{3,2},{4,3},{5,4},{6,5},{7,6},{8,7},{9,8},{10,9},{11,1... | collective-permute-start | bytes 98312 | tf_op jit(solution)/shard_map/ppermute | solution.py:101
  7.2 7.7 %collective-permute-start.9 = (bf16[4,1,32,128]{3,2,1,0:T(8,128)(2,1)S(1)}, bf16[4,1,32,128]{3,2,1,0:T(8,128)(2,1)S(1)}, u32[]{:S(2)}, u32[]{:S(2)}) collective-permute-start(bf16[4,1,32,128]{3,2,1,0:T(8,128)(2,1)S(1)} %get-tuple-element.73), channel_id=1, source_target_pairs={{0,1},{1,2},{2,3},{3,4},{4,5},{5,6},{6,7},{7,8},{8,9},{9,10},{10,1... | collective-permute-start | bytes 98312 | tf_op jit(solution)/shard_map/ppermute | solution.py:100
  7.2 6.7 %copy-start.2 = (bf16[4,8,32,128]{3,2,1,0:T(8,128)(2,1)S(1)}, bf16[4,8,32,128]{3,2,1,0:T(8,128)(2,1)}, u32[]{:S(2)}) copy-start(bf16[4,8,32,128]{3,2,1,0:T(8,128)(2,1)} %param.10) | copy-start | bytes 786436
  7.2 7.5 %copy-start.5 = (s32[4,8,5]{1,0,2:T(4,128)S(1)}, s32[4,8,5]{1,0,2:T(4,128)}, u32[]{:S(2)}) copy-start(s32[4,8,5]{1,0,2:T(4,128)} %param.12) | copy-start | bytes 1924
  12.9 1.9 %collective-permute-start.8 = (f32[112,128]{1,0:T(8,128)S(1)}, f32[112,128]{1,0:T(8,128)S(1)}, u32[]{:S(2)}, u32[]{:S(2)}) collective-permute-start(f32[112,128]{1,0:T(8,128)S(1)} %slice_select_fusion), channel_id=1, source_target_pairs={{0,16},{16,0},{32,48},{48,32},{64,80},{80,64},{96,112},{112,96},{1... | collective-permute-start | bytes 172040 | tf_op jit(solution)/shard_map/ppermute | solution.py:30
  14.9 7.4 %collective-permute-start.11 = (f32[56,128]{1,0:T(8,128)S(1)}, f32[56,128]{1,0:T(8,128)S(1)}, u32[]{:S(2)}, u32[]{:S(2)}) collective-permute-start(f32[56,128]{1,0:T(8,128)S(1)} %slice_select_fusion.1), channel_id=1, source_target_pairs={{0,32},{16,48},{32,0},{48,16},{64,96},{80,112},{96,64},{112,80},{1... | collective-permute-start | bytes 86024 | tf_op jit(solution)/shard_map/ppermute | solution.py:30
  16.6 5.8 %collective-permute-start.12 = (bf16[1,10,32,128]{3,2,1,0:T(8,128)(2,1)S(1)}, bf16[1,10,32,128]{3,2,1,0:T(8,128)(2,1)S(1)}, u32[]{:S(2)}, u32[]{:S(2)}) collective-permute-start(bf16[1,10,32,128]{3,2,1,0:T(8,128)(2,1)S(1)} %pad_maximum_fusion.5), channel_id=1, source_target_pairs={{16,0},{32,16},{48,32},{64,48},{80,64},{96,80},{112,96},{128,112},... | collective-permute-start | bytes 245768 | tf_op jit(solution)/shard_map/ppermute | solution.py:109
  19.3 4.4 %collective-permute-start.13 = (bf16[1,10,32,128]{3,2,1,0:T(8,128)(2,1)S(1)}, bf16[1,10,32,128]{3,2,1,0:T(8,128)(2,1)S(1)}, u32[]{:S(2)}, u32[]{:S(2)}) collective-permute-start(bf16[1,10,32,128]{3,2,1,0:T(8,128)(2,1)S(1)} %pad_maximum_fusion.6), channel_id=1, source_target_pairs={{0,16},{16,32},{32,48},{48,64},{64,80},{80,96},{96,112},{112,128},... | collective-permute-start | bytes 245768 | tf_op jit(solution)/shard_map/ppermute | solution.py:108
  25.2 4.2 %copy-start.4 = (bf16[4,8,5,128,128]{4,3,2,1,0:T(8,128)(2,1)S(1)}, bf16[4,8,5,128,128]{4,3,2,1,0:T(8,128)(2,1)}, u32[]{:S(2)}) copy-start(bf16[4,8,5,128,128]{4,3,2,1,0:T(8,128)(2,1)} %param.9) | copy-start | bytes 15728644
  29.5 4.2 %copy-start = (f32[4,8,192,128]{3,2,1,0:T(8,128)S(1)}, f32[4,8,192,128]{3,2,1,0:T(8,128)}, u32[]{:S(2)}) copy-start(f32[4,8,192,128]{3,2,1,0:T(8,128)} %param.11) | copy-start | bytes 9437188
  32.8 0.8 copy-start.1
  36.9 4.6 %collective-permute-start.14 = (f32[112,128]{1,0:T(8,128)S(1)}, f32[112,128]{1,0:T(8,128)S(1)}, u32[]{:S(2)}, u32[]{:S(2)}) collective-permute-start(f32[112,128]{1,0:T(8,128)S(1)} %pad_maximum_fusion.8), channel_id=1, source_target_pairs={{0,64},{16,80},{32,96},{48,112},{64,0},{80,16},{96,32},{112,48},{1... | collective-permute-start | bytes 172040 | tf_op jit(solution)/shard_map/ppermute | solution.py:24
  41.5 7.9 %collective-permute-start.15 = (f32[112,128]{1,0:T(8,128)S(1)}, f32[112,128]{1,0:T(8,128)S(1)}, u32[]{:S(2)}, u32[]{:S(2)}) collective-permute-start(f32[112,128]{1,0:T(8,128)S(1)} %fusion.19), channel_id=1, source_target_pairs={{0,128},{16,144},{32,160},{48,176},{64,192},{80,208},{96,224},{112... | collective-permute-start | bytes 172040 | tf_op jit(solution)/shard_map/ppermute | solution.py:24
  49.5 3.4 %collective-permute-start.16 = (f32[112,128]{1,0:T(8,128)S(1)}, f32[112,128]{1,0:T(8,128)S(1)}, u32[]{:S(2)}, u32[]{:S(2)}) collective-permute-start(f32[112,128]{1,0:T(8,128)S(1)} %add.81), channel_id=1, source_target_pairs={{0,1},{1,0},{2,3},{3,2},{4,5},{5,4},{6,7},{7,6},{8,9},{9,8},{10,11... | collective-permute-start | bytes 172040 | tf_op jit(solution)/shard_map/ppermute | solution.py:24
  52.9 4.6 %collective-permute-start.17 = (f32[112,128]{1,0:T(8,128)S(1)}, f32[112,128]{1,0:T(8,128)S(1)}, u32[]{:S(2)}, u32[]{:S(2)}) collective-permute-start(f32[112,128]{1,0:T(8,128)S(1)} %add.82), channel_id=1, source_target_pairs={{0,2},{1,3},{2,0},{3,1},{4,6},{5,7},{6,4},{7,5},{8,10},{9,11},{10,... | collective-permute-start | bytes 172040 | tf_op jit(solution)/shard_map/ppermute | solution.py:24
  57.5 3.1 %collective-permute-start.18 = (f32[112,128]{1,0:T(8,128)S(1)}, f32[112,128]{1,0:T(8,128)S(1)}, u32[]{:S(2)}, u32[]{:S(2)}) collective-permute-start(f32[112,128]{1,0:T(8,128)S(1)} %add.83), channel_id=1, source_target_pairs={{0,4},{1,5},{2,6},{3,7},{4,0},{5,1},{6,2},{7,3},{8,12},{9,13},{10,... | collective-permute-start | bytes 172040 | tf_op jit(solution)/shard_map/ppermute | solution.py:24
  60.7 4.6 %collective-permute-start.19 = (f32[112,128]{1,0:T(8,128)S(1)}, f32[112,128]{1,0:T(8,128)S(1)}, u32[]{:S(2)}, u32[]{:S(2)}) collective-permute-start(f32[112,128]{1,0:T(8,128)S(1)} %add.84), channel_id=1, source_target_pairs={{0,8},{1,9},{2,10},{3,11},{4,12},{5,13},{6,14},{7,15},{8,0},{9,1},... | collective-permute-start | bytes 172040 | tf_op jit(solution)/shard_map/ppermute | solution.py:24
  65.3 4.2 %collective-permute-start.20 = (f32[112,128]{1,0:T(8,128)S(1)}, f32[112,128]{1,0:T(8,128)S(1)}, u32[]{:S(2)}, u32[]{:S(2)}) collective-permute-start(f32[112,128]{1,0:T(8,128)S(1)} %add.85), channel_id=1, source_target_pairs={{0,32},{16,48},{32,0},{48,16},{64,96},{80,112},{96,64},{112,80},{1... | collective-permute-start | bytes 172040 | tf_op jit(solution)/shard_map/ppermute | solution.py:30
  69.5 10.1 %collective-permute-start.21 = (f32[168,128]{1,0:T(8,128)S(1)}, f32[168,128]{1,0:T(8,128)S(1)}, u32[]{:S(2)}, u32[]{:S(2)}) collective-permute-start(f32[168,128]{1,0:T(8,128)S(1)} %pad_maximum_fusion.4), channel_id=1, source_target_pairs={{0,16},{16,0},{32,48},{48,32},{64,80},{80,64},{96,112},{112,96},{1... | collective-permute-start | bytes 258056 | tf_op jit(solution)/shard_map/ppermute | solution.py:30
